TPU v7x, 32 devices: a whole 2x2x4 slice. The times are simulated.
32 devices in a mesh: seq: 16 (over z, x, core), head: 2 (over y).
Axes of the slice: x: 2, y: 2, z: 4, core: 2. Of those that a mesh axis runs over, the one named last changes fastest.
Arguments:
- step_tokens: bfloat16 [2, 12, 8, 2560], P(None, None, None, 'head'), may hold values from -6 to 6
- parents: int32 [2, 12, 8], replicated, may hold values from 0 to 7
- tail_cache: bfloat16 [12, 8, 64, 2048], P(None, 'head', 'seq'), may hold values from -192 to 192
- tail_len: int32 [12], replicated, may hold values from 0 to 62, as said below
- cache: bfloat16 [8, 2048, 2048], P(None, ('seq', 'head')), may hold values from -192 to 192
- cache_len: int32 [8], replicated, may hold values from 256 to 2048, as said below
- prompt_states: bfloat16 [4, 128, 2560], P(None, 'seq', 'head'), may hold values from -6 to 6
- prompt_len: int32 [4], replicated, may hold values from 32 to 128, as said below
- in_gain: float32 [2560], P('head'), may hold values from 0.5 to 1.5
- w_query: bfloat16 [2560, 2048], P('head', 'seq'), may hold values from -0.125 to 0.125
- w_keyval: bfloat16 [2560, 2048], P('head', 'seq'), may hold values from -0.125 to 0.125
- q_gain: float32 [256], replicated, may hold values from 0.6 to 32
- k_gain: float32 [256], replicated, may hold values from 0.6 to 32
- w_out: bfloat16 [2048, 2560], P('seq', 'head'), may hold values from -0.125 to 0.125
- post_gain: float32 [2560], P('head'), may hold values from 0.5 to 1.5
- ffn_gain: float32 [2560], P('head'), may hold values from 0.5 to 1.5
- w_gate: bfloat16 [2560, 10240], P('head', 'seq'), may hold values from -0.125 to 0.125
- w_up: bfloat16 [2560, 10240], P('head', 'seq'), may hold values from -0.125 to 0.125
- w_down: bfloat16 [10240, 2560], P('seq', 'head'), may hold values from -0.0625 to 0.0625
- final_gain: float32 [2560], P('head'), may hold values from 0.5 to 1.5
Outputs:
- decoded: bfloat16 [2, 12, 8, 2560], P(None, None, None, 'head')
Inputs may be any that keep to these rules, and one draw needn't show every extreme that they name: `tail_len`: the first 4 groups have 0; the largest entry is exactly 62. `cache_len`: the largest entry is exactly 2048. `prompt_len`: the largest entry is exactly 128.
All inputs are finite; a program needn't handle non-finite values.
Results may differ from a plain program's by a relative error of at most 0.0055.
The roundings to bfloat16 on the way count: a program that leaves them out, or rounds other values in their place, can miss the bound.
Values may be sent and summed in bfloat16 or wider, within the bound.
No kernel may reach another device: no remote copies, remote signals or barrier semaphores. Data moves between devices by JAX's collectives and lax.ppermute only.
A program may use at most 128 MiB of HBM per device.

v0:
```python
import jax
import jax.numpy as jnp
from jax import lax
from jax.sharding import PartitionSpec as P

D = 2560
QH = 8
KVH = 4
HD = 256
QD = 2048


EPS = 1e-06
NEG = -1e30
QSCALE = 0.0625


def norm_heads(values, gain, scale):
    shaped = values.reshape(values.shape[:-1] + (-1, gain.shape[0]))
    shaped = shaped * lax.rsqrt(jnp.mean(shaped * shaped, -1, keepdims=True) + EPS) * gain * scale
    return shaped.reshape(values.shape)


def finish_keys(pairs, k_gain):
    half = pairs.shape[-1] // 2
    keys = norm_heads(pairs[..., :half], k_gain, 1.0)
    return jnp.concatenate([keys, pairs[..., half:]], -1).astype(jnp.bfloat16)


def split_pairs(pairs):
    half = pairs.shape[-1] // 2
    keys = pairs[..., :half].reshape(pairs.shape[:-1] + (KVH, HD))
    values = pairs[..., half:].reshape(pairs.shape[:-1] + (KVH, HD))
    return (keys, values)


def exchange_sum(parts, axes):
    return jnp.sum(lax.all_to_all(parts, axes, 0, 0, tiled=True), 0)


def exchange_max(value, axes, count):
    spread = jnp.broadcast_to(value[None], (count,) + value.shape)
    return jnp.max(lax.all_to_all(spread, axes, 0, 0, tiled=True), 0)


def exchange_gather(piece, axes, count):
    spread = jnp.broadcast_to(piece[None], (count,) + piece.shape)
    return lax.all_to_all(spread, axes, 0, 0, tiled=True)


def project_tokens(tokens, in_gain, w_query, w_keyval, q_gain, k_gain):
    flat = tokens.reshape(-1, tokens.shape[-1]).astype(jnp.float32)
    scaled = (flat * in_gain).astype(jnp.bfloat16)
    q_part = jnp.dot(scaled, w_query, preferred_element_type=jnp.float32)
    kv_part = jnp.dot(scaled, w_keyval, preferred_element_type=jnp.float32)
    squares = jnp.sum(flat * flat, -1)
    n_head = lax.axis_size("head")
    n_seq = lax.axis_size("seq")
    rows = flat.shape[0]
    half = rows // n_head
    block = q_part.shape[1]
    packed = jnp.concatenate([q_part, kv_part, jnp.pad(squares[:, None], ((0, 0), (0, 127)))], 1)
    packed = exchange_sum(packed.reshape(n_head, half, -1), "head")
    factor = lax.rsqrt(packed[:, 2 * block] / D + EPS)[:, None]
    q_raw = (packed[:, :block] * factor).astype(jnp.bfloat16)
    kv_raw = (packed[:, block : 2 * block] * factor).astype(jnp.bfloat16)
    both = exchange_gather(
        jnp.concatenate([q_raw, kv_raw], 1), ("seq", "head"), n_seq * n_head
    ).reshape(n_seq, n_head, half, 2 * block)
    both = jnp.transpose(both, (1, 2, 0, 3)).reshape(rows, n_seq, 2 * block)
    q_raw = both[:, :, :block].reshape(rows, -1)
    kv_raw = both[:, :, block:].reshape(rows, -1)
    queries = norm_heads(q_raw.astype(jnp.float32), q_gain, QSCALE).astype(jnp.bfloat16)
    fresh = finish_keys(kv_raw.astype(jnp.float32), k_gain)
    return (queries, fresh)


def shards(
    step_tokens,
    parents,
    tail_cache,
    tail_len,
    cache,
    cache_len,
    prompt_states,
    prompt_len,
    in_gain,
    w_query,
    w_keyval,
    q_gain,
    k_gain,
    w_out,
    post_gain,
    ffn_gain,
    w_gate,
    w_up,
    w_down,
    final_gain,
):
    f32 = jnp.float32
    bf16 = jnp.bfloat16
    n_head = lax.axis_size("head")
    n_seq = lax.axis_size("seq")
    seq_at = lax.axis_index("seq")
    head_at = lax.axis_index("head")
    flat_at = seq_at * n_head + head_at
    steps, groups, beams, width = step_tokens.shape
    pre = prompt_states.shape[0]
    repeat = QH // KVH
    rows = jnp.transpose(prompt_states, (1, 0, 2)).astype(f32)
    prompt_scaled = (rows * in_gain).astype(bf16).reshape(-1, width)
    prompt_squares = jnp.sum(rows * rows, -1).reshape(-1)
    prompt_terms = jnp.dot(
        prompt_scaled,
        lax.all_gather(w_keyval, "seq", axis=1, tiled=True),
        preferred_element_type=f32,
    )
    prompt_sum, prompt_sq = (
        lax.psum_scatter(prompt_terms, "head", scatter_dimension=0, tiled=True),
        lax.psum_scatter(prompt_squares, "head", scatter_dimension=0, tiled=True),
    )
    prompt_pairs = finish_keys(prompt_sum * lax.rsqrt(prompt_sq / D + EPS)[:, None], k_gain)
    prompt_seg = prompt_pairs.shape[0] // pre
    prompt_pairs = jnp.transpose(prompt_pairs.reshape(prompt_seg, pre, -1), (1, 0, 2))
    prompt_keys, prompt_values = split_pairs(prompt_pairs)
    prompt_ok = (flat_at * prompt_seg + jnp.arange(prompt_seg))[None, :] < prompt_len[:, None]
    cache_seg = cache.shape[1]
    cache_keys, cache_values = split_pairs(cache)
    cache_ok = (flat_at * cache_seg + jnp.arange(cache_seg))[None, :] < cache_len[:, None]
    tail_seg = tail_cache.shape[2]
    local_beams = tail_cache.shape[1]
    offset = (seq_at * tail_seg + jnp.arange(tail_seg))[None, :] - tail_len[:, None]
    all_beams = jnp.arange(beams)
    every_query, every_fresh = project_tokens(
        step_tokens, in_gain, w_query, w_keyval, q_gain, k_gain
    )
    every_query = every_query.reshape(steps, groups, beams, -1)
    every_fresh = every_fresh.reshape(steps, groups, beams, -1)
    everyone = lax.all_gather(tail_cache, "head", axis=1, tiled=True)
    local_ids = head_at * local_beams + jnp.arange(local_beams)
    n_dev = n_seq * n_head
    owner = jnp.broadcast_to(all_beams[None, :, None], (groups, beams, tail_seg))
    source = jnp.broadcast_to(all_beams[None, :], (groups, beams))
    ancestors = []
    shaped_all, scores_all, tails_all = [], [], []
    for step in range(steps):
        link = parents[step]
        source = jnp.take_along_axis(source, link, axis=1)
        ancestors = [jnp.take_along_axis(a, link, axis=1) for a in ancestors]
        ancestors.append(jnp.broadcast_to(all_beams[None, :], (groups, beams)))
        picks = lax.dynamic_slice_in_dim(source, head_at * local_beams, local_beams, 1)
        tail_state = jnp.take_along_axis(everyone, picks[:, :, None, None], axis=1)
        for back, anc in enumerate(ancestors):
            mine = lax.dynamic_slice_in_dim(anc, head_at * local_beams, local_beams, 1)
            written = jnp.take_along_axis(every_fresh[back], mine[:, :, None], axis=1)
            tail_state = jnp.where(
                (offset == back)[:, None, :, None], written[:, :, None, :], tail_state
            )
        tail_ok = (offset <= step)[:, None, None, :] & (
            owner[:, :, None, :] == local_ids[None, None, :, None]
        )
        shaped = every_query[step].reshape(groups, beams, KVH, repeat, HD)
        tail_keys, tail_values = split_pairs(tail_state)
        pre_scores = jnp.einsum(
            "gbkrd,gtkd->gbkrt", shaped[:pre], prompt_keys, preferred_element_type=f32
        )
        dec_scores = jnp.einsum(
            "gbkrd,gtkd->gbkrt", shaped[pre:], cache_keys, preferred_element_type=f32
        )
        tail_scores = jnp.einsum(
            "gbkrd,gctkd->gbkrct", shaped, tail_keys, preferred_element_type=f32
        )
        pre_scores = jnp.where(prompt_ok[:, None, None, None, :], pre_scores, NEG)
        dec_scores = jnp.where(cache_ok[:, None, None, None, :], dec_scores, NEG)
        tail_scores = jnp.where(tail_ok[:, :, None, None, :, :], tail_scores, NEG)
        top = jnp.concatenate([jnp.max(pre_scores, -1), jnp.max(dec_scores, -1)], 0)
        top = jnp.maximum(top, jnp.max(tail_scores, (-2, -1)))
        scores_all.append((pre_scores, dec_scores, tail_scores))
        tails_all.append((tail_ok, tail_values))
        shaped_all.append(top)
    top_all = exchange_max(jnp.stack(shaped_all), ("seq", "head"), n_dev)
    weighted_all, total_all = [], []
    for step in range(steps):
        pre_scores, dec_scores, tail_scores = scores_all[step]
        tail_ok, tail_values = tails_all[step]
        top = top_all[step]
        pre_mask = prompt_ok[:, None, None, None, :]
        dec_mask = cache_ok[:, None, None, None, :]
        tail_mask = tail_ok[:, :, None, None, :, :]
        pre_weights = jnp.where(pre_mask, jnp.exp(pre_scores - top[:pre, ..., None]), 0.0)
        dec_weights = jnp.where(dec_mask, jnp.exp(dec_scores - top[pre:, ..., None]), 0.0)
        tail_weights = jnp.where(tail_mask, jnp.exp(tail_scores - top[..., None, None]), 0.0)
        total = jnp.concatenate([jnp.sum(pre_weights, -1), jnp.sum(dec_weights, -1)], 0)
        total = total + jnp.sum(tail_weights, (-2, -1))
        weighted = jnp.concatenate(
            [
                jnp.einsum(
                    "gbkrt,gtkd->gbkrd",
                    pre_weights.astype(bf16),
                    prompt_values,
                    preferred_element_type=f32,
                ),
                jnp.einsum(
                    "gbkrt,gtkd->gbkrd",
                    dec_weights.astype(bf16),
                    cache_values,
                    preferred_element_type=f32,
                ),
            ],
            0,
        )
        weighted = weighted + jnp.einsum(
            "gbkrct,gctkd->gbkrd",
            tail_weights.astype(bf16),
            tail_values,
            preferred_element_type=f32,
        )
        weighted_all.append(weighted.reshape(groups * beams, -1))
        total_all.append(total.reshape(groups * beams, -1))
    weighted = jnp.concatenate(weighted_all, 0)
    total = jnp.concatenate(total_all, 0)
    rows = weighted.shape[0]
    piece = QD // n_dev
    piece_head = jnp.arange(n_dev) * piece // HD
    lanes = -(-rows // 128) * 128
    packed = jnp.concatenate(
        [
            jnp.transpose(weighted.reshape(rows, n_dev, piece), (1, 0, 2)).reshape(n_dev, -1),
            jnp.pad(jnp.transpose(total[:, piece_head]), ((0, 0), (0, lanes - rows))),
        ],
        1,
    )
    packed = exchange_sum(packed, ("seq", "head"))
    share = packed[: rows * piece].reshape(rows, piece)
    own_total = packed[rows * piece : rows * piece + rows]
    attn = (share / own_total[:, None]).astype(bf16)
    attn = exchange_gather(attn, "head", n_head)
    attn = jnp.transpose(attn, (1, 0, 2)).reshape(rows, -1)
    partial_out = jnp.dot(attn, w_out, preferred_element_type=f32)
    per_dev = rows // n_seq
    out_proj = exchange_sum(partial_out.reshape(n_seq, per_dev, -1), "seq")
    out_sq = lax.psum(jnp.sum(out_proj * out_proj, -1), "head")
    x_all = step_tokens.reshape(rows, -1)
    x_f = lax.dynamic_slice_in_dim(x_all, seq_at * per_dev, per_dev, 0).astype(f32)
    state = (x_f + out_proj * lax.rsqrt(out_sq / D + EPS)[:, None] * post_gain).astype(bf16)
    state_all = exchange_gather(state, "seq", n_seq).reshape(rows, -1)
    state_f = state_all.astype(f32)
    scaled_two = (state_f * ffn_gain).astype(bf16)
    gate_part = jnp.dot(scaled_two, w_gate, preferred_element_type=f32)
    up_part = jnp.dot(scaled_two, w_up, preferred_element_type=f32)
    hidden = gate_part.shape[1]
    head_rows = rows // n_head
    packed = jnp.concatenate(
        [gate_part, up_part, jnp.pad(jnp.sum(state_f * state_f, -1)[:, None], ((0, 0), (0, 127)))],
        1,
    )
    packed = exchange_sum(packed.reshape(n_head, head_rows, -1), "head")
    norm_s = lax.rsqrt(packed[:, 2 * hidden] / D + EPS)[:, None]
    inner = (
        jax.nn.gelu(packed[:, :hidden] * norm_s, approximate=True)
        * (packed[:, hidden : 2 * hidden] * norm_s)
    ).astype(bf16)
    inner = exchange_gather(inner, "head", n_head).reshape(rows, hidden)
    ffn_out = exchange_sum(
        jnp.dot(inner, w_down, preferred_element_type=f32).reshape(n_seq, per_dev, -1), "seq"
    )
    ffn_sq = lax.psum(jnp.sum(ffn_out * ffn_out, -1), "head")
    result = (
        state.astype(f32) + ffn_out * lax.rsqrt(ffn_sq / D + EPS)[:, None] * final_gain
    ).astype(bf16)
    result = exchange_gather(result, "seq", n_seq)
    return result.reshape(steps, groups, beams, -1)


def solution(mesh):
    return jax.shard_map(
        shards,
        mesh=mesh,
        in_specs=(
            P(None, None, None, "head"),
            P(),
            P(None, "head", "seq", None),
            P(),
            P(None, ("seq", "head"), None),
            P(),
            P(None, "seq", "head"),
            P(),
            P("head"),
            P("head", "seq"),
            P("head", "seq"),
            P(),
            P(),
            P("seq", "head"),
            P("head"),
            P("head"),
            P("head", "seq"),
            P("head", "seq"),
            P("seq", "head"),
            P("head"),
        ),
        out_specs=P(None, None, None, "head"),
        check_vma=False,
    )
```

profile of v0, /device:TPU:0, one launch (start us, length us, event | category | flops | bytes accessed | tf_op | source)
XLA Modules:
  0.0 422.5 jit_solution(17496565796316060511)
XLA Ops:
  10.7 4.2 %all-to-all-start = ((f32[2,96,384]{2,1,0:T(8,128)}), f32[2,96,384]{2,1,0:T(8,128)S(1)}, u32[]{:S(2)}, u32[]{:S(2)}) async-start(f32[2,96,384]{2,1,0:T(8,128)} %bitcast.10), calls=%async_computation.1 | async-start | bytes 589824 | tf_op jit(solution)/shard_map/all_to_all | solution.py:38
  19.2 2.0 all-to-all-done
  22.9 5.2 %all-to-all-start.1 = ((bf16[32,96,256]{2,1,0:T(8,128)(2,1)}), bf16[32,96,256]{2,1,0:T(8,128)(2,1)}, u32[]{:S(2)}, u32[]{:S(2)}) async-start(bf16[32,96,256]{2,1,0:T(8,128)(2,1)} %broadcast_in_dim.258), calls=%async_computation.2 | async-start | bytes 3145728 | tf_op jit(solution)/shard_map/all_to_all | solution.py:48
  32.9 3.1 fusion.99
  36.0 1.9 reshape.536
  39.2 5.6 %all-reduce.3 = f32[32]{0:T(128)S(1)} all-reduce(f32[32]{0:T(128)S(1)} %reshape.530), channel_id=3, replica_groups=mesh['seq'=16,'head'=2] {'head'}, use_global_device_ids=true, to_apply=%region_2.0.clone | all-reduce | flops 32 | bytes 256
  47.4 4.3 %all-gather.5.cloned.1.call-done = bf16[12,8,4,2048]{3,2,1,0:T(4,128)(2,1)} async-done(((bf16[12,4,4,2048]{3,2,1,0:T(4,128)(2,1)}), bf16[12,8,4,2048]{3,2,1,0:T(4,128)(2,1)}) %all-gather.5.cloned.1.call-update) | async-done | bytes 1572880 | tf_op jit(solution)/shard_map/all_gather | solution.py:139
  51.7 3.9 gather_fusion.8
  55.6 3.9 gather_fusion.3
  59.4 6.2 %all-to-all-done.1 = bf16[32,96,256]{2,1,0:T(8,128)(2,1)} async-done(((bf16[32,96,256]{2,1,0:T(8,128)(2,1)}), bf16[32,96,256]{2,1,0:T(8,128)(2,1)}, u32[]{:S(2)}, u32[]{:S(2)}) %all-to-all-start.1) | async-done | bytes 1572896 | tf_op jit(solution)/shard_map/all_to_all | solution.py:48
  65.6 1.5 slice_bitcast_fusion
  72.7 2.4 mul.304
  75.1 2.1 reduce_sum.188
  79.4 2.3 gather_fusion.4
  81.8 1.7 reshape.649
  83.5 2.3 gather_fusion.1
  85.8 2.3 gather_fusion.6
  88.2 1.8 reshape.658
  89.9 1.7 reshape.635
  94.1 2.4 select_select_fusion.1
  97.9 1.9 reshape.537
  101.1 1.9 reshape.538
  107.7 1.9 fusion.34
  109.6 2.7 copy.462
  112.3 3.0 fusion.32
  115.3 2.7 copy.478
  118.1 1.7 fusion.20
  119.9 1.7 fusion.106
  121.6 1.7 fusion.108
  123.4 4.3 %fusion.110 = f32[32,2048]{1,0:T(8,128)} fusion(bf16[32,1280]{1,0:T(8,128)(2,1)S(1)} %copy-done.19, bf16[1280,2048]{1,0:T(8,128)(2,1)} %all-gather.3.cloned.1.call-done), kind=kOutput, calls=%fused_computation.242 | convolution fusion | flops 167772160 | bytes 5586944 | tf_op jit(solution)/shard_map/dot_general | solution.py:113
  128.8 9.8 %reduce-scatter.2.cloned.1.call-done = f32[16,2048]{1,0:T(8,128)} async-done(((f32[32,2048]{1,0:T(8,128)}), f32[16,2048]{1,0:T(8,128)}) %reduce-scatter.2.cloned.1.call-update) | async-done | bytes 131088 | tf_op jit(solution)/shard_map/reduce_scatter | solution.py:119
  142.5 1.6 broadcast_bitcast_fusion.2
  144.1 4.2 %reshape.690 = f32[32,1,1536]{2,1,0:T(1,128)} reshape(f32[32,2,4,2,8,12]{5,4,3,2,1,0:T(8,128)} %broadcast_bitcast_fusion.2) | data formatting | bytes 393216
  148.3 4.8 %all-to-all-start.2 = ((f32[32,1,1536]{2,1,0:T(1,128)}), f32[32,1,1536]{2,1,0:T(1,128)S(1)}, u32[]{:S(2)}, u32[]{:S(2)}) async-start(f32[32,1,1536]{2,1,0:T(1,128)} %reshape.690), calls=%async_computation.3 | async-start | bytes 393216 | tf_op jit(solution)/shard_map/all_to_all | solution.py:43
  153.2 1.6 reshape.539
  157.7 5.1 %all-to-all-done.2 = f32[32,1,1536]{2,1,0:T(1,128)S(1)} async-done(((f32[32,1,1536]{2,1,0:T(1,128)}), f32[32,1,1536]{2,1,0:T(1,128)S(1)}, u32[]{:S(2)}, u32[]{:S(2)}) %all-to-all-start.2) | async-done | bytes 196640 | tf_op jit(solution)/shard_map/all_to_all | solution.py:43
  164.4 3.6 reshape.691
  168.0 1.8 bitcast_reduce_fusion
  171.5 1.9 convolution_bitcast_fusion.4
  173.3 1.6 fusion.74
  175.0 1.8 convolution_bitcast_fusion.5
  178.6 2.4 convolution_bitcast_fusion.2
  185.5 2.0 copy.494
  187.6 2.0 copy.487
  189.6 1.7 fusion.6
  194.4 2.0 concatenate.89
  196.5 3.3 concatenate.91
  199.7 1.8 maximum_bitcast_fusion
  201.5 3.5 copy.496
  205.0 2.4 reshape.542
  208.3 1.7 copy.501
  210.0 39.9 %all_to_all.59 = f32[32,1,12544]{2,1,0:T(1,128)S(1)} all-to-all(f32[32,1,12544]{2,1,0:T(1,128)S(1)} %copy.501), channel_id=1, replica_groups=mesh['seq'=16,'head'=2] {'seq','head'}, dimensions={0} | all-to-all | bytes 3211264 | tf_op jit(solution)/shard_map/all_to_all | solution.py:38
  251.1 6.9 %all_to_all.60 = bf16[2,192,64]{1,2,0:T(8,128)(2,1)S(1)} all-to-all(bf16[2,192,64]{1,2,0:T(8,128)(2,1)S(1)} %broadcast_in_dim.281), channel_id=1, replica_groups=mesh['seq'=16,'head'=2] {'head'}, dimensions={0} | all-to-all | bytes 98304 | tf_op jit(solution)/shard_map/all_to_all | solution.py:48
  258.3 2.4 fusion.36
  260.7 3.8 all-to-all-start.5
  264.5 27.3 %all-to-all-done.5 = f32[16,12,1280]{2,1,0:T(8,128)S(1)} async-done(((f32[16,12,1280]{2,1,0:T(8,128)}), f32[16,12,1280]{2,1,0:T(8,128)S(1)}, u32[]{:S(2)}, u32[]{:S(2)}) %all-to-all-start.5) | async-done | bytes 983072 | tf_op jit(solution)/shard_map/all_to_all | solution.py:38
  292.0 4.9 %psum.14 = f32[12]{0:T(128)S(1)} all-reduce(f32[12]{0:T(128)S(1)} %multiply_reduce_fusion.4), channel_id=1, replica_groups=mesh['seq'=16,'head'=2] {'head'}, use_global_device_ids=true, to_apply=%region_25.29 | all-reduce | flops 12 | bytes 96 | tf_op jit(solution)/shard_map/psum | solution.py:242
  298.0 26.0 %all_to_all.61 = bf16[16,12,1280]{2,1,0:T(8,128)(2,1)S(1)} all-to-all(bf16[16,12,1280]{2,1,0:T(8,128)(2,1)S(1)} %broadcast_in_dim.282), channel_id=1, replica_groups=mesh['seq'=16,'head'=2] {'seq'}, dimensions={0} | all-to-all | bytes 983040 | tf_op jit(solution)/shard_map/all_to_all | solution.py:48
  324.4 2.1 fusion.51
  327.2 17.1 %all_to_all.62 = f32[2,96,1408]{2,1,0:T(8,128)S(1)} all-to-all(f32[2,96,1408]{2,1,0:T(8,128)S(1)} %bitcast.269), channel_id=1, replica_groups=mesh['seq'=16,'head'=2] {'head'}, dimensions={0} | all-to-all | bytes 2162688 | tf_op jit(solution)/shard_map/all_to_all | solution.py:38
  344.8 7.5 %all_to_all.63 = bf16[2,96,640]{2,1,0:T(8,128)(2,1)S(1)} all-to-all(bf16[2,96,640]{2,1,0:T(8,128)(2,1)S(1)} %broadcast_in_dim.284), channel_id=1, replica_groups=mesh['seq'=16,'head'=2] {'head'}, dimensions={0} | all-to-all | bytes 491520 | tf_op jit(solution)/shard_map/all_to_all | solution.py:48
  353.0 34.4 %all_to_all.64 = f32[16,12,1280]{2,1,0:T(8,128)S(1)} all-to-all(f32[16,12,1280]{2,1,0:T(8,128)S(1)} %fusion), channel_id=1, replica_groups=mesh['seq'=16,'head'=2] {'seq'}, dimensions={0} | all-to-all | bytes 1966080 | tf_op jit(solution)/shard_map/all_to_all | solution.py:38
  387.7 4.9 %psum.15 = f32[12]{0:T(128)S(1)} all-reduce(f32[12]{0:T(128)S(1)} %multiply_reduce_fusion.3), channel_id=1, replica_groups=mesh['seq'=16,'head'=2] {'head'}, use_global_device_ids=true, to_apply=%region_30.34 | all-reduce | flops 12 | bytes 96 | tf_op jit(solution)/shard_map/psum | solution.py:267
  392.8 22.0 %all_to_all.65 = bf16[16,12,1280]{2,1,0:T(8,128)(2,1)S(1)} all-to-all(bf16[16,12,1280]{2,1,0:T(8,128)(2,1)S(1)} %broadcast_in_dim.285), channel_id=1, replica_groups=mesh['seq'=16,'head'=2] {'seq'}, dimensions={0} | all-to-all | bytes 983040 | tf_op jit(solution)/shard_map/all_to_all | solution.py:48
  (299 shorter events, 62.6 us)
Async XLA Ops:
  6.5 345.8 %copy-start = (bf16[640,1280]{1,0:T(8,128)(2,1)S(1)}, bf16[640,1280]{1,0:T(8,128)(2,1)}, u32[]{:S(2)}) copy-start(bf16[640,1280]{1,0:T(8,128)(2,1)} %param.44) | copy-start | bytes 4915204
  6.5 2.8 copy-start.18
  6.5 2.8 copy-start.15
  6.5 2.9 copy-start.44
  6.5 3.2 copy-start.53
  6.5 45.2 %all-gather.5.cloned.1.call-start = ((), (), s32[]{:S(2)}) async-start(), calls=%async_computation.14 | async-start | bytes 2359296 | tf_op jit(solution)/shard_map/all_gather | solution.py:139
  7.3 116.1 %all-gather.3.cloned.1.call-start = ((), (), s32[]{:S(2)}) async-start(), calls=%async_computation.12 | async-start | bytes 5570560 | tf_op jit(solution)/shard_map/all_gather | solution.py:115
  9.3 5.7 %copy-start.48 = (f32[256]{0:T(256)S(1)}, f32[256]{0:T(256)}, u32[]{:S(2)}) copy-start(f32[256]{0:T(256)} %param.38) | copy-start | bytes 3076
  9.3 5.7 %copy-start.51 = (s32[12]{0:T(128)S(1)}, s32[12]{0:T(128)}, u32[]{:S(2)}) copy-start(s32[12]{0:T(128)} %param.29) | copy-start | bytes 148
  9.4 6.5 %copy-start.49 = (f32[256]{0:T(256)S(1)}, f32[256]{0:T(256)}, u32[]{:S(2)}) copy-start(f32[256]{0:T(256)} %param.37) | copy-start | bytes 3076
  9.4 6.5 %copy-start.38 = (s32[2,12,8]{1,2,0:T(8,128)S(1)}, s32[2,12,8]{1,2,0:T(8,128)}, u32[]{:S(2)}) copy-start(s32[2,12,8]{1,2,0:T(8,128)} %param.27) | copy-start | bytes 2308
  10.7 10.5 %all-to-all-start = ((f32[2,96,384]{2,1,0:T(8,128)}), f32[2,96,384]{2,1,0:T(8,128)S(1)}, u32[]{:S(2)}, u32[]{:S(2)}) async-start(f32[2,96,384]{2,1,0:T(8,128)} %bitcast.10), calls=%async_computation.1 | async-start | bytes 589824 | tf_op jit(solution)/shard_map/all_to_all | solution.py:38
  15.0 63.5 %copy-start.35 = (f32[1,2,4,128]{3,1,2,0:T(2,128)}, f32[1,2,4,128]{3,1,2,0:T(2,128)S(1)}, u32[]{:S(2)}) copy-start(f32[1,2,4,128]{3,1,2,0:T(2,128)S(1)} %copy.552) | copy-start | bytes 12292
  22.9 42.7 %all-to-all-start.1 = ((bf16[32,96,256]{2,1,0:T(8,128)(2,1)}), bf16[32,96,256]{2,1,0:T(8,128)(2,1)}, u32[]{:S(2)}, u32[]{:S(2)}) async-start(bf16[32,96,256]{2,1,0:T(8,128)(2,1)} %broadcast_in_dim.258), calls=%async_computation.2 | async-start | bytes 3145728 | tf_op jit(solution)/shard_map/all_to_all | solution.py:48
  28.1 110.5 %reduce-scatter.2.cloned.1.call-start = ((), (), s32[]{:S(2)}) async-start(), calls=%async_computation.13 | async-start | bytes 393216 | tf_op jit(solution)/shard_map/reduce_scatter | solution.py:119
  28.2 3.7 copy-start.33
  36.0 1.9 copy-start.55
  36.0 9.4 %copy-start.54 = (s32[4]{0:T(128)S(1)}, s32[4]{0:T(128)}, u32[]{:S(2)}) copy-start(s32[4]{0:T(128)} %param.33) | copy-start | bytes 52
  36.0 10.1 %copy-start.52 = (s32[8]{0:T(128)S(1)}, s32[8]{0:T(128)}, u32[]{:S(2)}) copy-start(s32[8]{0:T(128)} %param.31) | copy-start | bytes 100
  47.4 70.7 %copy-start.22 = (pred[12,8,4,4]{0,1,3,2:T(8,128)(4,1)}, pred[12,8,4,4]{0,1,3,2:T(8,128)(4,1)S(1)}, u32[]{:S(2)}) copy-start(pred[12,8,4,4]{0,1,3,2:T(8,128)(4,1)S(1)} %get-tuple-element.60) | copy-start | bytes 4612
  67.1 0.9 copy-start.1
  78.4 1.0 copy-start.10
  85.8 5.8 %copy-start.43 = (pred[12,4]{1,0:T(8,128)(4,1)S(1)}, pred[12,4]{1,0:T(8,128)(4,1)}, u32[]{:S(2)}) copy-start(pred[12,4]{1,0:T(8,128)(4,1)} %copy.471) | copy-start | bytes 148
  85.8 6.9 %copy-start.42 = (pred[12,4]{1,0:T(8,128)(4,1)S(1)}, pred[12,4]{1,0:T(8,128)(4,1)}, u32[]{:S(2)}) copy-start(pred[12,4]{1,0:T(8,128)(4,1)} %copy.452) | copy-start | bytes 148
  85.8 8.3 %copy-start.41 = (pred[12,4]{1,0:T(8,128)(4,1)S(1)}, pred[12,4]{1,0:T(8,128)(4,1)}, u32[]{:S(2)}) copy-start(pred[12,4]{1,0:T(8,128)(4,1)} %get-tuple-element.58) | copy-start | bytes 148
  88.2 5.9 %copy-start.6 = (bf16[48,4,2048]{2,1,0:T(4,128)(2,1)S(1)}, bf16[48,4,2048]{2,1,0:T(4,128)(2,1)}, u32[]{:S(2)}) copy-start(bf16[48,4,2048]{2,1,0:T(4,128)(2,1)} %gather_fusion.8) | copy-start | bytes 2359300
  91.6 2.5 copy-start.7
  96.6 3.2 copy-start.8
  104.2 1.2 copy-start.2
  106.6 1.0 copy-start.17
  118.1 1.8 copy-start.39
  119.9 3.5 copy-start.19
  123.3 4.3 %copy-start.3 = (f32[12,4,4,4,8,2]{0,4,3,2,5,1:T(8,128)S(1)}, f32[12,4,4,4,8,2]{0,4,3,2,5,1:T(8,128)}, u32[]{:S(2)}) copy-start(f32[12,4,4,4,8,2]{0,4,3,2,5,1:T(8,128)} %copy.462) | copy-start | bytes 147460
  123.3 4.3 %copy-start.20 = (pred[12,8,4,4]{0,1,3,2:T(8,128)(4,1)S(1)}, pred[12,8,4,4]{0,1,3,2:T(8,128)(4,1)}, u32[]{:S(2)}) copy-start(pred[12,8,4,4]{0,1,3,2:T(8,128)(4,1)} %get-tuple-element.59) | copy-start | bytes 4612
  123.3 4.4 %copy-start.24 = (f32[12,8,4,2]{0,1,3,2:T(8,128)S(1)}, f32[12,8,4,2]{0,1,3,2:T(8,128)}, u32[]{:S(2)}) copy-start(f32[12,8,4,2]{0,1,3,2:T(8,128)} %fusion.20) | copy-start | bytes 9220
  123.3 15.2 %copy-start.50 = (f32[16]{0:T(128)S(1)}, f32[16]{0:T(128)}, u32[]{:S(2)}) copy-start(f32[16]{0:T(128)} %fusion.93) | copy-start | bytes 196
  127.6 12.3 %copy-start.36 = (f32[1,2,4,128]{3,1,2,0:T(2,128)S(1)}, f32[1,2,4,128]{3,1,2,0:T(2,128)}, u32[]{:S(2)}) copy-start(f32[1,2,4,128]{3,1,2,0:T(2,128)} %copy-done.35) | copy-start | bytes 12292
  127.6 12.4 %copy-start.47 = (pred[4,4]{1,0:T(4,128)(4,1)S(1)}, pred[4,4]{1,0:T(4,128)(4,1)}, u32[]{:S(2)}) copy-start(pred[4,4]{1,0:T(4,128)(4,1)} %broadcast_compare_fusion.1) | copy-start | bytes 52
  127.7 14.5 %copy-start.26 = (f32[8,8,4,2]{1,3,2,0:T(2,128)S(1)}, f32[8,8,4,2]{1,3,2,0:T(2,128)}, u32[]{:S(2)}) copy-start(f32[8,8,4,2]{1,3,2,0:T(2,128)} %get-tuple-element.61) | copy-start | bytes 6148
  127.7 14.6 %copy-start.25 = (f32[8,8,4,2]{1,3,2,0:T(2,128)S(1)}, f32[8,8,4,2]{1,3,2,0:T(2,128)}, u32[]{:S(2)}) copy-start(f32[8,8,4,2]{1,3,2,0:T(2,128)} %get-tuple-element.65) | copy-start | bytes 6148
  128.8 11.3 %copy-start.30 = (bf16[32,2048]{1,0:T(8,128)(2,1)S(1)}, bf16[32,2048]{1,0:T(8,128)(2,1)}, u32[]{:S(2)}) copy-start(bf16[32,2048]{1,0:T(8,128)(2,1)} %get-tuple-element.26) | copy-start | bytes 393220
  128.8 12.3 %copy-start.29 = (bf16[32,2048]{1,0:T(8,128)(2,1)S(1)}, bf16[32,2048]{1,0:T(8,128)(2,1)}, u32[]{:S(2)}) copy-start(bf16[32,2048]{1,0:T(8,128)(2,1)} %get-tuple-element.27) | copy-start | bytes 393220
  144.1 9.1 %copy-start.5 = (bf16[8,64,1024]{2,1,0:T(8,128)(2,1)S(1)}, bf16[8,64,1024]{2,1,0:T(8,128)(2,1)}, u32[]{:S(2)}) copy-start(bf16[8,64,1024]{2,1,0:T(8,128)(2,1)} %get-tuple-element.16) | copy-start | bytes 3145732
  148.3 14.5 %all-to-all-start.2 = ((f32[32,1,1536]{2,1,0:T(1,128)}), f32[32,1,1536]{2,1,0:T(1,128)S(1)}, u32[]{:S(2)}, u32[]{:S(2)}) async-start(f32[32,1,1536]{2,1,0:T(1,128)} %reshape.690), calls=%async_computation.3 | async-start | bytes 393216 | tf_op jit(solution)/shard_map/all_to_all | solution.py:43
  168.0 10.5 %copy-start.13 = (f32[8,8,4,2,64]{4,1,3,2,0:T(8,128)S(1)}, f32[8,8,4,2,64]{4,1,3,2,0:T(8,128)}, u32[]{:S(2)}) copy-start(f32[8,8,4,2,64]{4,1,3,2,0:T(8,128)} %get-tuple-element.62) | copy-start | bytes 393220
  171.4 9.6 %copy-start.14 = (f32[8,8,4,2,64]{4,1,3,2,0:T(8,128)S(1)}, f32[8,8,4,2,64]{4,1,3,2,0:T(8,128)}, u32[]{:S(2)}) copy-start(f32[8,8,4,2,64]{4,1,3,2,0:T(8,128)} %get-tuple-element.66) | copy-start | bytes 393220
  178.5 2.5 copy-start.40
  178.5 3.6 copy-start.12
  181.0 2.3 copy-start.4
  181.0 2.3 copy-start.23
  181.0 2.3 copy-start.32
  182.1 2.0 copy-start.21
  182.1 2.0 copy-start.31
  182.1 3.1 copy-start.28
  182.1 3.1 copy-start.34
  183.2 2.1 copy-start.27
  189.6 3.0 copy-start.11
  189.6 3.0 copy-start.16
  260.6 36.3 %copy-start.45 = (f32[1280]{0:T(1024)S(1)}, f32[1280]{0:T(1024)}, u32[]{:S(2)}) copy-start(f32[1280]{0:T(1024)} %param.40) | copy-start | bytes 15364
  260.7 31.2 %all-to-all-start.5 = ((f32[16,12,1280]{2,1,0:T(8,128)}), f32[16,12,1280]{2,1,0:T(8,128)S(1)}, u32[]{:S(2)}, u32[]{:S(2)}) async-start(f32[16,12,1280]{2,1,0:T(8,128)} %fusion.36), calls=%async_computation.6 | async-start | bytes 2621440 | tf_op jit(solution)/shard_map/all_to_all | solution.py:38
  298.0 26.5 %copy-start.37 = (f32[1280]{0:T(1024)S(1)}, f32[1280]{0:T(1024)}, u32[]{:S(2)}) copy-start(f32[1280]{0:T(1024)} %param.41) | copy-start | bytes 15364
  324.4 2.1 copy-start.9
  353.0 39.6 %copy-start.46 = (f32[1280]{0:T(1024)S(1)}, f32[1280]{0:T(1024)}, u32[]{:S(2)}) copy-start(f32[1280]{0:T(1024)} %param.45) | copy-start | bytes 15364
Sparse Core Ops, SparseCore 0:
  8.9 42.7 all-gather.4
  53.9 61.2 all-gather.2
  127.8 10.7 reduce-scatter.1
where the time goes:
time: 428 us; the launch traced here: 422 us
  blocking collectives  169 us (39%)
  local copies, waits for them, and re-layouts  99.5 us (23%)
  waiting for transfers between devices  56.2 us (13%)
  other arithmetic  33.5 us (8%)
  matrix products  30.4 us (7%)
  starting transfers between devices  18.2 us (4%)
  between operations  15.3 us (4%)
    all_to_all x3, blocking collectives, exchange_sum(): return jnp.sum(lax.all_to_all(parts, axes, 0, 0, tiled=True), 0)  91.5 us
    all_to_all x4, blocking collectives, exchange_gather(): return lax.all_to_all(spread, axes, 0, 0, tiled=True)  62.4 us
    all_to_all x2, waiting for transfers between devices, exchange_sum(): return jnp.sum(lax.all_to_all(parts, axes, 0, 0, tiled=True), 0)  29.4 us
    unnamed x128, local copies, waits for them, and re-layouts  15.2 us
    gather x10, local copies, waits for them, and re-layouts, shards(): written = jnp.take_along_axis(every_fresh[back], mine[:, :, None], axis=1)  12.5 us
    reduce_scatter x1, waiting for transfers between devices, shards(): lax.psum_scatter(prompt_terms, 'head', scatter_dimension=0, tiled=True)  9.79 us
  transfers between devices with their start and end apart: 7, of which 6 were waited for; matrix products, arithmetic and copies ran while one was open for 21% of the time, Pallas kernels for 0%

commit v1 on v0

--- a/solution.py
+++ b/solution.py
@@ -34,7 +34,10 @@
     return (keys, values)
 
 
-def exchange_sum(parts, axes):
+def exchange_sum(parts, axes, narrow=False):
+    if narrow:
+        moved = lax.all_to_all(parts.astype(jnp.bfloat16), axes, 0, 0, tiled=True)
+        return jnp.sum(moved.astype(jnp.float32), 0)
     return jnp.sum(lax.all_to_all(parts, axes, 0, 0, tiled=True), 0)
 
 
@@ -122,11 +125,25 @@
     prompt_pairs = finish_keys(prompt_sum * lax.rsqrt(prompt_sq / D + EPS)[:, None], k_gain)
     prompt_seg = prompt_pairs.shape[0] // pre
     prompt_pairs = jnp.transpose(prompt_pairs.reshape(prompt_seg, pre, -1), (1, 0, 2))
-    prompt_keys, prompt_values = split_pairs(prompt_pairs)
     prompt_ok = (flat_at * prompt_seg + jnp.arange(prompt_seg))[None, :] < prompt_len[:, None]
     cache_seg = cache.shape[1]
-    cache_keys, cache_values = split_pairs(cache)
     cache_ok = (flat_at * cache_seg + jnp.arange(cache_seg))[None, :] < cache_len[:, None]
+    span = max(prompt_seg, cache_seg)
+    shared = jnp.concatenate(
+        [
+            jnp.pad(prompt_pairs, ((0, 0), (0, span - prompt_seg), (0, 0))),
+            jnp.pad(cache, ((0, 0), (0, span - cache_seg), (0, 0))),
+        ],
+        0,
+    )
+    shared_ok = jnp.concatenate(
+        [
+            jnp.pad(prompt_ok, ((0, 0), (0, span - prompt_seg))),
+            jnp.pad(cache_ok, ((0, 0), (0, span - cache_seg))),
+        ],
+        0,
+    )
+    shared_keys, shared_values = split_pairs(shared)
     tail_seg = tail_cache.shape[2]
     local_beams = tail_cache.shape[1]
     offset = (seq_at * tail_seg + jnp.arange(tail_seg))[None, :] - tail_len[:, None]
@@ -137,99 +154,90 @@
     every_query = every_query.reshape(steps, groups, beams, -1)
     every_fresh = every_fresh.reshape(steps, groups, beams, -1)
     everyone = lax.all_gather(tail_cache, "head", axis=1, tiled=True)
-    local_ids = head_at * local_beams + jnp.arange(local_beams)
     n_dev = n_seq * n_head
-    owner = jnp.broadcast_to(all_beams[None, :, None], (groups, beams, tail_seg))
+    first_beam = head_at * local_beams
+    many = steps * beams * repeat
+    grouped = jnp.transpose(
+        every_query.reshape(steps, groups, beams, KVH, repeat, HD), (1, 3, 0, 2, 4, 5)
+    ).reshape(groups, KVH, many, HD)
+    scores = jnp.einsum("gkmd,gtkd->gkmt", grouped, shared_keys, preferred_element_type=f32)
+    scores = jnp.where(shared_ok[:, None, None, :], scores, NEG)
+    top = jnp.max(scores, -1).reshape(groups, KVH, steps, beams, repeat)
     source = jnp.broadcast_to(all_beams[None, :], (groups, beams))
     ancestors = []
-    shaped_all, scores_all, tails_all = [], [], []
+    tail_parts = []
+    tail_tops = []
     for step in range(steps):
         link = parents[step]
         source = jnp.take_along_axis(source, link, axis=1)
         ancestors = [jnp.take_along_axis(a, link, axis=1) for a in ancestors]
         ancestors.append(jnp.broadcast_to(all_beams[None, :], (groups, beams)))
-        picks = lax.dynamic_slice_in_dim(source, head_at * local_beams, local_beams, 1)
+        picks = lax.dynamic_slice_in_dim(source, first_beam, local_beams, 1)
         tail_state = jnp.take_along_axis(everyone, picks[:, :, None, None], axis=1)
         for back, anc in enumerate(ancestors):
-            mine = lax.dynamic_slice_in_dim(anc, head_at * local_beams, local_beams, 1)
+            mine = lax.dynamic_slice_in_dim(anc, first_beam, local_beams, 1)
             written = jnp.take_along_axis(every_fresh[back], mine[:, :, None], axis=1)
             tail_state = jnp.where(
                 (offset == back)[:, None, :, None], written[:, :, None, :], tail_state
             )
-        tail_ok = (offset <= step)[:, None, None, :] & (
-            owner[:, :, None, :] == local_ids[None, None, :, None]
+        tail_keys, tail_values = split_pairs(tail_state)
+        local_query = lax.dynamic_slice_in_dim(every_query[step], first_beam, local_beams, 1)
+        local_query = local_query.reshape(groups, local_beams, KVH, repeat, HD)
+        tail_scores = jnp.einsum(
+            "gckrd,gctkd->gckrt", local_query, tail_keys, preferred_element_type=f32
         )
-        shaped = every_query[step].reshape(groups, beams, KVH, repeat, HD)
-        tail_keys, tail_values = split_pairs(tail_state)
-        pre_scores = jnp.einsum(
-            "gbkrd,gtkd->gbkrt", shaped[:pre], prompt_keys, preferred_element_type=f32
+        tail_ok = (offset <= step)[:, None, None, None, :]
+        tail_scores = jnp.where(tail_ok, tail_scores, NEG)
+        tail_parts.append((tail_scores, tail_ok, tail_values))
+        tail_top = lax.dynamic_update_slice(
+            jnp.full((groups, beams, KVH, repeat), NEG, f32),
+            jnp.max(tail_scores, -1),
+            (0, first_beam, 0, 0),
         )
-        dec_scores = jnp.einsum(
-            "gbkrd,gtkd->gbkrt", shaped[pre:], cache_keys, preferred_element_type=f32
+        tail_tops.append(jnp.transpose(tail_top, (0, 2, 1, 3)))
+    top = jnp.maximum(top, jnp.stack(tail_tops, 2))
+    top = exchange_max(top, ("seq", "head"), n_dev)
+    weights = jnp.where(
+        shared_ok[:, None, None, :], jnp.exp(scores - top.reshape(groups, KVH, many)[..., None]), 0.0
+    )
+    total = jnp.sum(weights, -1).reshape(groups, KVH, steps, beams, repeat)
+    weighted = jnp.einsum(
+        "gkmt,gtkd->gkmd", weights.astype(bf16), shared_values, preferred_element_type=f32
+    ).reshape(groups, KVH, steps, beams, repeat, HD)
+    tail_totals, tail_weighted = [], []
+    for step in range(steps):
+        tail_scores, tail_ok, tail_values = tail_parts[step]
+        local_top = lax.dynamic_slice_in_dim(top[:, :, step], first_beam, local_beams, 2)
+        local_top = jnp.transpose(local_top, (0, 2, 1, 3))
+        tail_weights = jnp.where(tail_ok, jnp.exp(tail_scores - local_top[..., None]), 0.0)
+        tail_total = lax.dynamic_update_slice(
+            jnp.zeros((groups, beams, KVH, repeat), f32),
+            jnp.sum(tail_weights, -1),
+            (0, first_beam, 0, 0),
         )
-        tail_scores = jnp.einsum(
-            "gbkrd,gctkd->gbkrct", shaped, tail_keys, preferred_element_type=f32
+        tail_sum = lax.dynamic_update_slice(
+            jnp.zeros((groups, beams, KVH, repeat, HD), f32),
+            jnp.einsum(
+                "gckrt,gctkd->gckrd",
+                tail_weights.astype(bf16),
+                tail_values,
+                preferred_element_type=f32,
+            ),
+            (0, first_beam, 0, 0, 0),
         )
-        pre_scores = jnp.where(prompt_ok[:, None, None, None, :], pre_scores, NEG)
-        dec_scores = jnp.where(cache_ok[:, None, None, None, :], dec_scores, NEG)
-        tail_scores = jnp.where(tail_ok[:, :, None, None, :, :], tail_scores, NEG)
-        top = jnp.concatenate([jnp.max(pre_scores, -1), jnp.max(dec_scores, -1)], 0)
-        top = jnp.maximum(top, jnp.max(tail_scores, (-2, -1)))
-        scores_all.append((pre_scores, dec_scores, tail_scores))
-        tails_all.append((tail_ok, tail_values))
-        shaped_all.append(top)
-    top_all = exchange_max(jnp.stack(shaped_all), ("seq", "head"), n_dev)
-    weighted_all, total_all = [], []
-    for step in range(steps):
-        pre_scores, dec_scores, tail_scores = scores_all[step]
-        tail_ok, tail_values = tails_all[step]
-        top = top_all[step]
-        pre_mask = prompt_ok[:, None, None, None, :]
-        dec_mask = cache_ok[:, None, None, None, :]
-        tail_mask = tail_ok[:, :, None, None, :, :]
-        pre_weights = jnp.where(pre_mask, jnp.exp(pre_scores - top[:pre, ..., None]), 0.0)
-        dec_weights = jnp.where(dec_mask, jnp.exp(dec_scores - top[pre:, ..., None]), 0.0)
-        tail_weights = jnp.where(tail_mask, jnp.exp(tail_scores - top[..., None, None]), 0.0)
-        total = jnp.concatenate([jnp.sum(pre_weights, -1), jnp.sum(dec_weights, -1)], 0)
-        total = total + jnp.sum(tail_weights, (-2, -1))
-        weighted = jnp.concatenate(
-            [
-                jnp.einsum(
-                    "gbkrt,gtkd->gbkrd",
-                    pre_weights.astype(bf16),
-                    prompt_values,
-                    preferred_element_type=f32,
-                ),
-                jnp.einsum(
-                    "gbkrt,gtkd->gbkrd",
-                    dec_weights.astype(bf16),
-                    cache_values,
-                    preferred_element_type=f32,
-                ),
-            ],
-            0,
-        )
-        weighted = weighted + jnp.einsum(
-            "gbkrct,gctkd->gbkrd",
-            tail_weights.astype(bf16),
-            tail_values,
-            preferred_element_type=f32,
-        )
-        weighted_all.append(weighted.reshape(groups * beams, -1))
-        total_all.append(total.reshape(groups * beams, -1))
-    weighted = jnp.concatenate(weighted_all, 0)
-    total = jnp.concatenate(total_all, 0)
-    rows = weighted.shape[0]
+        tail_totals.append(jnp.transpose(tail_total, (0, 2, 1, 3)))
+        tail_weighted.append(jnp.transpose(tail_sum, (0, 2, 1, 3, 4)))
+    total = total + jnp.stack(tail_totals, 2)
+    weighted = weighted + jnp.stack(tail_weighted, 2)
+    rows = steps * groups * beams
     piece = QD // n_dev
-    piece_head = jnp.arange(n_dev) * piece // HD
+    per_head = HD // piece
+    weighted = jnp.transpose(
+        weighted.reshape(groups, KVH, steps, beams, repeat, per_head, piece), (1, 4, 5, 2, 0, 3, 6)
+    ).reshape(n_dev, -1)
+    total = jnp.repeat(jnp.transpose(total, (1, 4, 2, 0, 3)).reshape(QH, rows), per_head, 0)
     lanes = -(-rows // 128) * 128
-    packed = jnp.concatenate(
-        [
-            jnp.transpose(weighted.reshape(rows, n_dev, piece), (1, 0, 2)).reshape(n_dev, -1),
-            jnp.pad(jnp.transpose(total[:, piece_head]), ((0, 0), (0, lanes - rows))),
-        ],
-        1,
-    )
+    packed = jnp.concatenate([weighted, jnp.pad(total, ((0, 0), (0, lanes - rows)))], 1)
     packed = exchange_sum(packed, ("seq", "head"))
     share = packed[: rows * piece].reshape(rows, piece)
     own_total = packed[rows * piece : rows * piece + rows]

time: 428 us -> 419 us (0.979)
  local copies, waits for them, and re-layouts: 99.5 us -> 73.6 us
  waiting for transfers between devices: 56.2 us -> 73.6 us
  blocking collectives: 169 us -> 185 us
  matrix products: 30.4 us -> 22 us
  starting transfers between devices: 18.2 us -> 13.3 us
    all_gather x1, waiting for transfers between devices: 0.02 us -> 21.2 us  [shards(): lax.all_gather(w_keyval, 'seq', axis=1, tiled=True)]
    all_to_all x0 -> x1, blocking collectives: none -> 14.4 us  [exchange_max(): return jnp.max(lax.all_to_all(spread, axes, 0, 0, tiled=True), 0)]
    dot_general x12 -> x6, matrix products: 19.9 us -> 10.4 us  [the longest x2 3.09 us: shards(): jnp.einsum('gckrd,gctkd->gckrt', local_query, tail_keys, preferred_elemen...]
    another operation x0 -> x8, local copies, waits for them, and re-layouts: none -> 7.76 us  [the longest x2 5.78 us: shards(): weighted = weighted + jnp.stack(tail_weighted, 2)]
    gather x10, local copies, waits for them, and re-layouts: 12.5 us -> 6.16 us  [shards(): written = jnp.take_along_axis(every_fresh[back], mine[:, :, None], axis=1)]
    dot_general x2 -> x0, local copies, waits for them, and re-layouts: 5.49 us -> none  [shards(): jnp.einsum('gbkrd,gctkd->gbkrct', shaped, tail_keys, preferred_element_ty...]
    concatenate x2 -> x0, local copies, waits for them, and re-layouts: 5.29 us -> none  [shards(): weighted = jnp.concatenate(weighted_all, 0)]
    all_to_all x1 -> x0, waiting for transfers between devices: 5.14 us -> none  [exchange_max(): return jnp.max(lax.all_to_all(spread, axes, 0, 0, tiled=True), 0)]
  transfers between devices with their start and end apart: 7 -> 6, of which waited for: 6 -> 6; matrix products, arithmetic and copies ran while one was open for 21% -> 13% of each run, Pallas kernels for 0% -> 0%
where the time goes in v1:
time: 419 us; the launch traced here: 414 us
  blocking collectives  185 us (44%)
  local copies, waits for them, and re-layouts  73.6 us (18%)
  waiting for transfers between devices  73.6 us (18%)
  other arithmetic  31.5 us (8%)
  matrix products  22 us (5%)
  between operations  15.2 us (4%)
  starting transfers between devices  13.3 us (3%)
    all_to_all x3, blocking collectives, exchange_sum(): return jnp.sum(lax.all_to_all(parts, axes, 0, 0, tiled=True), 0)  91.5 us
    all_to_all x4, blocking collectives, exchange_gather(): return lax.all_to_all(spread, axes, 0, 0, tiled=True)  62.4 us
    all_to_all x2, waiting for transfers between devices, exchange_sum(): return jnp.sum(lax.all_to_all(parts, axes, 0, 0, tiled=True), 0)  32.6 us
    all_gather x1, waiting for transfers between devices, shards(): lax.all_gather(w_keyval, 'seq', axis=1, tiled=True)  21.2 us
    all_to_all x1, blocking collectives, exchange_max(): return jnp.max(lax.all_to_all(spread, axes, 0, 0, tiled=True), 0)  14.4 us
    unnamed x84, local copies, waits for them, and re-layouts  13.9 us
  transfers between devices with their start and end apart: 6, of which 6 were waited for; matrix products, arithmetic and copies ran while one was open for 13% of the time, Pallas kernels for 0%

profile of v1, /device:TPU:0, one launch (start us, length us, event | category | flops | bytes accessed | tf_op | source)
XLA Modules:
  0.0 414.2 jit_solution(684152702623580658)
XLA Ops:
  8.0 1.4 fusion.25
  10.8 4.2 %all-to-all-start = ((f32[2,96,384]{2,1,0:T(8,128)}), f32[2,96,384]{2,1,0:T(8,128)S(1)}, u32[]{:S(2)}, u32[]{:S(2)}) async-start(f32[2,96,384]{2,1,0:T(8,128)} %bitcast.1), calls=%async_computation | async-start | bytes 589824 | tf_op jit(solution)/shard_map/all_to_all | solution.py:41
  16.0 5.2 %all-to-all-done = f32[2,96,384]{2,1,0:T(8,128)S(1)} async-done(((f32[2,96,384]{2,1,0:T(8,128)}), f32[2,96,384]{2,1,0:T(8,128)S(1)}, u32[]{:S(2)}, u32[]{:S(2)}) %all-to-all-start) | async-done | bytes 294944 | tf_op jit(solution)/shard_map/all_to_all | solution.py:41
  21.5 1.3 broadcast_in_dim.206
  22.9 5.1 %all-to-all-start.1 = ((bf16[32,96,256]{2,1,0:T(8,128)(2,1)}), bf16[32,96,256]{2,1,0:T(8,128)(2,1)S(1)}, u32[]{:S(2)}, u32[]{:S(2)}) async-start(bf16[32,96,256]{2,1,0:T(8,128)(2,1)} %broadcast_in_dim.206), calls=%async_computation.1 | async-start | bytes 3145728 | tf_op jit(solution)/shard_map/all_to_all | solution.py:51
  28.3 1.3 gather_fusion.4
  29.9 1.3 gather_fusion.1
  35.8 6.9 %all-reduce.5 = f32[32]{0:T(128)S(1)} all-reduce(f32[32]{0:T(128)S(1)} %reshape.385), channel_id=3, replica_groups=mesh['seq'=16,'head'=2] {'head'}, use_global_device_ids=true, to_apply=%region_6.7.clone | all-reduce | flops 32 | bytes 256
  44.2 7.5 %all-gather.5.cloned.1.call-done = bf16[12,8,4,2048]{3,2,1,0:T(4,128)(2,1)} async-done(((bf16[12,4,4,2048]{3,2,1,0:T(4,128)(2,1)}), bf16[12,8,4,2048]{3,2,1,0:T(4,128)(2,1)}) %all-gather.5.cloned.1.call-update) | async-done | bytes 1572880 | tf_op jit(solution)/shard_map/all_gather | solution.py:156
  51.7 3.9 gather_fusion.2
  55.6 3.9 gather_fusion.7
  59.5 6.0 %all-to-all-done.1 = bf16[32,96,256]{2,1,0:T(8,128)(2,1)S(1)} async-done(((bf16[32,96,256]{2,1,0:T(8,128)(2,1)}), bf16[32,96,256]{2,1,0:T(8,128)(2,1)S(1)}, u32[]{:S(2)}, u32[]{:S(2)}) %all-to-all-start.1) | async-done | bytes 1572896 | tf_op jit(solution)/shard_map/all_to_all | solution.py:51
  65.5 1.2 slice_bitcast_fusion
  68.4 1.6 copy_convert_fusion
  70.0 2.2 reshape.406
  72.2 1.4 copy.301
  78.5 1.5 mul.307
  81.7 1.6 gather_fusion
  83.3 1.6 gather_fusion.3
  85.7 1.7 gather_fusion.5
  87.7 1.3 broadcast_select_fusion.2
  89.0 1.5 select_select_fusion.1
  90.5 1.2 fusion.81
  91.7 1.2 fusion.80
  94.0 21.2 %all-gather.3.cloned.1.call-done = bf16[1280,2048]{1,0:T(8,128)(2,1)} async-done(((bf16[1280,128]{1,0:T(8,128)(2,1)}), bf16[1280,2048]{1,0:T(8,128)(2,1)}) %all-gather.3.cloned.1.call-update) | async-done | bytes 5242896 | tf_op jit(solution)/shard_map/all_gather | solution.py:118
  115.1 4.2 %fusion.86 = f32[32,2048]{1,0:T(8,128)} fusion(bf16[32,1280]{1,0:T(8,128)(2,1)S(1)} %copy-done.12, bf16[1280,2048]{1,0:T(8,128)(2,1)} %all-gather.3.cloned.1.call-done), kind=kOutput, calls=%fused_computation.205 | convolution fusion | flops 167772160 | bytes 5586944 | tf_op jit(solution)/shard_map/dot_general | solution.py:116
  119.4 2.0 fusion.84
  121.4 1.3 copy.302
  124.4 4.9 %reduce-scatter.2.cloned.1.call-done = f32[16,2048]{1,0:T(8,128)} async-done(((f32[32,2048]{1,0:T(8,128)}), f32[16,2048]{1,0:T(8,128)}) %reduce-scatter.2.cloned.1.call-update) | async-done | bytes 131088 | tf_op jit(solution)/shard_map/reduce_scatter | solution.py:122
  130.8 2.0 fusion.1
  133.9 1.5 fusion.83
  135.6 1.6 broadcast_bitcast_fusion.2
  137.2 3.6 reshape.524
  140.8 14.4 %all_to_all.59 = f32[32,1,1536]{2,1,0:T(1,128)} all-to-all(f32[32,1,1536]{2,1,0:T(1,128)S(1)} %reshape.524), channel_id=1, replica_groups=mesh['seq'=16,'head'=2] {'seq','head'}, dimensions={0} | all-to-all | bytes 393216 | tf_op jit(solution)/shard_map/all_to_all | solution.py:46
  155.6 2.0 reduce.10
  157.7 3.6 reshape.525
  161.3 1.8 bitcast_reduce_fusion
  163.3 1.7 fusion.23
  166.0 1.5 fusion.64
  167.9 1.5 fusion.63
  169.7 1.5 fusion.54
  172.3 1.5 fusion.49
  175.8 2.9 stack.31
  178.7 1.5 fusion.51
  182.2 2.9 stack.30
  185.1 2.7 fusion.9
  187.8 3.9 reshape.393
  191.7 3.5 fusion.2
  195.2 2.1 copy.342
  197.3 2.7 reshape.396
  200.1 1.7 copy.348
  201.8 39.9 %all_to_all.64 = f32[32,1,12544]{2,1,0:T(1,128)S(1)} all-to-all(f32[32,1,12544]{2,1,0:T(1,128)S(1)} %copy.348), channel_id=1, replica_groups=mesh['seq'=16,'head'=2] {'seq','head'}, dimensions={0} | all-to-all | bytes 3211264 | tf_op jit(solution)/shard_map/all_to_all | solution.py:41
  242.9 6.9 %all_to_all.60 = bf16[2,192,64]{1,2,0:T(8,128)(2,1)S(1)} all-to-all(bf16[2,192,64]{1,2,0:T(8,128)(2,1)S(1)} %broadcast_in_dim.226), channel_id=1, replica_groups=mesh['seq'=16,'head'=2] {'head'}, dimensions={0} | all-to-all | bytes 98304 | tf_op jit(solution)/shard_map/all_to_all | solution.py:51
  250.1 2.4 fusion.34
  252.4 3.8 all-to-all-start.5
  256.3 27.3 %all-to-all-done.5 = f32[16,12,1280]{2,1,0:T(8,128)S(1)} async-done(((f32[16,12,1280]{2,1,0:T(8,128)}), f32[16,12,1280]{2,1,0:T(8,128)S(1)}, u32[]{:S(2)}, u32[]{:S(2)}) %all-to-all-start.5) | async-done | bytes 983072 | tf_op jit(solution)/shard_map/all_to_all | solution.py:41
  283.8 4.9 %psum.14 = f32[12]{0:T(128)S(1)} all-reduce(f32[12]{0:T(128)S(1)} %multiply_reduce_fusion.4), channel_id=1, replica_groups=mesh['seq'=16,'head'=2] {'head'}, use_global_device_ids=true, to_apply=%region_19.23 | all-reduce | flops 12 | bytes 96 | tf_op jit(solution)/shard_map/psum | solution.py:250
  289.7 26.0 %all_to_all.61 = bf16[16,12,1280]{2,1,0:T(8,128)(2,1)S(1)} all-to-all(bf16[16,12,1280]{2,1,0:T(8,128)(2,1)S(1)} %broadcast_in_dim.227), channel_id=1, replica_groups=mesh['seq'=16,'head'=2] {'seq'}, dimensions={0} | all-to-all | bytes 983040 | tf_op jit(solution)/shard_map/all_to_all | solution.py:51
  316.2 2.1 fusion.45
  319.0 17.1 %all_to_all.65 = f32[2,96,1408]{2,1,0:T(8,128)S(1)} all-to-all(f32[2,96,1408]{2,1,0:T(8,128)S(1)} %bitcast.223), channel_id=1, replica_groups=mesh['seq'=16,'head'=2] {'head'}, dimensions={0} | all-to-all | bytes 2162688 | tf_op jit(solution)/shard_map/all_to_all | solution.py:41
  336.6 7.5 %all_to_all.62 = bf16[2,96,640]{2,1,0:T(8,128)(2,1)S(1)} all-to-all(bf16[2,96,640]{2,1,0:T(8,128)(2,1)S(1)} %broadcast_in_dim.229), channel_id=1, replica_groups=mesh['seq'=16,'head'=2] {'head'}, dimensions={0} | all-to-all | bytes 491520 | tf_op jit(solution)/shard_map/all_to_all | solution.py:51
  344.8 34.4 %all_to_all.66 = f32[16,12,1280]{2,1,0:T(8,128)S(1)} all-to-all(f32[16,12,1280]{2,1,0:T(8,128)S(1)} %fusion.3), channel_id=1, replica_groups=mesh['seq'=16,'head'=2] {'seq'}, dimensions={0} | all-to-all | bytes 1966080 | tf_op jit(solution)/shard_map/all_to_all | solution.py:41
  379.4 4.9 %psum.15 = f32[12]{0:T(128)S(1)} all-reduce(f32[12]{0:T(128)S(1)} %multiply_reduce_fusion.3), channel_id=1, replica_groups=mesh['seq'=16,'head'=2] {'head'}, use_global_device_ids=true, to_apply=%region_24.28 | all-reduce | flops 12 | bytes 96 | tf_op jit(solution)/shard_map/psum | solution.py:275
  384.5 22.0 %all_to_all.63 = bf16[16,12,1280]{2,1,0:T(8,128)(2,1)S(1)} all-to-all(bf16[16,12,1280]{2,1,0:T(8,128)(2,1)S(1)} %broadcast_in_dim.230), channel_id=1, replica_groups=mesh['seq'=16,'head'=2] {'seq'}, dimensions={0} | all-to-all | bytes 983040 | tf_op jit(solution)/shard_map/all_to_all | solution.py:51
  (247 shorter events, 38.0 us)
Async XLA Ops:
  6.5 337.6 %copy-start = (bf16[640,1280]{1,0:T(8,128)(2,1)S(1)}, bf16[640,1280]{1,0:T(8,128)(2,1)}, u32[]{:S(2)}) copy-start(bf16[640,1280]{1,0:T(8,128)(2,1)} %param.44) | copy-start | bytes 4915204
  6.5 2.9 copy-start.24
  6.5 2.9 copy-start.11
  6.5 2.9 copy-start.33
  6.5 45.1 %all-gather.5.cloned.1.call-start = ((), (), s32[]{:S(2)}) async-start(), calls=%async_computation.14 | async-start | bytes 2359296 | tf_op jit(solution)/shard_map/all_gather | solution.py:156
  7.3 107.8 %all-gather.3.cloned.1.call-start = ((), (), s32[]{:S(2)}) async-start(), calls=%async_computation.12 | async-start | bytes 5570560 | tf_op jit(solution)/shard_map/all_gather | solution.py:118
  9.5 5.6 %copy-start.15 = (bf16[4,8,1280]{2,1,0:T(8,128)(2,1)S(1)}, bf16[4,8,1280]{2,1,0:T(8,128)(2,1)}, u32[]{:S(2)}) copy-start(bf16[4,8,1280]{2,1,0:T(8,128)(2,1)} %param.32) | copy-start | bytes 245764
  9.5 6.5 %copy-start.29 = (f32[256]{0:T(256)S(1)}, f32[256]{0:T(256)}, u32[]{:S(2)}) copy-start(f32[256]{0:T(256)} %param.38) | copy-start | bytes 3076
  10.8 10.5 %all-to-all-start = ((f32[2,96,384]{2,1,0:T(8,128)}), f32[2,96,384]{2,1,0:T(8,128)S(1)}, u32[]{:S(2)}, u32[]{:S(2)}) async-start(f32[2,96,384]{2,1,0:T(8,128)} %bitcast.1), calls=%async_computation | async-start | bytes 589824 | tf_op jit(solution)/shard_map/all_to_all | solution.py:41
  22.8 5.2 %copy-start.27 = (f32[256]{0:T(256)S(1)}, f32[256]{0:T(256)}, u32[]{:S(2)}) copy-start(f32[256]{0:T(256)} %param.37) | copy-start | bytes 3076
  22.9 5.2 %copy-start.17 = (s32[2,12,8]{1,2,0:T(8,128)S(1)}, s32[2,12,8]{1,2,0:T(8,128)}, u32[]{:S(2)}) copy-start(s32[2,12,8]{1,2,0:T(8,128)} %param.27) | copy-start | bytes 2308
  22.9 42.6 %all-to-all-start.1 = ((bf16[32,96,256]{2,1,0:T(8,128)(2,1)}), bf16[32,96,256]{2,1,0:T(8,128)(2,1)S(1)}, u32[]{:S(2)}, u32[]{:S(2)}) async-start(bf16[32,96,256]{2,1,0:T(8,128)(2,1)} %broadcast_in_dim.206), calls=%async_computation.1 | async-start | bytes 3145728 | tf_op jit(solution)/shard_map/all_to_all | solution.py:51
  28.0 101.4 %reduce-scatter.2.cloned.1.call-start = ((), (), s32[]{:S(2)}) async-start(), calls=%async_computation.13 | async-start | bytes 393216 | tf_op jit(solution)/shard_map/reduce_scatter | solution.py:122
  31.4 3.2 copy-start.35
  31.4 12.0 %copy-start.34 = (s32[4]{0:T(128)S(1)}, s32[4]{0:T(128)}, u32[]{:S(2)}) copy-start(s32[4]{0:T(128)} %param.33) | copy-start | bytes 52
  31.4 12.1 %copy-start.32 = (s32[8]{0:T(128)S(1)}, s32[8]{0:T(128)}, u32[]{:S(2)}) copy-start(s32[8]{0:T(128)} %param.31) | copy-start | bytes 100
  31.4 12.1 %copy-start.31 = (s32[12]{0:T(128)S(1)}, s32[12]{0:T(128)}, u32[]{:S(2)}) copy-start(s32[12]{0:T(128)} %param.29) | copy-start | bytes 148
  43.5 119.8 %copy-start.18 = (pred[12,64]{1,0:T(8,128)(4,1)}, pred[12,64]{1,0:T(8,128)(4,1)S(1)}, u32[]{:S(2)}) copy-start(pred[12,64]{1,0:T(8,128)(4,1)S(1)} %pad_add_fusion) | copy-start | bytes 2308
  66.6 0.9 copy-start.1
  75.4 1.1 copy-start.6
  80.6 1.0 copy-start.9
  84.9 2.6 copy-start.20
  85.7 3.3 copy-start.4
  87.5 1.5 copy-start.5
  90.5 2.4 copy-start.2
  90.5 2.4 copy-start.8
  90.5 2.3 copy-start.28
  92.9 22.3 %copy-start.12 = (bf16[32,1280]{1,0:T(8,128)(2,1)S(1)}, bf16[32,1280]{1,0:T(8,128)(2,1)}, u32[]{:S(2)}) copy-start(bf16[32,1280]{1,0:T(8,128)(2,1)} %reshape.384) | copy-start | bytes 245764
  93.9 25.4 %copy-start.23 = (pred[12,4]{1,0:T(8,128)(4,1)S(1)}, pred[12,4]{1,0:T(8,128)(4,1)}, u32[]{:S(2)}) copy-start(pred[12,4]{1,0:T(8,128)(4,1)} %get-tuple-element.39) | copy-start | bytes 148
  119.4 3.7 copy-start.21
  122.7 6.7 %copy-start.30 = (f32[16]{0:T(128)S(1)}, f32[16]{0:T(128)}, u32[]{:S(2)}) copy-start(f32[16]{0:T(128)} %fusion.74) | copy-start | bytes 196
  132.8 1.1 copy-start.10
  163.3 2.7 copy-start.13
  174.9 3.8 copy-start.22
  181.2 3.9 copy-start.14
  181.2 3.9 copy-start.19
  187.8 3.9 copy-start.3
  252.4 36.3 %copy-start.25 = (f32[1280]{0:T(1024)S(1)}, f32[1280]{0:T(1024)}, u32[]{:S(2)}) copy-start(f32[1280]{0:T(1024)} %param.40) | copy-start | bytes 15364
  252.4 31.2 %all-to-all-start.5 = ((f32[16,12,1280]{2,1,0:T(8,128)}), f32[16,12,1280]{2,1,0:T(8,128)S(1)}, u32[]{:S(2)}, u32[]{:S(2)}) async-start(f32[16,12,1280]{2,1,0:T(8,128)} %fusion.34), calls=%async_computation.6 | async-start | bytes 2621440 | tf_op jit(solution)/shard_map/all_to_all | solution.py:41
  289.7 26.5 %copy-start.16 = (f32[1280]{0:T(1024)S(1)}, f32[1280]{0:T(1024)}, u32[]{:S(2)}) copy-start(f32[1280]{0:T(1024)} %param.41) | copy-start | bytes 15364
  316.2 2.1 copy-start.7
  344.8 39.6 %copy-start.26 = (f32[1280]{0:T(1024)S(1)}, f32[1280]{0:T(1024)}, u32[]{:S(2)}) copy-start(f32[1280]{0:T(1024)} %param.45) | copy-start | bytes 15364
Sparse Core Ops, SparseCore 0:
  8.9 42.7 all-gather.4
  53.8 61.2 all-gather.2
  119.5 9.8 reduce-scatter.1

commit v2 on v1

--- a/solution.py
+++ b/solution.py
@@ -10,6 +10,9 @@
 QD = 2048
 
 
+SEQ = ("seq", "pair")
+ALL = ("seq", "pair", "head")
+
 EPS = 1e-06
 NEG = -1e30
 QSCALE = 0.0625
@@ -49,6 +52,20 @@
 def exchange_gather(piece, axes, count):
     spread = jnp.broadcast_to(piece[None], (count,) + piece.shape)
     return lax.all_to_all(spread, axes, 0, 0, tiled=True)
+
+
+def seq_sum(parts):
+    pair = lax.axis_size("pair")
+    parts = parts.reshape((parts.shape[0] // pair, pair) + parts.shape[1:])
+    parts = exchange_sum(jnp.swapaxes(parts, 0, 1), "pair")
+    return exchange_sum(parts, "seq")
+
+
+def seq_gather(piece):
+    pair = lax.axis_size("pair")
+    outer = lax.axis_size("seq")
+    got = exchange_gather(exchange_gather(piece, "seq", outer), "pair", pair)
+    return jnp.swapaxes(got, 0, 1).reshape((outer * pair,) + piece.shape)
 
 
 def project_tokens(tokens, in_gain, w_query, w_keyval, q_gain, k_gain):
@@ -58,7 +75,7 @@
     kv_part = jnp.dot(scaled, w_keyval, preferred_element_type=jnp.float32)
     squares = jnp.sum(flat * flat, -1)
     n_head = lax.axis_size("head")
-    n_seq = lax.axis_size("seq")
+    n_seq = lax.axis_size("seq") * lax.axis_size("pair")
     rows = flat.shape[0]
     half = rows // n_head
     block = q_part.shape[1]
@@ -68,7 +85,7 @@
     q_raw = (packed[:, :block] * factor).astype(jnp.bfloat16)
     kv_raw = (packed[:, block : 2 * block] * factor).astype(jnp.bfloat16)
     both = exchange_gather(
-        jnp.concatenate([q_raw, kv_raw], 1), ("seq", "head"), n_seq * n_head
+        jnp.concatenate([q_raw, kv_raw], 1), ALL, n_seq * n_head
     ).reshape(n_seq, n_head, half, 2 * block)
     both = jnp.transpose(both, (1, 2, 0, 3)).reshape(rows, n_seq, 2 * block)
     q_raw = both[:, :, :block].reshape(rows, -1)
@@ -103,8 +120,8 @@
     f32 = jnp.float32
     bf16 = jnp.bfloat16
     n_head = lax.axis_size("head")
-    n_seq = lax.axis_size("seq")
-    seq_at = lax.axis_index("seq")
+    n_seq = lax.axis_size("seq") * lax.axis_size("pair")
+    seq_at = lax.axis_index("seq") * lax.axis_size("pair") + lax.axis_index("pair")
     head_at = lax.axis_index("head")
     flat_at = seq_at * n_head + head_at
     steps, groups, beams, width = step_tokens.shape
@@ -115,7 +132,7 @@
     prompt_squares = jnp.sum(rows * rows, -1).reshape(-1)
     prompt_terms = jnp.dot(
         prompt_scaled,
-        lax.all_gather(w_keyval, "seq", axis=1, tiled=True),
+        lax.all_gather(w_keyval, SEQ, axis=1, tiled=True),
         preferred_element_type=f32,
     )
     prompt_sum, prompt_sq = (
@@ -196,7 +213,7 @@
         )
         tail_tops.append(jnp.transpose(tail_top, (0, 2, 1, 3)))
     top = jnp.maximum(top, jnp.stack(tail_tops, 2))
-    top = exchange_max(top, ("seq", "head"), n_dev)
+    top = exchange_max(top, ALL, n_dev)
     weights = jnp.where(
         shared_ok[:, None, None, :], jnp.exp(scores - top.reshape(groups, KVH, many)[..., None]), 0.0
     )
@@ -238,6 +255,9 @@
     total = jnp.repeat(jnp.transpose(total, (1, 4, 2, 0, 3)).reshape(QH, rows), per_head, 0)
     lanes = -(-rows // 128) * 128
     packed = jnp.concatenate([weighted, jnp.pad(total, ((0, 0), (0, lanes - rows)))], 1)
+    pair = lax.axis_size("pair")
+    packed = packed.reshape(n_seq // pair, pair, n_head, -1)
+    packed = exchange_sum(jnp.swapaxes(packed, 0, 1), "pair").reshape(n_dev // pair, -1)
     packed = exchange_sum(packed, ("seq", "head"))
     share = packed[: rows * piece].reshape(rows, piece)
     own_total = packed[rows * piece : rows * piece + rows]
@@ -246,12 +266,12 @@
     attn = jnp.transpose(attn, (1, 0, 2)).reshape(rows, -1)
     partial_out = jnp.dot(attn, w_out, preferred_element_type=f32)
     per_dev = rows // n_seq
-    out_proj = exchange_sum(partial_out.reshape(n_seq, per_dev, -1), "seq")
+    out_proj = seq_sum(partial_out.reshape(n_seq, per_dev, -1))
     out_sq = lax.psum(jnp.sum(out_proj * out_proj, -1), "head")
     x_all = step_tokens.reshape(rows, -1)
     x_f = lax.dynamic_slice_in_dim(x_all, seq_at * per_dev, per_dev, 0).astype(f32)
     state = (x_f + out_proj * lax.rsqrt(out_sq / D + EPS)[:, None] * post_gain).astype(bf16)
-    state_all = exchange_gather(state, "seq", n_seq).reshape(rows, -1)
+    state_all = seq_gather(state).reshape(rows, -1)
     state_f = state_all.astype(f32)
     scaled_two = (state_f * ffn_gain).astype(bf16)
     gate_part = jnp.dot(scaled_two, w_gate, preferred_element_type=f32)
@@ -269,41 +289,43 @@
         * (packed[:, hidden : 2 * hidden] * norm_s)
     ).astype(bf16)
     inner = exchange_gather(inner, "head", n_head).reshape(rows, hidden)
-    ffn_out = exchange_sum(
-        jnp.dot(inner, w_down, preferred_element_type=f32).reshape(n_seq, per_dev, -1), "seq"
-    )
+    ffn_out = seq_sum(jnp.dot(inner, w_down, preferred_element_type=f32).reshape(n_seq, per_dev, -1))
     ffn_sq = lax.psum(jnp.sum(ffn_out * ffn_out, -1), "head")
     result = (
         state.astype(f32) + ffn_out * lax.rsqrt(ffn_sq / D + EPS)[:, None] * final_gain
     ).astype(bf16)
-    result = exchange_gather(result, "seq", n_seq)
+    result = seq_gather(result)
     return result.reshape(steps, groups, beams, -1)
 
 
 def solution(mesh):
+    devices = mesh.devices
+    fine = jax.sharding.Mesh(
+        devices.reshape(devices.shape[0] // 2, 2, devices.shape[1]), ("seq", "pair", "head")
+    )
     return jax.shard_map(
         shards,
-        mesh=mesh,
+        mesh=fine,
         in_specs=(
             P(None, None, None, "head"),
             P(),
-            P(None, "head", "seq", None),
-            P(),
-            P(None, ("seq", "head"), None),
-            P(),
-            P(None, "seq", "head"),
+            P(None, "head", SEQ, None),
+            P(),
+            P(None, ALL, None),
+            P(),
+            P(None, SEQ, "head"),
             P(),
             P("head"),
-            P("head", "seq"),
-            P("head", "seq"),
-            P(),
-            P(),
-            P("seq", "head"),
+            P("head", SEQ),
+            P("head", SEQ),
+            P(),
+            P(),
+            P(SEQ, "head"),
             P("head"),
             P("head"),
-            P("head", "seq"),
-            P("head", "seq"),
-            P("seq", "head"),
+            P("head", SEQ),
+            P("head", SEQ),
+            P(SEQ, "head"),
             P("head"),
         ),
         out_specs=P(None, None, None, "head"),

time: 419 us -> 385 us (0.919)
  blocking collectives: 185 us -> 156 us
  waiting for transfers between devices: 73.6 us -> 64.1 us
  local copies, waits for them, and re-layouts: 73.6 us -> 79.8 us
    all_to_all x3 -> x6, blocking collectives: 91.5 us -> 76.8 us  [exchange_sum(): return jnp.sum(lax.all_to_all(parts, axes, 0, 0, tiled=True), 0)]
    all_to_all x4 -> x6, blocking collectives: 62.4 us -> 48.2 us  [exchange_gather(): return lax.all_to_all(spread, axes, 0, 0, tiled=True)]
    all_to_all x2, waiting for transfers between devices: 32.6 us -> 23.1 us  [exchange_sum(): return jnp.sum(lax.all_to_all(parts, axes, 0, 0, tiled=True), 0)]
    unnamed x84 -> x86, local copies, waits for them, and re-layouts: 13.9 us -> 13.9 us
  transfers between devices with their start and end apart: 6 -> 6, of which waited for: 6 -> 6; matrix products, arithmetic and copies ran while one was open for 13% -> 14% of each run, Pallas kernels for 0% -> 0%
where the time goes in v2:
time: 385 us; the launch traced here: 381 us
  blocking collectives  156 us (41%)
  local copies, waits for them, and re-layouts  79.8 us (21%)
  waiting for transfers between devices  64.1 us (17%)
  other arithmetic  32.3 us (8%)
  matrix products  20 us (5%)
  between operations  15.3 us (4%)
  starting transfers between devices  13 us (3%)
    all_to_all x6, blocking collectives, exchange_sum(): return jnp.sum(lax.all_to_all(parts, axes, 0, 0, tiled=True), 0)  76.8 us
    all_to_all x6, blocking collectives, exchange_gather(): return lax.all_to_all(spread, axes, 0, 0, tiled=True)  48.2 us
    all_to_all x2, waiting for transfers between devices, exchange_sum(): return jnp.sum(lax.all_to_all(parts, axes, 0, 0, tiled=True), 0)  23.1 us
    all_gather x1, waiting for transfers between devices, shards(): lax.all_gather(w_keyval, SEQ, axis=1, tiled=True)  21.2 us
    all_to_all x1, blocking collectives, exchange_max(): return jnp.max(lax.all_to_all(spread, axes, 0, 0, tiled=True), 0)  14.4 us
    unnamed x86, local copies, waits for them, and re-layouts  13.9 us
    gather x6, local copies, waits for them, and re-layouts, shards(): tail_state = jnp.take_along_axis(everyone, picks[:, :, None, None], axis=1)  8.11 us
    all_to_all x2, starting transfers between devices, exchange_sum(): return jnp.sum(lax.all_to_all(parts, axes, 0, 0, tiled=True), 0)  7.77 us
  transfers between devices with their start and end apart: 6, of which 6 were waited for; matrix products, arithmetic and copies ran while one was open for 14% of the time, Pallas kernels for 0%

profile of v2, /device:TPU:0, one launch (start us, length us, event | category | flops | bytes accessed | tf_op | source)
XLA Modules:
  0.0 380.6 jit_solution(6101661912297657892)
XLA Ops:
  8.0 1.4 fusion.24
  10.8 4.2 %all-to-all-start = ((f32[2,96,384]{2,1,0:T(8,128)}), f32[2,96,384]{2,1,0:T(8,128)S(1)}, u32[]{:S(2)}, u32[]{:S(2)}) async-start(f32[2,96,384]{2,1,0:T(8,128)} %bitcast.1), calls=%async_computation | async-start | bytes 589824 | tf_op jit(solution)/shard_map/all_to_all | solution.py:44
  16.0 5.2 %all-to-all-done = f32[2,96,384]{2,1,0:T(8,128)S(1)} async-done(((f32[2,96,384]{2,1,0:T(8,128)}), f32[2,96,384]{2,1,0:T(8,128)S(1)}, u32[]{:S(2)}, u32[]{:S(2)}) %all-to-all-start) | async-done | bytes 294944 | tf_op jit(solution)/shard_map/all_to_all | solution.py:44
  21.5 1.3 broadcast_in_dim.218
  22.9 5.1 %all-to-all-start.1 = ((bf16[32,96,256]{2,1,0:T(8,128)(2,1)}), bf16[32,96,256]{2,1,0:T(8,128)(2,1)S(1)}, u32[]{:S(2)}, u32[]{:S(2)}) async-start(bf16[32,96,256]{2,1,0:T(8,128)(2,1)} %broadcast_in_dim.218), calls=%async_computation.1 | async-start | bytes 3145728 | tf_op jit(solution)/shard_map/all_to_all | solution.py:54
  35.8 6.9 %all-reduce.5 = f32[32]{0:T(128)S(1)} all-reduce(f32[32]{0:T(128)S(1)} %reshape.385), channel_id=3, replica_groups=mesh['seq'=8,'pair'=2,'head'=2] {'head'}, use_global_device_ids=true, to_apply=%region_6.7.clone | all-reduce | flops 32 | bytes 256
  44.2 7.5 %all-gather.5.cloned.1.call-done = bf16[12,8,4,2048]{3,2,1,0:T(4,128)(2,1)} async-done(((bf16[12,4,4,2048]{3,2,1,0:T(4,128)(2,1)}), bf16[12,8,4,2048]{3,2,1,0:T(4,128)(2,1)}) %all-gather.5.cloned.1.call-update) | async-done | bytes 1572880 | tf_op jit(solution)/shard_map/all_gather | solution.py:173
  51.7 3.9 %gather_fusion.2 = bf16[48,4,2048]{2,1,0:T(4,128)(2,1)} fusion(bf16[12,8,4,2048]{3,2,1,0:T(4,128)(2,1)} %all-gather.5.cloned.1.call-done, s32[48]{0:T(128)S(1)} %reshape.490), kind=kCustom, calls=%fused_computation.2.clone | custom fusion | bytes 1573248 | tf_op jit(solution)/shard_map/jit(take_along_axis)/gather | solution.py:193
  55.6 3.9 %gather_fusion.7 = bf16[48,4,2048]{2,1,0:T(4,128)(2,1)} fusion(bf16[12,8,4,2048]{3,2,1,0:T(4,128)(2,1)} %all-gather.5.cloned.1.call-done, s32[48]{0:T(128)S(1)} %reshape.513), kind=kCustom, calls=%fused_computation.7.clone | custom fusion | bytes 1573248 | tf_op jit(solution)/shard_map/jit(take_along_axis)/gather | solution.py:193
  59.5 6.0 %all-to-all-done.1 = bf16[32,96,256]{2,1,0:T(8,128)(2,1)S(1)} async-done(((bf16[32,96,256]{2,1,0:T(8,128)(2,1)}), bf16[32,96,256]{2,1,0:T(8,128)(2,1)S(1)}, u32[]{:S(2)}, u32[]{:S(2)}) %all-to-all-start.1) | async-done | bytes 1572896 | tf_op jit(solution)/shard_map/all_to_all | solution.py:54
  68.4 1.6 copy_convert_fusion
  70.0 2.2 reshape.404
  72.2 1.4 copy.431
  78.5 1.5 mul.312
  81.7 1.6 gather_fusion
  83.3 1.6 gather_fusion.3
  85.7 1.7 gather_fusion.5
  89.0 1.5 select_select_fusion.1
  94.0 21.2 %all-gather.3.cloned.1.call-done = bf16[1280,2048]{1,0:T(8,128)(2,1)} async-done(((bf16[1280,128]{1,0:T(8,128)(2,1)}), bf16[1280,2048]{1,0:T(8,128)(2,1)}) %all-gather.3.cloned.1.call-update) | async-done | bytes 5242896 | tf_op jit(solution)/shard_map/all_gather | solution.py:135
  115.1 4.2 %fusion.84 = f32[32,2048]{1,0:T(8,128)} fusion(bf16[32,1280]{1,0:T(8,128)(2,1)S(1)} %copy-done.13, bf16[1280,2048]{1,0:T(8,128)(2,1)} %all-gather.3.cloned.1.call-done), kind=kOutput, calls=%fused_computation.205 | convolution fusion | flops 167772160 | bytes 5586944 | tf_op jit(solution)/shard_map/dot_general | solution.py:133
  119.4 2.0 fusion.82
  121.4 1.3 copy.432
  124.4 4.9 %reduce-scatter.2.cloned.1.call-done = f32[16,2048]{1,0:T(8,128)} async-done(((f32[32,2048]{1,0:T(8,128)}), f32[16,2048]{1,0:T(8,128)}) %reduce-scatter.2.cloned.1.call-update) | async-done | bytes 131088 | tf_op jit(solution)/shard_map/reduce_scatter | solution.py:139
  130.8 2.0 fusion.1
  133.9 1.5 fusion.81
  135.6 1.6 broadcast_bitcast_fusion.2
  137.2 3.6 reshape.522
  140.8 14.4 %all_to_all.92 = f32[32,1,1536]{2,1,0:T(1,128)} all-to-all(f32[32,1,1536]{2,1,0:T(1,128)S(1)} %reshape.522), channel_id=1, replica_groups=mesh['seq'=8,'pair'=2,'head'=2] {'seq','pair','head'}, dimensions={0} | all-to-all | bytes 393216 | tf_op jit(solution)/shard_map/all_to_all | solution.py:49
  155.6 2.0 reduce.11
  157.7 3.6 reshape.523
  161.3 1.8 bitcast_reduce_fusion
  163.3 1.7 fusion.22
  166.0 1.5 fusion.62
  167.9 1.5 fusion.61
  169.7 1.5 fusion.52
  172.4 1.5 fusion.47
  175.9 2.9 stack.31
  178.7 1.5 fusion.49
  182.2 2.9 stack.30
  185.1 2.7 fusion.7
  187.9 3.9 %reshape.393 = f32[12,4,2,8,2,4,64]{6,5,4,3,2,1,0:T(4,128)} reshape(f32[12,4,32,256]{3,2,1,0:T(8,128)} %fusion.7) | data formatting | bytes 3145728 | tf_op jit(solution)/shard_map/reshape | solution.py:223
  191.7 3.5 fusion.2
  195.3 2.1 copy.472
  197.4 2.4 concatenate.49
  199.9 5.2 %all_to_all.85 = f32[2,8,2,12544]{3,1,2,0:T(8,128)S(1)} all-to-all(f32[2,8,2,12544]{3,1,2,0:T(8,128)S(1)} %maximum_bitcast_fusion), channel_id=1, replica_groups=mesh['seq'=8,'pair'=2,'head'=2] {'pair'}, dimensions={0} | all-to-all | bytes 3211264 | tf_op jit(solution)/shard_map/all_to_all | solution.py:44
  206.2 1.6 copy.479
  209.0 24.8 %all_to_all.93 = f32[16,1,12544]{2,1,0:T(1,128)S(1)} all-to-all(f32[16,1,12544]{2,1,0:T(1,128)S(1)} %all_to_all.68), channel_id=1, replica_groups=mesh['seq'=8,'pair'=2,'head'=2] {'seq','head'}, dimensions={0} | all-to-all | bytes 1605632 | tf_op jit(solution)/shard_map/all_to_all | solution.py:44
  234.6 6.5 %all_to_all.94 = bf16[2,192,64]{1,2,0:T(8,128)(2,1)S(1)} all-to-all(bf16[2,192,64]{1,2,0:T(8,128)(2,1)S(1)} %broadcast_in_dim.238), channel_id=1, replica_groups=mesh['seq'=8,'pair'=2,'head'=2] {'head'}, dimensions={0} | all-to-all | bytes 98304 | tf_op jit(solution)/shard_map/all_to_all | solution.py:54
  242.2 4.5 %all_to_all.86 = f32[2,8,12,1280]{3,1,2,0:T(8,128)S(1)} all-to-all(f32[2,8,12,1280]{3,1,2,0:T(8,128)S(1)} %copy.483), channel_id=1, replica_groups=mesh['seq'=8,'pair'=2,'head'=2] {'pair'}, dimensions={0} | all-to-all | bytes 1966080 | tf_op jit(solution)/shard_map/all_to_all | solution.py:44
  247.8 3.5 all-to-all-start.7
  251.4 17.8 %all-to-all-done.7 = f32[8,12,1280]{2,1,0:T(8,128)S(1)} async-done(((f32[8,12,1280]{2,1,0:T(8,128)}), f32[8,12,1280]{2,1,0:T(8,128)S(1)}, u32[]{:S(2)}, u32[]{:S(2)}) %all-to-all-start.7) | async-done | bytes 491552 | tf_op jit(solution)/shard_map/all_to_all | solution.py:44
  269.4 4.9 %psum.14 = f32[12]{0:T(128)S(1)} all-reduce(f32[12]{0:T(128)S(1)} %multiply_reduce_fusion.3), channel_id=1, replica_groups=mesh['seq'=8,'pair'=2,'head'=2] {'head'}, use_global_device_ids=true, to_apply=%region_21.25 | all-reduce | flops 12 | bytes 96 | tf_op jit(solution)/shard_map/psum | solution.py:270
  275.3 13.3 %all_to_all.87 = bf16[8,12,1280]{2,1,0:T(8,128)(2,1)S(1)} all-to-all(bf16[8,12,1280]{2,1,0:T(8,128)(2,1)S(1)} %broadcast_in_dim.239), channel_id=1, replica_groups=mesh['seq'=8,'pair'=2,'head'=2] {'seq'}, dimensions={0} | all-to-all | bytes 491520 | tf_op jit(solution)/shard_map/all_to_all | solution.py:54
  288.7 4.1 %all_to_all.88 = bf16[2,8,12,1280]{3,1,2,0:T(8,128)(2,1)S(1)} all-to-all(bf16[2,8,12,1280]{3,1,2,0:T(8,128)(2,1)S(1)} %broadcast_in_dim.240), channel_id=1, replica_groups=mesh['seq'=8,'pair'=2,'head'=2] {'pair'}, dimensions={0} | all-to-all | bytes 983040 | tf_op jit(solution)/shard_map/all_to_all | solution.py:54
  293.3 1.4 copy.486
  294.7 1.4 reshape.406
  296.1 2.1 fusion.43
  298.9 17.0 %all_to_all.95 = f32[2,96,1408]{2,1,0:T(8,128)S(1)} all-to-all(f32[2,96,1408]{2,1,0:T(8,128)S(1)} %bitcast.237), channel_id=1, replica_groups=mesh['seq'=8,'pair'=2,'head'=2] {'head'}, dimensions={0} | all-to-all | bytes 2162688 | tf_op jit(solution)/shard_map/all_to_all | solution.py:44
  316.3 7.5 %all_to_all.96 = bf16[2,96,640]{2,1,0:T(8,128)(2,1)S(1)} all-to-all(bf16[2,96,640]{2,1,0:T(8,128)(2,1)S(1)} %broadcast_in_dim.242), channel_id=1, replica_groups=mesh['seq'=8,'pair'=2,'head'=2] {'head'}, dimensions={0} | all-to-all | bytes 491520 | tf_op jit(solution)/shard_map/all_to_all | solution.py:54
  325.1 4.5 %all_to_all.89 = f32[2,8,12,1280]{3,1,2,0:T(8,128)S(1)} all-to-all(f32[2,8,12,1280]{3,1,2,0:T(8,128)S(1)} %copy.489), channel_id=1, replica_groups=mesh['seq'=8,'pair'=2,'head'=2] {'pair'}, dimensions={0} | all-to-all | bytes 1966080 | tf_op jit(solution)/shard_map/all_to_all | solution.py:44
  329.9 20.8 %all_to_all.97 = f32[8,12,1280]{2,1,0:T(8,128)S(1)} all-to-all(f32[8,12,1280]{2,1,0:T(8,128)S(1)} %copy.490), channel_id=1, replica_groups=mesh['seq'=8,'pair'=2,'head'=2] {'seq'}, dimensions={0} | all-to-all | bytes 983040 | tf_op jit(solution)/shard_map/all_to_all | solution.py:44
  350.9 4.9 %psum.15 = f32[12]{0:T(128)S(1)} all-reduce(f32[12]{0:T(128)S(1)} %multiply_reduce_fusion.2), channel_id=1, replica_groups=mesh['seq'=8,'pair'=2,'head'=2] {'head'}, use_global_device_ids=true, to_apply=%region_27.31 | all-reduce | flops 12 | bytes 96 | tf_op jit(solution)/shard_map/psum | solution.py:293
  355.9 12.6 %all_to_all.90 = bf16[8,12,1280]{2,1,0:T(8,128)(2,1)S(1)} all-to-all(bf16[8,12,1280]{2,1,0:T(8,128)(2,1)S(1)} %broadcast_in_dim.243), channel_id=1, replica_groups=mesh['seq'=8,'pair'=2,'head'=2] {'seq'}, dimensions={0} | all-to-all | bytes 491520 | tf_op jit(solution)/shard_map/all_to_all | solution.py:54
  368.7 4.1 %all_to_all.91 = bf16[2,8,12,1280]{3,1,2,0:T(8,128)(2,1)S(1)} all-to-all(bf16[2,8,12,1280]{3,1,2,0:T(8,128)(2,1)S(1)} %broadcast_in_dim.244), channel_id=1, replica_groups=mesh['seq'=8,'pair'=2,'head'=2] {'pair'}, dimensions={0} | all-to-all | bytes 983040 | tf_op jit(solution)/shard_map/all_to_all | solution.py:54
  (273 shorter events, 50.2 us)
Async XLA Ops:
  6.5 317.3 %copy-start = (bf16[640,1280]{1,0:T(8,128)(2,1)S(1)}, bf16[640,1280]{1,0:T(8,128)(2,1)}, u32[]{:S(2)}) copy-start(bf16[640,1280]{1,0:T(8,128)(2,1)} %param.44) | copy-start | bytes 4915204
  6.5 2.9 copy-start.25
  6.5 2.9 copy-start.11
  6.5 2.9 copy-start.34
  6.5 45.1 %all-gather.5.cloned.1.call-start = ((), (), s32[]{:S(2)}) async-start(), calls=%async_computation.19 | async-start | bytes 2359296 | tf_op jit(solution)/shard_map/all_gather | solution.py:173
  7.3 107.8 %all-gather.3.cloned.1.call-start = ((), (), s32[]{:S(2)}) async-start(), calls=%async_computation.17 | async-start | bytes 5570560 | tf_op jit(solution)/shard_map/all_gather | solution.py:135
  9.5 5.6 %copy-start.16 = (bf16[4,8,1280]{2,1,0:T(8,128)(2,1)S(1)}, bf16[4,8,1280]{2,1,0:T(8,128)(2,1)}, u32[]{:S(2)}) copy-start(bf16[4,8,1280]{2,1,0:T(8,128)(2,1)} %param.32) | copy-start | bytes 245764
  9.5 6.5 %copy-start.30 = (f32[256]{0:T(256)S(1)}, f32[256]{0:T(256)}, u32[]{:S(2)}) copy-start(f32[256]{0:T(256)} %param.38) | copy-start | bytes 3076
  10.8 10.5 %all-to-all-start = ((f32[2,96,384]{2,1,0:T(8,128)}), f32[2,96,384]{2,1,0:T(8,128)S(1)}, u32[]{:S(2)}, u32[]{:S(2)}) async-start(f32[2,96,384]{2,1,0:T(8,128)} %bitcast.1), calls=%async_computation | async-start | bytes 589824 | tf_op jit(solution)/shard_map/all_to_all | solution.py:44
  22.8 5.2 %copy-start.28 = (f32[256]{0:T(256)S(1)}, f32[256]{0:T(256)}, u32[]{:S(2)}) copy-start(f32[256]{0:T(256)} %param.37) | copy-start | bytes 3076
  22.9 5.2 %copy-start.18 = (s32[2,12,8]{1,2,0:T(8,128)S(1)}, s32[2,12,8]{1,2,0:T(8,128)}, u32[]{:S(2)}) copy-start(s32[2,12,8]{1,2,0:T(8,128)} %param.27) | copy-start | bytes 2308
  22.9 42.6 %all-to-all-start.1 = ((bf16[32,96,256]{2,1,0:T(8,128)(2,1)}), bf16[32,96,256]{2,1,0:T(8,128)(2,1)S(1)}, u32[]{:S(2)}, u32[]{:S(2)}) async-start(bf16[32,96,256]{2,1,0:T(8,128)(2,1)} %broadcast_in_dim.218), calls=%async_computation.1 | async-start | bytes 3145728 | tf_op jit(solution)/shard_map/all_to_all | solution.py:54
  28.0 101.4 %reduce-scatter.2.cloned.1.call-start = ((), (), s32[]{:S(2)}) async-start(), calls=%async_computation.18 | async-start | bytes 393216 | tf_op jit(solution)/shard_map/reduce_scatter | solution.py:139
  31.4 3.2 copy-start.36
  31.4 12.0 %copy-start.35 = (s32[4]{0:T(128)S(1)}, s32[4]{0:T(128)}, u32[]{:S(2)}) copy-start(s32[4]{0:T(128)} %param.33) | copy-start | bytes 52
  31.4 12.1 %copy-start.33 = (s32[8]{0:T(128)S(1)}, s32[8]{0:T(128)}, u32[]{:S(2)}) copy-start(s32[8]{0:T(128)} %param.31) | copy-start | bytes 100
  31.4 12.1 %copy-start.32 = (s32[12]{0:T(128)S(1)}, s32[12]{0:T(128)}, u32[]{:S(2)}) copy-start(s32[12]{0:T(128)} %param.29) | copy-start | bytes 148
  43.5 119.8 %copy-start.19 = (pred[12,64]{1,0:T(8,128)(4,1)}, pred[12,64]{1,0:T(8,128)(4,1)S(1)}, u32[]{:S(2)}) copy-start(pred[12,64]{1,0:T(8,128)(4,1)S(1)} %pad_add_fusion) | copy-start | bytes 2308
  66.6 0.9 copy-start.1
  75.4 1.1 copy-start.6
  80.6 1.0 copy-start.9
  84.9 2.6 copy-start.21
  85.7 3.3 copy-start.4
  87.5 1.5 copy-start.5
  90.5 2.4 copy-start.2
  90.5 2.4 copy-start.8
  90.5 2.3 copy-start.29
  92.9 22.3 %copy-start.13 = (bf16[32,1280]{1,0:T(8,128)(2,1)S(1)}, bf16[32,1280]{1,0:T(8,128)(2,1)}, u32[]{:S(2)}) copy-start(bf16[32,1280]{1,0:T(8,128)(2,1)} %reshape.384) | copy-start | bytes 245764
  93.9 25.4 %copy-start.24 = (pred[12,4]{1,0:T(8,128)(4,1)S(1)}, pred[12,4]{1,0:T(8,128)(4,1)}, u32[]{:S(2)}) copy-start(pred[12,4]{1,0:T(8,128)(4,1)} %get-tuple-element.39) | copy-start | bytes 148
  119.4 3.7 copy-start.22
  122.7 6.7 %copy-start.31 = (f32[16]{0:T(128)S(1)}, f32[16]{0:T(128)}, u32[]{:S(2)}) copy-start(f32[16]{0:T(128)} %fusion.72) | copy-start | bytes 196
  132.8 1.1 copy-start.10
  163.3 2.7 copy-start.14
  174.9 3.8 %copy-start.23 = (pred[12,4]{1,0:T(8,128)(4,1)S(1)}, pred[12,4]{1,0:T(8,128)(4,1)}, u32[]{:S(2)}) copy-start(pred[12,4]{1,0:T(8,128)(4,1)} %get-tuple-element.37) | copy-start | bytes 148
  181.3 3.9 %copy-start.15 = (f32[12,4,32]{2,1,0:T(4,128)S(1)}, f32[12,4,32]{2,1,0:T(4,128)}, u32[]{:S(2)}) copy-start(f32[12,4,32]{2,1,0:T(4,128)} %copy-done.14) | copy-start | bytes 18436
  181.3 3.9 %copy-start.20 = (pred[12,64]{1,0:T(8,128)(4,1)S(1)}, pred[12,64]{1,0:T(8,128)(4,1)}, u32[]{:S(2)}) copy-start(pred[12,64]{1,0:T(8,128)(4,1)} %copy-done.19) | copy-start | bytes 2308
  187.9 3.9 %copy-start.3 = (f32[12,4,1,8,2,4,64]{6,5,3,4,1,0,2:T(4,128)S(1)}, f32[12,4,1,8,2,4,64]{6,5,3,4,1,0,2:T(4,128)}, u32[]{:S(2)}) copy-start(f32[12,4,1,8,2,4,64]{6,5,3,4,1,0,2:T(4,128)} %stack.31) | copy-start | bytes 2359300
  233.7 7.6 %copy-start.12 = (bf16[128,1280]{1,0:T(8,128)(2,1)S(1)}, bf16[128,1280]{1,0:T(8,128)(2,1)}, u32[]{:S(2)}) copy-start(bf16[128,1280]{1,0:T(8,128)(2,1)} %param.39) | copy-start | bytes 983044
  246.8 27.5 %copy-start.26 = (f32[1280]{0:T(1024)S(1)}, f32[1280]{0:T(1024)}, u32[]{:S(2)}) copy-start(f32[1280]{0:T(1024)} %param.40) | copy-start | bytes 15364
  247.8 21.4 %all-to-all-start.7 = ((f32[8,12,1280]{2,1,0:T(8,128)}), f32[8,12,1280]{2,1,0:T(8,128)S(1)}, u32[]{:S(2)}, u32[]{:S(2)}) async-start(f32[8,12,1280]{2,1,0:T(8,128)} %copy.484), calls=%async_computation.8 | async-start | bytes 1310720 | tf_op jit(solution)/shard_map/all_to_all | solution.py:44
  294.7 1.4 copy-start.17
  296.1 2.1 copy-start.7
  329.7 26.1 %copy-start.27 = (f32[1280]{0:T(1024)S(1)}, f32[1280]{0:T(1024)}, u32[]{:S(2)}) copy-start(f32[1280]{0:T(1024)} %param.45) | copy-start | bytes 15364
Sparse Core Ops, SparseCore 0:
  8.9 42.7 all-gather.4
  53.8 61.2 all-gather.2
  119.5 9.8 reduce-scatter.1

commit v3 on v2

--- a/solution.py
+++ b/solution.py
@@ -10,8 +10,9 @@
 QD = 2048
 
 
-SEQ = ("seq", "pair")
-ALL = ("seq", "pair", "head")
+SEQ = ("seq", "mid", "pair")
+ALL = ("seq", "mid", "pair", "head")
+LEVELS = ("pair", "mid")
 
 EPS = 1e-06
 NEG = -1e30
@@ -54,18 +55,26 @@
     return lax.all_to_all(spread, axes, 0, 0, tiled=True)
 
 
+def seq_size():
+    size = lax.axis_size("seq")
+    for level in LEVELS:
+        size = size * lax.axis_size(level)
+    return size
+
+
 def seq_sum(parts):
-    pair = lax.axis_size("pair")
-    parts = parts.reshape((parts.shape[0] // pair, pair) + parts.shape[1:])
-    parts = exchange_sum(jnp.swapaxes(parts, 0, 1), "pair")
+    for level in LEVELS:
+        parts = parts.reshape((-1, lax.axis_size(level)) + parts.shape[1:])
+        parts = exchange_sum(jnp.swapaxes(parts, 0, 1), level)
     return exchange_sum(parts, "seq")
 
 
 def seq_gather(piece):
-    pair = lax.axis_size("pair")
-    outer = lax.axis_size("seq")
-    got = exchange_gather(exchange_gather(piece, "seq", outer), "pair", pair)
-    return jnp.swapaxes(got, 0, 1).reshape((outer * pair,) + piece.shape)
+    got = exchange_gather(piece, "seq", lax.axis_size("seq"))
+    for level in LEVELS[::-1]:
+        got = exchange_gather(got, level, lax.axis_size(level))
+        got = jnp.swapaxes(got, 0, 1).reshape((-1,) + piece.shape)
+    return got
 
 
 def project_tokens(tokens, in_gain, w_query, w_keyval, q_gain, k_gain):
@@ -75,7 +84,7 @@
     kv_part = jnp.dot(scaled, w_keyval, preferred_element_type=jnp.float32)
     squares = jnp.sum(flat * flat, -1)
     n_head = lax.axis_size("head")
-    n_seq = lax.axis_size("seq") * lax.axis_size("pair")
+    n_seq = seq_size()
     rows = flat.shape[0]
     half = rows // n_head
     block = q_part.shape[1]
@@ -120,8 +129,10 @@
     f32 = jnp.float32
     bf16 = jnp.bfloat16
     n_head = lax.axis_size("head")
-    n_seq = lax.axis_size("seq") * lax.axis_size("pair")
-    seq_at = lax.axis_index("seq") * lax.axis_size("pair") + lax.axis_index("pair")
+    n_seq = seq_size()
+    seq_at = lax.axis_index("seq")
+    for level in LEVELS[::-1]:
+        seq_at = seq_at * lax.axis_size(level) + lax.axis_index(level)
     head_at = lax.axis_index("head")
     flat_at = seq_at * n_head + head_at
     steps, groups, beams, width = step_tokens.shape
@@ -255,9 +266,9 @@
     total = jnp.repeat(jnp.transpose(total, (1, 4, 2, 0, 3)).reshape(QH, rows), per_head, 0)
     lanes = -(-rows // 128) * 128
     packed = jnp.concatenate([weighted, jnp.pad(total, ((0, 0), (0, lanes - rows)))], 1)
-    pair = lax.axis_size("pair")
-    packed = packed.reshape(n_seq // pair, pair, n_head, -1)
-    packed = exchange_sum(jnp.swapaxes(packed, 0, 1), "pair").reshape(n_dev // pair, -1)
+    for level in LEVELS:
+        packed = packed.reshape(-1, lax.axis_size(level), n_head, packed.shape[-1])
+        packed = exchange_sum(jnp.swapaxes(packed, 0, 1), level).reshape(-1, packed.shape[-1])
     packed = exchange_sum(packed, ("seq", "head"))
     share = packed[: rows * piece].reshape(rows, piece)
     own_total = packed[rows * piece : rows * piece + rows]
@@ -301,7 +312,7 @@
 def solution(mesh):
     devices = mesh.devices
     fine = jax.sharding.Mesh(
-        devices.reshape(devices.shape[0] // 2, 2, devices.shape[1]), ("seq", "pair", "head")
+        devices.reshape(devices.shape[0] // 4, 2, 2, devices.shape[1]), ALL
     )
     return jax.shard_map(
         shards,

time: 385 us -> 403 us (1.047)
  blocking collectives: 156 us -> 180 us
  waiting for transfers between devices: 64.1 us -> 56.1 us
    all_to_all x6 -> x9, blocking collectives: 76.8 us -> 93.1 us  [exchange_sum(): return jnp.sum(lax.all_to_all(parts, axes, 0, 0, tiled=True), 0)]
    all_to_all x2, waiting for transfers between devices: 23.1 us -> 15.3 us  [exchange_sum(): return jnp.sum(lax.all_to_all(parts, axes, 0, 0, tiled=True), 0)]
    all_to_all x6 -> x8, blocking collectives: 48.2 us -> 55.5 us  [exchange_gather(): return lax.all_to_all(spread, axes, 0, 0, tiled=True)]
  transfers between devices with their start and end apart: 6 -> 6, of which waited for: 6 -> 6; matrix products, arithmetic and copies ran while one was open for 14% -> 13% of each run, Pallas kernels for 0% -> 0%
where the time goes in v3:
time: 403 us; the launch traced here: 398 us
  blocking collectives  180 us (45%)
  local copies, waits for them, and re-layouts  81.2 us (20%)
  waiting for transfers between devices  56.1 us (14%)
  other arithmetic  33.1 us (8%)
  matrix products  20 us (5%)
  between operations  15.4 us (4%)
  starting transfers between devices  12.9 us (3%)
    all_to_all x9, blocking collectives, exchange_sum(): return jnp.sum(lax.all_to_all(parts, axes, 0, 0, tiled=True), 0)  93.1 us
    all_to_all x8, blocking collectives, exchange_gather(): return lax.all_to_all(spread, axes, 0, 0, tiled=True)  55.5 us
    all_gather x1, waiting for transfers between devices, shards(): lax.all_gather(w_keyval, SEQ, axis=1, tiled=True)  20.8 us
    all_to_all x2, waiting for transfers between devices, exchange_sum(): return jnp.sum(lax.all_to_all(parts, axes, 0, 0, tiled=True), 0)  15.3 us
    all_to_all x1, blocking collectives, exchange_max(): return jnp.max(lax.all_to_all(spread, axes, 0, 0, tiled=True), 0)  14.3 us
    unnamed x86, local copies, waits for them, and re-layouts  13.9 us
    gather x6, local copies, waits for them, and re-layouts, shards(): tail_state = jnp.take_along_axis(everyone, picks[:, :, None, None], axis=1)  8.11 us
  transfers between devices with their start and end apart: 6, of which 6 were waited for; matrix products, arithmetic and copies ran while one was open for 13% of the time, Pallas kernels for 0%

profile of v3, /device:TPU:0, one launch (start us, length us, event | category | flops | bytes accessed | tf_op | source)
XLA Modules:
  0.0 398.4 jit_solution(4759765070381839862)
XLA Ops:
  10.8 4.2 %all-to-all-start = ((f32[2,96,384]{2,1,0:T(8,128)}), f32[2,96,384]{2,1,0:T(8,128)S(1)}, u32[]{:S(2)}, u32[]{:S(2)}) async-start(f32[2,96,384]{2,1,0:T(8,128)} %bitcast.1), calls=%async_computation | async-start | bytes 589824 | tf_op jit(solution)/shard_map/all_to_all | solution.py:45
  16.0 5.2 %all-to-all-done = f32[2,96,384]{2,1,0:T(8,128)S(1)} async-done(((f32[2,96,384]{2,1,0:T(8,128)}), f32[2,96,384]{2,1,0:T(8,128)S(1)}, u32[]{:S(2)}, u32[]{:S(2)}) %all-to-all-start) | async-done | bytes 294944 | tf_op jit(solution)/shard_map/all_to_all | solution.py:45
  22.9 5.1 %all-to-all-start.1 = ((bf16[32,96,256]{2,1,0:T(8,128)(2,1)}), bf16[32,96,256]{2,1,0:T(8,128)(2,1)S(1)}, u32[]{:S(2)}, u32[]{:S(2)}) async-start(bf16[32,96,256]{2,1,0:T(8,128)(2,1)} %broadcast_in_dim.232), calls=%async_computation.1 | async-start | bytes 3145728 | tf_op jit(solution)/shard_map/all_to_all | solution.py:55
  35.8 6.8 %all-reduce.5 = f32[32]{0:T(128)S(1)} all-reduce(f32[32]{0:T(128)S(1)} %reshape.393), channel_id=3, replica_groups=mesh['seq'=4,'mid'=2,'pair'=2,'head'=2] {'head'}, use_global_device_ids=true, to_apply=%region_6.7.clone | all-reduce | flops 32 | bytes 256
  44.1 7.6 %all-gather.5.cloned.1.call-done = bf16[12,8,4,2048]{3,2,1,0:T(4,128)(2,1)} async-done(((bf16[12,4,4,2048]{3,2,1,0:T(4,128)(2,1)}), bf16[12,8,4,2048]{3,2,1,0:T(4,128)(2,1)}) %all-gather.5.cloned.1.call-update) | async-done | bytes 1572880 | tf_op jit(solution)/shard_map/all_gather | solution.py:184
  51.7 3.9 gather_fusion.2
  55.6 3.9 gather_fusion.7
  59.5 6.0 %all-to-all-done.1 = bf16[32,96,256]{2,1,0:T(8,128)(2,1)S(1)} async-done(((bf16[32,96,256]{2,1,0:T(8,128)(2,1)}), bf16[32,96,256]{2,1,0:T(8,128)(2,1)S(1)}, u32[]{:S(2)}, u32[]{:S(2)}) %all-to-all-start.1) | async-done | bytes 1572896 | tf_op jit(solution)/shard_map/all_to_all | solution.py:55
  68.4 1.6 copy_convert_fusion
  70.0 2.2 reshape.414
  78.5 1.5 mul.316
  81.6 1.6 gather_fusion
  83.3 1.6 gather_fusion.3
  85.7 2.1 gather_fusion.5
  89.3 1.5 select_select_fusion.1
  94.3 20.8 %all-gather.3.cloned.1.call-done = bf16[1280,2048]{1,0:T(8,128)(2,1)} async-done(((bf16[1280,128]{1,0:T(8,128)(2,1)}), bf16[1280,2048]{1,0:T(8,128)(2,1)}) %all-gather.3.cloned.1.call-update) | async-done | bytes 5242896 | tf_op jit(solution)/shard_map/all_gather | solution.py:146
  115.1 4.2 %fusion.84 = f32[32,2048]{1,0:T(8,128)} fusion(bf16[32,1280]{1,0:T(8,128)(2,1)S(1)} %copy-done.13, bf16[1280,2048]{1,0:T(8,128)(2,1)} %all-gather.3.cloned.1.call-done), kind=kOutput, calls=%fused_computation.206 | convolution fusion | flops 167772160 | bytes 5586944 | tf_op jit(solution)/shard_map/dot_general | solution.py:144
  119.4 2.0 fusion.82
  124.4 5.0 %reduce-scatter.2.cloned.1.call-done = f32[16,2048]{1,0:T(8,128)} async-done(((f32[32,2048]{1,0:T(8,128)}), f32[16,2048]{1,0:T(8,128)}) %reduce-scatter.2.cloned.1.call-update) | async-done | bytes 131088 | tf_op jit(solution)/shard_map/reduce_scatter | solution.py:150
  130.8 2.0 fusion.1
  134.0 1.5 fusion.81
  135.6 1.6 broadcast_bitcast_fusion.2
  137.2 3.6 reshape.532
  140.8 14.3 %all_to_all.118 = f32[32,1,1536]{2,1,0:T(1,128)} all-to-all(f32[32,1,1536]{2,1,0:T(1,128)S(1)} %reshape.532), channel_id=1, replica_groups=mesh['seq'=4,'mid'=2,'pair'=2,'head'=2] {'seq','mid','pair','head'}, dimensions={0} | all-to-all | bytes 393216 | tf_op jit(solution)/shard_map/all_to_all | solution.py:50
  155.6 2.0 reduce.11
  157.7 3.6 reshape.533
  161.3 1.8 bitcast_reduce_fusion
  163.3 1.7 fusion.22
  166.0 1.5 fusion.62
  167.9 1.5 fusion.61
  169.6 1.5 fusion.52
  172.4 1.5 fusion.47
  175.9 2.9 stack.31
  178.7 1.5 fusion.49
  182.2 2.9 stack.30
  185.1 2.7 fusion.7
  187.8 3.9 reshape.401
  191.7 3.5 fusion.2
  195.3 2.1 copy.490
  197.4 2.4 concatenate.49
  199.9 5.0 %all_to_all.109 = f32[2,8,2,12544]{3,1,2,0:T(8,128)S(1)} all-to-all(f32[2,8,2,12544]{3,1,2,0:T(8,128)S(1)} %maximum_bitcast_fusion), channel_id=1, replica_groups=mesh['seq'=4,'mid'=2,'pair'=2,'head'=2] {'pair'}, dimensions={0} | all-to-all | bytes 3211264 | tf_op jit(solution)/shard_map/all_to_all | solution.py:45
  206.0 1.6 reshape_reshape.4
  208.0 14.1 %all_to_all.119 = f32[2,4,2,12544]{3,2,1,0:T(2,128)S(1)} all-to-all(f32[2,4,2,12544]{3,2,1,0:T(2,128)S(1)} %bitcast.255), channel_id=1, replica_groups=mesh['seq'=4,'mid'=2,'pair'=2,'head'=2] {'mid'}, dimensions={0} | all-to-all | bytes 1605632 | tf_op jit(solution)/shard_map/all_to_all | solution.py:45
  223.5 14.4 %all_to_all.120 = f32[8,1,12544]{2,1,0:T(1,128)S(1)} all-to-all(f32[8,1,12544]{2,1,0:T(1,128)S(1)} %all_to_all.71), channel_id=1, replica_groups=mesh['seq'=4,'mid'=2,'pair'=2,'head'=2] {'seq','head'}, dimensions={0} | all-to-all | bytes 802816 | tf_op jit(solution)/shard_map/all_to_all | solution.py:45
  238.5 6.5 %all_to_all.121 = bf16[2,192,64]{1,2,0:T(8,128)(2,1)S(1)} all-to-all(bf16[2,192,64]{1,2,0:T(8,128)(2,1)S(1)} %broadcast_in_dim.252), channel_id=1, replica_groups=mesh['seq'=4,'mid'=2,'pair'=2,'head'=2] {'head'}, dimensions={0} | all-to-all | bytes 98304 | tf_op jit(solution)/shard_map/all_to_all | solution.py:55
  246.2 4.5 %all_to_all.110 = f32[2,8,12,1280]{3,1,2,0:T(8,128)S(1)} all-to-all(f32[2,8,12,1280]{3,1,2,0:T(8,128)S(1)} %copy.500), channel_id=1, replica_groups=mesh['seq'=4,'mid'=2,'pair'=2,'head'=2] {'pair'}, dimensions={0} | all-to-all | bytes 1966080 | tf_op jit(solution)/shard_map/all_to_all | solution.py:45
  251.2 10.6 %all_to_all.122 = f32[2,4,12,1280]{3,1,2,0:T(4,128)S(1)} all-to-all(f32[2,4,12,1280]{3,1,2,0:T(4,128)S(1)} %copy.501), channel_id=1, replica_groups=mesh['seq'=4,'mid'=2,'pair'=2,'head'=2] {'mid'}, dimensions={0} | all-to-all | bytes 983040 | tf_op jit(solution)/shard_map/all_to_all | solution.py:45
  262.8 3.5 all-to-all-start.9
  266.2 10.0 %all-to-all-done.9 = f32[4,12,1280]{2,1,0:T(8,128)S(1)} async-done(((f32[4,12,1280]{2,1,0:T(8,128)}), f32[4,12,1280]{2,1,0:T(8,128)S(1)}, u32[]{:S(2)}, u32[]{:S(2)}) %all-to-all-start.9) | async-done | bytes 245792 | tf_op jit(solution)/shard_map/all_to_all | solution.py:45
  276.4 4.9 %psum.14 = f32[12]{0:T(128)S(1)} all-reduce(f32[12]{0:T(128)S(1)} %multiply_reduce_fusion.3), channel_id=1, replica_groups=mesh['seq'=4,'mid'=2,'pair'=2,'head'=2] {'head'}, use_global_device_ids=true, to_apply=%region_23.27 | all-reduce | flops 12 | bytes 96 | tf_op jit(solution)/shard_map/psum | solution.py:281
  282.3 9.2 %all_to_all.111 = bf16[4,12,1280]{2,1,0:T(8,128)(2,1)S(1)} all-to-all(bf16[4,12,1280]{2,1,0:T(8,128)(2,1)S(1)} %broadcast_in_dim.253), channel_id=1, replica_groups=mesh['seq'=4,'mid'=2,'pair'=2,'head'=2] {'seq'}, dimensions={0} | all-to-all | bytes 245760 | tf_op jit(solution)/shard_map/all_to_all | solution.py:55
  291.6 7.5 %all_to_all.112 = bf16[2,4,12,1280]{3,1,2,0:T(4,128)(2,1)S(1)} all-to-all(bf16[2,4,12,1280]{3,1,2,0:T(4,128)(2,1)S(1)} %broadcast_in_dim.254), channel_id=1, replica_groups=mesh['seq'=4,'mid'=2,'pair'=2,'head'=2] {'mid'}, dimensions={0} | all-to-all | bytes 491520 | tf_op jit(solution)/shard_map/all_to_all | solution.py:55
  299.4 4.1 %all_to_all.113 = bf16[2,8,12,1280]{3,1,2,0:T(8,128)(2,1)S(1)} all-to-all(bf16[2,8,12,1280]{3,1,2,0:T(8,128)(2,1)S(1)} %broadcast_in_dim.256), channel_id=1, replica_groups=mesh['seq'=4,'mid'=2,'pair'=2,'head'=2] {'pair'}, dimensions={0} | all-to-all | bytes 983040 | tf_op jit(solution)/shard_map/all_to_all | solution.py:55
  305.4 1.4 reshape.416
  306.9 2.1 fusion.43
  309.6 17.0 %all_to_all.123 = f32[2,96,1408]{2,1,0:T(8,128)S(1)} all-to-all(f32[2,96,1408]{2,1,0:T(8,128)S(1)} %bitcast.254), channel_id=1, replica_groups=mesh['seq'=4,'mid'=2,'pair'=2,'head'=2] {'head'}, dimensions={0} | all-to-all | bytes 2162688 | tf_op jit(solution)/shard_map/all_to_all | solution.py:45
  327.1 7.5 %all_to_all.124 = bf16[2,96,640]{2,1,0:T(8,128)(2,1)S(1)} all-to-all(bf16[2,96,640]{2,1,0:T(8,128)(2,1)S(1)} %broadcast_in_dim.258), channel_id=1, replica_groups=mesh['seq'=4,'mid'=2,'pair'=2,'head'=2] {'head'}, dimensions={0} | all-to-all | bytes 491520 | tf_op jit(solution)/shard_map/all_to_all | solution.py:55
  335.9 4.5 %all_to_all.114 = f32[2,8,12,1280]{3,1,2,0:T(8,128)S(1)} all-to-all(f32[2,8,12,1280]{3,1,2,0:T(8,128)S(1)} %copy.508), channel_id=1, replica_groups=mesh['seq'=4,'mid'=2,'pair'=2,'head'=2] {'pair'}, dimensions={0} | all-to-all | bytes 1966080 | tf_op jit(solution)/shard_map/all_to_all | solution.py:45
  340.9 10.6 %all_to_all.125 = f32[2,4,12,1280]{3,1,2,0:T(4,128)S(1)} all-to-all(f32[2,4,12,1280]{3,1,2,0:T(4,128)S(1)} %copy.509), channel_id=1, replica_groups=mesh['seq'=4,'mid'=2,'pair'=2,'head'=2] {'mid'}, dimensions={0} | all-to-all | bytes 983040 | tf_op jit(solution)/shard_map/all_to_all | solution.py:45
  351.7 12.4 %all_to_all.126 = f32[4,12,1280]{2,1,0:T(8,128)S(1)} all-to-all(f32[4,12,1280]{2,1,0:T(8,128)S(1)} %copy.510), channel_id=1, replica_groups=mesh['seq'=4,'mid'=2,'pair'=2,'head'=2] {'seq'}, dimensions={0} | all-to-all | bytes 491520 | tf_op jit(solution)/shard_map/all_to_all | solution.py:45
  364.3 4.9 %psum.15 = f32[12]{0:T(128)S(1)} all-reduce(f32[12]{0:T(128)S(1)} %multiply_reduce_fusion.2), channel_id=1, replica_groups=mesh['seq'=4,'mid'=2,'pair'=2,'head'=2] {'head'}, use_global_device_ids=true, to_apply=%region_30.34 | all-reduce | flops 12 | bytes 96 | tf_op jit(solution)/shard_map/psum | solution.py:304
  369.3 9.2 %all_to_all.115 = bf16[4,12,1280]{2,1,0:T(8,128)(2,1)S(1)} all-to-all(bf16[4,12,1280]{2,1,0:T(8,128)(2,1)S(1)} %broadcast_in_dim.259), channel_id=1, replica_groups=mesh['seq'=4,'mid'=2,'pair'=2,'head'=2] {'seq'}, dimensions={0} | all-to-all | bytes 245760 | tf_op jit(solution)/shard_map/all_to_all | solution.py:55
  378.7 7.5 %all_to_all.116 = bf16[2,4,12,1280]{3,1,2,0:T(4,128)(2,1)S(1)} all-to-all(bf16[2,4,12,1280]{3,1,2,0:T(4,128)(2,1)S(1)} %broadcast_in_dim.260), channel_id=1, replica_groups=mesh['seq'=4,'mid'=2,'pair'=2,'head'=2] {'mid'}, dimensions={0} | all-to-all | bytes 491520 | tf_op jit(solution)/shard_map/all_to_all | solution.py:55
  386.5 4.1 %all_to_all.117 = bf16[2,8,12,1280]{3,1,2,0:T(8,128)(2,1)S(1)} all-to-all(bf16[2,8,12,1280]{3,1,2,0:T(8,128)(2,1)S(1)} %broadcast_in_dim.262), channel_id=1, replica_groups=mesh['seq'=4,'mid'=2,'pair'=2,'head'=2] {'pair'}, dimensions={0} | all-to-all | bytes 983040 | tf_op jit(solution)/shard_map/all_to_all | solution.py:55
  (292 shorter events, 58.8 us)
Async XLA Ops:
  6.5 328.0 %copy-start = (bf16[640,1280]{1,0:T(8,128)(2,1)S(1)}, bf16[640,1280]{1,0:T(8,128)(2,1)}, u32[]{:S(2)}) copy-start(bf16[640,1280]{1,0:T(8,128)(2,1)} %param.44) | copy-start | bytes 4915204
  6.5 2.9 copy-start.25
  6.5 2.9 copy-start.11
  6.5 2.9 copy-start.34
  6.5 45.2 %all-gather.5.cloned.1.call-start = ((), (), s32[]{:S(2)}) async-start(), calls=%async_computation.24 | async-start | bytes 2359296 | tf_op jit(solution)/shard_map/all_gather | solution.py:184
  7.3 107.8 %all-gather.3.cloned.1.call-start = ((), (), s32[]{:S(2)}) async-start(), calls=%async_computation.22 | async-start | bytes 5570560 | tf_op jit(solution)/shard_map/all_gather | solution.py:146
  9.5 5.6 %copy-start.16 = (bf16[4,8,1280]{2,1,0:T(8,128)(2,1)S(1)}, bf16[4,8,1280]{2,1,0:T(8,128)(2,1)}, u32[]{:S(2)}) copy-start(bf16[4,8,1280]{2,1,0:T(8,128)(2,1)} %param.32) | copy-start | bytes 245764
  9.5 6.5 %copy-start.30 = (f32[256]{0:T(256)S(1)}, f32[256]{0:T(256)}, u32[]{:S(2)}) copy-start(f32[256]{0:T(256)} %param.38) | copy-start | bytes 3076
  10.8 10.5 %all-to-all-start = ((f32[2,96,384]{2,1,0:T(8,128)}), f32[2,96,384]{2,1,0:T(8,128)S(1)}, u32[]{:S(2)}, u32[]{:S(2)}) async-start(f32[2,96,384]{2,1,0:T(8,128)} %bitcast.1), calls=%async_computation | async-start | bytes 589824 | tf_op jit(solution)/shard_map/all_to_all | solution.py:45
  22.8 5.2 %copy-start.28 = (f32[256]{0:T(256)S(1)}, f32[256]{0:T(256)}, u32[]{:S(2)}) copy-start(f32[256]{0:T(256)} %param.37) | copy-start | bytes 3076
  22.8 5.2 %copy-start.18 = (s32[2,12,8]{1,2,0:T(8,128)S(1)}, s32[2,12,8]{1,2,0:T(8,128)}, u32[]{:S(2)}) copy-start(s32[2,12,8]{1,2,0:T(8,128)} %param.27) | copy-start | bytes 2308
  22.9 42.6 %all-to-all-start.1 = ((bf16[32,96,256]{2,1,0:T(8,128)(2,1)}), bf16[32,96,256]{2,1,0:T(8,128)(2,1)S(1)}, u32[]{:S(2)}, u32[]{:S(2)}) async-start(bf16[32,96,256]{2,1,0:T(8,128)(2,1)} %broadcast_in_dim.232), calls=%async_computation.1 | async-start | bytes 3145728 | tf_op jit(solution)/shard_map/all_to_all | solution.py:55
  28.0 101.4 %reduce-scatter.2.cloned.1.call-start = ((), (), s32[]{:S(2)}) async-start(), calls=%async_computation.23 | async-start | bytes 393216 | tf_op jit(solution)/shard_map/reduce_scatter | solution.py:150
  31.3 3.2 copy-start.36
  31.4 11.9 %copy-start.35 = (s32[4]{0:T(128)S(1)}, s32[4]{0:T(128)}, u32[]{:S(2)}) copy-start(s32[4]{0:T(128)} %param.33) | copy-start | bytes 52
  31.4 12.0 %copy-start.33 = (s32[8]{0:T(128)S(1)}, s32[8]{0:T(128)}, u32[]{:S(2)}) copy-start(s32[8]{0:T(128)} %param.31) | copy-start | bytes 100
  31.4 12.1 %copy-start.32 = (s32[12]{0:T(128)S(1)}, s32[12]{0:T(128)}, u32[]{:S(2)}) copy-start(s32[12]{0:T(128)} %param.29) | copy-start | bytes 148
  43.4 119.9 %copy-start.19 = (pred[12,64]{1,0:T(8,128)(4,1)}, pred[12,64]{1,0:T(8,128)(4,1)S(1)}, u32[]{:S(2)}) copy-start(pred[12,64]{1,0:T(8,128)(4,1)S(1)} %pad_add_fusion) | copy-start | bytes 2308
  66.6 0.9 copy-start.1
  75.4 1.1 copy-start.6
  80.6 1.0 copy-start.9
  84.9 3.0 copy-start.21
  85.7 3.6 copy-start.4
  87.9 1.5 copy-start.5
  90.8 2.4 copy-start.2
  90.8 2.4 copy-start.8
  90.8 2.3 copy-start.29
  93.2 21.9 %copy-start.13 = (bf16[32,1280]{1,0:T(8,128)(2,1)S(1)}, bf16[32,1280]{1,0:T(8,128)(2,1)}, u32[]{:S(2)}) copy-start(bf16[32,1280]{1,0:T(8,128)(2,1)} %reshape.392) | copy-start | bytes 245764
  94.3 25.1 %copy-start.24 = (pred[12,4]{1,0:T(8,128)(4,1)S(1)}, pred[12,4]{1,0:T(8,128)(4,1)}, u32[]{:S(2)}) copy-start(pred[12,4]{1,0:T(8,128)(4,1)} %get-tuple-element.39) | copy-start | bytes 148
  119.4 3.7 copy-start.22
  122.7 6.7 %copy-start.31 = (f32[16]{0:T(128)S(1)}, f32[16]{0:T(128)}, u32[]{:S(2)}) copy-start(f32[16]{0:T(128)} %fusion.72) | copy-start | bytes 196
  132.8 1.1 copy-start.10
  163.3 2.7 copy-start.14
  174.9 3.8 copy-start.23
  181.3 3.9 copy-start.15
  181.3 3.9 copy-start.20
  187.8 3.9 copy-start.3
  222.9 22.4 %copy-start.12 = (bf16[128,1280]{1,0:T(8,128)(2,1)S(1)}, bf16[128,1280]{1,0:T(8,128)(2,1)}, u32[]{:S(2)}) copy-start(bf16[128,1280]{1,0:T(8,128)(2,1)} %param.39) | copy-start | bytes 983044
  251.2 30.1 %copy-start.26 = (f32[1280]{0:T(1024)S(1)}, f32[1280]{0:T(1024)}, u32[]{:S(2)}) copy-start(f32[1280]{0:T(1024)} %param.40) | copy-start | bytes 15364
  262.8 13.5 %all-to-all-start.9 = ((f32[4,12,1280]{2,1,0:T(8,128)}), f32[4,12,1280]{2,1,0:T(8,128)S(1)}, u32[]{:S(2)}, u32[]{:S(2)}) async-start(f32[4,12,1280]{2,1,0:T(8,128)} %copy.502), calls=%async_computation.10 | async-start | bytes 655360 | tf_op jit(solution)/shard_map/all_to_all | solution.py:45
  305.4 1.4 copy-start.17
  306.9 2.1 copy-start.7
  340.9 28.3 %copy-start.27 = (f32[1280]{0:T(1024)S(1)}, f32[1280]{0:T(1024)}, u32[]{:S(2)}) copy-start(f32[1280]{0:T(1024)} %param.45) | copy-start | bytes 15364
Sparse Core Ops, SparseCore 0:
  8.9 42.7 all-gather.4
  53.9 61.2 all-gather.2
  119.5 9.8 reduce-scatter.1

commit v4 on v2

--- a/solution.py
+++ b/solution.py
@@ -127,21 +127,31 @@
     steps, groups, beams, width = step_tokens.shape
     pre = prompt_states.shape[0]
     repeat = QH // KVH
-    rows = jnp.transpose(prompt_states, (1, 0, 2)).astype(f32)
-    prompt_scaled = (rows * in_gain).astype(bf16).reshape(-1, width)
-    prompt_squares = jnp.sum(rows * rows, -1).reshape(-1)
-    prompt_terms = jnp.dot(
-        prompt_scaled,
-        lax.all_gather(w_keyval, SEQ, axis=1, tiled=True),
-        preferred_element_type=f32,
-    )
-    prompt_sum, prompt_sq = (
-        lax.psum_scatter(prompt_terms, "head", scatter_dimension=0, tiled=True),
-        lax.psum_scatter(prompt_squares, "head", scatter_dimension=0, tiled=True),
-    )
+    owners = n_seq * n_head
+    prompt_all = lax.all_gather(prompt_states, SEQ, axis=1, tiled=True).astype(f32)
+    prompt_seg = prompt_all.shape[1] // owners
+    prompt_scaled = (prompt_all * in_gain).astype(bf16).reshape(-1, width)
+    prompt_terms = jnp.dot(prompt_scaled, w_keyval, preferred_element_type=f32)
+    kv_cols = prompt_terms.shape[1]
+    prompt_terms = jnp.transpose(
+        prompt_terms.reshape(pre, owners, prompt_seg, kv_cols), (1, 0, 2, 3)
+    ).reshape(owners, -1)
+    prompt_squares = jnp.transpose(
+        jnp.sum(prompt_all * prompt_all, -1).reshape(pre, owners, prompt_seg), (1, 0, 2)
+    ).reshape(owners, -1)
+    own_rows = pre * prompt_seg
+    pad_rows = -(-own_rows // 128) * 128
+    prompt_terms = jnp.concatenate(
+        [prompt_terms, jnp.pad(prompt_squares, ((0, 0), (0, pad_rows - own_rows)))], 1
+    )
+    prompt_terms = lax.all_to_all(prompt_terms, ALL, 0, 0, tiled=True)
+    prompt_terms = jnp.sum(prompt_terms.reshape(n_seq, n_head, -1), 1)
+    prompt_sq = prompt_terms[0, own_rows * kv_cols : own_rows * kv_cols + own_rows]
+    prompt_sum = jnp.transpose(
+        prompt_terms[:, : own_rows * kv_cols].reshape(n_seq, own_rows, kv_cols), (1, 0, 2)
+    ).reshape(own_rows, -1)
     prompt_pairs = finish_keys(prompt_sum * lax.rsqrt(prompt_sq / D + EPS)[:, None], k_gain)
-    prompt_seg = prompt_pairs.shape[0] // pre
-    prompt_pairs = jnp.transpose(prompt_pairs.reshape(prompt_seg, pre, -1), (1, 0, 2))
+    prompt_pairs = prompt_pairs.reshape(pre, prompt_seg, -1)
     prompt_ok = (flat_at * prompt_seg + jnp.arange(prompt_seg))[None, :] < prompt_len[:, None]
     cache_seg = cache.shape[1]
     cache_ok = (flat_at * cache_seg + jnp.arange(cache_seg))[None, :] < cache_len[:, None]

time: 385 us -> 391 us (1.016)
  waiting for transfers between devices: 64.1 us -> 72.4 us
  blocking collectives: 156 us -> 148 us
  other arithmetic: 32.3 us -> 39.4 us
  matrix products: 20 us -> 14.5 us
    all_to_all x0 -> x1, waiting for transfers between devices: none -> 10.2 us  [shards(): prompt_terms = lax.all_to_all(prompt_terms, ALL, 0, 0, tiled=True)]
    all_gather x1, waiting for transfers between devices: 21.2 us -> 29.1 us  [shards(): lax.all_gather(prompt_states, SEQ, axis=1, tiled=True).astype(f32)]
    unnamed x1 -> x0, blocking collectives: 6.92 us -> none
    all_to_all x2, waiting for transfers between devices: 23.1 us -> 17.8 us  [exchange_sum(): return jnp.sum(lax.all_to_all(parts, axes, 0, 0, tiled=True), 0)]
    reduce_scatter x1 -> x0, waiting for transfers between devices: 4.95 us -> none  [shards(): lax.psum_scatter(prompt_terms, 'head', scatter_dimension=0, tiled=True)]
    unnamed x86 -> x93, local copies, waits for them, and re-layouts: 13.9 us -> 13.9 us
  transfers between devices with their start and end apart: 6 -> 6, of which waited for: 6 -> 5; matrix products, arithmetic and copies ran while one was open for 14% -> 11% of each run, Pallas kernels for 0% -> 0%
where the time goes in v4:
time: 391 us; the launch traced here: 386 us
  blocking collectives  148 us (38%)
  local copies, waits for them, and re-layouts  82.1 us (21%)
  waiting for transfers between devices  72.4 us (19%)
  other arithmetic  39.4 us (10%)
  between operations  14.9 us (4%)
  matrix products  14.5 us (4%)
  starting transfers between devices  14.3 us (4%)
    all_to_all x6, blocking collectives, exchange_sum(): return jnp.sum(lax.all_to_all(parts, axes, 0, 0, tiled=True), 0)  76.7 us
    all_to_all x6, blocking collectives, exchange_gather(): return lax.all_to_all(spread, axes, 0, 0, tiled=True)  48.2 us
    all_gather x1, waiting for transfers between devices, shards(): lax.all_gather(prompt_states, SEQ, axis=1, tiled=True).astype(f32)  29.1 us
    all_to_all x2, waiting for transfers between devices, exchange_sum(): return jnp.sum(lax.all_to_all(parts, axes, 0, 0, tiled=True), 0)  17.8 us
    unnamed x93, local copies, waits for them, and re-layouts  13.9 us
    all_to_all x1, blocking collectives, exchange_max(): return jnp.max(lax.all_to_all(spread, axes, 0, 0, tiled=True), 0)  13.1 us
    all_to_all x1, waiting for transfers between devices, shards(): prompt_terms = lax.all_to_all(prompt_terms, ALL, 0, 0, tiled=True)  10.2 us
    gather x6, local copies, waits for them, and re-layouts, shards(): tail_state = jnp.take_along_axis(everyone, picks[:, :, None, None], axis=1)  8.1 us
  transfers between devices with their start and end apart: 6, of which 5 were waited for; matrix products, arithmetic and copies ran while one was open for 11% of the time, Pallas kernels for 0%

profile of v4, /device:TPU:0, one launch (start us, length us, event | category | flops | bytes accessed | tf_op | source)
XLA Modules:
  0.0 385.5 jit_solution(5594856617778486727)
XLA Ops:
  7.3 1.2 multiply_reduce_fusion.1
  8.6 1.4 fusion.33
  11.1 4.2 %all-to-all-start = ((f32[2,96,384]{2,1,0:T(8,128)}), f32[2,96,384]{2,1,0:T(8,128)S(1)}, u32[]{:S(2)}, u32[]{:S(2)}) async-start(f32[2,96,384]{2,1,0:T(8,128)} %bitcast.1), calls=%async_computation | async-start | bytes 589824 | tf_op jit(solution)/shard_map/all_to_all | solution.py:44
  16.4 1.3 gather_fusion.4
  18.0 1.3 gather_fusion.1
  22.0 29.1 %all-gather.3.cloned.1.call-done = bf16[4,128,1280]{2,1,0:T(8,128)(2,1)} async-done(((bf16[4,8,1280]{2,1,0:T(8,128)(2,1)}), bf16[4,128,1280]{2,1,0:T(8,128)(2,1)}) %all-gather.3.cloned.1.call-update) | async-done | bytes 1310736 | tf_op jit(solution)/shard_map/all_gather | solution.py:131
  51.1 1.8 fusion.1
  53.1 1.2 dot_general.47
  54.4 1.9 fusion.21
  57.6 3.6 all-to-all-start.2
  62.0 10.2 %all-to-all-done.2 = f32[32,1,2176]{2,1,0:T(1,128)S(1)} async-done(((f32[32,1,2176]{2,1,0:T(1,128)}), f32[32,1,2176]{2,1,0:T(1,128)S(1)}, u32[]{:S(2)}, u32[]{:S(2)}) %all-to-all-start.2) | async-done | bytes 278560 | tf_op jit(solution)/shard_map/all_to_all | solution.py:147
  72.2 1.4 broadcast_in_dim.218
  73.6 2.9 all-to-all-start.1
  81.5 1.3 subtract_compare_fusion.3
  82.9 6.3 %all-gather.5.cloned.1.call-done = bf16[12,8,4,2048]{3,2,1,0:T(4,128)(2,1)} async-done(((bf16[12,4,4,2048]{3,2,1,0:T(4,128)(2,1)}), bf16[12,8,4,2048]{3,2,1,0:T(4,128)(2,1)}) %all-gather.5.cloned.1.call-update) | async-done | bytes 1572880 | tf_op jit(solution)/shard_map/all_gather | solution.py:183
  89.2 3.9 %gather_fusion.2 = bf16[48,4,2048]{2,1,0:T(4,128)(2,1)} fusion(bf16[12,8,4,2048]{3,2,1,0:T(4,128)(2,1)} %all-gather.5.cloned.1.call-done, s32[48]{0:T(128)S(1)} %reshape.524), kind=kCustom, calls=%fused_computation.2.clone | custom fusion | bytes 1573248 | tf_op jit(solution)/shard_map/jit(take_along_axis)/gather | solution.py:203
  93.1 3.9 %gather_fusion.7 = bf16[48,4,2048]{2,1,0:T(4,128)(2,1)} fusion(bf16[12,8,4,2048]{3,2,1,0:T(4,128)(2,1)} %all-gather.5.cloned.1.call-done, s32[48]{0:T(128)S(1)} %reshape.547), kind=kCustom, calls=%fused_computation.7.clone | custom fusion | bytes 1573248 | tf_op jit(solution)/shard_map/jit(take_along_axis)/gather | solution.py:203
  96.9 1.4 reduce.7
  102.7 3.7 pad_maximum_fusion
  106.4 7.6 %all-to-all-done.1 = bf16[32,96,256]{2,1,0:T(8,128)(2,1)S(1)} async-done(((bf16[32,96,256]{2,1,0:T(8,128)(2,1)}), bf16[32,96,256]{2,1,0:T(8,128)(2,1)S(1)}, u32[]{:S(2)}, u32[]{:S(2)}) %all-to-all-start.1) | async-done | bytes 1572896 | tf_op jit(solution)/shard_map/all_to_all | solution.py:54
  116.5 1.3 copy.555
  119.8 2.2 reshape.438
  122.0 1.4 copy.445
  123.4 2.8 fusion.30
  126.6 1.5 fusion.89
  131.5 1.7 reshape.424
  135.4 1.6 gather_fusion
  137.0 1.6 gather_fusion.3
  139.4 1.6 gather_fusion.5
  141.2 1.2 broadcast_select_fusion.2
  142.5 2.2 select_select_fusion.1
  150.1 1.6 broadcast_bitcast_fusion.2
  151.8 3.7 reshape.557
  155.5 13.1 %all_to_all.101 = f32[32,1,1536]{2,1,0:T(1,128)S(1)} all-to-all(f32[32,1,1536]{2,1,0:T(1,128)S(1)} %reshape.557), channel_id=1, replica_groups=mesh['seq'=8,'pair'=2,'head'=2] {'seq','pair','head'}, dimensions={0} | all-to-all | bytes 393216 | tf_op jit(solution)/shard_map/all_to_all | solution.py:49
  170.1 3.6 reshape.558
  173.7 1.9 bitcast_reduce_fusion
  179.1 1.5 fusion.69
  182.7 1.9 stack.31
  186.9 2.9 stack.30
  189.8 2.7 fusion.10
  192.6 3.9 %reshape.427 = f32[12,4,2,8,2,4,64]{6,5,4,3,2,1,0:T(4,128)} reshape(f32[12,4,32,256]{3,2,1,0:T(8,128)} %fusion.10) | data formatting | bytes 3145728 | tf_op jit(solution)/shard_map/reshape | solution.py:233
  196.4 3.5 fusion
  200.0 2.1 copy.488
  202.1 2.4 concatenate.53
  204.6 5.2 %all_to_all.94 = f32[2,8,2,12544]{3,1,2,0:T(8,128)S(1)} all-to-all(f32[2,8,2,12544]{3,1,2,0:T(8,128)S(1)} %maximum_bitcast_fusion), channel_id=1, replica_groups=mesh['seq'=8,'pair'=2,'head'=2] {'pair'}, dimensions={0} | all-to-all | bytes 3211264 | tf_op jit(solution)/shard_map/all_to_all | solution.py:44
  210.9 1.6 copy.495
  213.7 24.8 %all_to_all.102 = f32[16,1,12544]{2,1,0:T(1,128)S(1)} all-to-all(f32[16,1,12544]{2,1,0:T(1,128)S(1)} %all_to_all.76), channel_id=1, replica_groups=mesh['seq'=8,'pair'=2,'head'=2] {'seq','head'}, dimensions={0} | all-to-all | bytes 1605632 | tf_op jit(solution)/shard_map/all_to_all | solution.py:44
  239.2 6.5 %all_to_all.103 = bf16[2,192,64]{1,2,0:T(8,128)(2,1)S(1)} all-to-all(bf16[2,192,64]{1,2,0:T(8,128)(2,1)S(1)} %broadcast_in_dim.238), channel_id=1, replica_groups=mesh['seq'=8,'pair'=2,'head'=2] {'head'}, dimensions={0} | all-to-all | bytes 98304 | tf_op jit(solution)/shard_map/all_to_all | solution.py:54
  246.9 4.5 %all_to_all.95 = f32[2,8,12,1280]{3,1,2,0:T(8,128)S(1)} all-to-all(f32[2,8,12,1280]{3,1,2,0:T(8,128)S(1)} %copy.499), channel_id=1, replica_groups=mesh['seq'=8,'pair'=2,'head'=2] {'pair'}, dimensions={0} | all-to-all | bytes 1966080 | tf_op jit(solution)/shard_map/all_to_all | solution.py:44
  252.5 3.5 all-to-all-start.8
  256.1 17.8 %all-to-all-done.8 = f32[8,12,1280]{2,1,0:T(8,128)S(1)} async-done(((f32[8,12,1280]{2,1,0:T(8,128)}), f32[8,12,1280]{2,1,0:T(8,128)S(1)}, u32[]{:S(2)}, u32[]{:S(2)}) %all-to-all-start.8) | async-done | bytes 491552 | tf_op jit(solution)/shard_map/all_to_all | solution.py:44
  274.0 4.9 %psum.14 = f32[12]{0:T(128)S(1)} all-reduce(f32[12]{0:T(128)S(1)} %multiply_reduce_fusion.3), channel_id=1, replica_groups=mesh['seq'=8,'pair'=2,'head'=2] {'head'}, use_global_device_ids=true, to_apply=%region_20.24 | all-reduce | flops 12 | bytes 96 | tf_op jit(solution)/shard_map/psum | solution.py:280
  279.9 13.3 %all_to_all.96 = bf16[8,12,1280]{2,1,0:T(8,128)(2,1)S(1)} all-to-all(bf16[8,12,1280]{2,1,0:T(8,128)(2,1)S(1)} %broadcast_in_dim.239), channel_id=1, replica_groups=mesh['seq'=8,'pair'=2,'head'=2] {'seq'}, dimensions={0} | all-to-all | bytes 491520 | tf_op jit(solution)/shard_map/all_to_all | solution.py:54
  293.4 4.1 %all_to_all.97 = bf16[2,8,12,1280]{3,1,2,0:T(8,128)(2,1)S(1)} all-to-all(bf16[2,8,12,1280]{3,1,2,0:T(8,128)(2,1)S(1)} %broadcast_in_dim.240), channel_id=1, replica_groups=mesh['seq'=8,'pair'=2,'head'=2] {'pair'}, dimensions={0} | all-to-all | bytes 983040 | tf_op jit(solution)/shard_map/all_to_all | solution.py:54
  298.0 1.4 copy.502
  299.3 1.4 reshape.440
  300.8 2.1 fusion.54
  303.6 17.0 %all_to_all.104 = f32[2,96,1408]{2,1,0:T(8,128)S(1)} all-to-all(f32[2,96,1408]{2,1,0:T(8,128)S(1)} %bitcast.250), channel_id=1, replica_groups=mesh['seq'=8,'pair'=2,'head'=2] {'head'}, dimensions={0} | all-to-all | bytes 2162688 | tf_op jit(solution)/shard_map/all_to_all | solution.py:44
  321.0 7.5 %all_to_all.105 = bf16[2,96,640]{2,1,0:T(8,128)(2,1)S(1)} all-to-all(bf16[2,96,640]{2,1,0:T(8,128)(2,1)S(1)} %broadcast_in_dim.242), channel_id=1, replica_groups=mesh['seq'=8,'pair'=2,'head'=2] {'head'}, dimensions={0} | all-to-all | bytes 491520 | tf_op jit(solution)/shard_map/all_to_all | solution.py:54
  329.8 4.5 %all_to_all.98 = f32[2,8,12,1280]{3,1,2,0:T(8,128)S(1)} all-to-all(f32[2,8,12,1280]{3,1,2,0:T(8,128)S(1)} %copy.505), channel_id=1, replica_groups=mesh['seq'=8,'pair'=2,'head'=2] {'pair'}, dimensions={0} | all-to-all | bytes 1966080 | tf_op jit(solution)/shard_map/all_to_all | solution.py:44
  334.6 20.8 %all_to_all.106 = f32[8,12,1280]{2,1,0:T(8,128)S(1)} all-to-all(f32[8,12,1280]{2,1,0:T(8,128)S(1)} %copy.506), channel_id=1, replica_groups=mesh['seq'=8,'pair'=2,'head'=2] {'seq'}, dimensions={0} | all-to-all | bytes 983040 | tf_op jit(solution)/shard_map/all_to_all | solution.py:44
  355.5 4.9 %psum.15 = f32[12]{0:T(128)S(1)} all-reduce(f32[12]{0:T(128)S(1)} %multiply_reduce_fusion.2), channel_id=1, replica_groups=mesh['seq'=8,'pair'=2,'head'=2] {'head'}, use_global_device_ids=true, to_apply=%region_26.30 | all-reduce | flops 12 | bytes 96 | tf_op jit(solution)/shard_map/psum | solution.py:303
  360.6 12.6 %all_to_all.99 = bf16[8,12,1280]{2,1,0:T(8,128)(2,1)S(1)} all-to-all(bf16[8,12,1280]{2,1,0:T(8,128)(2,1)S(1)} %broadcast_in_dim.243), channel_id=1, replica_groups=mesh['seq'=8,'pair'=2,'head'=2] {'seq'}, dimensions={0} | all-to-all | bytes 491520 | tf_op jit(solution)/shard_map/all_to_all | solution.py:54
  373.4 4.1 %all_to_all.100 = bf16[2,8,12,1280]{3,1,2,0:T(8,128)(2,1)S(1)} all-to-all(bf16[2,8,12,1280]{3,1,2,0:T(8,128)(2,1)S(1)} %broadcast_in_dim.244), channel_id=1, replica_groups=mesh['seq'=8,'pair'=2,'head'=2] {'pair'}, dimensions={0} | all-to-all | bytes 983040 | tf_op jit(solution)/shard_map/all_to_all | solution.py:54
  (282 shorter events, 54.6 us)
Async XLA Ops:
  6.5 322.0 %copy-start = (bf16[640,1280]{1,0:T(8,128)(2,1)S(1)}, bf16[640,1280]{1,0:T(8,128)(2,1)}, u32[]{:S(2)}) copy-start(bf16[640,1280]{1,0:T(8,128)(2,1)} %param.44) | copy-start | bytes 4915204
  6.5 3.5 copy-start.13
  6.5 3.5 copy-start.24
  6.5 3.5 copy-start.39
  6.5 44.5 %all-gather.3.cloned.1.call-start = ((), (), s32[]{:S(2)}) async-start(), calls=%async_computation.17 | async-start | bytes 1392640 | tf_op jit(solution)/shard_map/all_gather | solution.py:131
  10.1 6.0 %copy-start.38 = (f32[256]{0:T(256)S(1)}, f32[256]{0:T(256)}, u32[]{:S(2)}) copy-start(f32[256]{0:T(256)} %param.38) | copy-start | bytes 3076
  10.1 6.1 %copy-start.33 = (f32[256]{0:T(256)S(1)}, f32[256]{0:T(256)}, u32[]{:S(2)}) copy-start(f32[256]{0:T(256)} %param.37) | copy-start | bytes 3076
  10.1 6.1 %copy-start.22 = (s32[2,12,8]{1,2,0:T(8,128)S(1)}, s32[2,12,8]{1,2,0:T(8,128)}, u32[]{:S(2)}) copy-start(s32[2,12,8]{1,2,0:T(8,128)} %param.27) | copy-start | bytes 2308
  11.1 46.4 %all-to-all-start = ((f32[2,96,384]{2,1,0:T(8,128)}), f32[2,96,384]{2,1,0:T(8,128)S(1)}, u32[]{:S(2)}, u32[]{:S(2)}) async-start(f32[2,96,384]{2,1,0:T(8,128)} %bitcast.1), calls=%async_computation | async-start | bytes 589824 | tf_op jit(solution)/shard_map/all_to_all | solution.py:44
  15.4 73.8 %all-gather.5.cloned.1.call-start = ((), (), s32[]{:S(2)}) async-start(), calls=%async_computation.18 | async-start | bytes 2359296 | tf_op jit(solution)/shard_map/all_gather | solution.py:183
  57.6 14.6 %all-to-all-start.2 = ((f32[32,1,2176]{2,1,0:T(1,128)}), f32[32,1,2176]{2,1,0:T(1,128)S(1)}, u32[]{:S(2)}, u32[]{:S(2)}) async-start(f32[32,1,2176]{2,1,0:T(1,128)} %copy.451), calls=%async_computation.2 | async-start | bytes 557056 | tf_op jit(solution)/shard_map/all_to_all | solution.py:147
  73.5 3.7 copy-start.37
  73.6 3.8 copy-start.30
  73.6 4.0 %copy-start.36 = (pred[12,4]{0,1:T(4,128)(4,1)S(1)}, pred[12,4]{0,1:T(4,128)(4,1)}, u32[]{:S(2)}) copy-start(pred[12,4]{0,1:T(4,128)(4,1)} %get-tuple-element.53) | copy-start | bytes 148
  73.6 4.7 %copy-start.29 = (s32[12,4,1]{0,1,2:T(4,128)S(1)}, s32[12,4,1]{0,1,2:T(4,128)}, u32[]{:S(2)}) copy-start(s32[12,4,1]{0,1,2:T(4,128)} %get-tuple-element.50) | copy-start | bytes 580
  73.6 5.8 %copy-start.35 = (pred[12,4]{0,1:T(4,128)(4,1)S(1)}, pred[12,4]{0,1:T(4,128)(4,1)}, u32[]{:S(2)}) copy-start(pred[12,4]{0,1:T(4,128)(4,1)} %get-tuple-element.54) | copy-start | bytes 148
  73.6 40.4 %all-to-all-start.1 = ((bf16[32,96,256]{2,1,0:T(8,128)(2,1)}), bf16[32,96,256]{2,1,0:T(8,128)(2,1)S(1)}, u32[]{:S(2)}, u32[]{:S(2)}) async-start(bf16[32,96,256]{2,1,0:T(8,128)(2,1)} %broadcast_in_dim.218), calls=%async_computation.1 | async-start | bytes 3145728 | tf_op jit(solution)/shard_map/all_to_all | solution.py:54
  117.8 1.0 copy-start.3
  119.8 3.5 copy-start.34
  123.4 3.2 copy-start.12
  130.6 2.7 copy-start.9
  133.7 1.1 copy-start.4
  134.2 1.1 copy-start.11
  138.6 2.4 copy-start.26
  138.6 2.6 copy-start.25
  139.4 3.1 copy-start.6
  139.4 3.1 copy-start.23
  141.0 1.4 copy-start.7
  144.7 0.9 copy-start.18
  144.7 0.9 copy-start.28
  145.2 2.6 copy-start.8
  145.7 2.5 copy-start.27
  147.8 0.9 copy-start.19
  147.8 2.3 copy-start.15
  173.7 2.7 copy-start.5
  173.7 4.3 %copy-start.16 = (f32[12,4,4,2,4]{4,3,2,1,0:T(2,128)S(1)}, f32[12,4,4,2,4]{4,3,2,1,0:T(2,128)}, u32[]{:S(2)}) copy-start(f32[12,4,4,2,4]{4,3,2,1,0:T(2,128)} %get-tuple-element.44) | copy-start | bytes 18436
  182.4 2.1 copy-start.17
  186.0 3.9 %copy-start.1 = (bf16[12,64,1024]{2,1,0:T(8,128)(2,1)S(1)}, bf16[12,64,1024]{2,1,0:T(8,128)(2,1)}, u32[]{:S(2)}) copy-start(bf16[12,64,1024]{2,1,0:T(8,128)(2,1)} %get-tuple-element.12) | copy-start | bytes 4718596
  192.6 3.9 %copy-start.2 = (f32[12,4,1,8,2,4,64]{6,5,3,4,1,0,2:T(4,128)S(1)}, f32[12,4,1,8,2,4,64]{6,5,3,4,1,0,2:T(4,128)}, u32[]{:S(2)}) copy-start(f32[12,4,1,8,2,4,64]{6,5,3,4,1,0,2:T(4,128)} %stack.31) | copy-start | bytes 2359300
  202.1 2.4 copy-start.20
  238.4 7.6 %copy-start.14 = (bf16[128,1280]{1,0:T(8,128)(2,1)S(1)}, bf16[128,1280]{1,0:T(8,128)(2,1)}, u32[]{:S(2)}) copy-start(bf16[128,1280]{1,0:T(8,128)(2,1)} %param.39) | copy-start | bytes 983044
  251.5 27.5 %copy-start.31 = (f32[1280]{0:T(1024)S(1)}, f32[1280]{0:T(1024)}, u32[]{:S(2)}) copy-start(f32[1280]{0:T(1024)} %param.40) | copy-start | bytes 15364
  252.5 21.4 %all-to-all-start.8 = ((f32[8,12,1280]{2,1,0:T(8,128)}), f32[8,12,1280]{2,1,0:T(8,128)S(1)}, u32[]{:S(2)}, u32[]{:S(2)}) async-start(f32[8,12,1280]{2,1,0:T(8,128)} %copy.500), calls=%async_computation.8 | async-start | bytes 1310720 | tf_op jit(solution)/shard_map/all_to_all | solution.py:44
  299.3 1.4 copy-start.21
  300.8 2.1 copy-start.10
  334.4 26.1 %copy-start.32 = (f32[1280]{0:T(1024)S(1)}, f32[1280]{0:T(1024)}, u32[]{:S(2)}) copy-start(f32[1280]{0:T(1024)} %param.45) | copy-start | bytes 15364
Sparse Core Ops, SparseCore 0:
  9.6 41.4 all-gather.2
  52.6 36.5 all-gather.4

commit v5 on v2

--- a/solution.py
+++ b/solution.py
@@ -177,13 +177,9 @@
     grouped = jnp.transpose(
         every_query.reshape(steps, groups, beams, KVH, repeat, HD), (1, 3, 0, 2, 4, 5)
     ).reshape(groups, KVH, many, HD)
-    scores = jnp.einsum("gkmd,gtkd->gkmt", grouped, shared_keys, preferred_element_type=f32)
-    scores = jnp.where(shared_ok[:, None, None, :], scores, NEG)
-    top = jnp.max(scores, -1).reshape(groups, KVH, steps, beams, repeat)
     source = jnp.broadcast_to(all_beams[None, :], (groups, beams))
     ancestors = []
-    tail_parts = []
-    tail_tops = []
+    tail_states = []
     for step in range(steps):
         link = parents[step]
         source = jnp.take_along_axis(source, link, axis=1)
@@ -197,55 +193,32 @@
             tail_state = jnp.where(
                 (offset == back)[:, None, :, None], written[:, :, None, :], tail_state
             )
-        tail_keys, tail_values = split_pairs(tail_state)
-        local_query = lax.dynamic_slice_in_dim(every_query[step], first_beam, local_beams, 1)
-        local_query = local_query.reshape(groups, local_beams, KVH, repeat, HD)
-        tail_scores = jnp.einsum(
-            "gckrd,gctkd->gckrt", local_query, tail_keys, preferred_element_type=f32
-        )
-        tail_ok = (offset <= step)[:, None, None, None, :]
-        tail_scores = jnp.where(tail_ok, tail_scores, NEG)
-        tail_parts.append((tail_scores, tail_ok, tail_values))
-        tail_top = lax.dynamic_update_slice(
-            jnp.full((groups, beams, KVH, repeat), NEG, f32),
-            jnp.max(tail_scores, -1),
-            (0, first_beam, 0, 0),
-        )
-        tail_tops.append(jnp.transpose(tail_top, (0, 2, 1, 3)))
-    top = jnp.maximum(top, jnp.stack(tail_tops, 2))
+        tail_states.append(tail_state)
+    tails = jnp.stack(tail_states, 1).reshape(groups, steps * local_beams * tail_seg, -1)
+    all_keys, all_values = split_pairs(jnp.concatenate([shared, tails], 1))
+    step_id = jnp.arange(steps)
+    same_step = step_id[:, None, None, None, None, None] == step_id[None, None, None, :, None, None]
+    same_beam = (
+        all_beams[None, :, None, None, None, None]
+        == (first_beam + jnp.arange(local_beams))[None, None, None, None, :, None]
+    )
+    live = offset[:, None, None, None, None, None, :] <= step_id[None, None, None, None, :, None, None]
+    tail_mask = jnp.broadcast_to(
+        (same_step & same_beam)[None] & live,
+        (groups, steps, beams, repeat, steps, local_beams, tail_seg),
+    ).reshape(groups, many, -1)
+    mask = jnp.concatenate(
+        [jnp.broadcast_to(shared_ok[:, None, :], (groups, many, span)), tail_mask], -1
+    )[:, None]
+    scores = jnp.einsum("gkmd,gtkd->gkmt", grouped, all_keys, preferred_element_type=f32)
+    scores = jnp.where(mask, scores, NEG)
+    top = jnp.max(scores, -1).reshape(groups, KVH, steps, beams, repeat)
     top = exchange_max(top, ALL, n_dev)
-    weights = jnp.where(
-        shared_ok[:, None, None, :], jnp.exp(scores - top.reshape(groups, KVH, many)[..., None]), 0.0
-    )
+    weights = jnp.where(mask, jnp.exp(scores - top.reshape(groups, KVH, many)[..., None]), 0.0)
     total = jnp.sum(weights, -1).reshape(groups, KVH, steps, beams, repeat)
     weighted = jnp.einsum(
-        "gkmt,gtkd->gkmd", weights.astype(bf16), shared_values, preferred_element_type=f32
+        "gkmt,gtkd->gkmd", weights.astype(bf16), all_values, preferred_element_type=f32
     ).reshape(groups, KVH, steps, beams, repeat, HD)
-    tail_totals, tail_weighted = [], []
-    for step in range(steps):
-        tail_scores, tail_ok, tail_values = tail_parts[step]
-        local_top = lax.dynamic_slice_in_dim(top[:, :, step], first_beam, local_beams, 2)
-        local_top = jnp.transpose(local_top, (0, 2, 1, 3))
-        tail_weights = jnp.where(tail_ok, jnp.exp(tail_scores - local_top[..., None]), 0.0)
-        tail_total = lax.dynamic_update_slice(
-            jnp.zeros((groups, beams, KVH, repeat), f32),
-            jnp.sum(tail_weights, -1),
-            (0, first_beam, 0, 0),
-        )
-        tail_sum = lax.dynamic_update_slice(
-            jnp.zeros((groups, beams, KVH, repeat, HD), f32),
-            jnp.einsum(
-                "gckrt,gctkd->gckrd",
-                tail_weights.astype(bf16),
-                tail_values,
-                preferred_element_type=f32,
-            ),
-            (0, first_beam, 0, 0, 0),
-        )
-        tail_totals.append(jnp.transpose(tail_total, (0, 2, 1, 3)))
-        tail_weighted.append(jnp.transpose(tail_sum, (0, 2, 1, 3, 4)))
-    total = total + jnp.stack(tail_totals, 2)
-    weighted = weighted + jnp.stack(tail_weighted, 2)
     rows = steps * groups * beams
     piece = QD // n_dev
     per_head = HD // piece

time: 385 us -> 365 us (0.948)
  waiting for transfers between devices: 64.1 us -> 57.4 us
  matrix products: 20 us -> 13.5 us
  local copies, waits for them, and re-layouts: 79.8 us -> 73.8 us
    dot_general x6 -> x2, matrix products: 10.4 us -> 3.52 us  [the longest x1 2.44 us: shards(): jnp.einsum('gkmt,gtkd->gkmd', weights.astype(bf16), all_values, preferred...]
    transpose x2 -> x0, other arithmetic: 5.05 us -> none  [the longest x1 3.53 us: shards(): jnp.transpose(weighted.reshape(groups, KVH, steps, beams, repeat, per_hea...]
    reduce_scatter x1, waiting for transfers between devices: 4.95 us -> 0.01 us  [shards(): lax.psum_scatter(prompt_terms, 'head', scatter_dimension=0, tiled=True)]
    unnamed x86 -> x68, local copies, waits for them, and re-layouts: 13.9 us -> 12 us
    another operation x8 -> x2, local copies, waits for them, and re-layouts: 7.76 us -> 6.69 us  [shards(): weighted.reshape(groups, KVH, steps, beams, repeat, per_head, piece)]
  transfers between devices with their start and end apart: 6 -> 6, of which waited for: 6 -> 5; matrix products, arithmetic and copies ran while one was open for 14% -> 16% of each run, Pallas kernels for 0% -> 0%
where the time goes in v5:
time: 365 us; the launch traced here: 360 us
  blocking collectives  157 us (43%)
  local copies, waits for them, and re-layouts  73.8 us (20%)
  waiting for transfers between devices  57.4 us (16%)
  other arithmetic  30.1 us (8%)
  between operations  15.1 us (4%)
  matrix products  13.5 us (4%)
  starting transfers between devices  13.4 us (4%)
    all_to_all x6, blocking collectives, exchange_sum(): return jnp.sum(lax.all_to_all(parts, axes, 0, 0, tiled=True), 0)  76.5 us
    all_to_all x6, blocking collectives, exchange_gather(): return lax.all_to_all(spread, axes, 0, 0, tiled=True)  48.4 us
    all_gather x1, waiting for transfers between devices, shards(): lax.all_gather(w_keyval, SEQ, axis=1, tiled=True)  23.8 us
    all_to_all x2, waiting for transfers between devices, exchange_sum(): return jnp.sum(lax.all_to_all(parts, axes, 0, 0, tiled=True), 0)  19.3 us
    all_to_all x1, blocking collectives, exchange_max(): return jnp.max(lax.all_to_all(spread, axes, 0, 0, tiled=True), 0)  13.7 us
    unnamed x68, local copies, waits for them, and re-layouts  12 us
    gather x6, local copies, waits for them, and re-layouts, shards(): tail_state = jnp.take_along_axis(everyone, picks[:, :, None, None], axis=1)  8.11 us
    unnamed x1, blocking collectives  8.04 us
  transfers between devices with their start and end apart: 6, of which 5 were waited for; matrix products, arithmetic and copies ran while one was open for 16% of the time, Pallas kernels for 0%

profile of v5, /device:TPU:0, one launch (start us, length us, event | category | flops | bytes accessed | tf_op | source)
XLA Modules:
  0.0 359.9 jit_solution(18089564338209539268)
XLA Ops:
  8.0 1.2 multiply_reduce_fusion.1
  10.7 4.2 %all-to-all-start = ((f32[2,96,384]{2,1,0:T(8,128)}), f32[2,96,384]{2,1,0:T(8,128)S(1)}, u32[]{:S(2)}, u32[]{:S(2)}) async-start(f32[2,96,384]{2,1,0:T(8,128)} %bitcast.2), calls=%async_computation | async-start | bytes 589824 | tf_op jit(solution)/shard_map/all_to_all | solution.py:44
  15.1 1.3 gather_fusion.4
  16.8 1.3 gather_fusion.1
  19.7 1.5 all-to-all-done
  21.4 1.3 broadcast_in_dim.111
  22.8 5.5 %all-to-all-start.1 = ((bf16[32,96,256]{2,1,0:T(8,128)(2,1)}), bf16[32,96,256]{2,1,0:T(8,128)(2,1)S(1)}, u32[]{:S(2)}, u32[]{:S(2)}) async-start(bf16[32,96,256]{2,1,0:T(8,128)(2,1)} %broadcast_in_dim.111), calls=%async_computation.1 | async-start | bytes 3145728 | tf_op jit(solution)/shard_map/all_to_all | solution.py:54
  34.9 8.0 %all-reduce.5 = f32[32]{0:T(128)S(1)} all-reduce(f32[32]{0:T(128)S(1)} %reshape.374), channel_id=3, replica_groups=mesh['seq'=8,'pair'=2,'head'=2] {'head'}, use_global_device_ids=true, to_apply=%region_6.7.clone | all-reduce | flops 32 | bytes 256
  43.8 1.3 subtract_compare_fusion.1
  45.1 6.5 %all-gather.5.cloned.1.call-done = bf16[12,8,4,2048]{3,2,1,0:T(4,128)(2,1)} async-done(((bf16[12,4,4,2048]{3,2,1,0:T(4,128)(2,1)}), bf16[12,8,4,2048]{3,2,1,0:T(4,128)(2,1)}) %all-gather.5.cloned.1.call-update) | async-done | bytes 1572880 | tf_op jit(solution)/shard_map/all_gather | solution.py:173
  51.6 3.9 %gather_fusion.7 = bf16[48,4,2048]{2,1,0:T(4,128)(2,1)} fusion(bf16[12,8,4,2048]{3,2,1,0:T(4,128)(2,1)} %all-gather.5.cloned.1.call-done, s32[48]{0:T(128)S(1)} %reshape.494), kind=kCustom, calls=%fused_computation.7.clone | custom fusion | bytes 1573248 | tf_op jit(solution)/shard_map/jit(take_along_axis)/gather | solution.py:189
  55.5 3.9 %gather_fusion.2 = bf16[48,4,2048]{2,1,0:T(4,128)(2,1)} fusion(bf16[12,8,4,2048]{3,2,1,0:T(4,128)(2,1)} %all-gather.5.cloned.1.call-done, s32[48]{0:T(128)S(1)} %reshape.471), kind=kCustom, calls=%fused_computation.2.clone | custom fusion | bytes 1573248 | tf_op jit(solution)/shard_map/jit(take_along_axis)/gather | solution.py:189
  59.4 6.4 %all-to-all-done.1 = bf16[32,96,256]{2,1,0:T(8,128)(2,1)S(1)} async-done(((bf16[32,96,256]{2,1,0:T(8,128)(2,1)}), bf16[32,96,256]{2,1,0:T(8,128)(2,1)S(1)}, u32[]{:S(2)}, u32[]{:S(2)}) %all-to-all-start.1) | async-done | bytes 1572896 | tf_op jit(solution)/shard_map/all_to_all | solution.py:54
  65.8 1.2 copy-done.1
  67.0 1.5 fusion.67
  70.5 2.4 mul.285
  72.9 1.4 reduce_sum.172
  75.6 1.6 gather_fusion
  78.0 1.6 gather_fusion.3
  80.3 1.6 gather_fusion.5
  84.5 1.3 broadcast_select_fusion.2
  85.8 1.7 fusion.21
  87.5 2.2 pad_maximum_fusion
  89.7 1.7 copy_convert_fusion
  91.3 23.8 %all-gather.3.cloned.1.call-done = bf16[1280,2048]{1,0:T(8,128)(2,1)} async-done(((bf16[1280,128]{1,0:T(8,128)(2,1)}), bf16[1280,2048]{1,0:T(8,128)(2,1)}) %all-gather.3.cloned.1.call-update) | async-done | bytes 5242896 | tf_op jit(solution)/shard_map/all_gather | solution.py:135
  115.1 4.2 %fusion.69 = f32[32,2048]{1,0:T(8,128)} fusion(bf16[32,1280]{1,0:T(8,128)(2,1)S(1)} %reshape.373, bf16[1280,2048]{1,0:T(8,128)(2,1)} %all-gather.3.cloned.1.call-done), kind=kOutput, calls=%fused_computation.175 | convolution fusion | flops 167772160 | bytes 5586944 | tf_op jit(solution)/shard_map/dot_general | solution.py:133
  119.4 2.4 reshape.375
  121.8 3.1 reshape.386
  124.9 1.4 copy.375
  126.3 2.2 fusion.22
  128.6 1.4 copy.376
  132.8 1.8 fusion.4
  134.6 1.9 fusion.66
  137.8 1.6 broadcast_bitcast_fusion.1
  139.3 3.6 reshape.503
  142.9 13.7 %all_to_all.85 = f32[32,1,1536]{2,1,0:T(1,128)S(1)} all-to-all(f32[32,1,1536]{2,1,0:T(1,128)S(1)} %reshape.503), channel_id=1, replica_groups=mesh['seq'=8,'pair'=2,'head'=2] {'seq','pair','head'}, dimensions={0} | all-to-all | bytes 393216 | tf_op jit(solution)/shard_map/all_to_all | solution.py:49
  158.2 3.6 %reshape.504 = f32[32,4,2,2,8,12]{5,4,3,2,1,0:T(8,128)} reshape(f32[32,1536]{1,0:T(8,128)S(1)} %reduce.11) | data formatting | bytes 393216
  161.8 1.8 bitcast_reduce_fusion
  164.4 2.4 fusion.5
  166.8 2.5 reshape_reshape.4
  169.3 4.2 %copy.457 = f32[12,4,2,8,2,4,64]{6,3,0,2,4,1,5:T(8,128)} copy(f32[12,4,2,8,2,4,64]{6,5,4,3,2,1,0:T(4,128)} %reshape_reshape.4) | data formatting | bytes 3145728 | tf_op jit(solution)/shard_map/reshape;reshape | solution.py:226
  173.5 2.4 concatenate.52
  176.5 5.0 %all_to_all.86 = f32[2,8,2,12544]{3,1,2,0:T(8,128)S(1)} all-to-all(f32[2,8,2,12544]{3,1,2,0:T(8,128)S(1)} %maximum_bitcast_fusion), channel_id=1, replica_groups=mesh['seq'=8,'pair'=2,'head'=2] {'pair'}, dimensions={0} | all-to-all | bytes 3211264 | tf_op jit(solution)/shard_map/all_to_all | solution.py:44
  182.6 1.6 copy.412
  185.3 24.8 %all_to_all.87 = f32[16,1,12544]{2,1,0:T(1,128)S(1)} all-to-all(f32[16,1,12544]{2,1,0:T(1,128)S(1)} %all_to_all.68), channel_id=1, replica_groups=mesh['seq'=8,'pair'=2,'head'=2] {'seq','head'}, dimensions={0} | all-to-all | bytes 1605632 | tf_op jit(solution)/shard_map/all_to_all | solution.py:44
  210.9 6.5 %all_to_all.88 = bf16[2,192,64]{1,2,0:T(8,128)(2,1)S(1)} all-to-all(bf16[2,192,64]{1,2,0:T(8,128)(2,1)S(1)} %broadcast_in_dim.223), channel_id=1, replica_groups=mesh['seq'=8,'pair'=2,'head'=2] {'head'}, dimensions={0} | all-to-all | bytes 98304 | tf_op jit(solution)/shard_map/all_to_all | solution.py:54
  218.6 4.5 %all_to_all.89 = f32[2,8,12,1280]{3,1,2,0:T(8,128)S(1)} all-to-all(f32[2,8,12,1280]{3,1,2,0:T(8,128)S(1)} %copy.416), channel_id=1, replica_groups=mesh['seq'=8,'pair'=2,'head'=2] {'pair'}, dimensions={0} | all-to-all | bytes 1966080 | tf_op jit(solution)/shard_map/all_to_all | solution.py:44
  224.2 3.5 all-to-all-start.7
  227.7 17.8 %all-to-all-done.7 = f32[8,12,1280]{2,1,0:T(8,128)S(1)} async-done(((f32[8,12,1280]{2,1,0:T(8,128)}), f32[8,12,1280]{2,1,0:T(8,128)S(1)}, u32[]{:S(2)}, u32[]{:S(2)}) %all-to-all-start.7) | async-done | bytes 491552 | tf_op jit(solution)/shard_map/all_to_all | solution.py:44
  245.7 4.9 %psum.14 = f32[12]{0:T(128)S(1)} all-reduce(f32[12]{0:T(128)S(1)} %multiply_reduce_fusion.3), channel_id=1, replica_groups=mesh['seq'=8,'pair'=2,'head'=2] {'head'}, use_global_device_ids=true, to_apply=%region_17.21 | all-reduce | flops 12 | bytes 96 | tf_op jit(solution)/shard_map/psum | solution.py:243
  251.6 13.3 %all_to_all.90 = bf16[8,12,1280]{2,1,0:T(8,128)(2,1)S(1)} all-to-all(bf16[8,12,1280]{2,1,0:T(8,128)(2,1)S(1)} %broadcast_in_dim.224), channel_id=1, replica_groups=mesh['seq'=8,'pair'=2,'head'=2] {'seq'}, dimensions={0} | all-to-all | bytes 491520 | tf_op jit(solution)/shard_map/all_to_all | solution.py:54
  265.1 4.3 %all_to_all.91 = bf16[2,8,12,1280]{3,1,2,0:T(8,128)(2,1)S(1)} all-to-all(bf16[2,8,12,1280]{3,1,2,0:T(8,128)(2,1)S(1)} %broadcast_in_dim.225), channel_id=1, replica_groups=mesh['seq'=8,'pair'=2,'head'=2] {'pair'}, dimensions={0} | all-to-all | bytes 983040 | tf_op jit(solution)/shard_map/all_to_all | solution.py:54
  269.5 1.4 copy.419
  270.9 1.4 reshape.387
  272.3 2.9 fusion.44
  275.2 1.3 fusion.45
  277.0 1.3 select_maximum_fusion
  278.2 17.0 %all_to_all.92 = f32[2,96,1408]{2,1,0:T(8,128)S(1)} all-to-all(f32[2,96,1408]{2,1,0:T(8,128)S(1)} %bitcast.175), channel_id=1, replica_groups=mesh['seq'=8,'pair'=2,'head'=2] {'head'}, dimensions={0} | all-to-all | bytes 2162688 | tf_op jit(solution)/shard_map/all_to_all | solution.py:44
  295.6 7.5 %all_to_all.93 = bf16[2,96,640]{2,1,0:T(8,128)(2,1)S(1)} all-to-all(bf16[2,96,640]{2,1,0:T(8,128)(2,1)S(1)} %broadcast_in_dim.227), channel_id=1, replica_groups=mesh['seq'=8,'pair'=2,'head'=2] {'head'}, dimensions={0} | all-to-all | bytes 491520 | tf_op jit(solution)/shard_map/all_to_all | solution.py:54
  304.4 4.5 %all_to_all.94 = f32[2,8,12,1280]{3,1,2,0:T(8,128)S(1)} all-to-all(f32[2,8,12,1280]{3,1,2,0:T(8,128)S(1)} %copy.422), channel_id=1, replica_groups=mesh['seq'=8,'pair'=2,'head'=2] {'pair'}, dimensions={0} | all-to-all | bytes 1966080 | tf_op jit(solution)/shard_map/all_to_all | solution.py:44
  309.2 20.8 %all_to_all.95 = f32[8,12,1280]{2,1,0:T(8,128)S(1)} all-to-all(f32[8,12,1280]{2,1,0:T(8,128)S(1)} %copy.423), channel_id=1, replica_groups=mesh['seq'=8,'pair'=2,'head'=2] {'seq'}, dimensions={0} | all-to-all | bytes 983040 | tf_op jit(solution)/shard_map/all_to_all | solution.py:44
  330.2 4.9 %psum.15 = f32[12]{0:T(128)S(1)} all-reduce(f32[12]{0:T(128)S(1)} %multiply_reduce_fusion.2), channel_id=1, replica_groups=mesh['seq'=8,'pair'=2,'head'=2] {'head'}, use_global_device_ids=true, to_apply=%region_23.27 | all-reduce | flops 12 | bytes 96 | tf_op jit(solution)/shard_map/psum | solution.py:266
  335.2 12.6 %all_to_all.96 = bf16[8,12,1280]{2,1,0:T(8,128)(2,1)S(1)} all-to-all(bf16[8,12,1280]{2,1,0:T(8,128)(2,1)S(1)} %broadcast_in_dim.228), channel_id=1, replica_groups=mesh['seq'=8,'pair'=2,'head'=2] {'seq'}, dimensions={0} | all-to-all | bytes 491520 | tf_op jit(solution)/shard_map/all_to_all | solution.py:54
  348.0 4.1 %all_to_all.97 = bf16[2,8,12,1280]{3,1,2,0:T(8,128)(2,1)S(1)} all-to-all(bf16[2,8,12,1280]{3,1,2,0:T(8,128)(2,1)S(1)} %broadcast_in_dim.229), channel_id=1, replica_groups=mesh['seq'=8,'pair'=2,'head'=2] {'pair'}, dimensions={0} | all-to-all | bytes 983040 | tf_op jit(solution)/shard_map/all_to_all | solution.py:54
  (229 shorter events, 36.5 us)
Async XLA Ops:
  6.5 296.6 %copy-start = (bf16[640,1280]{1,0:T(8,128)(2,1)S(1)}, bf16[640,1280]{1,0:T(8,128)(2,1)}, u32[]{:S(2)}) copy-start(bf16[640,1280]{1,0:T(8,128)(2,1)} %param.44) | copy-start | bytes 4915204
  6.5 2.8 copy-start.9
  6.5 2.8 copy-start.8
  6.5 2.8 copy-start.18
  6.5 3.1 copy-start.27
  6.5 45.1 %all-gather.5.cloned.1.call-start = ((), (), s32[]{:S(2)}) async-start(), calls=%async_computation.19 | async-start | bytes 2359296 | tf_op jit(solution)/shard_map/all_gather | solution.py:173
  7.3 107.9 %all-gather.3.cloned.1.call-start = ((), (), s32[]{:S(2)}) async-start(), calls=%async_computation.17 | async-start | bytes 5570560 | tf_op jit(solution)/shard_map/all_gather | solution.py:135
  9.2 5.7 %copy-start.13 = (s32[2,12,8]{1,2,0:T(8,128)S(1)}, s32[2,12,8]{1,2,0:T(8,128)}, u32[]{:S(2)}) copy-start(s32[2,12,8]{1,2,0:T(8,128)} %param.27) | copy-start | bytes 2308
  10.7 10.5 %all-to-all-start = ((f32[2,96,384]{2,1,0:T(8,128)}), f32[2,96,384]{2,1,0:T(8,128)S(1)}, u32[]{:S(2)}, u32[]{:S(2)}) async-start(f32[2,96,384]{2,1,0:T(8,128)} %bitcast.2), calls=%async_computation | async-start | bytes 589824 | tf_op jit(solution)/shard_map/all_to_all | solution.py:44
  18.2 1.3 copy-start.24
  22.7 9.1 %copy-start.11 = (bf16[4,8,1280]{2,1,0:T(8,128)(2,1)S(1)}, bf16[4,8,1280]{2,1,0:T(8,128)(2,1)}, u32[]{:S(2)}) copy-start(bf16[4,8,1280]{2,1,0:T(8,128)(2,1)} %param.32) | copy-start | bytes 245764
  22.7 10.0 %copy-start.21 = (s32[12]{0:T(128)S(1)}, s32[12]{0:T(128)}, u32[]{:S(2)}) copy-start(s32[12]{0:T(128)} %param.29) | copy-start | bytes 148
  22.7 10.9 %copy-start.29 = (u32[32]{0:T(128)S(1)}, u32[32]{0:T(128)}, u32[]{:S(2)}) copy-start(u32[32]{0:T(128)} %constant.271) | copy-start | bytes 388
  22.7 20.8 %copy-start.28 = (s32[4]{0:T(128)S(1)}, s32[4]{0:T(128)}, u32[]{:S(2)}) copy-start(s32[4]{0:T(128)} %param.33) | copy-start | bytes 52
  22.7 20.8 %copy-start.26 = (s32[8]{0:T(128)S(1)}, s32[8]{0:T(128)}, u32[]{:S(2)}) copy-start(s32[8]{0:T(128)} %param.31) | copy-start | bytes 100
  22.8 43.0 %all-to-all-start.1 = ((bf16[32,96,256]{2,1,0:T(8,128)(2,1)}), bf16[32,96,256]{2,1,0:T(8,128)(2,1)S(1)}, u32[]{:S(2)}, u32[]{:S(2)}) async-start(bf16[32,96,256]{2,1,0:T(8,128)(2,1)} %broadcast_in_dim.111), calls=%async_computation.1 | async-start | bytes 3145728 | tf_op jit(solution)/shard_map/all_to_all | solution.py:54
  28.3 101.7 %reduce-scatter.2.cloned.1.call-start = ((), (), s32[]{:S(2)}) async-start(), calls=%async_computation.18 | async-start | bytes 393216 | tf_op jit(solution)/shard_map/reduce_scatter | solution.py:139
  32.2 0.5 copy-start.22
  65.8 1.2 copy-start.1
  74.6 1.0 copy-start.6
  81.9 3.9 %copy-start.2 = (bf16[48,4,2048]{2,1,0:T(4,128)(2,1)S(1)}, bf16[48,4,2048]{2,1,0:T(4,128)(2,1)}, u32[]{:S(2)}) copy-start(bf16[48,4,2048]{2,1,0:T(4,128)(2,1)} %gather_fusion.7) | copy-start | bytes 2359300
  82.6 3.2 copy-start.14
  82.6 3.2 copy-start.15
  82.6 3.2 copy-start.16
  82.6 3.2 copy-start.17
  83.3 2.5 copy-start.3
  121.8 4.6 %copy-start.23 = (f32[256]{0:T(256)S(1)}, f32[256]{0:T(256)}, u32[]{:S(2)}) copy-start(f32[256]{0:T(256)} %param.37) | copy-start | bytes 3076
  126.3 3.7 %copy-start.25 = (f32[16]{0:T(128)S(1)}, f32[16]{0:T(128)}, u32[]{:S(2)}) copy-start(f32[16]{0:T(128)} %fusion.63) | copy-start | bytes 196
  134.6 1.9 copy-start.7
  137.6 26.2 %copy-start.4 = (f32[12,4,32,96]{3,2,1,0:T(8,128)}, f32[12,4,32,96]{3,2,1,0:T(8,128)S(1)}, u32[]{:S(2)}) copy-start(f32[12,4,32,96]{3,2,1,0:T(8,128)S(1)} %get-tuple-element.32) | copy-start | bytes 1769476
  210.1 7.6 %copy-start.10 = (bf16[128,1280]{1,0:T(8,128)(2,1)S(1)}, bf16[128,1280]{1,0:T(8,128)(2,1)}, u32[]{:S(2)}) copy-start(bf16[128,1280]{1,0:T(8,128)(2,1)} %param.39) | copy-start | bytes 983044
  223.2 27.5 %copy-start.19 = (f32[1280]{0:T(1024)S(1)}, f32[1280]{0:T(1024)}, u32[]{:S(2)}) copy-start(f32[1280]{0:T(1024)} %param.40) | copy-start | bytes 15364
  224.2 21.4 %all-to-all-start.7 = ((f32[8,12,1280]{2,1,0:T(8,128)}), f32[8,12,1280]{2,1,0:T(8,128)S(1)}, u32[]{:S(2)}, u32[]{:S(2)}) async-start(f32[8,12,1280]{2,1,0:T(8,128)} %copy.417), calls=%async_computation.8 | async-start | bytes 1310720 | tf_op jit(solution)/shard_map/all_to_all | solution.py:44
  270.9 1.4 copy-start.12
  272.3 2.9 copy-start.5
  309.0 26.1 %copy-start.20 = (f32[1280]{0:T(1024)S(1)}, f32[1280]{0:T(1024)}, u32[]{:S(2)}) copy-start(f32[1280]{0:T(1024)} %param.45) | copy-start | bytes 15364
Sparse Core Ops, SparseCore 0:
  8.9 42.6 all-gather.4
  53.7 61.3 all-gather.2
  119.5 9.8 reduce-scatter.1

commit v6 on v5

--- a/solution.py
+++ b/solution.py
@@ -127,21 +127,40 @@
     steps, groups, beams, width = step_tokens.shape
     pre = prompt_states.shape[0]
     repeat = QH // KVH
-    rows = jnp.transpose(prompt_states, (1, 0, 2)).astype(f32)
-    prompt_scaled = (rows * in_gain).astype(bf16).reshape(-1, width)
-    prompt_squares = jnp.sum(rows * rows, -1).reshape(-1)
-    prompt_terms = jnp.dot(
-        prompt_scaled,
-        lax.all_gather(w_keyval, SEQ, axis=1, tiled=True),
-        preferred_element_type=f32,
-    )
-    prompt_sum, prompt_sq = (
-        lax.psum_scatter(prompt_terms, "head", scatter_dimension=0, tiled=True),
-        lax.psum_scatter(prompt_squares, "head", scatter_dimension=0, tiled=True),
-    )
+    every_query, every_fresh = project_tokens(
+        step_tokens, in_gain, w_query, w_keyval, q_gain, k_gain
+    )
+    every_query = every_query.reshape(steps, groups, beams, -1)
+    every_fresh = every_fresh.reshape(steps, groups, beams, -1)
+    owners = n_seq * n_head
+    prompt_all = lax.all_gather(prompt_states, SEQ, axis=1, tiled=True)
+    prompt_all, every_query, every_fresh = lax.optimization_barrier(
+        (prompt_all, every_query, every_fresh)
+    )
+    prompt_all = prompt_all.astype(f32)
+    prompt_seg = prompt_all.shape[1] // owners
+    prompt_scaled = (prompt_all * in_gain).astype(bf16).reshape(-1, width)
+    prompt_terms = jnp.dot(prompt_scaled, w_keyval, preferred_element_type=f32)
+    kv_cols = prompt_terms.shape[1]
+    prompt_terms = jnp.transpose(
+        prompt_terms.reshape(pre, owners, prompt_seg, kv_cols), (1, 0, 2, 3)
+    ).reshape(owners, -1)
+    prompt_squares = jnp.transpose(
+        jnp.sum(prompt_all * prompt_all, -1).reshape(pre, owners, prompt_seg), (1, 0, 2)
+    ).reshape(owners, -1)
+    own_rows = pre * prompt_seg
+    pad_rows = -(-own_rows // 128) * 128
+    prompt_terms = jnp.concatenate(
+        [prompt_terms, jnp.pad(prompt_squares, ((0, 0), (0, pad_rows - own_rows)))], 1
+    )
+    prompt_terms = lax.all_to_all(prompt_terms, ALL, 0, 0, tiled=True)
+    prompt_terms = jnp.sum(prompt_terms.reshape(n_seq, n_head, -1), 1)
+    prompt_sq = prompt_terms[0, own_rows * kv_cols : own_rows * kv_cols + own_rows]
+    prompt_sum = jnp.transpose(
+        prompt_terms[:, : own_rows * kv_cols].reshape(n_seq, own_rows, kv_cols), (1, 0, 2)
+    ).reshape(own_rows, -1)
     prompt_pairs = finish_keys(prompt_sum * lax.rsqrt(prompt_sq / D + EPS)[:, None], k_gain)
-    prompt_seg = prompt_pairs.shape[0] // pre
-    prompt_pairs = jnp.transpose(prompt_pairs.reshape(prompt_seg, pre, -1), (1, 0, 2))
+    prompt_pairs = prompt_pairs.reshape(pre, prompt_seg, -1)
     prompt_ok = (flat_at * prompt_seg + jnp.arange(prompt_seg))[None, :] < prompt_len[:, None]
     cache_seg = cache.shape[1]
     cache_ok = (flat_at * cache_seg + jnp.arange(cache_seg))[None, :] < cache_len[:, None]
@@ -165,11 +184,6 @@
     local_beams = tail_cache.shape[1]
     offset = (seq_at * tail_seg + jnp.arange(tail_seg))[None, :] - tail_len[:, None]
     all_beams = jnp.arange(beams)
-    every_query, every_fresh = project_tokens(
-        step_tokens, in_gain, w_query, w_keyval, q_gain, k_gain
-    )
-    every_query = every_query.reshape(steps, groups, beams, -1)
-    every_fresh = every_fresh.reshape(steps, groups, beams, -1)
     everyone = lax.all_gather(tail_cache, "head", axis=1, tiled=True)
     n_dev = n_seq * n_head
     first_beam = head_at * local_beams

time: 365 us -> 366 us (level)
  blocking collectives: 157 us -> 150 us
  local copies, waits for them, and re-layouts: 73.8 us -> 80.3 us
  waiting for transfers between devices: 57.4 us -> 51.9 us
  starting transfers between devices: 13.4 us -> 17.9 us
  other arithmetic: 30.1 us -> 34.5 us
    all_gather x1, waiting for transfers between devices: 23.8 us -> 7.16 us  [shards(): prompt_all = lax.all_gather(prompt_states, SEQ, axis=1, tiled=True)]
    all_gather x1, waiting for transfers between devices: 6.45 us -> 15.9 us  [shards(): everyone = lax.all_gather(tail_cache, 'head', axis=1, tiled=True)]
    unnamed x1 -> x0, blocking collectives: 8.04 us -> none
    reshape x2 -> x5, local copies, waits for them, and re-layouts: 0.11 us -> 4.65 us  [the longest x1 3.25 us: shards(): every_query.reshape(steps, groups, beams, KVH, repeat, HD)]
    all_to_all x0 -> x1, starting transfers between devices: none -> 3.75 us  [shards(): prompt_terms = lax.all_to_all(prompt_terms, ALL, 0, 0, tiled=True)]
    unnamed x68 -> x65, local copies, waits for them, and re-layouts: 12 us -> 11.3 us
  transfers between devices with their start and end apart: 6 -> 6, of which waited for: 5 -> 5; matrix products, arithmetic and copies ran while one was open for 16% -> 17% of each run, Pallas kernels for 0% -> 0%
where the time goes in v6:
time: 366 us; the launch traced here: 362 us
  blocking collectives  150 us (41%)
  local copies, waits for them, and re-layouts  80.3 us (22%)
  waiting for transfers between devices  51.9 us (14%)
  other arithmetic  34.5 us (9%)
  starting transfers between devices  17.9 us (5%)
  between operations  14.8 us (4%)
  matrix products  12.3 us (3%)
    all_to_all x6, blocking collectives, exchange_sum(): return jnp.sum(lax.all_to_all(parts, axes, 0, 0, tiled=True), 0)  76.5 us
    all_to_all x6, blocking collectives, exchange_gather(): return lax.all_to_all(spread, axes, 0, 0, tiled=True)  48.2 us
    all_to_all x2, waiting for transfers between devices, exchange_sum(): return jnp.sum(lax.all_to_all(parts, axes, 0, 0, tiled=True), 0)  19.7 us
    all_gather x1, waiting for transfers between devices, shards(): everyone = lax.all_gather(tail_cache, 'head', axis=1, tiled=True)  15.9 us
    all_to_all x1, blocking collectives, exchange_max(): return jnp.max(lax.all_to_all(spread, axes, 0, 0, tiled=True), 0)  15.4 us
    unnamed x65, local copies, waits for them, and re-layouts  11.3 us
    gather x6, local copies, waits for them, and re-layouts, shards(): tail_state = jnp.take_along_axis(everyone, picks[:, :, None, None], axis=1)  8.09 us
    all_to_all x2, starting transfers between devices, exchange_sum(): return jnp.sum(lax.all_to_all(parts, axes, 0, 0, tiled=True), 0)  8.03 us
  transfers between devices with their start and end apart: 6, of which 5 were waited for; matrix products, arithmetic and copies ran while one was open for 17% of the time, Pallas kernels for 0%

profile of v6, /device:TPU:0, one launch (start us, length us, event | category | flops | bytes accessed | tf_op | source)
XLA Modules:
  0.0 361.7 jit_solution(12790799549181467007)
XLA Ops:
  8.6 1.4 fusion.29
  11.1 4.2 %all-to-all-start = ((f32[2,96,384]{2,1,0:T(8,128)}), f32[2,96,384]{2,1,0:T(8,128)S(1)}, u32[]{:S(2)}, u32[]{:S(2)}) async-start(f32[2,96,384]{2,1,0:T(8,128)} %bitcast.2), calls=%async_computation | async-start | bytes 589824 | tf_op jit(solution)/shard_map/all_to_all | solution.py:44
  17.9 1.3 gather_fusion.1
  19.7 1.9 all-to-all-done
  21.8 1.3 broadcast_in_dim.111
  23.1 6.1 %all-to-all-start.1 = ((bf16[32,96,256]{2,1,0:T(8,128)(2,1)}), bf16[32,96,256]{2,1,0:T(8,128)(2,1)S(1)}, u32[]{:S(2)}, u32[]{:S(2)}) async-start(bf16[32,96,256]{2,1,0:T(8,128)(2,1)} %broadcast_in_dim.111), calls=%async_computation.1 | async-start | bytes 3145728 | tf_op jit(solution)/shard_map/all_to_all | solution.py:54
  35.4 15.9 %all-gather.5.cloned.1.call-done = bf16[12,8,4,2048]{3,2,1,0:T(4,128)(2,1)} async-done(((bf16[12,4,4,2048]{3,2,1,0:T(4,128)(2,1)}), bf16[12,8,4,2048]{3,2,1,0:T(4,128)(2,1)}) %all-gather.5.cloned.1.call-update) | async-done | bytes 1572880 | tf_op jit(solution)/shard_map/all_gather | solution.py:187
  51.2 3.9 %gather_fusion.7 = bf16[48,4,2048]{2,1,0:T(4,128)(2,1)} fusion(bf16[12,8,4,2048]{3,2,1,0:T(4,128)(2,1)} %all-gather.5.cloned.1.call-done, s32[48]{0:T(128)S(1)} %reshape.525), kind=kCustom, calls=%fused_computation.7.clone | custom fusion | bytes 1573248 | tf_op jit(solution)/shard_map/jit(take_along_axis)/gather | solution.py:203
  55.1 3.9 %gather_fusion.2 = bf16[48,4,2048]{2,1,0:T(4,128)(2,1)} fusion(bf16[12,8,4,2048]{3,2,1,0:T(4,128)(2,1)} %all-gather.5.cloned.1.call-done, s32[48]{0:T(128)S(1)} %reshape.502), kind=kCustom, calls=%fused_computation.2.clone | custom fusion | bytes 1573248 | tf_op jit(solution)/shard_map/jit(take_along_axis)/gather | solution.py:203
  59.0 7.8 %all-to-all-done.1 = bf16[32,96,256]{2,1,0:T(8,128)(2,1)S(1)} async-done(((bf16[32,96,256]{2,1,0:T(8,128)(2,1)}), bf16[32,96,256]{2,1,0:T(8,128)(2,1)S(1)}, u32[]{:S(2)}, u32[]{:S(2)}) %all-to-all-start.1) | async-done | bytes 1572896 | tf_op jit(solution)/shard_map/all_to_all | solution.py:54
  66.8 1.4 slice_bitcast_fusion
  70.4 2.4 mul.278
  72.8 1.4 reduce_sum.176
  75.6 2.1 copy.380
  77.7 2.6 reshape.417
  81.3 1.4 mul.269
  82.7 1.5 fusion.22
  84.2 2.0 pad_maximum_fusion.2
  87.4 7.2 %all-gather.3.cloned.1.call-done = bf16[4,128,1280]{2,1,0:T(8,128)(2,1)} async-done(((bf16[4,8,1280]{2,1,0:T(8,128)(2,1)}), bf16[4,128,1280]{2,1,0:T(8,128)(2,1)}) %all-gather.3.cloned.1.call-update) | async-done | bytes 1310736 | tf_op jit(solution)/shard_map/all_gather | solution.py:136
  94.5 1.8 fusion
  97.5 1.9 fusion.16
  101.0 3.8 %all-to-all-start.2 = ((f32[32,1,2176]{2,1,0:T(1,128)}), f32[32,1,2176]{2,1,0:T(1,128)S(1)}, u32[]{:S(2)}, u32[]{:S(2)}) async-start(f32[32,1,2176]{2,1,0:T(1,128)} %copy.390), calls=%async_computation.2 | async-start | bytes 557056 | tf_op jit(solution)/shard_map/all_to_all | solution.py:156
  104.9 1.6 gather_fusion
  107.2 1.6 gather_fusion.3
  109.6 1.6 gather_fusion.5
  112.1 1.3 broadcast_select_fusion.2
  113.5 1.5 fusion.26
  115.0 2.2 pad_maximum_fusion.1
  117.1 2.3 reshape.406
  119.5 3.3 reshape.398
  122.7 2.6 copy.385
  125.3 1.4 reduce.7
  132.4 1.8 pad_maximum_fusion
  134.2 1.9 fusion.67
  137.3 1.6 broadcast_bitcast_fusion.2
  138.9 3.7 %reshape.535 = f32[32,1,1536]{2,1,0:T(1,128)S(1)} reshape(f32[32,4,2,2,8,12]{5,4,3,2,1,0:T(8,128)} %broadcast_bitcast_fusion.2) | data formatting | bytes 393216
  142.7 15.4 %all_to_all.94 = f32[32,1,1536]{2,1,0:T(1,128)S(1)} all-to-all(f32[32,1,1536]{2,1,0:T(1,128)S(1)} %reshape.535), channel_id=1, replica_groups=mesh['seq'=8,'pair'=2,'head'=2] {'seq','pair','head'}, dimensions={0} | all-to-all | bytes 393216 | tf_op jit(solution)/shard_map/all_to_all | solution.py:49
  159.7 3.6 reshape.536
  163.3 1.8 bitcast_reduce_fusion
  165.8 2.4 fusion.2
  168.3 2.5 reshape_reshape.4
  170.8 4.2 %copy.471 = f32[12,4,2,8,2,4,64]{6,3,0,2,4,1,5:T(8,128)} copy(f32[12,4,2,8,2,4,64]{6,5,4,3,2,1,0:T(4,128)} %reshape_reshape.4) | data formatting | bytes 3145728 | tf_op jit(solution)/shard_map/reshape;reshape | solution.py:240
  175.0 2.4 concatenate.63
  178.0 5.0 %all_to_all.95 = f32[2,8,2,12544]{3,1,2,0:T(8,128)S(1)} all-to-all(f32[2,8,2,12544]{3,1,2,0:T(8,128)S(1)} %maximum_bitcast_fusion), channel_id=1, replica_groups=mesh['seq'=8,'pair'=2,'head'=2] {'pair'}, dimensions={0} | all-to-all | bytes 3211264 | tf_op jit(solution)/shard_map/all_to_all | solution.py:44
  184.1 1.6 copy.420
  186.8 24.8 %all_to_all.96 = f32[16,1,12544]{2,1,0:T(1,128)S(1)} all-to-all(f32[16,1,12544]{2,1,0:T(1,128)S(1)} %all_to_all.76), channel_id=1, replica_groups=mesh['seq'=8,'pair'=2,'head'=2] {'seq','head'}, dimensions={0} | all-to-all | bytes 1605632 | tf_op jit(solution)/shard_map/all_to_all | solution.py:44
  212.4 6.5 %all_to_all.97 = bf16[2,192,64]{1,2,0:T(8,128)(2,1)S(1)} all-to-all(bf16[2,192,64]{1,2,0:T(8,128)(2,1)S(1)} %broadcast_in_dim.223), channel_id=1, replica_groups=mesh['seq'=8,'pair'=2,'head'=2] {'head'}, dimensions={0} | all-to-all | bytes 98304 | tf_op jit(solution)/shard_map/all_to_all | solution.py:54
  220.1 4.5 %all_to_all.98 = f32[2,8,12,1280]{3,1,2,0:T(8,128)S(1)} all-to-all(f32[2,8,12,1280]{3,1,2,0:T(8,128)S(1)} %copy.424), channel_id=1, replica_groups=mesh['seq'=8,'pair'=2,'head'=2] {'pair'}, dimensions={0} | all-to-all | bytes 1966080 | tf_op jit(solution)/shard_map/all_to_all | solution.py:44
  225.7 3.8 %all-to-all-start.8 = ((f32[8,12,1280]{2,1,0:T(8,128)}), f32[8,12,1280]{2,1,0:T(8,128)S(1)}, u32[]{:S(2)}, u32[]{:S(2)}) async-start(f32[8,12,1280]{2,1,0:T(8,128)} %copy.425), calls=%async_computation.8 | async-start | bytes 1310720 | tf_op jit(solution)/shard_map/all_to_all | solution.py:44
  229.5 17.8 %all-to-all-done.8 = f32[8,12,1280]{2,1,0:T(8,128)S(1)} async-done(((f32[8,12,1280]{2,1,0:T(8,128)}), f32[8,12,1280]{2,1,0:T(8,128)S(1)}, u32[]{:S(2)}, u32[]{:S(2)}) %all-to-all-start.8) | async-done | bytes 491552 | tf_op jit(solution)/shard_map/all_to_all | solution.py:44
  247.4 4.9 %psum.14 = f32[12]{0:T(128)S(1)} all-reduce(f32[12]{0:T(128)S(1)} %multiply_reduce_fusion.3), channel_id=1, replica_groups=mesh['seq'=8,'pair'=2,'head'=2] {'head'}, use_global_device_ids=true, to_apply=%region_16.20 | all-reduce | flops 12 | bytes 96 | tf_op jit(solution)/shard_map/psum | solution.py:257
  253.3 13.3 %all_to_all.99 = bf16[8,12,1280]{2,1,0:T(8,128)(2,1)S(1)} all-to-all(bf16[8,12,1280]{2,1,0:T(8,128)(2,1)S(1)} %broadcast_in_dim.224), channel_id=1, replica_groups=mesh['seq'=8,'pair'=2,'head'=2] {'seq'}, dimensions={0} | all-to-all | bytes 491520 | tf_op jit(solution)/shard_map/all_to_all | solution.py:54
  266.8 4.1 %all_to_all.100 = bf16[2,8,12,1280]{3,1,2,0:T(8,128)(2,1)S(1)} all-to-all(bf16[2,8,12,1280]{3,1,2,0:T(8,128)(2,1)S(1)} %broadcast_in_dim.225), channel_id=1, replica_groups=mesh['seq'=8,'pair'=2,'head'=2] {'pair'}, dimensions={0} | all-to-all | bytes 983040 | tf_op jit(solution)/shard_map/all_to_all | solution.py:54
  271.0 1.4 copy.427
  272.4 1.4 reshape.418
  273.8 2.9 fusion.47
  276.8 1.3 fusion.48
  279.7 17.0 %all_to_all.101 = f32[2,96,1408]{2,1,0:T(8,128)S(1)} all-to-all(f32[2,96,1408]{2,1,0:T(8,128)S(1)} %bitcast.193), channel_id=1, replica_groups=mesh['seq'=8,'pair'=2,'head'=2] {'head'}, dimensions={0} | all-to-all | bytes 2162688 | tf_op jit(solution)/shard_map/all_to_all | solution.py:44
  297.1 7.5 %all_to_all.102 = bf16[2,96,640]{2,1,0:T(8,128)(2,1)S(1)} all-to-all(bf16[2,96,640]{2,1,0:T(8,128)(2,1)S(1)} %broadcast_in_dim.227), channel_id=1, replica_groups=mesh['seq'=8,'pair'=2,'head'=2] {'head'}, dimensions={0} | all-to-all | bytes 491520 | tf_op jit(solution)/shard_map/all_to_all | solution.py:54
  305.9 4.5 %all_to_all.103 = f32[2,8,12,1280]{3,1,2,0:T(8,128)S(1)} all-to-all(f32[2,8,12,1280]{3,1,2,0:T(8,128)S(1)} %copy.430), channel_id=1, replica_groups=mesh['seq'=8,'pair'=2,'head'=2] {'pair'}, dimensions={0} | all-to-all | bytes 1966080 | tf_op jit(solution)/shard_map/all_to_all | solution.py:44
  310.7 20.8 %all_to_all.104 = f32[8,12,1280]{2,1,0:T(8,128)S(1)} all-to-all(f32[8,12,1280]{2,1,0:T(8,128)S(1)} %copy.431), channel_id=1, replica_groups=mesh['seq'=8,'pair'=2,'head'=2] {'seq'}, dimensions={0} | all-to-all | bytes 983040 | tf_op jit(solution)/shard_map/all_to_all | solution.py:44
  331.7 4.9 %psum.15 = f32[12]{0:T(128)S(1)} all-reduce(f32[12]{0:T(128)S(1)} %multiply_reduce_fusion.2), channel_id=1, replica_groups=mesh['seq'=8,'pair'=2,'head'=2] {'head'}, use_global_device_ids=true, to_apply=%region_22.26 | all-reduce | flops 12 | bytes 96 | tf_op jit(solution)/shard_map/psum | solution.py:280
  336.7 12.6 %all_to_all.105 = bf16[8,12,1280]{2,1,0:T(8,128)(2,1)S(1)} all-to-all(bf16[8,12,1280]{2,1,0:T(8,128)(2,1)S(1)} %broadcast_in_dim.228), channel_id=1, replica_groups=mesh['seq'=8,'pair'=2,'head'=2] {'seq'}, dimensions={0} | all-to-all | bytes 491520 | tf_op jit(solution)/shard_map/all_to_all | solution.py:54
  349.5 4.1 %all_to_all.106 = bf16[2,8,12,1280]{3,1,2,0:T(8,128)(2,1)S(1)} all-to-all(bf16[2,8,12,1280]{3,1,2,0:T(8,128)(2,1)S(1)} %broadcast_in_dim.229), channel_id=1, replica_groups=mesh['seq'=8,'pair'=2,'head'=2] {'pair'}, dimensions={0} | all-to-all | bytes 983040 | tf_op jit(solution)/shard_map/all_to_all | solution.py:54
  (231 shorter events, 44.5 us)
Async XLA Ops:
  6.5 298.1 %copy-start = (bf16[640,1280]{1,0:T(8,128)(2,1)S(1)}, bf16[640,1280]{1,0:T(8,128)(2,1)}, u32[]{:S(2)}) copy-start(bf16[640,1280]{1,0:T(8,128)(2,1)} %param.44) | copy-start | bytes 4915204
  6.5 3.5 copy-start.11
  6.5 3.5 copy-start.18
  6.5 3.5 copy-start.25
  6.5 44.7 %all-gather.5.cloned.1.call-start = ((), (), s32[]{:S(2)}) async-start(), calls=%async_computation.18 | async-start | bytes 2359296 | tf_op jit(solution)/shard_map/all_gather | solution.py:187
  8.6 7.5 %copy-start.14 = (s32[2,12,8]{1,2,0:T(8,128)S(1)}, s32[2,12,8]{1,2,0:T(8,128)}, u32[]{:S(2)}) copy-start(s32[2,12,8]{1,2,0:T(8,128)} %param.27) | copy-start | bytes 2308
  11.1 10.5 %all-to-all-start = ((f32[2,96,384]{2,1,0:T(8,128)}), f32[2,96,384]{2,1,0:T(8,128)S(1)}, u32[]{:S(2)}, u32[]{:S(2)}) async-start(f32[2,96,384]{2,1,0:T(8,128)} %bitcast.2), calls=%async_computation | async-start | bytes 589824 | tf_op jit(solution)/shard_map/all_to_all | solution.py:44
  15.3 79.2 %all-gather.3.cloned.1.call-start = ((), (), s32[]{:S(2)}) async-start(), calls=%async_computation.17 | async-start | bytes 1392640 | tf_op jit(solution)/shard_map/all_gather | solution.py:136
  17.9 1.5 copy-start.21
  23.1 43.6 %all-to-all-start.1 = ((bf16[32,96,256]{2,1,0:T(8,128)(2,1)}), bf16[32,96,256]{2,1,0:T(8,128)(2,1)S(1)}, u32[]{:S(2)}, u32[]{:S(2)}) async-start(bf16[32,96,256]{2,1,0:T(8,128)(2,1)} %broadcast_in_dim.111), calls=%async_computation.1 | async-start | bytes 3145728 | tf_op jit(solution)/shard_map/all_to_all | solution.py:54
  29.3 2.0 copy-start.26
  29.3 2.1 copy-start.24
  29.3 2.4 copy-start.22
  29.3 2.5 copy-start.23
  68.4 1.0 copy-start.4
  74.2 1.4 copy-start.2
  82.7 3.5 copy-start.1
  82.7 3.5 copy-start.3
  99.4 5.4 %copy-start.8 = (bf16[2,12,8,2048]{3,2,1,0:T(8,128)(2,1)S(1)}, bf16[2,12,8,2048]{3,2,1,0:T(8,128)(2,1)}, u32[]{:S(2)}) copy-start(bf16[2,12,8,2048]{3,2,1,0:T(8,128)(2,1)} %pad_maximum_fusion.2) | copy-start | bytes 2359300
  101.0 24.3 %all-to-all-start.2 = ((f32[32,1,2176]{2,1,0:T(1,128)}), f32[32,1,2176]{2,1,0:T(1,128)S(1)}, u32[]{:S(2)}, u32[]{:S(2)}) async-start(f32[32,1,2176]{2,1,0:T(1,128)} %copy.390), calls=%async_computation.2 | async-start | bytes 557056 | tf_op jit(solution)/shard_map/all_to_all | solution.py:156
  109.5 3.9 %copy-start.5 = (bf16[48,4,2048]{2,1,0:T(4,128)(2,1)S(1)}, bf16[48,4,2048]{2,1,0:T(4,128)(2,1)}, u32[]{:S(2)}) copy-start(bf16[48,4,2048]{2,1,0:T(4,128)(2,1)} %gather_fusion.7) | copy-start | bytes 2359300
  109.5 3.9 %copy-start.15 = (pred[12,4]{1,0:T(8,128)(4,1)S(1)}, pred[12,4]{1,0:T(8,128)(4,1)}, u32[]{:S(2)}) copy-start(pred[12,4]{1,0:T(8,128)(4,1)} %copy.406) | copy-start | bytes 148
  111.1 2.3 copy-start.16
  111.1 2.3 copy-start.17
  111.2 2.2 copy-start.6
  134.2 1.9 copy-start.10
  137.2 28.1 %copy-start.7 = (f32[12,4,32,96]{3,2,1,0:T(8,128)}, f32[12,4,32,96]{3,2,1,0:T(8,128)S(1)}, u32[]{:S(2)}) copy-start(f32[12,4,32,96]{3,2,1,0:T(8,128)S(1)} %get-tuple-element.38) | copy-start | bytes 1769476
  211.6 7.6 %copy-start.12 = (bf16[128,1280]{1,0:T(8,128)(2,1)S(1)}, bf16[128,1280]{1,0:T(8,128)(2,1)}, u32[]{:S(2)}) copy-start(bf16[128,1280]{1,0:T(8,128)(2,1)} %param.39) | copy-start | bytes 983044
  224.7 27.7 %copy-start.19 = (f32[1280]{0:T(1024)S(1)}, f32[1280]{0:T(1024)}, u32[]{:S(2)}) copy-start(f32[1280]{0:T(1024)} %param.40) | copy-start | bytes 15364
  225.7 21.6 %all-to-all-start.8 = ((f32[8,12,1280]{2,1,0:T(8,128)}), f32[8,12,1280]{2,1,0:T(8,128)S(1)}, u32[]{:S(2)}, u32[]{:S(2)}) async-start(f32[8,12,1280]{2,1,0:T(8,128)} %copy.425), calls=%async_computation.8 | async-start | bytes 1310720 | tf_op jit(solution)/shard_map/all_to_all | solution.py:44
  272.4 1.4 copy-start.13
  273.8 2.9 copy-start.9
  310.5 26.1 %copy-start.20 = (f32[1280]{0:T(1024)S(1)}, f32[1280]{0:T(1024)}, u32[]{:S(2)}) copy-start(f32[1280]{0:T(1024)} %param.45) | copy-start | bytes 15364
Sparse Core Ops, SparseCore 0:
  8.9 42.2 all-gather.4
  53.4 41.0 all-gather.2

commit v7 on v5

--- a/solution.py
+++ b/solution.py
@@ -45,8 +45,9 @@
 
 
 def exchange_max(value, axes, count):
-    spread = jnp.broadcast_to(value[None], (count,) + value.shape)
-    return jnp.max(lax.all_to_all(spread, axes, 0, 0, tiled=True), 0)
+    flat = value.reshape(-1, 128)
+    spread = jnp.broadcast_to(flat[None], (count,) + flat.shape)
+    return jnp.max(lax.all_to_all(spread, axes, 0, 0, tiled=True), 0).reshape(value.shape)
 
 
 def exchange_gather(piece, axes, count):
@@ -229,9 +230,9 @@
     lanes = -(-rows // 128) * 128
     packed = jnp.concatenate([weighted, jnp.pad(total, ((0, 0), (0, lanes - rows)))], 1)
     pair = lax.axis_size("pair")
-    packed = packed.reshape(n_seq // pair, pair, n_head, -1)
-    packed = exchange_sum(jnp.swapaxes(packed, 0, 1), "pair").reshape(n_dev // pair, -1)
-    packed = exchange_sum(packed, ("seq", "head"))
+    packed = packed.reshape(n_seq // pair, pair, n_head, -1, 128)
+    packed = exchange_sum(jnp.swapaxes(packed, 0, 1), "pair").reshape(n_dev // pair, -1, 128)
+    packed = exchange_sum(packed, ("seq", "head")).reshape(-1)
     share = packed[: rows * piece].reshape(rows, piece)
     own_total = packed[rows * piece : rows * piece + rows]
     attn = (share / own_total[:, None]).astype(bf16)

time: 365 us -> 353 us (0.967); the launches traced: 360 us -> 352 us
  local copies, waits for them, and re-layouts: 73.8 us -> 66 us
    unnamed x68 -> x65, local copies, waits for them, and re-layouts: 12 us -> 3.27 us
    reshape x0 -> x3, local copies, waits for them, and re-layouts: none -> 4.25 us  [the longest x1 2.42 us: shards(): weighted = jnp.transpose(weighted.reshape(groups, KVH, steps, beams, repe...]
  transfers between devices with their start and end apart: 6 -> 6, of which waited for: 5 -> 5; matrix products, arithmetic and copies ran while one was open for 16% -> 17% of each run, Pallas kernels for 0% -> 0%
where the time goes in v7:
time: 353 us; the launch traced here: 352 us
  blocking collectives  159 us (45%)
  local copies, waits for them, and re-layouts  66 us (19%)
  waiting for transfers between devices  57.3 us (16%)
  other arithmetic  28 us (8%)
  between operations  14.8 us (4%)
  matrix products  13.5 us (4%)
  starting transfers between devices  13.4 us (4%)
    all_to_all x6, blocking collectives, exchange_sum(): return jnp.sum(lax.all_to_all(parts, axes, 0, 0, tiled=True), 0)  78 us
    all_to_all x6, blocking collectives, exchange_gather(): return lax.all_to_all(spread, axes, 0, 0, tiled=True)  48.2 us
    all_gather x1, waiting for transfers between devices, shards(): lax.all_gather(w_keyval, SEQ, axis=1, tiled=True)  23.7 us
    all_to_all x2, waiting for transfers between devices, exchange_sum(): return jnp.sum(lax.all_to_all(parts, axes, 0, 0, tiled=True), 0)  19.3 us
    all_to_all x1, blocking collectives, exchange_max(): lax.all_to_all(spread, axes, 0, 0, tiled=True)  14.5 us
    gather x6, local copies, waits for them, and re-layouts, shards(): tail_state = jnp.take_along_axis(everyone, picks[:, :, None, None], axis=1)  8.11 us
    unnamed x1, blocking collectives  8.04 us
    all_to_all x2, starting transfers between devices, exchange_sum(): return jnp.sum(lax.all_to_all(parts, axes, 0, 0, tiled=True), 0)  7.77 us
  transfers between devices with their start and end apart: 6, of which 5 were waited for; matrix products, arithmetic and copies ran while one was open for 17% of the time, Pallas kernels for 0%

profile of v7, /device:TPU:0, one launch (start us, length us, event | category | flops | bytes accessed | tf_op | source)
XLA Modules:
  0.0 351.7 jit_solution(14616395222462093316)
XLA Ops:
  8.0 1.2 multiply_reduce_fusion.1
  10.7 4.2 %all-to-all-start = ((f32[2,96,384]{2,1,0:T(8,128)}), f32[2,96,384]{2,1,0:T(8,128)S(1)}, u32[]{:S(2)}, u32[]{:S(2)}) async-start(f32[2,96,384]{2,1,0:T(8,128)} %bitcast.2), calls=%async_computation | async-start | bytes 589824 | tf_op jit(solution)/shard_map/all_to_all | solution.py:44
  15.1 1.3 gather_fusion.4
  16.8 1.3 gather_fusion.1
  19.7 1.5 all-to-all-done
  21.4 1.3 broadcast_in_dim.111
  22.8 5.5 %all-to-all-start.1 = ((bf16[32,96,256]{2,1,0:T(8,128)(2,1)}), bf16[32,96,256]{2,1,0:T(8,128)(2,1)S(1)}, u32[]{:S(2)}, u32[]{:S(2)}) async-start(bf16[32,96,256]{2,1,0:T(8,128)(2,1)} %broadcast_in_dim.111), calls=%async_computation.1 | async-start | bytes 3145728 | tf_op jit(solution)/shard_map/all_to_all | solution.py:55
  34.9 8.0 %all-reduce.5 = f32[32]{0:T(128)S(1)} all-reduce(f32[32]{0:T(128)S(1)} %reshape.372), channel_id=3, replica_groups=mesh['seq'=8,'pair'=2,'head'=2] {'head'}, use_global_device_ids=true, to_apply=%region_6.7.clone | all-reduce | flops 32 | bytes 256
  43.8 1.3 subtract_compare_fusion.1
  45.2 6.4 %all-gather.5.cloned.1.call-done = bf16[12,8,4,2048]{3,2,1,0:T(4,128)(2,1)} async-done(((bf16[12,4,4,2048]{3,2,1,0:T(4,128)(2,1)}), bf16[12,8,4,2048]{3,2,1,0:T(4,128)(2,1)}) %all-gather.5.cloned.1.call-update) | async-done | bytes 1572880 | tf_op jit(solution)/shard_map/all_gather | solution.py:174
  51.6 3.9 %gather_fusion.7 = bf16[48,4,2048]{2,1,0:T(4,128)(2,1)} fusion(bf16[12,8,4,2048]{3,2,1,0:T(4,128)(2,1)} %all-gather.5.cloned.1.call-done, s32[48]{0:T(128)S(1)} %reshape.496), kind=kCustom, calls=%fused_computation.7.clone | custom fusion | bytes 1573248 | tf_op jit(solution)/shard_map/jit(take_along_axis)/gather | solution.py:190
  55.5 3.9 %gather_fusion.2 = bf16[48,4,2048]{2,1,0:T(4,128)(2,1)} fusion(bf16[12,8,4,2048]{3,2,1,0:T(4,128)(2,1)} %all-gather.5.cloned.1.call-done, s32[48]{0:T(128)S(1)} %reshape.473), kind=kCustom, calls=%fused_computation.2.clone | custom fusion | bytes 1573248 | tf_op jit(solution)/shard_map/jit(take_along_axis)/gather | solution.py:190
  59.4 6.4 %all-to-all-done.1 = bf16[32,96,256]{2,1,0:T(8,128)(2,1)S(1)} async-done(((bf16[32,96,256]{2,1,0:T(8,128)(2,1)}), bf16[32,96,256]{2,1,0:T(8,128)(2,1)S(1)}, u32[]{:S(2)}, u32[]{:S(2)}) %all-to-all-start.1) | async-done | bytes 1572896 | tf_op jit(solution)/shard_map/all_to_all | solution.py:55
  65.8 1.2 copy-done.1
  67.0 1.5 fusion.67
  70.5 2.4 mul.285
  72.9 1.4 reduce_sum.172
  75.6 1.6 gather_fusion
  78.0 1.6 gather_fusion.3
  80.3 1.6 gather_fusion.5
  83.3 1.2 broadcast_select_fusion
  84.5 1.3 broadcast_select_fusion.2
  85.8 1.7 fusion.21
  87.6 2.2 pad_maximum_fusion
  89.7 1.7 copy_convert_fusion
  91.4 23.7 %all-gather.3.cloned.1.call-done = bf16[1280,2048]{1,0:T(8,128)(2,1)} async-done(((bf16[1280,128]{1,0:T(8,128)(2,1)}), bf16[1280,2048]{1,0:T(8,128)(2,1)}) %all-gather.3.cloned.1.call-update) | async-done | bytes 5242896 | tf_op jit(solution)/shard_map/all_gather | solution.py:136
  115.1 4.2 %fusion.69 = f32[32,2048]{1,0:T(8,128)} fusion(bf16[32,1280]{1,0:T(8,128)(2,1)S(1)} %reshape.371, bf16[1280,2048]{1,0:T(8,128)(2,1)} %all-gather.3.cloned.1.call-done), kind=kOutput, calls=%fused_computation.174 | convolution fusion | flops 167772160 | bytes 5586944 | tf_op jit(solution)/shard_map/dot_general | solution.py:134
  119.4 2.4 reshape.373
  121.8 3.1 reshape.388
  124.9 1.4 copy.497
  126.3 2.2 fusion.22
  128.6 1.4 copy.498
  132.8 1.8 fusion.4
  134.6 1.9 fusion.66
  136.6 1.1 fusion.68
  137.8 14.5 %all_to_all.80 = f32[32,12,128]{2,1,0:T(8,128)S(1)} all-to-all(f32[32,12,128]{2,1,0:T(8,128)S(1)} %broadcast_in_dim.220), channel_id=1, replica_groups=mesh['seq'=8,'pair'=2,'head'=2] {'seq','pair','head'}, dimensions={0} | all-to-all | bytes 393216 | tf_op jit(solution)/shard_map/all_to_all | solution.py:50
  153.0 2.4 fusion.5
  155.4 2.5 reshape_reshape.4
  157.9 4.1 %copy.577 = f32[12,4,2,8,2,4,64]{6,3,0,2,5,4,1:T(8,128)} copy(f32[12,4,2,8,2,4,64]{6,5,4,3,2,1,0:T(4,128)} %reshape_reshape.4) | data formatting | bytes 3145728 | tf_op jit(solution)/shard_map/reshape;reshape | solution.py:227
  162.0 2.4 reshape.376
  164.9 1.3 select_maximum_fusion
  166.2 1.6 reshape.380
  168.7 5.0 %all_to_all.81 = f32[2,8,2,98,128]{4,1,3,2,0:T(8,128)S(1)} all-to-all(f32[2,8,2,98,128]{4,1,3,2,0:T(8,128)S(1)} %copy.530), channel_id=1, replica_groups=mesh['seq'=8,'pair'=2,'head'=2] {'pair'}, dimensions={0} | all-to-all | bytes 3211264 | tf_op jit(solution)/shard_map/all_to_all | solution.py:44
  174.8 1.6 copy.531
  176.6 26.3 %all_to_all.82 = f32[16,98,128]{2,1,0:T(8,128)S(1)} all-to-all(f32[16,98,128]{2,1,0:T(8,128)S(1)} %copy.532), channel_id=1, replica_groups=mesh['seq'=8,'pair'=2,'head'=2] {'seq','head'}, dimensions={0} | all-to-all | bytes 1605632 | tf_op jit(solution)/shard_map/all_to_all | solution.py:44
  203.2 6.5 %all_to_all.83 = bf16[2,192,64]{1,2,0:T(8,128)(2,1)S(1)} all-to-all(bf16[2,192,64]{1,2,0:T(8,128)(2,1)S(1)} %broadcast_in_dim.223), channel_id=1, replica_groups=mesh['seq'=8,'pair'=2,'head'=2] {'head'}, dimensions={0} | all-to-all | bytes 98304 | tf_op jit(solution)/shard_map/all_to_all | solution.py:55
  210.8 4.5 %all_to_all.84 = f32[2,8,12,1280]{3,1,2,0:T(8,128)S(1)} all-to-all(f32[2,8,12,1280]{3,1,2,0:T(8,128)S(1)} %copy.535), channel_id=1, replica_groups=mesh['seq'=8,'pair'=2,'head'=2] {'pair'}, dimensions={0} | all-to-all | bytes 1966080 | tf_op jit(solution)/shard_map/all_to_all | solution.py:44
  216.5 3.5 %all-to-all-start.7 = ((f32[8,12,1280]{2,1,0:T(8,128)}), f32[8,12,1280]{2,1,0:T(8,128)S(1)}, u32[]{:S(2)}, u32[]{:S(2)}) async-start(f32[8,12,1280]{2,1,0:T(8,128)} %copy.536), calls=%async_computation.8 | async-start | bytes 1310720 | tf_op jit(solution)/shard_map/all_to_all | solution.py:44
  220.0 17.8 %all-to-all-done.7 = f32[8,12,1280]{2,1,0:T(8,128)S(1)} async-done(((f32[8,12,1280]{2,1,0:T(8,128)}), f32[8,12,1280]{2,1,0:T(8,128)S(1)}, u32[]{:S(2)}, u32[]{:S(2)}) %all-to-all-start.7) | async-done | bytes 491552 | tf_op jit(solution)/shard_map/all_to_all | solution.py:44
  238.0 4.9 %psum.14 = f32[12]{0:T(128)S(1)} all-reduce(f32[12]{0:T(128)S(1)} %multiply_reduce_fusion.3), channel_id=1, replica_groups=mesh['seq'=8,'pair'=2,'head'=2] {'head'}, use_global_device_ids=true, to_apply=%region_17.21 | all-reduce | flops 12 | bytes 96 | tf_op jit(solution)/shard_map/psum | solution.py:244
  243.9 13.3 %all_to_all.85 = bf16[8,12,1280]{2,1,0:T(8,128)(2,1)S(1)} all-to-all(bf16[8,12,1280]{2,1,0:T(8,128)(2,1)S(1)} %broadcast_in_dim.224), channel_id=1, replica_groups=mesh['seq'=8,'pair'=2,'head'=2] {'seq'}, dimensions={0} | all-to-all | bytes 491520 | tf_op jit(solution)/shard_map/all_to_all | solution.py:55
  257.4 4.1 %all_to_all.86 = bf16[2,8,12,1280]{3,1,2,0:T(8,128)(2,1)S(1)} all-to-all(bf16[2,8,12,1280]{3,1,2,0:T(8,128)(2,1)S(1)} %broadcast_in_dim.225), channel_id=1, replica_groups=mesh['seq'=8,'pair'=2,'head'=2] {'pair'}, dimensions={0} | all-to-all | bytes 983040 | tf_op jit(solution)/shard_map/all_to_all | solution.py:55
  261.5 1.4 copy.538
  262.9 1.4 reshape.389
  264.4 2.9 fusion.44
  267.3 1.3 fusion.45
  269.0 1.3 select_maximum_fusion.1
  270.3 17.0 %all_to_all.87 = f32[2,96,1408]{2,1,0:T(8,128)S(1)} all-to-all(f32[2,96,1408]{2,1,0:T(8,128)S(1)} %bitcast.169), channel_id=1, replica_groups=mesh['seq'=8,'pair'=2,'head'=2] {'head'}, dimensions={0} | all-to-all | bytes 2162688 | tf_op jit(solution)/shard_map/all_to_all | solution.py:44
  287.7 7.5 %all_to_all.88 = bf16[2,96,640]{2,1,0:T(8,128)(2,1)S(1)} all-to-all(bf16[2,96,640]{2,1,0:T(8,128)(2,1)S(1)} %broadcast_in_dim.227), channel_id=1, replica_groups=mesh['seq'=8,'pair'=2,'head'=2] {'head'}, dimensions={0} | all-to-all | bytes 491520 | tf_op jit(solution)/shard_map/all_to_all | solution.py:55
  296.5 4.5 %all_to_all.89 = f32[2,8,12,1280]{3,1,2,0:T(8,128)S(1)} all-to-all(f32[2,8,12,1280]{3,1,2,0:T(8,128)S(1)} %copy.541), channel_id=1, replica_groups=mesh['seq'=8,'pair'=2,'head'=2] {'pair'}, dimensions={0} | all-to-all | bytes 1966080 | tf_op jit(solution)/shard_map/all_to_all | solution.py:44
  301.3 20.8 %all_to_all.90 = f32[8,12,1280]{2,1,0:T(8,128)S(1)} all-to-all(f32[8,12,1280]{2,1,0:T(8,128)S(1)} %copy.542), channel_id=1, replica_groups=mesh['seq'=8,'pair'=2,'head'=2] {'seq'}, dimensions={0} | all-to-all | bytes 983040 | tf_op jit(solution)/shard_map/all_to_all | solution.py:44
  322.2 4.9 %psum.15 = f32[12]{0:T(128)S(1)} all-reduce(f32[12]{0:T(128)S(1)} %multiply_reduce_fusion.2), channel_id=1, replica_groups=mesh['seq'=8,'pair'=2,'head'=2] {'head'}, use_global_device_ids=true, to_apply=%region_23.27 | all-reduce | flops 12 | bytes 96 | tf_op jit(solution)/shard_map/psum | solution.py:267
  327.3 12.6 %all_to_all.91 = bf16[8,12,1280]{2,1,0:T(8,128)(2,1)S(1)} all-to-all(bf16[8,12,1280]{2,1,0:T(8,128)(2,1)S(1)} %broadcast_in_dim.228), channel_id=1, replica_groups=mesh['seq'=8,'pair'=2,'head'=2] {'seq'}, dimensions={0} | all-to-all | bytes 491520 | tf_op jit(solution)/shard_map/all_to_all | solution.py:55
  340.0 4.1 %all_to_all.92 = bf16[2,8,12,1280]{3,1,2,0:T(8,128)(2,1)S(1)} all-to-all(bf16[2,8,12,1280]{3,1,2,0:T(8,128)(2,1)S(1)} %broadcast_in_dim.229), channel_id=1, replica_groups=mesh['seq'=8,'pair'=2,'head'=2] {'pair'}, dimensions={0} | all-to-all | bytes 983040 | tf_op jit(solution)/shard_map/all_to_all | solution.py:55
  (222 shorter events, 32.0 us)
Async XLA Ops:
  6.5 288.7 %copy-start = (bf16[640,1280]{1,0:T(8,128)(2,1)S(1)}, bf16[640,1280]{1,0:T(8,128)(2,1)}, u32[]{:S(2)}) copy-start(bf16[640,1280]{1,0:T(8,128)(2,1)} %param.44) | copy-start | bytes 4915204
  6.5 2.8 copy-start.9
  6.5 2.8 copy-start.8
  6.5 2.8 copy-start.18
  6.5 3.1 copy-start.27
  6.5 45.1 %all-gather.5.cloned.1.call-start = ((), (), s32[]{:S(2)}) async-start(), calls=%async_computation.19 | async-start | bytes 2359296 | tf_op jit(solution)/shard_map/all_gather | solution.py:174
  7.3 107.9 %all-gather.3.cloned.1.call-start = ((), (), s32[]{:S(2)}) async-start(), calls=%async_computation.17 | async-start | bytes 5570560 | tf_op jit(solution)/shard_map/all_gather | solution.py:136
  9.2 5.7 %copy-start.13 = (s32[2,12,8]{1,2,0:T(8,128)S(1)}, s32[2,12,8]{1,2,0:T(8,128)}, u32[]{:S(2)}) copy-start(s32[2,12,8]{1,2,0:T(8,128)} %param.27) | copy-start | bytes 2308
  10.7 10.5 %all-to-all-start = ((f32[2,96,384]{2,1,0:T(8,128)}), f32[2,96,384]{2,1,0:T(8,128)S(1)}, u32[]{:S(2)}, u32[]{:S(2)}) async-start(f32[2,96,384]{2,1,0:T(8,128)} %bitcast.2), calls=%async_computation | async-start | bytes 589824 | tf_op jit(solution)/shard_map/all_to_all | solution.py:44
  18.2 1.3 copy-start.24
  22.7 9.1 %copy-start.11 = (bf16[4,8,1280]{2,1,0:T(8,128)(2,1)S(1)}, bf16[4,8,1280]{2,1,0:T(8,128)(2,1)}, u32[]{:S(2)}) copy-start(bf16[4,8,1280]{2,1,0:T(8,128)(2,1)} %param.32) | copy-start | bytes 245764
  22.7 9.9 %copy-start.21 = (s32[12]{0:T(128)S(1)}, s32[12]{0:T(128)}, u32[]{:S(2)}) copy-start(s32[12]{0:T(128)} %param.29) | copy-start | bytes 148
  22.7 10.9 %copy-start.29 = (u32[32]{0:T(128)S(1)}, u32[32]{0:T(128)}, u32[]{:S(2)}) copy-start(u32[32]{0:T(128)} %constant.271) | copy-start | bytes 388
  22.8 20.8 %copy-start.28 = (s32[4]{0:T(128)S(1)}, s32[4]{0:T(128)}, u32[]{:S(2)}) copy-start(s32[4]{0:T(128)} %param.33) | copy-start | bytes 52
  22.8 20.8 %copy-start.26 = (s32[8]{0:T(128)S(1)}, s32[8]{0:T(128)}, u32[]{:S(2)}) copy-start(s32[8]{0:T(128)} %param.31) | copy-start | bytes 100
  22.8 43.0 %all-to-all-start.1 = ((bf16[32,96,256]{2,1,0:T(8,128)(2,1)}), bf16[32,96,256]{2,1,0:T(8,128)(2,1)S(1)}, u32[]{:S(2)}, u32[]{:S(2)}) async-start(bf16[32,96,256]{2,1,0:T(8,128)(2,1)} %broadcast_in_dim.111), calls=%async_computation.1 | async-start | bytes 3145728 | tf_op jit(solution)/shard_map/all_to_all | solution.py:55
  28.3 101.7 %reduce-scatter.2.cloned.1.call-start = ((), (), s32[]{:S(2)}) async-start(), calls=%async_computation.18 | async-start | bytes 393216 | tf_op jit(solution)/shard_map/reduce_scatter | solution.py:140
  32.2 0.5 copy-start.22
  65.8 1.2 copy-start.1
  74.6 1.0 copy-start.6
  81.9 3.9 %copy-start.2 = (bf16[48,4,2048]{2,1,0:T(4,128)(2,1)S(1)}, bf16[48,4,2048]{2,1,0:T(4,128)(2,1)}, u32[]{:S(2)}) copy-start(bf16[48,4,2048]{2,1,0:T(4,128)(2,1)} %gather_fusion.7) | copy-start | bytes 2359300
  82.6 3.2 copy-start.14
  82.6 3.2 copy-start.15
  82.6 3.2 copy-start.16
  82.6 3.2 copy-start.17
  83.3 2.5 copy-start.3
  121.8 4.6 %copy-start.23 = (f32[256]{0:T(256)S(1)}, f32[256]{0:T(256)}, u32[]{:S(2)}) copy-start(f32[256]{0:T(256)} %param.37) | copy-start | bytes 3076
  126.3 3.7 %copy-start.25 = (f32[16]{0:T(128)S(1)}, f32[16]{0:T(128)}, u32[]{:S(2)}) copy-start(f32[16]{0:T(128)} %fusion.63) | copy-start | bytes 196
  134.6 1.9 copy-start.7
  137.6 15.3 %copy-start.4 = (f32[12,4,32,96]{3,2,1,0:T(8,128)}, f32[12,4,32,96]{3,2,1,0:T(8,128)S(1)}, u32[]{:S(2)}) copy-start(f32[12,4,32,96]{3,2,1,0:T(8,128)S(1)} %get-tuple-element.32) | copy-start | bytes 1769476
  176.6 33.4 %copy-start.10 = (bf16[128,1280]{1,0:T(8,128)(2,1)S(1)}, bf16[128,1280]{1,0:T(8,128)(2,1)}, u32[]{:S(2)}) copy-start(bf16[128,1280]{1,0:T(8,128)(2,1)} %param.39) | copy-start | bytes 983044
  215.5 27.5 %copy-start.19 = (f32[1280]{0:T(1024)S(1)}, f32[1280]{0:T(1024)}, u32[]{:S(2)}) copy-start(f32[1280]{0:T(1024)} %param.40) | copy-start | bytes 15364
  216.5 21.4 %all-to-all-start.7 = ((f32[8,12,1280]{2,1,0:T(8,128)}), f32[8,12,1280]{2,1,0:T(8,128)S(1)}, u32[]{:S(2)}, u32[]{:S(2)}) async-start(f32[8,12,1280]{2,1,0:T(8,128)} %copy.536), calls=%async_computation.8 | async-start | bytes 1310720 | tf_op jit(solution)/shard_map/all_to_all | solution.py:44
  262.9 1.4 copy-start.12
  264.4 2.9 copy-start.5
  301.1 26.1 %copy-start.20 = (f32[1280]{0:T(1024)S(1)}, f32[1280]{0:T(1024)}, u32[]{:S(2)}) copy-start(f32[1280]{0:T(1024)} %param.45) | copy-start | bytes 15364
Sparse Core Ops, SparseCore 0:
  8.9 42.6 all-gather.4
  53.8 61.3 all-gather.2
  119.5 9.8 reduce-scatter.1

commit v8 on v7

--- a/solution.py
+++ b/solution.py
@@ -37,11 +37,21 @@
     return (keys, values)
 
 
-def exchange_sum(parts, axes, narrow=False):
-    if narrow:
-        moved = lax.all_to_all(parts.astype(jnp.bfloat16), axes, 0, 0, tiled=True)
-        return jnp.sum(moved.astype(jnp.float32), 0)
-    return jnp.sum(lax.all_to_all(parts, axes, 0, 0, tiled=True), 0)
+def lane_shape(shape, dtype):
+    rows = 8 if jnp.dtype(dtype).itemsize == 4 else 16
+    size = 1
+    for n in shape:
+        size = size * n
+    aligned = len(shape) >= 2 and shape[-1] % 128 == 0 and shape[-2] % rows == 0
+    if aligned or size % 128:
+        return shape
+    return (size // 128, 128)
+
+
+def exchange_sum(parts, axes):
+    shape = lane_shape(parts.shape[1:], parts.dtype)
+    moved = lax.all_to_all(parts.reshape((parts.shape[0],) + shape), axes, 0, 0, tiled=True)
+    return jnp.sum(moved, 0).reshape(parts.shape[1:])
 
 
 def exchange_max(value, axes, count):
@@ -51,8 +61,9 @@
 
 
 def exchange_gather(piece, axes, count):
-    spread = jnp.broadcast_to(piece[None], (count,) + piece.shape)
-    return lax.all_to_all(spread, axes, 0, 0, tiled=True)
+    flat = piece.reshape(lane_shape(piece.shape, piece.dtype))
+    spread = jnp.broadcast_to(flat[None], (count,) + flat.shape)
+    return lax.all_to_all(spread, axes, 0, 0, tiled=True).reshape((count,) + piece.shape)
 
 
 def seq_sum(parts):

time: 353 us -> 355 us (level)
  local copies, waits for them, and re-layouts: 66 us -> 73.5 us
  blocking collectives: 159 us -> 154 us
    slice x1 -> x3, local copies, waits for them, and re-layouts: 0.01 us -> 5.78 us  [shards(): own_total = packed[rows * piece:rows * piece + rows]]
    all_to_all x12, blocking collectives: 126 us -> 122 us  [the longest x6 76.4 us: exchange_sum(): lax.all_to_all(parts.reshape((parts.shape[0],) + shape), axes, 0, 0, tile...]
  transfers between devices with their start and end apart: 6 -> 6, of which waited for: 5 -> 5; matrix products, arithmetic and copies ran while one was open for 17% -> 16% of each run, Pallas kernels for 0% -> 0%
where the time goes in v8:
time: 355 us; the launch traced here: 353 us
  blocking collectives  154 us (43%)
  local copies, waits for them, and re-layouts  73.5 us (21%)
  waiting for transfers between devices  53.8 us (15%)
  other arithmetic  29.7 us (8%)
  between operations  14.8 us (4%)
  matrix products  13.5 us (4%)
  starting transfers between devices  13.4 us (4%)
    all_to_all x6, blocking collectives, exchange_sum(): lax.all_to_all(parts.reshape((parts.shape[0],) + shape), axes, 0, 0, tile...  76.4 us
    all_to_all x6, blocking collectives, exchange_gather(): lax.all_to_all(spread, axes, 0, 0, tiled=True)  45.2 us
    all_gather x1, waiting for transfers between devices, shards(): lax.all_gather(w_keyval, SEQ, axis=1, tiled=True)  23.7 us
    all_to_all x2, waiting for transfers between devices, exchange_sum(): lax.all_to_all(parts.reshape((parts.shape[0],) + shape), axes, 0, 0, tile...  15.8 us
    all_to_all x1, blocking collectives, exchange_max(): lax.all_to_all(spread, axes, 0, 0, tiled=True)  14.5 us
    gather x6, local copies, waits for them, and re-layouts, shards(): tail_state = jnp.take_along_axis(everyone, picks[:, :, None, None], axis=1)  8.11 us
    unnamed x1, blocking collectives  8.04 us
    all_to_all x2, starting transfers between devices, exchange_sum(): lax.all_to_all(parts.reshape((parts.shape[0],) + shape), axes, 0, 0, tile...  7.72 us
  transfers between devices with their start and end apart: 6, of which 5 were waited for; matrix products, arithmetic and copies ran while one was open for 16% of the time, Pallas kernels for 0%

profile of v8, /device:TPU:0, one launch (start us, length us, event | category | flops | bytes accessed | tf_op | source)
XLA Modules:
  0.0 352.7 jit_solution(8038298823944206329)
XLA Ops:
  8.0 1.2 multiply_reduce_fusion.1
  10.7 4.2 %all-to-all-start = ((f32[2,96,384]{2,1,0:T(8,128)}), f32[2,96,384]{2,1,0:T(8,128)S(1)}, u32[]{:S(2)}, u32[]{:S(2)}) async-start(f32[2,96,384]{2,1,0:T(8,128)} %bitcast.2), calls=%async_computation | async-start | bytes 589824 | tf_op jit(solution)/shard_map/all_to_all | solution.py:53
  15.1 1.3 gather_fusion.4
  16.8 1.3 gather_fusion.1
  19.7 1.5 all-to-all-done
  21.4 1.3 broadcast_in_dim.119
  22.8 5.5 %all-to-all-start.1 = ((bf16[32,96,256]{2,1,0:T(8,128)(2,1)}), bf16[32,96,256]{2,1,0:T(8,128)(2,1)S(1)}, u32[]{:S(2)}, u32[]{:S(2)}) async-start(bf16[32,96,256]{2,1,0:T(8,128)(2,1)} %broadcast_in_dim.119), calls=%async_computation.1 | async-start | bytes 3145728 | tf_op jit(solution)/shard_map/all_to_all | solution.py:66
  34.9 8.0 %all-reduce.5 = f32[32]{0:T(128)S(1)} all-reduce(f32[32]{0:T(128)S(1)} %reshape.390), channel_id=3, replica_groups=mesh['seq'=8,'pair'=2,'head'=2] {'head'}, use_global_device_ids=true, to_apply=%region_6.7.clone | all-reduce | flops 32 | bytes 256
  43.8 1.3 subtract_compare_fusion.1
  45.2 6.4 %all-gather.5.cloned.1.call-done = bf16[12,8,4,2048]{3,2,1,0:T(4,128)(2,1)} async-done(((bf16[12,4,4,2048]{3,2,1,0:T(4,128)(2,1)}), bf16[12,8,4,2048]{3,2,1,0:T(4,128)(2,1)}) %all-gather.5.cloned.1.call-update) | async-done | bytes 1572880 | tf_op jit(solution)/shard_map/all_gather | solution.py:185
  51.6 3.9 %gather_fusion.7 = bf16[48,4,2048]{2,1,0:T(4,128)(2,1)} fusion(bf16[12,8,4,2048]{3,2,1,0:T(4,128)(2,1)} %all-gather.5.cloned.1.call-done, s32[48]{0:T(128)S(1)} %reshape.519), kind=kCustom, calls=%fused_computation.7.clone | custom fusion | bytes 1573248 | tf_op jit(solution)/shard_map/jit(take_along_axis)/gather | solution.py:201
  55.5 3.9 %gather_fusion.2 = bf16[48,4,2048]{2,1,0:T(4,128)(2,1)} fusion(bf16[12,8,4,2048]{3,2,1,0:T(4,128)(2,1)} %all-gather.5.cloned.1.call-done, s32[48]{0:T(128)S(1)} %reshape.496), kind=kCustom, calls=%fused_computation.2.clone | custom fusion | bytes 1573248 | tf_op jit(solution)/shard_map/jit(take_along_axis)/gather | solution.py:201
  59.4 6.4 %all-to-all-done.1 = bf16[32,96,256]{2,1,0:T(8,128)(2,1)S(1)} async-done(((bf16[32,96,256]{2,1,0:T(8,128)(2,1)}), bf16[32,96,256]{2,1,0:T(8,128)(2,1)S(1)}, u32[]{:S(2)}, u32[]{:S(2)}) %all-to-all-start.1) | async-done | bytes 1572896 | tf_op jit(solution)/shard_map/all_to_all | solution.py:66
  65.8 1.2 copy-done.1
  67.0 1.5 fusion.67
  70.5 2.4 mul.290
  72.9 1.4 reduce_sum.186
  75.6 1.6 gather_fusion
  78.0 1.6 gather_fusion.3
  80.3 1.6 gather_fusion.5
  83.3 1.2 broadcast_select_fusion
  84.5 1.3 broadcast_select_fusion.2
  85.8 1.7 fusion.20
  87.6 2.2 pad_maximum_fusion
  89.7 1.7 copy_convert_fusion
  91.4 23.7 %all-gather.3.cloned.1.call-done = bf16[1280,2048]{1,0:T(8,128)(2,1)} async-done(((bf16[1280,128]{1,0:T(8,128)(2,1)}), bf16[1280,2048]{1,0:T(8,128)(2,1)}) %all-gather.3.cloned.1.call-update) | async-done | bytes 5242896 | tf_op jit(solution)/shard_map/all_gather | solution.py:147
  115.1 4.2 %fusion.69 = f32[32,2048]{1,0:T(8,128)} fusion(bf16[32,1280]{1,0:T(8,128)(2,1)S(1)} %reshape.389, bf16[1280,2048]{1,0:T(8,128)(2,1)} %all-gather.3.cloned.1.call-done), kind=kOutput, calls=%fused_computation.173 | convolution fusion | flops 167772160 | bytes 5586944 | tf_op jit(solution)/shard_map/dot_general | solution.py:145
  119.4 2.4 reshape.391
  121.8 3.1 reshape.410
  124.9 1.4 copy.366
  126.3 2.2 fusion.21
  128.6 1.4 copy.367
  132.8 1.8 fusion.4
  134.6 1.9 fusion.66
  137.8 14.5 %all_to_all.80 = f32[32,12,128]{2,1,0:T(8,128)S(1)} all-to-all(f32[32,12,128]{2,1,0:T(8,128)S(1)} %broadcast_in_dim.223), channel_id=1, replica_groups=mesh['seq'=8,'pair'=2,'head'=2] {'seq','pair','head'}, dimensions={0} | all-to-all | bytes 393216 | tf_op jit(solution)/shard_map/all_to_all | solution.py:60
  153.0 2.4 fusion.5
  155.4 2.5 reshape_reshape.19
  157.9 4.1 %copy.442 = f32[12,4,2,8,2,4,64]{6,3,0,2,5,4,1:T(8,128)} copy(f32[12,4,2,8,2,4,64]{6,5,4,3,2,1,0:T(4,128)} %reshape_reshape.19) | data formatting | bytes 3145728 | tf_op jit(solution)/shard_map/reshape;reshape | solution.py:238
  162.0 2.4 reshape.394
  164.9 1.3 select_maximum_fusion
  166.2 1.6 reshape.398
  168.7 5.3 %all_to_all.81 = f32[2,1568,128]{2,1,0:T(8,128)S(1)} all-to-all(f32[2,1568,128]{2,1,0:T(8,128)S(1)} %copy.400), channel_id=1, replica_groups=mesh['seq'=8,'pair'=2,'head'=2] {'pair'}, dimensions={0} | all-to-all | bytes 3211264 | tf_op jit(solution)/shard_map/all_to_all | solution.py:53
  175.0 1.2 reshape_reshape.20
  176.2 26.0 %all_to_all.82 = f32[16,98,128]{2,1,0:T(8,128)S(1)} all-to-all(f32[16,98,128]{2,1,0:T(8,128)S(1)} %reshape_reshape.20), channel_id=1, replica_groups=mesh['seq'=8,'pair'=2,'head'=2] {'seq','head'}, dimensions={0} | all-to-all | bytes 1605632 | tf_op jit(solution)/shard_map/all_to_all | solution.py:53
  202.3 4.9 %slice.89 = f32[6272,2]{1,0:T(8,128)} reshape(f32[98,128]{1,0:T(8,128)S(1)} %reduce_sum.189) | data formatting | bytes 100352 | tf_op jit(solution)/shard_map/slice | solution.py:248
  208.2 6.4 %all_to_all.83 = bf16[2,96,128]{2,1,0:T(8,128)(2,1)S(1)} all-to-all(bf16[2,96,128]{2,1,0:T(8,128)(2,1)S(1)} %broadcast_in_dim.226), channel_id=1, replica_groups=mesh['seq'=8,'pair'=2,'head'=2] {'head'}, dimensions={0} | all-to-all | bytes 98304 | tf_op jit(solution)/shard_map/all_to_all | solution.py:66
  216.4 5.6 %all_to_all.84 = f32[2,960,128]{2,1,0:T(8,128)S(1)} all-to-all(f32[2,960,128]{2,1,0:T(8,128)} %reshape.401), channel_id=1, replica_groups=mesh['seq'=8,'pair'=2,'head'=2] {'pair'}, dimensions={0} | all-to-all | bytes 1966080 | tf_op jit(solution)/shard_map/all_to_all | solution.py:53
  222.9 3.5 all-to-all-start.7
  226.4 14.3 %all-to-all-done.7 = f32[8,120,128]{2,1,0:T(8,128)S(1)} async-done(((f32[8,120,128]{2,1,0:T(8,128)}), f32[8,120,128]{2,1,0:T(8,128)S(1)}, u32[]{:S(2)}, u32[]{:S(2)}) %all-to-all-start.7) | async-done | bytes 491552 | tf_op jit(solution)/shard_map/all_to_all | solution.py:53
  241.0 4.9 %psum.14 = f32[12]{0:T(128)S(1)} all-reduce(f32[12]{0:T(128)S(1)} %reduce_sum.194), channel_id=1, replica_groups=mesh['seq'=8,'pair'=2,'head'=2] {'head'}, use_global_device_ids=true, to_apply=%region_18.22 | all-reduce | flops 12 | bytes 96 | tf_op jit(solution)/shard_map/psum | solution.py:255
  247.0 11.5 %all_to_all.85 = bf16[8,120,128]{2,1,0:T(8,128)(2,1)S(1)} all-to-all(bf16[8,120,128]{2,1,0:T(8,128)(2,1)S(1)} %broadcast_in_dim.228), channel_id=1, replica_groups=mesh['seq'=8,'pair'=2,'head'=2] {'seq'}, dimensions={0} | all-to-all | bytes 491520 | tf_op jit(solution)/shard_map/all_to_all | solution.py:66
  258.6 4.1 %all_to_all.86 = bf16[2,960,128]{2,1,0:T(8,128)(2,1)S(1)} all-to-all(bf16[2,960,128]{2,1,0:T(8,128)(2,1)S(1)} %broadcast_in_dim.230), channel_id=1, replica_groups=mesh['seq'=8,'pair'=2,'head'=2] {'pair'}, dimensions={0} | all-to-all | bytes 983040 | tf_op jit(solution)/shard_map/all_to_all | solution.py:66
  263.2 1.2 copy.405
  264.4 1.4 reshape.411
  265.9 2.9 fusion.43
  268.8 1.4 fusion.44
  271.1 1.5 mul.304
  274.0 17.0 %all_to_all.87 = f32[2,96,1408]{2,1,0:T(8,128)S(1)} all-to-all(f32[2,96,1408]{2,1,0:T(8,128)S(1)} %bitcast.174), channel_id=1, replica_groups=mesh['seq'=8,'pair'=2,'head'=2] {'head'}, dimensions={0} | all-to-all | bytes 2162688 | tf_op jit(solution)/shard_map/all_to_all | solution.py:53
  291.4 7.5 %all_to_all.88 = bf16[2,96,640]{2,1,0:T(8,128)(2,1)S(1)} all-to-all(bf16[2,96,640]{2,1,0:T(8,128)(2,1)S(1)} %broadcast_in_dim.232), channel_id=1, replica_groups=mesh['seq'=8,'pair'=2,'head'=2] {'head'}, dimensions={0} | all-to-all | bytes 491520 | tf_op jit(solution)/shard_map/all_to_all | solution.py:66
  300.8 5.6 %all_to_all.89 = f32[2,960,128]{2,1,0:T(8,128)S(1)} all-to-all(f32[2,960,128]{2,1,0:T(8,128)} %reshape.404), channel_id=1, replica_groups=mesh['seq'=8,'pair'=2,'head'=2] {'pair'}, dimensions={0} | all-to-all | bytes 1966080 | tf_op jit(solution)/shard_map/all_to_all | solution.py:53
  306.5 17.0 %all_to_all.90 = f32[8,120,128]{2,1,0:T(8,128)S(1)} all-to-all(f32[8,120,128]{2,1,0:T(8,128)S(1)} %bitcast.181), channel_id=1, replica_groups=mesh['seq'=8,'pair'=2,'head'=2] {'seq'}, dimensions={0} | all-to-all | bytes 983040 | tf_op jit(solution)/shard_map/all_to_all | solution.py:53
  323.8 4.9 %psum.15 = f32[12]{0:T(128)S(1)} all-reduce(f32[12]{0:T(128)S(1)} %reduce_sum.202), channel_id=1, replica_groups=mesh['seq'=8,'pair'=2,'head'=2] {'head'}, use_global_device_ids=true, to_apply=%region_25.29 | all-reduce | flops 12 | bytes 96 | tf_op jit(solution)/shard_map/psum | solution.py:278
  329.0 11.5 %all_to_all.91 = bf16[8,120,128]{2,1,0:T(8,128)(2,1)S(1)} all-to-all(bf16[8,120,128]{2,1,0:T(8,128)(2,1)S(1)} %broadcast_in_dim.234), channel_id=1, replica_groups=mesh['seq'=8,'pair'=2,'head'=2] {'seq'}, dimensions={0} | all-to-all | bytes 491520 | tf_op jit(solution)/shard_map/all_to_all | solution.py:66
  340.6 4.1 %all_to_all.92 = bf16[2,960,128]{2,1,0:T(8,128)(2,1)S(1)} all-to-all(bf16[2,960,128]{2,1,0:T(8,128)(2,1)S(1)} %broadcast_in_dim.236), channel_id=1, replica_groups=mesh['seq'=8,'pair'=2,'head'=2] {'pair'}, dimensions={0} | all-to-all | bytes 983040 | tf_op jit(solution)/shard_map/all_to_all | solution.py:66
  (235 shorter events, 37.8 us)
Async XLA Ops:
  6.5 292.4 %copy-start = (bf16[640,1280]{1,0:T(8,128)(2,1)S(1)}, bf16[640,1280]{1,0:T(8,128)(2,1)}, u32[]{:S(2)}) copy-start(bf16[640,1280]{1,0:T(8,128)(2,1)} %param.44) | copy-start | bytes 4915204
  6.5 2.8 copy-start.10
  6.5 2.8 copy-start.9
  6.5 2.8 copy-start.19
  6.5 3.1 copy-start.28
  6.5 45.1 %all-gather.5.cloned.1.call-start = ((), (), s32[]{:S(2)}) async-start(), calls=%async_computation.19 | async-start | bytes 2359296 | tf_op jit(solution)/shard_map/all_gather | solution.py:185
  7.3 107.9 %all-gather.3.cloned.1.call-start = ((), (), s32[]{:S(2)}) async-start(), calls=%async_computation.17 | async-start | bytes 5570560 | tf_op jit(solution)/shard_map/all_gather | solution.py:147
  9.2 5.7 %copy-start.14 = (s32[2,12,8]{1,2,0:T(8,128)S(1)}, s32[2,12,8]{1,2,0:T(8,128)}, u32[]{:S(2)}) copy-start(s32[2,12,8]{1,2,0:T(8,128)} %param.27) | copy-start | bytes 2308
  10.7 10.5 %all-to-all-start = ((f32[2,96,384]{2,1,0:T(8,128)}), f32[2,96,384]{2,1,0:T(8,128)S(1)}, u32[]{:S(2)}, u32[]{:S(2)}) async-start(f32[2,96,384]{2,1,0:T(8,128)} %bitcast.2), calls=%async_computation | async-start | bytes 589824 | tf_op jit(solution)/shard_map/all_to_all | solution.py:53
  18.2 1.3 copy-start.25
  22.7 9.1 %copy-start.12 = (bf16[4,8,1280]{2,1,0:T(8,128)(2,1)S(1)}, bf16[4,8,1280]{2,1,0:T(8,128)(2,1)}, u32[]{:S(2)}) copy-start(bf16[4,8,1280]{2,1,0:T(8,128)(2,1)} %param.32) | copy-start | bytes 245764
  22.7 9.9 %copy-start.22 = (s32[12]{0:T(128)S(1)}, s32[12]{0:T(128)}, u32[]{:S(2)}) copy-start(s32[12]{0:T(128)} %param.29) | copy-start | bytes 148
  22.7 10.9 %copy-start.30 = (u32[32]{0:T(128)S(1)}, u32[32]{0:T(128)}, u32[]{:S(2)}) copy-start(u32[32]{0:T(128)} %constant.271) | copy-start | bytes 388
  22.8 20.8 %copy-start.29 = (s32[4]{0:T(128)S(1)}, s32[4]{0:T(128)}, u32[]{:S(2)}) copy-start(s32[4]{0:T(128)} %param.33) | copy-start | bytes 52
  22.8 20.8 %copy-start.27 = (s32[8]{0:T(128)S(1)}, s32[8]{0:T(128)}, u32[]{:S(2)}) copy-start(s32[8]{0:T(128)} %param.31) | copy-start | bytes 100
  22.8 43.0 %all-to-all-start.1 = ((bf16[32,96,256]{2,1,0:T(8,128)(2,1)}), bf16[32,96,256]{2,1,0:T(8,128)(2,1)S(1)}, u32[]{:S(2)}, u32[]{:S(2)}) async-start(bf16[32,96,256]{2,1,0:T(8,128)(2,1)} %broadcast_in_dim.119), calls=%async_computation.1 | async-start | bytes 3145728 | tf_op jit(solution)/shard_map/all_to_all | solution.py:66
  28.3 101.7 %reduce-scatter.2.cloned.1.call-start = ((), (), s32[]{:S(2)}) async-start(), calls=%async_computation.18 | async-start | bytes 393216 | tf_op jit(solution)/shard_map/reduce_scatter | solution.py:151
  32.2 0.5 copy-start.23
  65.8 1.2 copy-start.1
  74.6 1.0 copy-start.7
  81.9 3.9 %copy-start.2 = (bf16[48,4,2048]{2,1,0:T(4,128)(2,1)S(1)}, bf16[48,4,2048]{2,1,0:T(4,128)(2,1)}, u32[]{:S(2)}) copy-start(bf16[48,4,2048]{2,1,0:T(4,128)(2,1)} %gather_fusion.7) | copy-start | bytes 2359300
  82.6 3.2 copy-start.15
  82.6 3.2 copy-start.16
  82.6 3.2 copy-start.17
  82.6 3.2 copy-start.18
  83.3 2.5 copy-start.3
  121.8 4.6 %copy-start.24 = (f32[256]{0:T(256)S(1)}, f32[256]{0:T(256)}, u32[]{:S(2)}) copy-start(f32[256]{0:T(256)} %param.37) | copy-start | bytes 3076
  126.3 3.7 %copy-start.26 = (f32[16]{0:T(128)S(1)}, f32[16]{0:T(128)}, u32[]{:S(2)}) copy-start(f32[16]{0:T(128)} %fusion.63) | copy-start | bytes 196
  134.6 1.9 copy-start.8
  137.6 15.3 %copy-start.4 = (f32[12,4,32,96]{3,2,1,0:T(8,128)}, f32[12,4,32,96]{3,2,1,0:T(8,128)S(1)}, u32[]{:S(2)}) copy-start(f32[12,4,32,96]{3,2,1,0:T(8,128)S(1)} %get-tuple-element.32) | copy-start | bytes 1769476
  202.3 12.7 %copy-start.11 = (bf16[128,1280]{1,0:T(8,128)(2,1)S(1)}, bf16[128,1280]{1,0:T(8,128)(2,1)}, u32[]{:S(2)}) copy-start(bf16[128,1280]{1,0:T(8,128)(2,1)} %param.39) | copy-start | bytes 983044
  222.0 24.0 %copy-start.20 = (f32[1280]{0:T(1024)S(1)}, f32[1280]{0:T(1024)}, u32[]{:S(2)}) copy-start(f32[1280]{0:T(1024)} %param.40) | copy-start | bytes 15364
  222.9 17.8 %all-to-all-start.7 = ((f32[8,120,128]{2,1,0:T(8,128)}), f32[8,120,128]{2,1,0:T(8,128)S(1)}, u32[]{:S(2)}, u32[]{:S(2)}) async-start(f32[8,120,128]{2,1,0:T(8,128)} %bitcast.46), calls=%async_computation.8 | async-start | bytes 983040 | tf_op jit(solution)/shard_map/all_to_all | solution.py:53
  264.4 1.4 copy-start.13
  265.8 2.9 copy-start.6
  271.1 1.7 copy-start.5
  306.4 22.4 %copy-start.21 = (f32[1280]{0:T(1024)S(1)}, f32[1280]{0:T(1024)}, u32[]{:S(2)}) copy-start(f32[1280]{0:T(1024)} %param.45) | copy-start | bytes 15364
Sparse Core Ops, SparseCore 0:
  8.9 42.6 all-gather.4
  53.8 61.3 all-gather.2
  119.5 9.8 reduce-scatter.1

commit v9 on v8

--- a/solution.py
+++ b/solution.py
@@ -37,19 +37,15 @@
     return (keys, values)
 
 
-def lane_shape(shape, dtype):
-    rows = 8 if jnp.dtype(dtype).itemsize == 4 else 16
+def lane_shape(shape):
     size = 1
     for n in shape:
         size = size * n
-    aligned = len(shape) >= 2 and shape[-1] % 128 == 0 and shape[-2] % rows == 0
-    if aligned or size % 128:
-        return shape
-    return (size // 128, 128)
-
-
-def exchange_sum(parts, axes):
-    shape = lane_shape(parts.shape[1:], parts.dtype)
+    return shape if size % 128 else (size // 128, 128)
+
+
+def exchange_sum(parts, axes, align=False):
+    shape = lane_shape(parts.shape[1:]) if align else parts.shape[1:]
     moved = lax.all_to_all(parts.reshape((parts.shape[0],) + shape), axes, 0, 0, tiled=True)
     return jnp.sum(moved, 0).reshape(parts.shape[1:])
 
@@ -60,8 +56,8 @@
     return jnp.max(lax.all_to_all(spread, axes, 0, 0, tiled=True), 0).reshape(value.shape)
 
 
-def exchange_gather(piece, axes, count):
-    flat = piece.reshape(lane_shape(piece.shape, piece.dtype))
+def exchange_gather(piece, axes, count, align=False):
+    flat = piece.reshape(lane_shape(piece.shape)) if align else piece
     spread = jnp.broadcast_to(flat[None], (count,) + flat.shape)
     return lax.all_to_all(spread, axes, 0, 0, tiled=True).reshape((count,) + piece.shape)
 
@@ -70,13 +66,13 @@
     pair = lax.axis_size("pair")
     parts = parts.reshape((parts.shape[0] // pair, pair) + parts.shape[1:])
     parts = exchange_sum(jnp.swapaxes(parts, 0, 1), "pair")
-    return exchange_sum(parts, "seq")
+    return exchange_sum(parts, "seq", True)
 
 
 def seq_gather(piece):
     pair = lax.axis_size("pair")
     outer = lax.axis_size("seq")
-    got = exchange_gather(exchange_gather(piece, "seq", outer), "pair", pair)
+    got = exchange_gather(exchange_gather(piece, "seq", outer, True), "pair", pair)
     return jnp.swapaxes(got, 0, 1).reshape((outer * pair,) + piece.shape)
 
 

time: 355 us -> 344 us (0.969)
  local copies, waits for them, and re-layouts: 73.5 us -> 67 us
    slice x3 -> x1, local copies, waits for them, and re-layouts: 5.78 us -> 0.01 us  [shards(): own_total = packed[rows * piece:rows * piece + rows]]
  transfers between devices with their start and end apart: 6 -> 6, of which waited for: 5 -> 5; matrix products, arithmetic and copies ran while one was open for 16% -> 17% of each run, Pallas kernels for 0% -> 0%
where the time goes in v9:
time: 344 us; the launch traced here: 343 us
  blocking collectives  152 us (44%)
  local copies, waits for them, and re-layouts  67 us (19%)
  waiting for transfers between devices  53.8 us (16%)
  other arithmetic  28.2 us (8%)
  between operations  14.8 us (4%)
  matrix products  13.5 us (4%)
  starting transfers between devices  13.4 us (4%)
    all_to_all x6, blocking collectives, exchange_sum(): lax.all_to_all(parts.reshape((parts.shape[0],) + shape), axes, 0, 0, tile...  74.2 us
    all_to_all x6, blocking collectives, exchange_gather(): lax.all_to_all(spread, axes, 0, 0, tiled=True)  45.3 us
    all_gather x1, waiting for transfers between devices, shards(): lax.all_gather(w_keyval, SEQ, axis=1, tiled=True)  23.7 us
    all_to_all x2, waiting for transfers between devices, exchange_sum(): lax.all_to_all(parts.reshape((parts.shape[0],) + shape), axes, 0, 0, tile...  15.8 us
    all_to_all x1, blocking collectives, exchange_max(): lax.all_to_all(spread, axes, 0, 0, tiled=True)  14.5 us
    gather x6, local copies, waits for them, and re-layouts, shards(): tail_state = jnp.take_along_axis(everyone, picks[:, :, None, None], axis=1)  8.11 us
    unnamed x1, blocking collectives  8.04 us
    all_to_all x2, starting transfers between devices, exchange_sum(): lax.all_to_all(parts.reshape((parts.shape[0],) + shape), axes, 0, 0, tile...  7.72 us
  transfers between devices with their start and end apart: 6, of which 5 were waited for; matrix products, arithmetic and copies ran while one was open for 17% of the time, Pallas kernels for 0%

profile of v9, /device:TPU:0, one launch (start us, length us, event | category | flops | bytes accessed | tf_op | source)
XLA Modules:
  0.0 342.7 jit_solution(3954063168441502576)
XLA Ops:
  8.0 1.2 multiply_reduce_fusion.1
  10.7 4.2 %all-to-all-start = ((f32[2,96,384]{2,1,0:T(8,128)}), f32[2,96,384]{2,1,0:T(8,128)S(1)}, u32[]{:S(2)}, u32[]{:S(2)}) async-start(f32[2,96,384]{2,1,0:T(8,128)} %bitcast.2), calls=%async_computation | async-start | bytes 589824 | tf_op jit(solution)/shard_map/all_to_all | solution.py:49
  15.1 1.3 gather_fusion.4
  16.8 1.3 gather_fusion.1
  19.7 1.5 all-to-all-done
  21.4 1.3 broadcast_in_dim.119
  22.8 5.5 %all-to-all-start.1 = ((bf16[32,96,256]{2,1,0:T(8,128)(2,1)}), bf16[32,96,256]{2,1,0:T(8,128)(2,1)S(1)}, u32[]{:S(2)}, u32[]{:S(2)}) async-start(bf16[32,96,256]{2,1,0:T(8,128)(2,1)} %broadcast_in_dim.119), calls=%async_computation.1 | async-start | bytes 3145728 | tf_op jit(solution)/shard_map/all_to_all | solution.py:62
  34.9 8.0 %all-reduce.5 = f32[32]{0:T(128)S(1)} all-reduce(f32[32]{0:T(128)S(1)} %reshape.386), channel_id=3, replica_groups=mesh['seq'=8,'pair'=2,'head'=2] {'head'}, use_global_device_ids=true, to_apply=%region_6.7.clone | all-reduce | flops 32 | bytes 256
  43.8 1.3 subtract_compare_fusion.1
  45.2 6.4 %all-gather.5.cloned.1.call-done = bf16[12,8,4,2048]{3,2,1,0:T(4,128)(2,1)} async-done(((bf16[12,4,4,2048]{3,2,1,0:T(4,128)(2,1)}), bf16[12,8,4,2048]{3,2,1,0:T(4,128)(2,1)}) %all-gather.5.cloned.1.call-update) | async-done | bytes 1572880 | tf_op jit(solution)/shard_map/all_gather | solution.py:181
  51.6 3.9 %gather_fusion.7 = bf16[48,4,2048]{2,1,0:T(4,128)(2,1)} fusion(bf16[12,8,4,2048]{3,2,1,0:T(4,128)(2,1)} %all-gather.5.cloned.1.call-done, s32[48]{0:T(128)S(1)} %reshape.514), kind=kCustom, calls=%fused_computation.7.clone | custom fusion | bytes 1573248 | tf_op jit(solution)/shard_map/jit(take_along_axis)/gather | solution.py:197
  55.5 3.9 %gather_fusion.2 = bf16[48,4,2048]{2,1,0:T(4,128)(2,1)} fusion(bf16[12,8,4,2048]{3,2,1,0:T(4,128)(2,1)} %all-gather.5.cloned.1.call-done, s32[48]{0:T(128)S(1)} %reshape.491), kind=kCustom, calls=%fused_computation.2.clone | custom fusion | bytes 1573248 | tf_op jit(solution)/shard_map/jit(take_along_axis)/gather | solution.py:197
  59.4 6.4 %all-to-all-done.1 = bf16[32,96,256]{2,1,0:T(8,128)(2,1)S(1)} async-done(((bf16[32,96,256]{2,1,0:T(8,128)(2,1)}), bf16[32,96,256]{2,1,0:T(8,128)(2,1)S(1)}, u32[]{:S(2)}, u32[]{:S(2)}) %all-to-all-start.1) | async-done | bytes 1572896 | tf_op jit(solution)/shard_map/all_to_all | solution.py:62
  65.8 1.2 copy-done.1
  67.0 1.5 fusion.67
  70.5 2.4 mul.287
  72.9 1.4 reduce_sum.186
  75.6 1.6 gather_fusion
  78.0 1.6 gather_fusion.3
  80.3 1.6 gather_fusion.5
  83.3 1.2 broadcast_select_fusion
  84.5 1.3 broadcast_select_fusion.2
  85.8 1.7 fusion.21
  87.6 2.2 pad_maximum_fusion
  89.7 1.7 copy_convert_fusion
  91.4 23.7 %all-gather.3.cloned.1.call-done = bf16[1280,2048]{1,0:T(8,128)(2,1)} async-done(((bf16[1280,128]{1,0:T(8,128)(2,1)}), bf16[1280,2048]{1,0:T(8,128)(2,1)}) %all-gather.3.cloned.1.call-update) | async-done | bytes 5242896 | tf_op jit(solution)/shard_map/all_gather | solution.py:143
  115.1 4.2 %fusion.69 = f32[32,2048]{1,0:T(8,128)} fusion(bf16[32,1280]{1,0:T(8,128)(2,1)S(1)} %reshape.385, bf16[1280,2048]{1,0:T(8,128)(2,1)} %all-gather.3.cloned.1.call-done), kind=kOutput, calls=%fused_computation.174 | convolution fusion | flops 167772160 | bytes 5586944 | tf_op jit(solution)/shard_map/dot_general | solution.py:141
  119.4 2.4 reshape.387
  121.8 3.1 reshape.406
  124.9 1.4 copy.505
  126.3 2.2 fusion.22
  128.6 1.4 copy.506
  132.8 1.8 fusion.4
  134.6 1.9 fusion.66
  136.6 1.1 fusion.68
  137.8 14.5 %all_to_all.80 = f32[32,12,128]{2,1,0:T(8,128)S(1)} all-to-all(f32[32,12,128]{2,1,0:T(8,128)S(1)} %broadcast_in_dim.224), channel_id=1, replica_groups=mesh['seq'=8,'pair'=2,'head'=2] {'seq','pair','head'}, dimensions={0} | all-to-all | bytes 393216 | tf_op jit(solution)/shard_map/all_to_all | solution.py:56
  153.0 2.4 fusion.5
  155.4 2.5 reshape_reshape.4
  157.9 4.1 %copy.585 = f32[12,4,2,8,2,4,64]{6,3,0,2,5,4,1:T(8,128)} copy(f32[12,4,2,8,2,4,64]{6,5,4,3,2,1,0:T(4,128)} %reshape_reshape.4) | data formatting | bytes 3145728 | tf_op jit(solution)/shard_map/reshape;reshape | solution.py:234
  162.0 2.4 reshape.390
  164.9 1.3 select_maximum_fusion
  166.2 1.6 reshape.394
  168.7 5.0 %all_to_all.81 = f32[2,8,2,98,128]{4,1,3,2,0:T(8,128)S(1)} all-to-all(f32[2,8,2,98,128]{4,1,3,2,0:T(8,128)S(1)} %copy.538), channel_id=1, replica_groups=mesh['seq'=8,'pair'=2,'head'=2] {'pair'}, dimensions={0} | all-to-all | bytes 3211264 | tf_op jit(solution)/shard_map/all_to_all | solution.py:49
  174.8 1.6 copy.539
  176.6 26.3 %all_to_all.82 = f32[16,98,128]{2,1,0:T(8,128)S(1)} all-to-all(f32[16,98,128]{2,1,0:T(8,128)S(1)} %copy.540), channel_id=1, replica_groups=mesh['seq'=8,'pair'=2,'head'=2] {'seq','head'}, dimensions={0} | all-to-all | bytes 1605632 | tf_op jit(solution)/shard_map/all_to_all | solution.py:49
  203.2 6.5 %all_to_all.83 = bf16[2,192,64]{1,2,0:T(8,128)(2,1)S(1)} all-to-all(bf16[2,192,64]{1,2,0:T(8,128)(2,1)S(1)} %broadcast_in_dim.227), channel_id=1, replica_groups=mesh['seq'=8,'pair'=2,'head'=2] {'head'}, dimensions={0} | all-to-all | bytes 98304 | tf_op jit(solution)/shard_map/all_to_all | solution.py:62
  210.8 4.5 %all_to_all.84 = f32[2,8,12,1280]{3,1,2,0:T(8,128)S(1)} all-to-all(f32[2,8,12,1280]{3,1,2,0:T(8,128)S(1)} %copy.543), channel_id=1, replica_groups=mesh['seq'=8,'pair'=2,'head'=2] {'pair'}, dimensions={0} | all-to-all | bytes 1966080 | tf_op jit(solution)/shard_map/all_to_all | solution.py:49
  216.5 3.5 %all-to-all-start.7 = ((f32[8,120,128]{2,1,0:T(8,128)}), f32[8,120,128]{2,1,0:T(8,128)S(1)}, u32[]{:S(2)}, u32[]{:S(2)}) async-start(f32[8,120,128]{2,1,0:T(8,128)} %reshape.398), calls=%async_computation.8 | async-start | bytes 983040 | tf_op jit(solution)/shard_map/all_to_all | solution.py:49
  220.0 14.3 %all-to-all-done.7 = f32[8,120,128]{2,1,0:T(8,128)S(1)} async-done(((f32[8,120,128]{2,1,0:T(8,128)}), f32[8,120,128]{2,1,0:T(8,128)S(1)}, u32[]{:S(2)}, u32[]{:S(2)}) %all-to-all-start.7) | async-done | bytes 491552 | tf_op jit(solution)/shard_map/all_to_all | solution.py:49
  234.6 4.9 %psum.14 = f32[12]{0:T(128)S(1)} all-reduce(f32[12]{0:T(128)S(1)} %reduce_sum.194), channel_id=1, replica_groups=mesh['seq'=8,'pair'=2,'head'=2] {'head'}, use_global_device_ids=true, to_apply=%region_18.22 | all-reduce | flops 12 | bytes 96 | tf_op jit(solution)/shard_map/psum | solution.py:251
  240.6 11.5 %all_to_all.85 = bf16[8,120,128]{2,1,0:T(8,128)(2,1)S(1)} all-to-all(bf16[8,120,128]{2,1,0:T(8,128)(2,1)S(1)} %broadcast_in_dim.229), channel_id=1, replica_groups=mesh['seq'=8,'pair'=2,'head'=2] {'seq'}, dimensions={0} | all-to-all | bytes 491520 | tf_op jit(solution)/shard_map/all_to_all | solution.py:62
  252.6 4.1 %all_to_all.86 = bf16[2,8,12,1280]{3,1,2,0:T(8,128)(2,1)S(1)} all-to-all(bf16[2,8,12,1280]{3,1,2,0:T(8,128)(2,1)S(1)} %broadcast_in_dim.231), channel_id=1, replica_groups=mesh['seq'=8,'pair'=2,'head'=2] {'pair'}, dimensions={0} | all-to-all | bytes 983040 | tf_op jit(solution)/shard_map/all_to_all | solution.py:62
  256.8 1.4 copy.546
  258.1 1.4 reshape.407
  259.6 2.9 fusion.44
  262.5 1.3 fusion.45
  264.2 1.3 select_maximum_fusion.1
  265.5 17.0 %all_to_all.87 = f32[2,96,1408]{2,1,0:T(8,128)S(1)} all-to-all(f32[2,96,1408]{2,1,0:T(8,128)S(1)} %bitcast.169), channel_id=1, replica_groups=mesh['seq'=8,'pair'=2,'head'=2] {'head'}, dimensions={0} | all-to-all | bytes 2162688 | tf_op jit(solution)/shard_map/all_to_all | solution.py:49
  282.9 7.5 %all_to_all.88 = bf16[2,96,640]{2,1,0:T(8,128)(2,1)S(1)} all-to-all(bf16[2,96,640]{2,1,0:T(8,128)(2,1)S(1)} %broadcast_in_dim.233), channel_id=1, replica_groups=mesh['seq'=8,'pair'=2,'head'=2] {'head'}, dimensions={0} | all-to-all | bytes 491520 | tf_op jit(solution)/shard_map/all_to_all | solution.py:62
  291.7 4.5 %all_to_all.89 = f32[2,8,12,1280]{3,1,2,0:T(8,128)S(1)} all-to-all(f32[2,8,12,1280]{3,1,2,0:T(8,128)S(1)} %copy.549), channel_id=1, replica_groups=mesh['seq'=8,'pair'=2,'head'=2] {'pair'}, dimensions={0} | all-to-all | bytes 1966080 | tf_op jit(solution)/shard_map/all_to_all | solution.py:49
  296.6 17.0 %all_to_all.90 = f32[8,120,128]{2,1,0:T(8,128)S(1)} all-to-all(f32[8,120,128]{2,1,0:T(8,128)S(1)} %reshape.401), channel_id=1, replica_groups=mesh['seq'=8,'pair'=2,'head'=2] {'seq'}, dimensions={0} | all-to-all | bytes 983040 | tf_op jit(solution)/shard_map/all_to_all | solution.py:49
  313.9 4.9 %psum.15 = f32[12]{0:T(128)S(1)} all-reduce(f32[12]{0:T(128)S(1)} %reduce_sum.202), channel_id=1, replica_groups=mesh['seq'=8,'pair'=2,'head'=2] {'head'}, use_global_device_ids=true, to_apply=%region_25.29 | all-reduce | flops 12 | bytes 96 | tf_op jit(solution)/shard_map/psum | solution.py:274
  319.1 11.5 %all_to_all.91 = bf16[8,120,128]{2,1,0:T(8,128)(2,1)S(1)} all-to-all(bf16[8,120,128]{2,1,0:T(8,128)(2,1)S(1)} %broadcast_in_dim.235), channel_id=1, replica_groups=mesh['seq'=8,'pair'=2,'head'=2] {'seq'}, dimensions={0} | all-to-all | bytes 491520 | tf_op jit(solution)/shard_map/all_to_all | solution.py:62
  331.0 4.1 %all_to_all.92 = bf16[2,8,12,1280]{3,1,2,0:T(8,128)(2,1)S(1)} all-to-all(bf16[2,8,12,1280]{3,1,2,0:T(8,128)(2,1)S(1)} %broadcast_in_dim.237), channel_id=1, replica_groups=mesh['seq'=8,'pair'=2,'head'=2] {'pair'}, dimensions={0} | all-to-all | bytes 983040 | tf_op jit(solution)/shard_map/all_to_all | solution.py:62
  (234 shorter events, 33.2 us)
Async XLA Ops:
  6.5 283.9 %copy-start = (bf16[640,1280]{1,0:T(8,128)(2,1)S(1)}, bf16[640,1280]{1,0:T(8,128)(2,1)}, u32[]{:S(2)}) copy-start(bf16[640,1280]{1,0:T(8,128)(2,1)} %param.44) | copy-start | bytes 4915204
  6.5 2.8 copy-start.9
  6.5 2.8 copy-start.8
  6.5 2.8 copy-start.18
  6.5 3.1 copy-start.27
  6.5 45.1 %all-gather.5.cloned.1.call-start = ((), (), s32[]{:S(2)}) async-start(), calls=%async_computation.19 | async-start | bytes 2359296 | tf_op jit(solution)/shard_map/all_gather | solution.py:181
  7.3 107.9 %all-gather.3.cloned.1.call-start = ((), (), s32[]{:S(2)}) async-start(), calls=%async_computation.17 | async-start | bytes 5570560 | tf_op jit(solution)/shard_map/all_gather | solution.py:143
  9.2 5.7 %copy-start.13 = (s32[2,12,8]{1,2,0:T(8,128)S(1)}, s32[2,12,8]{1,2,0:T(8,128)}, u32[]{:S(2)}) copy-start(s32[2,12,8]{1,2,0:T(8,128)} %param.27) | copy-start | bytes 2308
  10.7 10.5 %all-to-all-start = ((f32[2,96,384]{2,1,0:T(8,128)}), f32[2,96,384]{2,1,0:T(8,128)S(1)}, u32[]{:S(2)}, u32[]{:S(2)}) async-start(f32[2,96,384]{2,1,0:T(8,128)} %bitcast.2), calls=%async_computation | async-start | bytes 589824 | tf_op jit(solution)/shard_map/all_to_all | solution.py:49
  18.2 1.3 copy-start.24
  22.7 9.1 %copy-start.11 = (bf16[4,8,1280]{2,1,0:T(8,128)(2,1)S(1)}, bf16[4,8,1280]{2,1,0:T(8,128)(2,1)}, u32[]{:S(2)}) copy-start(bf16[4,8,1280]{2,1,0:T(8,128)(2,1)} %param.32) | copy-start | bytes 245764
  22.7 9.9 %copy-start.21 = (s32[12]{0:T(128)S(1)}, s32[12]{0:T(128)}, u32[]{:S(2)}) copy-start(s32[12]{0:T(128)} %param.29) | copy-start | bytes 148
  22.7 10.9 %copy-start.29 = (u32[32]{0:T(128)S(1)}, u32[32]{0:T(128)}, u32[]{:S(2)}) copy-start(u32[32]{0:T(128)} %constant.271) | copy-start | bytes 388
  22.8 20.8 %copy-start.28 = (s32[4]{0:T(128)S(1)}, s32[4]{0:T(128)}, u32[]{:S(2)}) copy-start(s32[4]{0:T(128)} %param.33) | copy-start | bytes 52
  22.8 20.8 %copy-start.26 = (s32[8]{0:T(128)S(1)}, s32[8]{0:T(128)}, u32[]{:S(2)}) copy-start(s32[8]{0:T(128)} %param.31) | copy-start | bytes 100
  22.8 43.0 %all-to-all-start.1 = ((bf16[32,96,256]{2,1,0:T(8,128)(2,1)}), bf16[32,96,256]{2,1,0:T(8,128)(2,1)S(1)}, u32[]{:S(2)}, u32[]{:S(2)}) async-start(bf16[32,96,256]{2,1,0:T(8,128)(2,1)} %broadcast_in_dim.119), calls=%async_computation.1 | async-start | bytes 3145728 | tf_op jit(solution)/shard_map/all_to_all | solution.py:62
  28.3 101.7 %reduce-scatter.2.cloned.1.call-start = ((), (), s32[]{:S(2)}) async-start(), calls=%async_computation.18 | async-start | bytes 393216 | tf_op jit(solution)/shard_map/reduce_scatter | solution.py:147
  32.2 0.5 copy-start.22
  65.8 1.2 copy-start.1
  74.6 1.0 copy-start.6
  81.9 3.9 %copy-start.2 = (bf16[48,4,2048]{2,1,0:T(4,128)(2,1)S(1)}, bf16[48,4,2048]{2,1,0:T(4,128)(2,1)}, u32[]{:S(2)}) copy-start(bf16[48,4,2048]{2,1,0:T(4,128)(2,1)} %gather_fusion.7) | copy-start | bytes 2359300
  82.6 3.2 copy-start.14
  82.6 3.2 copy-start.15
  82.6 3.2 copy-start.16
  82.6 3.2 copy-start.17
  83.3 2.5 copy-start.3
  121.8 4.6 %copy-start.23 = (f32[256]{0:T(256)S(1)}, f32[256]{0:T(256)}, u32[]{:S(2)}) copy-start(f32[256]{0:T(256)} %param.37) | copy-start | bytes 3076
  126.3 3.7 %copy-start.25 = (f32[16]{0:T(128)S(1)}, f32[16]{0:T(128)}, u32[]{:S(2)}) copy-start(f32[16]{0:T(128)} %fusion.63) | copy-start | bytes 196
  134.6 1.9 copy-start.7
  137.6 15.3 %copy-start.4 = (f32[12,4,32,96]{3,2,1,0:T(8,128)}, f32[12,4,32,96]{3,2,1,0:T(8,128)S(1)}, u32[]{:S(2)}) copy-start(f32[12,4,32,96]{3,2,1,0:T(8,128)S(1)} %get-tuple-element.32) | copy-start | bytes 1769476
  176.6 33.4 %copy-start.10 = (bf16[128,1280]{1,0:T(8,128)(2,1)S(1)}, bf16[128,1280]{1,0:T(8,128)(2,1)}, u32[]{:S(2)}) copy-start(bf16[128,1280]{1,0:T(8,128)(2,1)} %param.39) | copy-start | bytes 983044
  215.6 24.0 %copy-start.19 = (f32[1280]{0:T(1024)S(1)}, f32[1280]{0:T(1024)}, u32[]{:S(2)}) copy-start(f32[1280]{0:T(1024)} %param.40) | copy-start | bytes 15364
  216.5 17.8 %all-to-all-start.7 = ((f32[8,120,128]{2,1,0:T(8,128)}), f32[8,120,128]{2,1,0:T(8,128)S(1)}, u32[]{:S(2)}, u32[]{:S(2)}) async-start(f32[8,120,128]{2,1,0:T(8,128)} %reshape.398), calls=%async_computation.8 | async-start | bytes 983040 | tf_op jit(solution)/shard_map/all_to_all | solution.py:49
  258.1 1.4 copy-start.12
  259.6 2.9 copy-start.5
  296.5 22.4 %copy-start.20 = (f32[1280]{0:T(1024)S(1)}, f32[1280]{0:T(1024)}, u32[]{:S(2)}) copy-start(f32[1280]{0:T(1024)} %param.45) | copy-start | bytes 15364
Sparse Core Ops, SparseCore 0:
  8.9 42.6 all-gather.4
  53.8 61.3 all-gather.2
  119.5 9.8 reduce-scatter.1

commit v10 on v9

--- a/solution.py
+++ b/solution.py
@@ -243,7 +243,7 @@
     share = packed[: rows * piece].reshape(rows, piece)
     own_total = packed[rows * piece : rows * piece + rows]
     attn = (share / own_total[:, None]).astype(bf16)
-    attn = exchange_gather(attn, "head", n_head)
+    attn = exchange_gather(attn, "head", n_head, True)
     attn = jnp.transpose(attn, (1, 0, 2)).reshape(rows, -1)
     partial_out = jnp.dot(attn, w_out, preferred_element_type=f32)
     per_dev = rows // n_seq

time: 344 us -> 350 us (1.017)
  local copies, waits for them, and re-layouts: 67 us -> 72.8 us
    slice x1 -> x3, local copies, waits for them, and re-layouts: 0.01 us -> 5.78 us  [shards(): own_total = packed[rows * piece:rows * piece + rows]]
where the time goes in v10:
time: 350 us; the launch traced here: 348 us
  blocking collectives  152 us (43%)
  local copies, waits for them, and re-layouts  72.8 us (21%)
  waiting for transfers between devices  53.8 us (15%)
  other arithmetic  28.1 us (8%)
  between operations  14.8 us (4%)
  matrix products  13.5 us (4%)
  starting transfers between devices  13.4 us (4%)
    all_to_all x6, blocking collectives, exchange_sum(): lax.all_to_all(parts.reshape((parts.shape[0],) + shape), axes, 0, 0, tile...  74.1 us
    all_to_all x6, blocking collectives, exchange_gather(): lax.all_to_all(spread, axes, 0, 0, tiled=True)  45.2 us
    all_gather x1, waiting for transfers between devices, shards(): lax.all_gather(w_keyval, SEQ, axis=1, tiled=True)  23.7 us
    all_to_all x2, waiting for transfers between devices, exchange_sum(): lax.all_to_all(parts.reshape((parts.shape[0],) + shape), axes, 0, 0, tile...  15.8 us
    all_to_all x1, blocking collectives, exchange_max(): lax.all_to_all(spread, axes, 0, 0, tiled=True)  14.5 us
    gather x6, local copies, waits for them, and re-layouts, shards(): tail_state = jnp.take_along_axis(everyone, picks[:, :, None, None], axis=1)  8.11 us
    unnamed x1, blocking collectives  8.04 us
    all_to_all x2, starting transfers between devices, exchange_sum(): lax.all_to_all(parts.reshape((parts.shape[0],) + shape), axes, 0, 0, tile...  7.72 us
  transfers between devices with their start and end apart: 6, of which 5 were waited for; matrix products, arithmetic and copies ran while one was open for 17% of the time, Pallas kernels for 0%

profile of v10, /device:TPU:0, one launch (start us, length us, event | category | flops | bytes accessed | tf_op | source)
XLA Modules:
  0.0 348.1 jit_solution(4206021512240342855)
XLA Ops:
  8.0 1.2 multiply_reduce_fusion.1
  10.7 4.2 %all-to-all-start = ((f32[2,96,384]{2,1,0:T(8,128)}), f32[2,96,384]{2,1,0:T(8,128)S(1)}, u32[]{:S(2)}, u32[]{:S(2)}) async-start(f32[2,96,384]{2,1,0:T(8,128)} %bitcast.2), calls=%async_computation | async-start | bytes 589824 | tf_op jit(solution)/shard_map/all_to_all | solution.py:49
  15.1 1.3 gather_fusion.4
  16.8 1.3 gather_fusion.1
  19.7 1.5 all-to-all-done
  21.4 1.3 broadcast_in_dim.119
  22.8 5.5 %all-to-all-start.1 = ((bf16[32,96,256]{2,1,0:T(8,128)(2,1)}), bf16[32,96,256]{2,1,0:T(8,128)(2,1)S(1)}, u32[]{:S(2)}, u32[]{:S(2)}) async-start(bf16[32,96,256]{2,1,0:T(8,128)(2,1)} %broadcast_in_dim.119), calls=%async_computation.1 | async-start | bytes 3145728 | tf_op jit(solution)/shard_map/all_to_all | solution.py:62
  34.9 8.0 %all-reduce.5 = f32[32]{0:T(128)S(1)} all-reduce(f32[32]{0:T(128)S(1)} %reshape.382), channel_id=3, replica_groups=mesh['seq'=8,'pair'=2,'head'=2] {'head'}, use_global_device_ids=true, to_apply=%region_6.7.clone | all-reduce | flops 32 | bytes 256
  43.8 1.3 subtract_compare_fusion.1
  45.2 6.4 %all-gather.5.cloned.1.call-done = bf16[12,8,4,2048]{3,2,1,0:T(4,128)(2,1)} async-done(((bf16[12,4,4,2048]{3,2,1,0:T(4,128)(2,1)}), bf16[12,8,4,2048]{3,2,1,0:T(4,128)(2,1)}) %all-gather.5.cloned.1.call-update) | async-done | bytes 1572880 | tf_op jit(solution)/shard_map/all_gather | solution.py:181
  51.6 3.9 %gather_fusion.7 = bf16[48,4,2048]{2,1,0:T(4,128)(2,1)} fusion(bf16[12,8,4,2048]{3,2,1,0:T(4,128)(2,1)} %all-gather.5.cloned.1.call-done, s32[48]{0:T(128)S(1)} %reshape.509), kind=kCustom, calls=%fused_computation.7.clone | custom fusion | bytes 1573248 | tf_op jit(solution)/shard_map/jit(take_along_axis)/gather | solution.py:197
  55.5 3.9 %gather_fusion.2 = bf16[48,4,2048]{2,1,0:T(4,128)(2,1)} fusion(bf16[12,8,4,2048]{3,2,1,0:T(4,128)(2,1)} %all-gather.5.cloned.1.call-done, s32[48]{0:T(128)S(1)} %reshape.486), kind=kCustom, calls=%fused_computation.2.clone | custom fusion | bytes 1573248 | tf_op jit(solution)/shard_map/jit(take_along_axis)/gather | solution.py:197
  59.4 6.4 %all-to-all-done.1 = bf16[32,96,256]{2,1,0:T(8,128)(2,1)S(1)} async-done(((bf16[32,96,256]{2,1,0:T(8,128)(2,1)}), bf16[32,96,256]{2,1,0:T(8,128)(2,1)S(1)}, u32[]{:S(2)}, u32[]{:S(2)}) %all-to-all-start.1) | async-done | bytes 1572896 | tf_op jit(solution)/shard_map/all_to_all | solution.py:62
  65.8 1.2 copy-done.1
  67.0 1.5 fusion.68
  70.5 2.4 mul.287
  72.9 1.4 reduce_sum.186
  75.6 1.6 gather_fusion
  78.0 1.6 gather_fusion.3
  80.3 1.6 gather_fusion.5
  83.3 1.2 broadcast_select_fusion
  84.5 1.3 broadcast_select_fusion.2
  85.8 1.7 fusion.21
  87.6 2.2 pad_maximum_fusion
  89.7 1.7 copy_convert_fusion
  91.4 23.7 %all-gather.3.cloned.1.call-done = bf16[1280,2048]{1,0:T(8,128)(2,1)} async-done(((bf16[1280,128]{1,0:T(8,128)(2,1)}), bf16[1280,2048]{1,0:T(8,128)(2,1)}) %all-gather.3.cloned.1.call-update) | async-done | bytes 5242896 | tf_op jit(solution)/shard_map/all_gather | solution.py:143
  115.1 4.2 %fusion.70 = f32[32,2048]{1,0:T(8,128)} fusion(bf16[32,1280]{1,0:T(8,128)(2,1)S(1)} %reshape.381, bf16[1280,2048]{1,0:T(8,128)(2,1)} %all-gather.3.cloned.1.call-done), kind=kOutput, calls=%fused_computation.175 | convolution fusion | flops 167772160 | bytes 5586944 | tf_op jit(solution)/shard_map/dot_general | solution.py:141
  119.4 2.4 reshape.383
  121.8 3.1 reshape.401
  124.9 1.4 copy.529
  126.3 2.2 fusion.22
  128.6 1.4 copy.530
  132.8 1.8 fusion.4
  134.6 1.9 fusion.67
  137.8 14.5 %all_to_all.80 = f32[32,12,128]{2,1,0:T(8,128)S(1)} all-to-all(f32[32,12,128]{2,1,0:T(8,128)S(1)} %broadcast_in_dim.223), channel_id=1, replica_groups=mesh['seq'=8,'pair'=2,'head'=2] {'seq','pair','head'}, dimensions={0} | all-to-all | bytes 393216 | tf_op jit(solution)/shard_map/all_to_all | solution.py:56
  153.0 2.4 fusion.5
  155.4 2.5 reshape_reshape.4
  157.9 4.1 %copy.612 = f32[12,4,2,8,2,4,64]{6,3,0,2,5,4,1:T(8,128)} copy(f32[12,4,2,8,2,4,64]{6,5,4,3,2,1,0:T(4,128)} %reshape_reshape.4) | data formatting | bytes 3145728 | tf_op jit(solution)/shard_map/reshape;reshape | solution.py:234
  162.0 2.4 reshape.386
  164.9 1.3 select_maximum_fusion
  166.2 1.6 reshape.390
  168.7 5.0 %all_to_all.81 = f32[2,8,2,98,128]{4,1,3,2,0:T(8,128)S(1)} all-to-all(f32[2,8,2,98,128]{4,1,3,2,0:T(8,128)S(1)} %copy.562), channel_id=1, replica_groups=mesh['seq'=8,'pair'=2,'head'=2] {'pair'}, dimensions={0} | all-to-all | bytes 3211264 | tf_op jit(solution)/shard_map/all_to_all | solution.py:49
  174.8 1.6 copy.563
  176.6 26.1 %all_to_all.82 = f32[16,98,128]{2,1,0:T(8,128)S(1)} all-to-all(f32[16,98,128]{2,1,0:T(8,128)S(1)} %copy.564), channel_id=1, replica_groups=mesh['seq'=8,'pair'=2,'head'=2] {'seq','head'}, dimensions={0} | all-to-all | bytes 1605632 | tf_op jit(solution)/shard_map/all_to_all | solution.py:49
  202.8 4.9 %slice.89 = f32[6272,2]{1,0:T(8,128)} reshape(f32[98,128]{1,0:T(8,128)S(1)} %reduce_sum.189) | data formatting | bytes 100352 | tf_op jit(solution)/shard_map/slice | solution.py:244
  208.7 6.4 %all_to_all.83 = bf16[2,96,128]{2,1,0:T(8,128)(2,1)S(1)} all-to-all(bf16[2,96,128]{2,1,0:T(8,128)(2,1)S(1)} %broadcast_in_dim.226), channel_id=1, replica_groups=mesh['seq'=8,'pair'=2,'head'=2] {'head'}, dimensions={0} | all-to-all | bytes 98304 | tf_op jit(solution)/shard_map/all_to_all | solution.py:62
  216.3 4.5 %all_to_all.84 = f32[2,8,12,1280]{3,1,2,0:T(8,128)S(1)} all-to-all(f32[2,8,12,1280]{3,1,2,0:T(8,128)S(1)} %copy.569), channel_id=1, replica_groups=mesh['seq'=8,'pair'=2,'head'=2] {'pair'}, dimensions={0} | all-to-all | bytes 1966080 | tf_op jit(solution)/shard_map/all_to_all | solution.py:49
  222.0 3.5 %all-to-all-start.7 = ((f32[8,120,128]{2,1,0:T(8,128)}), f32[8,120,128]{2,1,0:T(8,128)S(1)}, u32[]{:S(2)}, u32[]{:S(2)}) async-start(f32[8,120,128]{2,1,0:T(8,128)} %reshape.393), calls=%async_computation.8 | async-start | bytes 983040 | tf_op jit(solution)/shard_map/all_to_all | solution.py:49
  225.4 14.3 %all-to-all-done.7 = f32[8,120,128]{2,1,0:T(8,128)S(1)} async-done(((f32[8,120,128]{2,1,0:T(8,128)}), f32[8,120,128]{2,1,0:T(8,128)S(1)}, u32[]{:S(2)}, u32[]{:S(2)}) %all-to-all-start.7) | async-done | bytes 491552 | tf_op jit(solution)/shard_map/all_to_all | solution.py:49
  240.1 4.9 %psum.14 = f32[12]{0:T(128)S(1)} all-reduce(f32[12]{0:T(128)S(1)} %reduce_sum.194), channel_id=1, replica_groups=mesh['seq'=8,'pair'=2,'head'=2] {'head'}, use_global_device_ids=true, to_apply=%region_18.22 | all-reduce | flops 12 | bytes 96 | tf_op jit(solution)/shard_map/psum | solution.py:251
  246.1 11.5 %all_to_all.85 = bf16[8,120,128]{2,1,0:T(8,128)(2,1)S(1)} all-to-all(bf16[8,120,128]{2,1,0:T(8,128)(2,1)S(1)} %broadcast_in_dim.228), channel_id=1, replica_groups=mesh['seq'=8,'pair'=2,'head'=2] {'seq'}, dimensions={0} | all-to-all | bytes 491520 | tf_op jit(solution)/shard_map/all_to_all | solution.py:62
  258.0 4.1 %all_to_all.86 = bf16[2,8,12,1280]{3,1,2,0:T(8,128)(2,1)S(1)} all-to-all(bf16[2,8,12,1280]{3,1,2,0:T(8,128)(2,1)S(1)} %broadcast_in_dim.230), channel_id=1, replica_groups=mesh['seq'=8,'pair'=2,'head'=2] {'pair'}, dimensions={0} | all-to-all | bytes 983040 | tf_op jit(solution)/shard_map/all_to_all | solution.py:62
  262.2 1.4 copy.572
  263.6 1.4 reshape.402
  265.1 2.9 fusion.44
  268.0 1.3 fusion.45
  269.7 1.3 select_maximum_fusion.1
  271.0 17.0 %all_to_all.87 = f32[2,96,1408]{2,1,0:T(8,128)S(1)} all-to-all(f32[2,96,1408]{2,1,0:T(8,128)S(1)} %bitcast.169), channel_id=1, replica_groups=mesh['seq'=8,'pair'=2,'head'=2] {'head'}, dimensions={0} | all-to-all | bytes 2162688 | tf_op jit(solution)/shard_map/all_to_all | solution.py:49
  288.4 7.5 %all_to_all.88 = bf16[2,96,640]{2,1,0:T(8,128)(2,1)S(1)} all-to-all(bf16[2,96,640]{2,1,0:T(8,128)(2,1)S(1)} %broadcast_in_dim.232), channel_id=1, replica_groups=mesh['seq'=8,'pair'=2,'head'=2] {'head'}, dimensions={0} | all-to-all | bytes 491520 | tf_op jit(solution)/shard_map/all_to_all | solution.py:62
  297.2 4.5 %all_to_all.89 = f32[2,8,12,1280]{3,1,2,0:T(8,128)S(1)} all-to-all(f32[2,8,12,1280]{3,1,2,0:T(8,128)S(1)} %copy.575), channel_id=1, replica_groups=mesh['seq'=8,'pair'=2,'head'=2] {'pair'}, dimensions={0} | all-to-all | bytes 1966080 | tf_op jit(solution)/shard_map/all_to_all | solution.py:49
  302.0 17.0 %all_to_all.90 = f32[8,120,128]{2,1,0:T(8,128)S(1)} all-to-all(f32[8,120,128]{2,1,0:T(8,128)S(1)} %reshape.396), channel_id=1, replica_groups=mesh['seq'=8,'pair'=2,'head'=2] {'seq'}, dimensions={0} | all-to-all | bytes 983040 | tf_op jit(solution)/shard_map/all_to_all | solution.py:49
  319.4 4.9 %psum.15 = f32[12]{0:T(128)S(1)} all-reduce(f32[12]{0:T(128)S(1)} %reduce_sum.202), channel_id=1, replica_groups=mesh['seq'=8,'pair'=2,'head'=2] {'head'}, use_global_device_ids=true, to_apply=%region_25.29 | all-reduce | flops 12 | bytes 96 | tf_op jit(solution)/shard_map/psum | solution.py:274
  324.5 11.5 %all_to_all.91 = bf16[8,120,128]{2,1,0:T(8,128)(2,1)S(1)} all-to-all(bf16[8,120,128]{2,1,0:T(8,128)(2,1)S(1)} %broadcast_in_dim.234), channel_id=1, replica_groups=mesh['seq'=8,'pair'=2,'head'=2] {'seq'}, dimensions={0} | all-to-all | bytes 491520 | tf_op jit(solution)/shard_map/all_to_all | solution.py:62
  336.5 4.1 %all_to_all.92 = bf16[2,8,12,1280]{3,1,2,0:T(8,128)(2,1)S(1)} all-to-all(bf16[2,8,12,1280]{3,1,2,0:T(8,128)(2,1)S(1)} %broadcast_in_dim.236), channel_id=1, replica_groups=mesh['seq'=8,'pair'=2,'head'=2] {'pair'}, dimensions={0} | all-to-all | bytes 983040 | tf_op jit(solution)/shard_map/all_to_all | solution.py:62
  (236 shorter events, 35.1 us)
Async XLA Ops:
  6.5 289.4 %copy-start = (bf16[640,1280]{1,0:T(8,128)(2,1)S(1)}, bf16[640,1280]{1,0:T(8,128)(2,1)}, u32[]{:S(2)}) copy-start(bf16[640,1280]{1,0:T(8,128)(2,1)} %param.44) | copy-start | bytes 4915204
  6.5 2.8 copy-start.9
  6.5 2.8 copy-start.8
  6.5 2.8 copy-start.18
  6.5 3.1 copy-start.27
  6.5 45.1 %all-gather.5.cloned.1.call-start = ((), (), s32[]{:S(2)}) async-start(), calls=%async_computation.19 | async-start | bytes 2359296 | tf_op jit(solution)/shard_map/all_gather | solution.py:181
  7.3 107.9 %all-gather.3.cloned.1.call-start = ((), (), s32[]{:S(2)}) async-start(), calls=%async_computation.17 | async-start | bytes 5570560 | tf_op jit(solution)/shard_map/all_gather | solution.py:143
  9.2 5.7 %copy-start.13 = (s32[2,12,8]{1,2,0:T(8,128)S(1)}, s32[2,12,8]{1,2,0:T(8,128)}, u32[]{:S(2)}) copy-start(s32[2,12,8]{1,2,0:T(8,128)} %param.27) | copy-start | bytes 2308
  10.7 10.5 %all-to-all-start = ((f32[2,96,384]{2,1,0:T(8,128)}), f32[2,96,384]{2,1,0:T(8,128)S(1)}, u32[]{:S(2)}, u32[]{:S(2)}) async-start(f32[2,96,384]{2,1,0:T(8,128)} %bitcast.2), calls=%async_computation | async-start | bytes 589824 | tf_op jit(solution)/shard_map/all_to_all | solution.py:49
  18.2 1.3 copy-start.24
  22.7 9.1 %copy-start.11 = (bf16[4,8,1280]{2,1,0:T(8,128)(2,1)S(1)}, bf16[4,8,1280]{2,1,0:T(8,128)(2,1)}, u32[]{:S(2)}) copy-start(bf16[4,8,1280]{2,1,0:T(8,128)(2,1)} %param.32) | copy-start | bytes 245764
  22.7 9.9 %copy-start.21 = (s32[12]{0:T(128)S(1)}, s32[12]{0:T(128)}, u32[]{:S(2)}) copy-start(s32[12]{0:T(128)} %param.29) | copy-start | bytes 148
  22.7 10.9 %copy-start.29 = (u32[32]{0:T(128)S(1)}, u32[32]{0:T(128)}, u32[]{:S(2)}) copy-start(u32[32]{0:T(128)} %constant.271) | copy-start | bytes 388
  22.8 20.8 %copy-start.28 = (s32[4]{0:T(128)S(1)}, s32[4]{0:T(128)}, u32[]{:S(2)}) copy-start(s32[4]{0:T(128)} %param.33) | copy-start | bytes 52
  22.8 20.8 %copy-start.26 = (s32[8]{0:T(128)S(1)}, s32[8]{0:T(128)}, u32[]{:S(2)}) copy-start(s32[8]{0:T(128)} %param.31) | copy-start | bytes 100
  22.8 43.0 %all-to-all-start.1 = ((bf16[32,96,256]{2,1,0:T(8,128)(2,1)}), bf16[32,96,256]{2,1,0:T(8,128)(2,1)S(1)}, u32[]{:S(2)}, u32[]{:S(2)}) async-start(bf16[32,96,256]{2,1,0:T(8,128)(2,1)} %broadcast_in_dim.119), calls=%async_computation.1 | async-start | bytes 3145728 | tf_op jit(solution)/shard_map/all_to_all | solution.py:62
  28.3 101.7 %reduce-scatter.2.cloned.1.call-start = ((), (), s32[]{:S(2)}) async-start(), calls=%async_computation.18 | async-start | bytes 393216 | tf_op jit(solution)/shard_map/reduce_scatter | solution.py:147
  32.2 0.5 copy-start.22
  65.8 1.2 copy-start.1
  74.6 1.0 copy-start.6
  81.9 3.9 %copy-start.2 = (bf16[48,4,2048]{2,1,0:T(4,128)(2,1)S(1)}, bf16[48,4,2048]{2,1,0:T(4,128)(2,1)}, u32[]{:S(2)}) copy-start(bf16[48,4,2048]{2,1,0:T(4,128)(2,1)} %gather_fusion.7) | copy-start | bytes 2359300
  82.6 3.2 copy-start.14
  82.6 3.2 copy-start.15
  82.6 3.2 copy-start.16
  82.6 3.2 copy-start.17
  83.3 2.5 copy-start.3
  121.8 4.6 %copy-start.23 = (f32[256]{0:T(256)S(1)}, f32[256]{0:T(256)}, u32[]{:S(2)}) copy-start(f32[256]{0:T(256)} %param.37) | copy-start | bytes 3076
  126.3 3.7 %copy-start.25 = (f32[16]{0:T(128)S(1)}, f32[16]{0:T(128)}, u32[]{:S(2)}) copy-start(f32[16]{0:T(128)} %fusion.64) | copy-start | bytes 196
  134.6 1.9 copy-start.7
  137.6 15.3 %copy-start.4 = (f32[12,4,32,96]{3,2,1,0:T(8,128)}, f32[12,4,32,96]{3,2,1,0:T(8,128)S(1)}, u32[]{:S(2)}) copy-start(f32[12,4,32,96]{3,2,1,0:T(8,128)S(1)} %get-tuple-element.32) | copy-start | bytes 1769476
  202.7 12.7 %copy-start.10 = (bf16[128,1280]{1,0:T(8,128)(2,1)S(1)}, bf16[128,1280]{1,0:T(8,128)(2,1)}, u32[]{:S(2)}) copy-start(bf16[128,1280]{1,0:T(8,128)(2,1)} %param.39) | copy-start | bytes 983044
  221.1 24.0 %copy-start.19 = (f32[1280]{0:T(1024)S(1)}, f32[1280]{0:T(1024)}, u32[]{:S(2)}) copy-start(f32[1280]{0:T(1024)} %param.40) | copy-start | bytes 15364
  222.0 17.8 %all-to-all-start.7 = ((f32[8,120,128]{2,1,0:T(8,128)}), f32[8,120,128]{2,1,0:T(8,128)S(1)}, u32[]{:S(2)}, u32[]{:S(2)}) async-start(f32[8,120,128]{2,1,0:T(8,128)} %reshape.393), calls=%async_computation.8 | async-start | bytes 983040 | tf_op jit(solution)/shard_map/all_to_all | solution.py:49
  263.6 1.4 copy-start.12
  265.1 2.9 copy-start.5
  302.0 22.4 %copy-start.20 = (f32[1280]{0:T(1024)S(1)}, f32[1280]{0:T(1024)}, u32[]{:S(2)}) copy-start(f32[1280]{0:T(1024)} %param.45) | copy-start | bytes 15364
Sparse Core Ops, SparseCore 0:
  8.9 42.6 all-gather.4
  53.8 61.3 all-gather.2
  119.5 9.8 reduce-scatter.1

commit v11 on v9

--- a/solution.py
+++ b/solution.py
@@ -178,7 +178,10 @@
     )
     every_query = every_query.reshape(steps, groups, beams, -1)
     every_fresh = every_fresh.reshape(steps, groups, beams, -1)
-    everyone = lax.all_gather(tail_cache, "head", axis=1, tiled=True)
+    everyone = exchange_gather(tail_cache, "head", n_head, True)
+    everyone = jnp.moveaxis(everyone, 0, 1).reshape(
+        (groups, beams) + tail_cache.shape[2:]
+    )
     n_dev = n_seq * n_head
     first_beam = head_at * local_beams
     many = steps * beams * repeat

time: 344 us -> 360 us (1.047); the launches traced: 343 us -> 355 us
  local copies, waits for them, and re-layouts: 67 us -> 71.1 us
  blocking collectives: 152 us -> 148 us
  waiting for transfers between devices: 53.8 us -> 57.8 us
    all_to_all x1 -> x2, waiting for transfers between devices: 6.43 us -> 41.6 us  [exchange_gather(): lax.all_to_all(spread, axes, 0, 0, tiled=True)]
    all_gather x1, waiting for transfers between devices: 23.7 us -> 0.01 us  [shards(): lax.all_gather(w_keyval, SEQ, axis=1, tiled=True)]
    all_gather x1 -> x0, waiting for transfers between devices: 6.45 us -> none  [shards(): everyone = lax.all_gather(tail_cache, 'head', axis=1, tiled=True)]
    all_to_all x1 -> x2, starting transfers between devices: 5.52 us -> 8.8 us  [exchange_gather(): lax.all_to_all(spread, axes, 0, 0, tiled=True)]
  transfers between devices with their start and end apart: 6 -> 6, of which waited for: 5 -> 4; matrix products, arithmetic and copies ran while one was open for 17% -> 19% of each run, Pallas kernels for 0% -> 0%
where the time goes in v11:
time: 360 us; the launch traced here: 355 us
  blocking collectives  148 us (41%)
  local copies, waits for them, and re-layouts  71.1 us (20%)
  waiting for transfers between devices  57.8 us (16%)
  other arithmetic  31.2 us (9%)
  starting transfers between devices  16.6 us (5%)
  between operations  15.6 us (4%)
  matrix products  14.8 us (4%)
    all_to_all x6, blocking collectives, exchange_sum(): lax.all_to_all(parts.reshape((parts.shape[0],) + shape), axes, 0, 0, tile...  74.1 us
    all_to_all x6, blocking collectives, exchange_gather(): lax.all_to_all(spread, axes, 0, 0, tiled=True)  45.3 us
    all_to_all x2, waiting for transfers between devices, exchange_gather(): lax.all_to_all(spread, axes, 0, 0, tiled=True)  41.6 us
    all_to_all x2, waiting for transfers between devices, exchange_sum(): lax.all_to_all(parts.reshape((parts.shape[0],) + shape), axes, 0, 0, tile...  15.4 us
    all_to_all x1, blocking collectives, exchange_max(): lax.all_to_all(spread, axes, 0, 0, tiled=True)  13.4 us
    all_to_all x2, starting transfers between devices, exchange_gather(): lax.all_to_all(spread, axes, 0, 0, tiled=True)  8.8 us
    all_to_all x2, starting transfers between devices, exchange_sum(): lax.all_to_all(parts.reshape((parts.shape[0],) + shape), axes, 0, 0, tile...  7.72 us
    gather x10, local copies, waits for them, and re-layouts, shards(): written = jnp.take_along_axis(every_fresh[back], mine[:, :, None], axis=1)  7.32 us
  transfers between devices with their start and end apart: 6, of which 4 were waited for; matrix products, arithmetic and copies ran while one was open for 19% of the time, Pallas kernels for 0%

profile of v11, /device:TPU:0, one launch (start us, length us, event | category | flops | bytes accessed | tf_op | source)
XLA Modules:
  0.0 354.8 jit_solution(13739762702119207355)
XLA Ops:
  8.6 1.4 fusion.25
  11.1 4.2 %all-to-all-start = ((f32[2,96,384]{2,1,0:T(8,128)}), f32[2,96,384]{2,1,0:T(8,128)S(1)}, u32[]{:S(2)}, u32[]{:S(2)}) async-start(f32[2,96,384]{2,1,0:T(8,128)} %bitcast.2), calls=%async_computation | async-start | bytes 589824 | tf_op jit(solution)/shard_map/all_to_all | solution.py:49
  15.5 1.3 gather_fusion.4
  17.1 1.3 gather_fusion.1
  21.6 1.3 broadcast_in_dim.222
  22.9 3.7 %all-to-all-start.2 = ((bf16[2,3072,128]{2,1,0:T(8,128)(2,1)}), bf16[2,3072,128]{2,1,0:T(8,128)(2,1)S(1)}, u32[]{:S(2)}, u32[]{:S(2)}) async-start(bf16[2,3072,128]{2,1,0:T(8,128)(2,1)} %broadcast_in_dim.222), calls=%async_computation.3 | async-start | bytes 3145728 | tf_op jit(solution)/shard_map/all_to_all | solution.py:62
  29.8 15.7 %all-to-all-done.2 = bf16[2,3072,128]{2,1,0:T(8,128)(2,1)S(1)} async-done(((bf16[2,3072,128]{2,1,0:T(8,128)(2,1)}), bf16[2,3072,128]{2,1,0:T(8,128)(2,1)S(1)}, u32[]{:S(2)}, u32[]{:S(2)}) %all-to-all-start.2) | async-done | bytes 1572896 | tf_op jit(solution)/shard_map/all_to_all | solution.py:62
  45.5 1.3 broadcast_in_dim.123
  46.8 5.1 %all-to-all-start.1 = ((bf16[32,96,256]{2,1,0:T(8,128)(2,1)}), bf16[32,96,256]{2,1,0:T(8,128)(2,1)}, u32[]{:S(2)}, u32[]{:S(2)}) async-start(bf16[32,96,256]{2,1,0:T(8,128)(2,1)} %broadcast_in_dim.123), calls=%async_computation.1 | async-start | bytes 3145728 | tf_op jit(solution)/shard_map/all_to_all | solution.py:62
  58.3 5.1 %all-reduce.5 = f32[32]{0:T(128)S(1)} all-reduce(f32[32]{0:T(128)S(1)} %reshape.393), channel_id=3, replica_groups=mesh['seq'=8,'pair'=2,'head'=2] {'head'}, use_global_device_ids=true, to_apply=%region_6.7.clone | all-reduce | flops 32 | bytes 256
  64.3 1.3 subtract_compare_fusion.1
  65.6 1.9 reshape.394
  67.5 2.5 copy.528
  70.0 2.4 gather_fusion.7
  72.5 2.5 gather_fusion.2
  74.9 25.9 %all-to-all-done.1 = bf16[32,96,256]{2,1,0:T(8,128)(2,1)} async-done(((bf16[32,96,256]{2,1,0:T(8,128)(2,1)}), bf16[32,96,256]{2,1,0:T(8,128)(2,1)}, u32[]{:S(2)}, u32[]{:S(2)}) %all-to-all-start.1) | async-done | bytes 1572896 | tf_op jit(solution)/shard_map/all_to_all | solution.py:62
  100.9 1.5 fusion.67
  104.3 2.4 mul.287
  106.7 1.4 reduce_sum.186
  109.5 1.6 gather_fusion
  111.8 1.6 gather_fusion.3
  114.2 1.6 gather_fusion.5
  118.4 1.3 broadcast_select_fusion.2
  119.7 1.7 fusion.21
  121.4 2.3 pad_maximum_fusion
  123.7 1.7 copy_convert_fusion
  125.4 4.3 %fusion.69 = f32[32,2048]{1,0:T(8,128)} fusion(bf16[32,1280]{1,0:T(8,128)(2,1)S(1)} %reshape.392, bf16[1280,2048]{1,0:T(8,128)(2,1)} %all-gather.2.cloned.1.call-done), kind=kOutput, calls=%fused_computation.174 | convolution fusion | flops 167772160 | bytes 5586944 | tf_op jit(solution)/shard_map/dot_general | solution.py:141
  129.8 2.2 copy.540
  132.0 2.4 reshape.396
  134.4 3.1 reshape.415
  137.6 1.4 copy.514
  139.0 2.3 fusion.22
  141.2 1.4 copy.515
  145.4 1.8 fusion.4
  147.3 1.9 fusion.66
  150.4 13.4 %all_to_all.85 = f32[32,12,128]{2,1,0:T(8,128)S(1)} all-to-all(f32[32,12,128]{2,1,0:T(8,128)S(1)} %broadcast_in_dim.233), channel_id=1, replica_groups=mesh['seq'=8,'pair'=2,'head'=2] {'seq','pair','head'}, dimensions={0} | all-to-all | bytes 393216 | tf_op jit(solution)/shard_map/all_to_all | solution.py:56
  164.5 2.4 fusion.5
  167.0 2.5 reshape_reshape.4
  169.5 4.1 %copy.595 = f32[12,4,2,8,2,4,64]{6,3,0,2,5,4,1:T(8,128)} copy(f32[12,4,2,8,2,4,64]{6,5,4,3,2,1,0:T(4,128)} %reshape_reshape.4) | data formatting | bytes 3145728 | tf_op jit(solution)/shard_map/reshape;reshape | solution.py:237
  173.6 2.4 reshape.399
  176.5 1.3 select_maximum_fusion
  177.7 1.6 reshape.403
  180.3 5.0 %all_to_all.86 = f32[2,8,2,98,128]{4,1,3,2,0:T(8,128)S(1)} all-to-all(f32[2,8,2,98,128]{4,1,3,2,0:T(8,128)S(1)} %copy.548), channel_id=1, replica_groups=mesh['seq'=8,'pair'=2,'head'=2] {'pair'}, dimensions={0} | all-to-all | bytes 3211264 | tf_op jit(solution)/shard_map/all_to_all | solution.py:49
  186.3 1.6 copy.549
  188.2 26.1 %all_to_all.87 = f32[16,98,128]{2,1,0:T(8,128)S(1)} all-to-all(f32[16,98,128]{2,1,0:T(8,128)S(1)} %copy.550), channel_id=1, replica_groups=mesh['seq'=8,'pair'=2,'head'=2] {'seq','head'}, dimensions={0} | all-to-all | bytes 1605632 | tf_op jit(solution)/shard_map/all_to_all | solution.py:49
  214.6 6.5 %all_to_all.88 = bf16[2,192,64]{1,2,0:T(8,128)(2,1)S(1)} all-to-all(bf16[2,192,64]{1,2,0:T(8,128)(2,1)S(1)} %broadcast_in_dim.236), channel_id=1, replica_groups=mesh['seq'=8,'pair'=2,'head'=2] {'head'}, dimensions={0} | all-to-all | bytes 98304 | tf_op jit(solution)/shard_map/all_to_all | solution.py:62
  222.3 4.5 %all_to_all.89 = f32[2,8,12,1280]{3,1,2,0:T(8,128)S(1)} all-to-all(f32[2,8,12,1280]{3,1,2,0:T(8,128)S(1)} %copy.553), channel_id=1, replica_groups=mesh['seq'=8,'pair'=2,'head'=2] {'pair'}, dimensions={0} | all-to-all | bytes 1966080 | tf_op jit(solution)/shard_map/all_to_all | solution.py:49
  227.9 3.5 all-to-all-start.8
  231.4 14.3 %all-to-all-done.8 = f32[8,120,128]{2,1,0:T(8,128)S(1)} async-done(((f32[8,120,128]{2,1,0:T(8,128)}), f32[8,120,128]{2,1,0:T(8,128)S(1)}, u32[]{:S(2)}, u32[]{:S(2)}) %all-to-all-start.8) | async-done | bytes 491552 | tf_op jit(solution)/shard_map/all_to_all | solution.py:49
  246.1 4.9 %psum.14 = f32[12]{0:T(128)S(1)} all-reduce(f32[12]{0:T(128)S(1)} %reduce_sum.194), channel_id=1, replica_groups=mesh['seq'=8,'pair'=2,'head'=2] {'head'}, use_global_device_ids=true, to_apply=%region_18.22 | all-reduce | flops 12 | bytes 96 | tf_op jit(solution)/shard_map/psum | solution.py:254
  252.0 11.5 %all_to_all.90 = bf16[8,120,128]{2,1,0:T(8,128)(2,1)S(1)} all-to-all(bf16[8,120,128]{2,1,0:T(8,128)(2,1)S(1)} %broadcast_in_dim.238), channel_id=1, replica_groups=mesh['seq'=8,'pair'=2,'head'=2] {'seq'}, dimensions={0} | all-to-all | bytes 491520 | tf_op jit(solution)/shard_map/all_to_all | solution.py:62
  264.0 4.1 %all_to_all.91 = bf16[2,8,12,1280]{3,1,2,0:T(8,128)(2,1)S(1)} all-to-all(bf16[2,8,12,1280]{3,1,2,0:T(8,128)(2,1)S(1)} %broadcast_in_dim.240), channel_id=1, replica_groups=mesh['seq'=8,'pair'=2,'head'=2] {'pair'}, dimensions={0} | all-to-all | bytes 983040 | tf_op jit(solution)/shard_map/all_to_all | solution.py:62
  268.2 1.4 copy.556
  269.6 1.4 reshape.416
  271.0 2.9 fusion.44
  273.9 1.3 fusion.45
  275.6 1.3 select_maximum_fusion.1
  276.9 17.0 %all_to_all.92 = f32[2,96,1408]{2,1,0:T(8,128)S(1)} all-to-all(f32[2,96,1408]{2,1,0:T(8,128)S(1)} %bitcast.171), channel_id=1, replica_groups=mesh['seq'=8,'pair'=2,'head'=2] {'head'}, dimensions={0} | all-to-all | bytes 2162688 | tf_op jit(solution)/shard_map/all_to_all | solution.py:49
  294.3 7.5 %all_to_all.93 = bf16[2,96,640]{2,1,0:T(8,128)(2,1)S(1)} all-to-all(bf16[2,96,640]{2,1,0:T(8,128)(2,1)S(1)} %broadcast_in_dim.242), channel_id=1, replica_groups=mesh['seq'=8,'pair'=2,'head'=2] {'head'}, dimensions={0} | all-to-all | bytes 491520 | tf_op jit(solution)/shard_map/all_to_all | solution.py:62
  303.1 4.5 %all_to_all.94 = f32[2,8,12,1280]{3,1,2,0:T(8,128)S(1)} all-to-all(f32[2,8,12,1280]{3,1,2,0:T(8,128)S(1)} %copy.559), channel_id=1, replica_groups=mesh['seq'=8,'pair'=2,'head'=2] {'pair'}, dimensions={0} | all-to-all | bytes 1966080 | tf_op jit(solution)/shard_map/all_to_all | solution.py:49
  308.0 17.0 %all_to_all.95 = f32[8,120,128]{2,1,0:T(8,128)S(1)} all-to-all(f32[8,120,128]{2,1,0:T(8,128)S(1)} %reshape.410), channel_id=1, replica_groups=mesh['seq'=8,'pair'=2,'head'=2] {'seq'}, dimensions={0} | all-to-all | bytes 983040 | tf_op jit(solution)/shard_map/all_to_all | solution.py:49
  325.3 4.9 %psum.15 = f32[12]{0:T(128)S(1)} all-reduce(f32[12]{0:T(128)S(1)} %reduce_sum.202), channel_id=1, replica_groups=mesh['seq'=8,'pair'=2,'head'=2] {'head'}, use_global_device_ids=true, to_apply=%region_25.29 | all-reduce | flops 12 | bytes 96 | tf_op jit(solution)/shard_map/psum | solution.py:277
  330.5 11.5 %all_to_all.96 = bf16[8,120,128]{2,1,0:T(8,128)(2,1)S(1)} all-to-all(bf16[8,120,128]{2,1,0:T(8,128)(2,1)S(1)} %broadcast_in_dim.244), channel_id=1, replica_groups=mesh['seq'=8,'pair'=2,'head'=2] {'seq'}, dimensions={0} | all-to-all | bytes 491520 | tf_op jit(solution)/shard_map/all_to_all | solution.py:62
  342.5 4.1 %all_to_all.97 = bf16[2,8,12,1280]{3,1,2,0:T(8,128)(2,1)S(1)} all-to-all(bf16[2,8,12,1280]{3,1,2,0:T(8,128)(2,1)S(1)} %broadcast_in_dim.246), channel_id=1, replica_groups=mesh['seq'=8,'pair'=2,'head'=2] {'pair'}, dimensions={0} | all-to-all | bytes 983040 | tf_op jit(solution)/shard_map/all_to_all | solution.py:62
  (242 shorter events, 39.8 us)
Async XLA Ops:
  6.5 295.3 %copy-start = (bf16[640,1280]{1,0:T(8,128)(2,1)S(1)}, bf16[640,1280]{1,0:T(8,128)(2,1)}, u32[]{:S(2)}) copy-start(bf16[640,1280]{1,0:T(8,128)(2,1)} %param.44) | copy-start | bytes 4915204
  6.5 3.5 copy-start.9
  6.5 3.5 copy-start.18
  6.5 3.5 copy-start.29
  6.5 118.8 %all-gather.2.cloned.1.call-start = ((), (), s32[]{:S(2)}) async-start(), calls=%async_computation.18 | async-start | bytes 5570560 | tf_op jit(solution)/shard_map/all_gather | solution.py:143
  8.5 6.8 %copy-start.13 = (s32[2,12,8]{1,2,0:T(8,128)S(1)}, s32[2,12,8]{1,2,0:T(8,128)}, u32[]{:S(2)}) copy-start(s32[2,12,8]{1,2,0:T(8,128)} %param.27) | copy-start | bytes 2308
  11.1 10.5 %all-to-all-start = ((f32[2,96,384]{2,1,0:T(8,128)}), f32[2,96,384]{2,1,0:T(8,128)S(1)}, u32[]{:S(2)}, u32[]{:S(2)}) async-start(f32[2,96,384]{2,1,0:T(8,128)} %bitcast.2), calls=%async_computation | async-start | bytes 589824 | tf_op jit(solution)/shard_map/all_to_all | solution.py:49
  18.6 1.2 copy-start.7
  18.6 1.8 copy-start.26
  22.9 22.6 %all-to-all-start.2 = ((bf16[2,3072,128]{2,1,0:T(8,128)(2,1)}), bf16[2,3072,128]{2,1,0:T(8,128)(2,1)S(1)}, u32[]{:S(2)}, u32[]{:S(2)}) async-start(bf16[2,3072,128]{2,1,0:T(8,128)(2,1)} %broadcast_in_dim.222), calls=%async_computation.3 | async-start | bytes 3145728 | tf_op jit(solution)/shard_map/all_to_all | solution.py:62
  46.8 5.5 %copy-start.23 = (pred[12,4]{0,1:T(4,128)(4,1)S(1)}, pred[12,4]{0,1:T(4,128)(4,1)}, u32[]{:S(2)}) copy-start(pred[12,4]{0,1:T(4,128)(4,1)} %get-tuple-element.37) | copy-start | bytes 148
  46.8 6.3 %copy-start.22 = (pred[12,4]{0,1:T(4,128)(4,1)S(1)}, pred[12,4]{0,1:T(4,128)(4,1)}, u32[]{:S(2)}) copy-start(pred[12,4]{0,1:T(4,128)(4,1)} %get-tuple-element.38) | copy-start | bytes 148
  46.8 8.7 %copy-start.11 = (bf16[4,8,1280]{2,1,0:T(8,128)(2,1)S(1)}, bf16[4,8,1280]{2,1,0:T(8,128)(2,1)}, u32[]{:S(2)}) copy-start(bf16[4,8,1280]{2,1,0:T(8,128)(2,1)} %param.32) | copy-start | bytes 245764
  46.8 9.1 %copy-start.21 = (s32[12]{0:T(128)S(1)}, s32[12]{0:T(128)}, u32[]{:S(2)}) copy-start(s32[12]{0:T(128)} %param.29) | copy-start | bytes 148
  46.8 10.2 %copy-start.31 = (u32[32]{0:T(128)S(1)}, u32[32]{0:T(128)}, u32[]{:S(2)}) copy-start(u32[32]{0:T(128)} %constant.271) | copy-start | bytes 388
  46.8 17.2 %copy-start.30 = (s32[4]{0:T(128)S(1)}, s32[4]{0:T(128)}, u32[]{:S(2)}) copy-start(s32[4]{0:T(128)} %param.33) | copy-start | bytes 52
  46.8 17.2 %copy-start.28 = (s32[8]{0:T(128)S(1)}, s32[8]{0:T(128)}, u32[]{:S(2)}) copy-start(s32[8]{0:T(128)} %param.31) | copy-start | bytes 100
  46.8 54.0 %all-to-all-start.1 = ((bf16[32,96,256]{2,1,0:T(8,128)(2,1)}), bf16[32,96,256]{2,1,0:T(8,128)(2,1)}, u32[]{:S(2)}, u32[]{:S(2)}) async-start(bf16[32,96,256]{2,1,0:T(8,128)(2,1)} %broadcast_in_dim.123), calls=%async_computation.1 | async-start | bytes 3145728 | tf_op jit(solution)/shard_map/all_to_all | solution.py:62
  52.0 90.7 %reduce-scatter.2.cloned.1.call-start = ((), (), s32[]{:S(2)}) async-start(), calls=%async_computation.19 | async-start | bytes 393216 | tf_op jit(solution)/shard_map/reduce_scatter | solution.py:147
  55.9 0.5 copy-start.24
  108.5 1.0 copy-start.6
  115.7 3.9 %copy-start.2 = (bf16[48,4,2048]{2,1,0:T(4,128)(2,1)S(1)}, bf16[48,4,2048]{2,1,0:T(4,128)(2,1)}, u32[]{:S(2)}) copy-start(bf16[48,4,2048]{2,1,0:T(4,128)(2,1)} %gather_fusion.7) | copy-start | bytes 2359300
  116.5 3.2 copy-start.14
  116.5 3.2 copy-start.15
  116.5 3.2 copy-start.16
  116.5 3.2 copy-start.17
  117.2 2.5 copy-start.3
  125.4 4.4 %copy-start.1 = (bf16[12,2,4,4,2048]{4,3,2,0,1:T(4,128)(2,1)S(1)}, bf16[12,2,4,4,2048]{4,3,2,0,1:T(4,128)(2,1)}, u32[]{:S(2)}) copy-start(bf16[12,2,4,4,2048]{4,3,2,0,1:T(4,128)(2,1)} %pad_maximum_fusion) | copy-start | bytes 4718596
  134.4 4.6 %copy-start.25 = (f32[256]{0:T(256)S(1)}, f32[256]{0:T(256)}, u32[]{:S(2)}) copy-start(f32[256]{0:T(256)} %param.37) | copy-start | bytes 3076
  139.0 3.7 %copy-start.27 = (f32[16]{0:T(128)S(1)}, f32[16]{0:T(128)}, u32[]{:S(2)}) copy-start(f32[16]{0:T(128)} %fusion.63) | copy-start | bytes 196
  147.3 1.9 copy-start.8
  150.3 14.2 %copy-start.4 = (f32[12,4,32,96]{3,2,1,0:T(8,128)}, f32[12,4,32,96]{3,2,1,0:T(8,128)S(1)}, u32[]{:S(2)}) copy-start(f32[12,4,32,96]{3,2,1,0:T(8,128)S(1)} %get-tuple-element.32) | copy-start | bytes 1769476
  188.1 33.2 %copy-start.10 = (bf16[128,1280]{1,0:T(8,128)(2,1)S(1)}, bf16[128,1280]{1,0:T(8,128)(2,1)}, u32[]{:S(2)}) copy-start(bf16[128,1280]{1,0:T(8,128)(2,1)} %param.39) | copy-start | bytes 983044
  227.1 24.0 %copy-start.19 = (f32[1280]{0:T(1024)S(1)}, f32[1280]{0:T(1024)}, u32[]{:S(2)}) copy-start(f32[1280]{0:T(1024)} %param.40) | copy-start | bytes 15364
  227.9 17.8 %all-to-all-start.8 = ((f32[8,120,128]{2,1,0:T(8,128)}), f32[8,120,128]{2,1,0:T(8,128)S(1)}, u32[]{:S(2)}, u32[]{:S(2)}) async-start(f32[8,120,128]{2,1,0:T(8,128)} %reshape.407), calls=%async_computation.9 | async-start | bytes 983040 | tf_op jit(solution)/shard_map/all_to_all | solution.py:49
  269.6 1.4 copy-start.12
  271.0 2.9 copy-start.5
  307.9 22.4 %copy-start.20 = (f32[1280]{0:T(1024)S(1)}, f32[1280]{0:T(1024)}, u32[]{:S(2)}) copy-start(f32[1280]{0:T(1024)} %param.45) | copy-start | bytes 15364
Sparse Core Ops, SparseCore 0:
  9.5 79.6 all-gather.1
  129.9 9.7 reduce-scatter.1

commit v12 on v9

--- a/solution.py
+++ b/solution.py
@@ -74,6 +74,14 @@
     outer = lax.axis_size("seq")
     got = exchange_gather(exchange_gather(piece, "seq", outer, True), "pair", pair)
     return jnp.swapaxes(got, 0, 1).reshape((outer * pair,) + piece.shape)
+
+
+def gather_columns(weight):
+    pair = lax.axis_size("pair")
+    outer = lax.axis_size("seq")
+    part = lax.all_gather(weight, "seq", axis=1, tiled=True)
+    both = exchange_gather(part, "pair", pair).reshape(pair, weight.shape[0], outer, -1)
+    return jnp.transpose(both, (1, 2, 0, 3)).reshape(weight.shape[0], -1)
 
 
 def project_tokens(tokens, in_gain, w_query, w_keyval, q_gain, k_gain):
@@ -140,7 +148,7 @@
     prompt_squares = jnp.sum(rows * rows, -1).reshape(-1)
     prompt_terms = jnp.dot(
         prompt_scaled,
-        lax.all_gather(w_keyval, SEQ, axis=1, tiled=True),
+        gather_columns(w_keyval),
         preferred_element_type=f32,
     )
     prompt_sum, prompt_sq = (

time: 344 us -> 352 us (1.023)
  local copies, waits for them, and re-layouts: 67 us -> 74.6 us
  blocking collectives: 152 us -> 158 us
  waiting for transfers between devices: 53.8 us -> 49 us
    all_to_all x6 -> x7, blocking collectives: 45.3 us -> 53.2 us  [exchange_gather(): lax.all_to_all(spread, axes, 0, 0, tiled=True)]
    all_gather x0 -> x1, local copies, waits for them, and re-layouts: none -> 4.4 us  [gather_columns(): part = lax.all_gather(weight, 'seq', axis=1, tiled=True)]
  transfers between devices with their start and end apart: 6 -> 6, of which waited for: 5 -> 5; matrix products, arithmetic and copies ran while one was open for 17% -> 18% of each run, Pallas kernels for 0% -> 0%
where the time goes in v12:
time: 352 us; the launch traced here: 350 us
  blocking collectives  158 us (45%)
  local copies, waits for them, and re-layouts  74.6 us (21%)
  waiting for transfers between devices  49 us (14%)
  other arithmetic  30 us (9%)
  between operations  14.8 us (4%)
  starting transfers between devices  14 us (4%)
  matrix products  10.1 us (3%)
    all_to_all x6, blocking collectives, exchange_sum(): lax.all_to_all(parts.reshape((parts.shape[0],) + shape), axes, 0, 0, tile...  74.1 us
    all_to_all x7, blocking collectives, exchange_gather(): lax.all_to_all(spread, axes, 0, 0, tiled=True)  53.2 us
    all_gather x1, waiting for transfers between devices, gather_columns(): part = lax.all_gather(weight, 'seq', axis=1, tiled=True)  20.9 us
    all_to_all x2, waiting for transfers between devices, exchange_sum(): lax.all_to_all(parts.reshape((parts.shape[0],) + shape), axes, 0, 0, tile...  15.1 us
    all_to_all x1, blocking collectives, exchange_max(): lax.all_to_all(spread, axes, 0, 0, tiled=True)  14.5 us
    gather x6, local copies, waits for them, and re-layouts, shards(): tail_state = jnp.take_along_axis(everyone, picks[:, :, None, None], axis=1)  8.08 us
    all_to_all x2, starting transfers between devices, exchange_sum(): lax.all_to_all(parts.reshape((parts.shape[0],) + shape), axes, 0, 0, tile...  7.72 us
    all_to_all x1, waiting for transfers between devices, exchange_gather(): lax.all_to_all(spread, axes, 0, 0, tiled=True)  7.31 us
  transfers between devices with their start and end apart: 6, of which 5 were waited for; matrix products, arithmetic and copies ran while one was open for 18% of the time, Pallas kernels for 0%

profile of v12, /device:TPU:0, one launch (start us, length us, event | category | flops | bytes accessed | tf_op | source)
XLA Modules:
  0.0 350.4 jit_solution(7921452419111686315)
XLA Ops:
  8.0 1.2 multiply_reduce_fusion.1
  10.7 4.2 %all-to-all-start = ((f32[2,96,384]{2,1,0:T(8,128)}), f32[2,96,384]{2,1,0:T(8,128)S(1)}, u32[]{:S(2)}, u32[]{:S(2)}) async-start(f32[2,96,384]{2,1,0:T(8,128)} %bitcast.2), calls=%async_computation | async-start | bytes 589824 | tf_op jit(solution)/shard_map/all_to_all | solution.py:49
  15.3 1.3 gather_fusion.4
  16.9 1.3 gather_fusion.1
  21.4 1.4 broadcast_in_dim.121
  22.8 6.2 %all-to-all-start.1 = ((bf16[32,96,256]{2,1,0:T(8,128)(2,1)}), bf16[32,96,256]{2,1,0:T(8,128)(2,1)S(1)}, u32[]{:S(2)}, u32[]{:S(2)}) async-start(bf16[32,96,256]{2,1,0:T(8,128)(2,1)} %broadcast_in_dim.121), calls=%async_computation.1 | async-start | bytes 3145728 | tf_op jit(solution)/shard_map/all_to_all | solution.py:62
  30.6 1.3 copy.538
  33.0 1.4 copy.548
  35.6 1.2 dynamic-slice.2
  37.5 6.2 %all-reduce.5 = f32[32]{0:T(128)S(1)} all-reduce(f32[32]{0:T(128)S(1)} %reshape.395), channel_id=3, replica_groups=mesh['seq'=8,'pair'=2,'head'=2] {'head'}, use_global_device_ids=true, to_apply=%region_6.7.clone | all-reduce | flops 32 | bytes 256
  45.9 1.3 subtract_compare_fusion.1
  47.2 4.2 %all-gather.5.cloned.1.call-done = bf16[12,8,4,2048]{3,2,1,0:T(4,128)(2,1)} async-done(((bf16[12,4,4,2048]{3,2,1,0:T(4,128)(2,1)}), bf16[12,8,4,2048]{3,2,1,0:T(4,128)(2,1)}) %all-gather.5.cloned.1.call-update) | async-done | bytes 1572880 | tf_op jit(solution)/shard_map/all_gather | solution.py:189
  51.4 3.9 %gather_fusion.2 = bf16[48,4,2048]{2,1,0:T(4,128)(2,1)} fusion(bf16[12,8,4,2048]{3,2,1,0:T(4,128)(2,1)} %all-gather.5.cloned.1.call-done, s32[48]{0:T(128)S(1)} %reshape.500), kind=kCustom, calls=%fused_computation.2.clone | custom fusion | bytes 1573248 | tf_op jit(solution)/shard_map/jit(take_along_axis)/gather | solution.py:205
  55.3 3.8 %gather_fusion.7 = bf16[48,4,2048]{2,1,0:T(4,128)(2,1)} fusion(bf16[12,8,4,2048]{3,2,1,0:T(4,128)(2,1)} %all-gather.5.cloned.1.call-done, s32[48]{0:T(128)S(1)} %reshape.523), kind=kCustom, calls=%fused_computation.7.clone | custom fusion | bytes 1573248 | tf_op jit(solution)/shard_map/jit(take_along_axis)/gather | solution.py:205
  59.1 7.3 %all-to-all-done.1 = bf16[32,96,256]{2,1,0:T(8,128)(2,1)S(1)} async-done(((bf16[32,96,256]{2,1,0:T(8,128)(2,1)}), bf16[32,96,256]{2,1,0:T(8,128)(2,1)S(1)}, u32[]{:S(2)}, u32[]{:S(2)}) %all-to-all-start.1) | async-done | bytes 1572896 | tf_op jit(solution)/shard_map/all_to_all | solution.py:62
  67.6 1.5 fusion.67
  71.0 2.4 mul.287
  73.4 1.4 reduce_sum.186
  76.2 1.6 gather_fusion
  78.5 1.6 gather_fusion.3
  80.9 1.6 gather_fusion.5
  85.1 1.3 broadcast_select_fusion.2
  86.4 1.5 fusion.21
  87.9 2.2 pad_maximum_fusion
  90.1 1.7 copy_convert_fusion
  91.8 20.9 %all-gather.3.cloned.1.call-done = bf16[1280,1024]{1,0:T(8,128)(2,1)} async-done(((bf16[1280,128]{1,0:T(8,128)(2,1)}), bf16[1280,1024]{1,0:T(8,128)(2,1)}) %all-gather.3.cloned.1.call-update) | async-done | bytes 2621456 | tf_op jit(solution)/shard_map/all_gather | solution.py:82
  112.7 4.4 %copy.526 = bf16[1280,1024]{0,1:T(8,128)(2,1)} copy(bf16[1280,1024]{1,0:T(8,128)(2,1)} %all-gather.3.cloned.1.call-done) | data formatting | bytes 5242880 | tf_op jit(solution)/shard_map/all_gather | solution.py:82
  117.1 2.1 broadcast_in_dim.122
  119.2 7.9 %all_to_all.85 = bf16[2,1280,1024]{1,2,0:T(8,128)(2,1)S(1)} all-to-all(bf16[2,1280,1024]{1,2,0:T(8,128)(2,1)S(1)} %broadcast_in_dim.122), channel_id=1, replica_groups=mesh['seq'=8,'pair'=2,'head'=2] {'pair'}, dimensions={0} | all-to-all | bytes 10485760 | tf_op jit(solution)/shard_map/all_to_all | solution.py:62
  127.6 2.3 fusion.69
  130.0 2.4 reshape.396
  132.4 3.1 reshape.415
  135.5 1.4 copy.523
  136.9 2.2 fusion.22
  139.2 1.4 copy.524
  143.4 1.8 fusion.4
  145.2 1.9 fusion.66
  148.4 14.5 %all_to_all.86 = f32[32,12,128]{2,1,0:T(8,128)S(1)} all-to-all(f32[32,12,128]{2,1,0:T(8,128)S(1)} %broadcast_in_dim.231), channel_id=1, replica_groups=mesh['seq'=8,'pair'=2,'head'=2] {'seq','pair','head'}, dimensions={0} | all-to-all | bytes 393216 | tf_op jit(solution)/shard_map/all_to_all | solution.py:56
  164.0 2.4 fusion.5
  166.4 2.5 reshape_reshape.4
  168.9 4.1 %copy.605 = f32[12,4,2,8,2,4,64]{6,3,0,2,5,4,1:T(8,128)} copy(f32[12,4,2,8,2,4,64]{6,5,4,3,2,1,0:T(4,128)} %reshape_reshape.4) | data formatting | bytes 3145728 | tf_op jit(solution)/shard_map/reshape;reshape | solution.py:242
  173.1 2.4 reshape.399
  175.5 1.3 select_maximum_fusion
  176.8 1.6 reshape.403
  179.3 5.0 %all_to_all.87 = f32[2,8,2,98,128]{4,1,3,2,0:T(8,128)S(1)} all-to-all(f32[2,8,2,98,128]{4,1,3,2,0:T(8,128)S(1)} %copy.558), channel_id=1, replica_groups=mesh['seq'=8,'pair'=2,'head'=2] {'pair'}, dimensions={0} | all-to-all | bytes 3211264 | tf_op jit(solution)/shard_map/all_to_all | solution.py:49
  185.4 1.6 copy.559
  187.2 26.1 %all_to_all.88 = f32[16,98,128]{2,1,0:T(8,128)S(1)} all-to-all(f32[16,98,128]{2,1,0:T(8,128)S(1)} %copy.560), channel_id=1, replica_groups=mesh['seq'=8,'pair'=2,'head'=2] {'seq','head'}, dimensions={0} | all-to-all | bytes 1605632 | tf_op jit(solution)/shard_map/all_to_all | solution.py:49
  213.7 6.5 %all_to_all.89 = bf16[2,192,64]{1,2,0:T(8,128)(2,1)S(1)} all-to-all(bf16[2,192,64]{1,2,0:T(8,128)(2,1)S(1)} %broadcast_in_dim.234), channel_id=1, replica_groups=mesh['seq'=8,'pair'=2,'head'=2] {'head'}, dimensions={0} | all-to-all | bytes 98304 | tf_op jit(solution)/shard_map/all_to_all | solution.py:62
  221.3 4.5 %all_to_all.90 = f32[2,8,12,1280]{3,1,2,0:T(8,128)S(1)} all-to-all(f32[2,8,12,1280]{3,1,2,0:T(8,128)S(1)} %copy.563), channel_id=1, replica_groups=mesh['seq'=8,'pair'=2,'head'=2] {'pair'}, dimensions={0} | all-to-all | bytes 1966080 | tf_op jit(solution)/shard_map/all_to_all | solution.py:49
  226.9 3.5 all-to-all-start.8
  230.4 14.3 %all-to-all-done.8 = f32[8,120,128]{2,1,0:T(8,128)S(1)} async-done(((f32[8,120,128]{2,1,0:T(8,128)}), f32[8,120,128]{2,1,0:T(8,128)S(1)}, u32[]{:S(2)}, u32[]{:S(2)}) %all-to-all-start.8) | async-done | bytes 491552 | tf_op jit(solution)/shard_map/all_to_all | solution.py:49
  245.1 4.9 %psum.14 = f32[12]{0:T(128)S(1)} all-reduce(f32[12]{0:T(128)S(1)} %reduce_sum.194), channel_id=1, replica_groups=mesh['seq'=8,'pair'=2,'head'=2] {'head'}, use_global_device_ids=true, to_apply=%region_18.22 | all-reduce | flops 12 | bytes 96 | tf_op jit(solution)/shard_map/psum | solution.py:259
  251.1 11.5 %all_to_all.91 = bf16[8,120,128]{2,1,0:T(8,128)(2,1)S(1)} all-to-all(bf16[8,120,128]{2,1,0:T(8,128)(2,1)S(1)} %broadcast_in_dim.236), channel_id=1, replica_groups=mesh['seq'=8,'pair'=2,'head'=2] {'seq'}, dimensions={0} | all-to-all | bytes 491520 | tf_op jit(solution)/shard_map/all_to_all | solution.py:62
  263.0 4.1 %all_to_all.92 = bf16[2,8,12,1280]{3,1,2,0:T(8,128)(2,1)S(1)} all-to-all(bf16[2,8,12,1280]{3,1,2,0:T(8,128)(2,1)S(1)} %broadcast_in_dim.238), channel_id=1, replica_groups=mesh['seq'=8,'pair'=2,'head'=2] {'pair'}, dimensions={0} | all-to-all | bytes 983040 | tf_op jit(solution)/shard_map/all_to_all | solution.py:62
  267.6 1.4 copy.566
  269.0 1.4 reshape.416
  270.5 2.1 fusion.44
  273.2 17.0 %all_to_all.93 = f32[2,96,1408]{2,1,0:T(8,128)S(1)} all-to-all(f32[2,96,1408]{2,1,0:T(8,128)S(1)} %bitcast.175), channel_id=1, replica_groups=mesh['seq'=8,'pair'=2,'head'=2] {'head'}, dimensions={0} | all-to-all | bytes 2162688 | tf_op jit(solution)/shard_map/all_to_all | solution.py:49
  290.6 7.5 %all_to_all.94 = bf16[2,96,640]{2,1,0:T(8,128)(2,1)S(1)} all-to-all(bf16[2,96,640]{2,1,0:T(8,128)(2,1)S(1)} %broadcast_in_dim.240), channel_id=1, replica_groups=mesh['seq'=8,'pair'=2,'head'=2] {'head'}, dimensions={0} | all-to-all | bytes 491520 | tf_op jit(solution)/shard_map/all_to_all | solution.py:62
  299.5 4.5 %all_to_all.95 = f32[2,8,12,1280]{3,1,2,0:T(8,128)S(1)} all-to-all(f32[2,8,12,1280]{3,1,2,0:T(8,128)S(1)} %copy.569), channel_id=1, replica_groups=mesh['seq'=8,'pair'=2,'head'=2] {'pair'}, dimensions={0} | all-to-all | bytes 1966080 | tf_op jit(solution)/shard_map/all_to_all | solution.py:49
  304.3 17.0 %all_to_all.96 = f32[8,120,128]{2,1,0:T(8,128)S(1)} all-to-all(f32[8,120,128]{2,1,0:T(8,128)S(1)} %reshape.410), channel_id=1, replica_groups=mesh['seq'=8,'pair'=2,'head'=2] {'seq'}, dimensions={0} | all-to-all | bytes 983040 | tf_op jit(solution)/shard_map/all_to_all | solution.py:49
  321.7 4.9 %psum.15 = f32[12]{0:T(128)S(1)} all-reduce(f32[12]{0:T(128)S(1)} %reduce_sum.202), channel_id=1, replica_groups=mesh['seq'=8,'pair'=2,'head'=2] {'head'}, use_global_device_ids=true, to_apply=%region_25.29 | all-reduce | flops 12 | bytes 96 | tf_op jit(solution)/shard_map/psum | solution.py:282
  326.8 11.5 %all_to_all.97 = bf16[8,120,128]{2,1,0:T(8,128)(2,1)S(1)} all-to-all(bf16[8,120,128]{2,1,0:T(8,128)(2,1)S(1)} %broadcast_in_dim.242), channel_id=1, replica_groups=mesh['seq'=8,'pair'=2,'head'=2] {'seq'}, dimensions={0} | all-to-all | bytes 491520 | tf_op jit(solution)/shard_map/all_to_all | solution.py:62
  338.8 4.1 %all_to_all.98 = bf16[2,8,12,1280]{3,1,2,0:T(8,128)(2,1)S(1)} all-to-all(bf16[2,8,12,1280]{3,1,2,0:T(8,128)(2,1)S(1)} %broadcast_in_dim.244), channel_id=1, replica_groups=mesh['seq'=8,'pair'=2,'head'=2] {'pair'}, dimensions={0} | all-to-all | bytes 983040 | tf_op jit(solution)/shard_map/all_to_all | solution.py:62
  (232 shorter events, 38.5 us)
Async XLA Ops:
  6.5 291.6 %copy-start = (bf16[640,1280]{1,0:T(8,128)(2,1)S(1)}, bf16[640,1280]{1,0:T(8,128)(2,1)}, u32[]{:S(2)}) copy-start(bf16[640,1280]{1,0:T(8,128)(2,1)} %param.44) | copy-start | bytes 4915204
  6.5 2.8 copy-start.9
  6.5 2.8 copy-start.8
  6.5 2.8 copy-start.18
  6.5 3.1 copy-start.26
  6.5 44.9 %all-gather.5.cloned.1.call-start = ((), (), s32[]{:S(2)}) async-start(), calls=%async_computation.20 | async-start | bytes 2359296 | tf_op jit(solution)/shard_map/all_gather | solution.py:189
  7.3 105.4 %all-gather.3.cloned.1.call-start = ((), (), s32[]{:S(2)}) async-start(), calls=%async_computation.18 | async-start | bytes 2949120 | tf_op jit(solution)/shard_map/all_gather | solution.py:82
  9.2 5.7 %copy-start.11 = (bf16[4,8,1280]{2,1,0:T(8,128)(2,1)S(1)}, bf16[4,8,1280]{2,1,0:T(8,128)(2,1)}, u32[]{:S(2)}) copy-start(bf16[4,8,1280]{2,1,0:T(8,128)(2,1)} %param.32) | copy-start | bytes 245764
  9.3 5.7 %copy-start.13 = (s32[2,12,8]{1,2,0:T(8,128)S(1)}, s32[2,12,8]{1,2,0:T(8,128)}, u32[]{:S(2)}) copy-start(s32[2,12,8]{1,2,0:T(8,128)} %param.27) | copy-start | bytes 2308
  10.7 10.5 %all-to-all-start = ((f32[2,96,384]{2,1,0:T(8,128)}), f32[2,96,384]{2,1,0:T(8,128)S(1)}, u32[]{:S(2)}, u32[]{:S(2)}) async-start(f32[2,96,384]{2,1,0:T(8,128)} %bitcast.2), calls=%async_computation | async-start | bytes 589824 | tf_op jit(solution)/shard_map/all_to_all | solution.py:49
  18.3 1.8 copy-start.21
  19.5 1.9 copy-start.22
  22.8 7.2 %copy-start.24 = (f32[256]{0:T(256)S(1)}, f32[256]{0:T(256)}, u32[]{:S(2)}) copy-start(f32[256]{0:T(256)} %param.38) | copy-start | bytes 3076
  22.8 43.7 %all-to-all-start.1 = ((bf16[32,96,256]{2,1,0:T(8,128)(2,1)}), bf16[32,96,256]{2,1,0:T(8,128)(2,1)S(1)}, u32[]{:S(2)}, u32[]{:S(2)}) async-start(bf16[32,96,256]{2,1,0:T(8,128)(2,1)} %broadcast_in_dim.121), calls=%async_computation.1 | async-start | bytes 3145728 | tf_op jit(solution)/shard_map/all_to_all | solution.py:62
  29.0 111.6 %reduce-scatter.2.cloned.1.call-start = ((), (), s32[]{:S(2)}) async-start(), calls=%async_computation.19 | async-start | bytes 393216 | tf_op jit(solution)/shard_map/reduce_scatter | solution.py:155
  66.4 1.1 copy-start.1
  75.2 1.0 copy-start.6
  82.4 3.9 %copy-start.2 = (bf16[48,4,2048]{2,1,0:T(4,128)(2,1)S(1)}, bf16[48,4,2048]{2,1,0:T(4,128)(2,1)}, u32[]{:S(2)}) copy-start(bf16[48,4,2048]{2,1,0:T(4,128)(2,1)} %gather_fusion.2) | copy-start | bytes 2359300
  83.2 3.2 copy-start.14
  83.2 3.2 copy-start.15
  83.2 3.2 copy-start.16
  83.2 3.2 copy-start.17
  83.9 2.5 copy-start.3
  132.4 4.6 %copy-start.23 = (f32[256]{0:T(256)S(1)}, f32[256]{0:T(256)}, u32[]{:S(2)}) copy-start(f32[256]{0:T(256)} %param.37) | copy-start | bytes 3076
  136.9 3.7 %copy-start.25 = (f32[16]{0:T(128)S(1)}, f32[16]{0:T(128)}, u32[]{:S(2)}) copy-start(f32[16]{0:T(128)} %fusion.63) | copy-start | bytes 196
  145.2 1.9 copy-start.7
  148.2 15.7 %copy-start.4 = (f32[12,4,32,96]{3,2,1,0:T(8,128)}, f32[12,4,32,96]{3,2,1,0:T(8,128)S(1)}, u32[]{:S(2)}) copy-start(f32[12,4,32,96]{3,2,1,0:T(8,128)S(1)} %get-tuple-element.32) | copy-start | bytes 1769476
  187.2 33.2 %copy-start.10 = (bf16[128,1280]{1,0:T(8,128)(2,1)S(1)}, bf16[128,1280]{1,0:T(8,128)(2,1)}, u32[]{:S(2)}) copy-start(bf16[128,1280]{1,0:T(8,128)(2,1)} %param.39) | copy-start | bytes 983044
  226.1 24.0 %copy-start.19 = (f32[1280]{0:T(1024)S(1)}, f32[1280]{0:T(1024)}, u32[]{:S(2)}) copy-start(f32[1280]{0:T(1024)} %param.40) | copy-start | bytes 15364
  226.9 17.8 %all-to-all-start.8 = ((f32[8,120,128]{2,1,0:T(8,128)}), f32[8,120,128]{2,1,0:T(8,128)S(1)}, u32[]{:S(2)}, u32[]{:S(2)}) async-start(f32[8,120,128]{2,1,0:T(8,128)} %reshape.407), calls=%async_computation.9 | async-start | bytes 983040 | tf_op jit(solution)/shard_map/all_to_all | solution.py:49
  269.0 1.4 copy-start.12
  270.4 2.1 copy-start.5
  304.2 22.4 %copy-start.20 = (f32[1280]{0:T(1024)S(1)}, f32[1280]{0:T(1024)}, u32[]{:S(2)}) copy-start(f32[1280]{0:T(1024)} %param.45) | copy-start | bytes 15364
Sparse Core Ops, SparseCore 0:
  8.9 42.4 all-gather.4
  53.5 59.1 all-gather.2
  130.1 9.8 reduce-scatter.1

commit v13 on v9

--- a/solution.py
+++ b/solution.py
@@ -248,7 +248,7 @@
     partial_out = jnp.dot(attn, w_out, preferred_element_type=f32)
     per_dev = rows // n_seq
     out_proj = seq_sum(partial_out.reshape(n_seq, per_dev, -1))
-    out_sq = lax.psum(jnp.sum(out_proj * out_proj, -1), "head")
+    out_sq = jnp.sum(exchange_gather(jnp.sum(out_proj * out_proj, -1), "head", n_head), 0)
     x_all = step_tokens.reshape(rows, -1)
     x_f = lax.dynamic_slice_in_dim(x_all, seq_at * per_dev, per_dev, 0).astype(f32)
     state = (x_f + out_proj * lax.rsqrt(out_sq / D + EPS)[:, None] * post_gain).astype(bf16)
@@ -271,7 +271,7 @@
     ).astype(bf16)
     inner = exchange_gather(inner, "head", n_head).reshape(rows, hidden)
     ffn_out = seq_sum(jnp.dot(inner, w_down, preferred_element_type=f32).reshape(n_seq, per_dev, -1))
-    ffn_sq = lax.psum(jnp.sum(ffn_out * ffn_out, -1), "head")
+    ffn_sq = jnp.sum(exchange_gather(jnp.sum(ffn_out * ffn_out, -1), "head", n_head), 0)
     result = (
         state.astype(f32) + ffn_out * lax.rsqrt(ffn_sq / D + EPS)[:, None] * final_gain
     ).astype(bf16)

time: 344 us -> 347 us (level)
    all_to_all x6 -> x8, blocking collectives: 45.3 us -> 57.4 us  [exchange_gather(): lax.all_to_all(spread, axes, 0, 0, tiled=True)]
    psum x2 -> x0, blocking collectives: 9.88 us -> none  [the longest x1 4.94 us: shards(): out_sq = lax.psum(jnp.sum(out_proj * out_proj, -1), 'head')]
where the time goes in v13:
time: 347 us; the launch traced here: 345 us
  blocking collectives  154 us (44%)
  local copies, waits for them, and re-layouts  67 us (19%)
  waiting for transfers between devices  53.8 us (16%)
  other arithmetic  28.3 us (8%)
  between operations  14.9 us (4%)
  matrix products  13.5 us (4%)
  starting transfers between devices  13.4 us (4%)
    all_to_all x6, blocking collectives, exchange_sum(): lax.all_to_all(parts.reshape((parts.shape[0],) + shape), axes, 0, 0, tile...  74.2 us
    all_to_all x8, blocking collectives, exchange_gather(): lax.all_to_all(spread, axes, 0, 0, tiled=True)  57.4 us
    all_gather x1, waiting for transfers between devices, shards(): lax.all_gather(w_keyval, SEQ, axis=1, tiled=True)  23.7 us
    all_to_all x2, waiting for transfers between devices, exchange_sum(): lax.all_to_all(parts.reshape((parts.shape[0],) + shape), axes, 0, 0, tile...  15.8 us
    all_to_all x1, blocking collectives, exchange_max(): lax.all_to_all(spread, axes, 0, 0, tiled=True)  14.5 us
    gather x6, local copies, waits for them, and re-layouts, shards(): tail_state = jnp.take_along_axis(everyone, picks[:, :, None, None], axis=1)  8.11 us
    unnamed x1, blocking collectives  8.04 us
    all_to_all x2, starting transfers between devices, exchange_sum(): lax.all_to_all(parts.reshape((parts.shape[0],) + shape), axes, 0, 0, tile...  7.72 us
  transfers between devices with their start and end apart: 6, of which 5 were waited for; matrix products, arithmetic and copies ran while one was open for 17% of the time, Pallas kernels for 0%

profile of v13, /device:TPU:0, one launch (start us, length us, event | category | flops | bytes accessed | tf_op | source)
XLA Modules:
  0.0 345.0 jit_solution(2244966891943489790)
XLA Ops:
  8.0 1.2 multiply_reduce_fusion.1
  10.7 4.2 %all-to-all-start = ((f32[2,96,384]{2,1,0:T(8,128)}), f32[2,96,384]{2,1,0:T(8,128)S(1)}, u32[]{:S(2)}, u32[]{:S(2)}) async-start(f32[2,96,384]{2,1,0:T(8,128)} %bitcast.2), calls=%async_computation | async-start | bytes 589824 | tf_op jit(solution)/shard_map/all_to_all | solution.py:49
  15.1 1.3 gather_fusion.4
  16.8 1.3 gather_fusion.1
  19.7 1.5 all-to-all-done
  21.4 1.3 broadcast_in_dim.123
  22.8 5.5 %all-to-all-start.1 = ((bf16[32,96,256]{2,1,0:T(8,128)(2,1)}), bf16[32,96,256]{2,1,0:T(8,128)(2,1)S(1)}, u32[]{:S(2)}, u32[]{:S(2)}) async-start(bf16[32,96,256]{2,1,0:T(8,128)(2,1)} %broadcast_in_dim.123), calls=%async_computation.1 | async-start | bytes 3145728 | tf_op jit(solution)/shard_map/all_to_all | solution.py:62
  34.9 8.0 %all-reduce.5 = f32[32]{0:T(128)S(1)} all-reduce(f32[32]{0:T(128)S(1)} %reshape.406), channel_id=3, replica_groups=mesh['seq'=8,'pair'=2,'head'=2] {'head'}, use_global_device_ids=true, to_apply=%region_6.7.clone | all-reduce | flops 32 | bytes 256
  43.8 1.3 subtract_compare_fusion.1
  45.2 6.4 %all-gather.5.cloned.1.call-done = bf16[12,8,4,2048]{3,2,1,0:T(4,128)(2,1)} async-done(((bf16[12,4,4,2048]{3,2,1,0:T(4,128)(2,1)}), bf16[12,8,4,2048]{3,2,1,0:T(4,128)(2,1)}) %all-gather.5.cloned.1.call-update) | async-done | bytes 1572880 | tf_op jit(solution)/shard_map/all_gather | solution.py:181
  51.6 3.9 %gather_fusion.7 = bf16[48,4,2048]{2,1,0:T(4,128)(2,1)} fusion(bf16[12,8,4,2048]{3,2,1,0:T(4,128)(2,1)} %all-gather.5.cloned.1.call-done, s32[48]{0:T(128)S(1)} %reshape.534), kind=kCustom, calls=%fused_computation.7.clone | custom fusion | bytes 1573248 | tf_op jit(solution)/shard_map/jit(take_along_axis)/gather | solution.py:197
  55.5 3.9 %gather_fusion.2 = bf16[48,4,2048]{2,1,0:T(4,128)(2,1)} fusion(bf16[12,8,4,2048]{3,2,1,0:T(4,128)(2,1)} %all-gather.5.cloned.1.call-done, s32[48]{0:T(128)S(1)} %reshape.511), kind=kCustom, calls=%fused_computation.2.clone | custom fusion | bytes 1573248 | tf_op jit(solution)/shard_map/jit(take_along_axis)/gather | solution.py:197
  59.4 6.4 %all-to-all-done.1 = bf16[32,96,256]{2,1,0:T(8,128)(2,1)S(1)} async-done(((bf16[32,96,256]{2,1,0:T(8,128)(2,1)}), bf16[32,96,256]{2,1,0:T(8,128)(2,1)S(1)}, u32[]{:S(2)}, u32[]{:S(2)}) %all-to-all-start.1) | async-done | bytes 1572896 | tf_op jit(solution)/shard_map/all_to_all | solution.py:62
  65.8 1.2 copy-done.1
  67.0 1.5 fusion.67
  70.5 2.4 mul.287
  72.9 1.4 reduce_sum.204
  75.6 1.6 gather_fusion
  78.0 1.6 gather_fusion.3
  80.3 1.6 gather_fusion.5
  83.3 1.2 broadcast_select_fusion
  84.5 1.3 broadcast_select_fusion.2
  85.8 1.7 fusion.21
  87.6 2.2 pad_maximum_fusion
  89.7 1.7 copy_convert_fusion
  91.4 23.7 %all-gather.3.cloned.1.call-done = bf16[1280,2048]{1,0:T(8,128)(2,1)} async-done(((bf16[1280,128]{1,0:T(8,128)(2,1)}), bf16[1280,2048]{1,0:T(8,128)(2,1)}) %all-gather.3.cloned.1.call-update) | async-done | bytes 5242896 | tf_op jit(solution)/shard_map/all_gather | solution.py:143
  115.1 4.2 %fusion.69 = f32[32,2048]{1,0:T(8,128)} fusion(bf16[32,1280]{1,0:T(8,128)(2,1)S(1)} %reshape.405, bf16[1280,2048]{1,0:T(8,128)(2,1)} %all-gather.3.cloned.1.call-done), kind=kOutput, calls=%fused_computation.174 | convolution fusion | flops 167772160 | bytes 5586944 | tf_op jit(solution)/shard_map/dot_general | solution.py:141
  119.4 2.4 reshape.407
  121.8 3.1 reshape.426
  124.9 1.4 copy.509
  126.3 2.2 fusion.22
  128.6 1.4 copy.510
  132.8 1.8 fusion.4
  134.6 1.9 fusion.66
  136.6 1.1 fusion.68
  137.8 14.5 %all_to_all.92 = f32[32,12,128]{2,1,0:T(8,128)S(1)} all-to-all(f32[32,12,128]{2,1,0:T(8,128)S(1)} %broadcast_in_dim.236), channel_id=1, replica_groups=mesh['seq'=8,'pair'=2,'head'=2] {'seq','pair','head'}, dimensions={0} | all-to-all | bytes 393216 | tf_op jit(solution)/shard_map/all_to_all | solution.py:56
  153.0 2.4 fusion.5
  155.4 2.5 reshape_reshape.4
  157.9 4.1 %copy.591 = f32[12,4,2,8,2,4,64]{6,3,0,2,5,4,1:T(8,128)} copy(f32[12,4,2,8,2,4,64]{6,5,4,3,2,1,0:T(4,128)} %reshape_reshape.4) | data formatting | bytes 3145728 | tf_op jit(solution)/shard_map/reshape;reshape | solution.py:234
  162.0 2.4 reshape.410
  164.9 1.3 select_maximum_fusion
  166.2 1.6 reshape.414
  168.7 5.0 %all_to_all.93 = f32[2,8,2,98,128]{4,1,3,2,0:T(8,128)S(1)} all-to-all(f32[2,8,2,98,128]{4,1,3,2,0:T(8,128)S(1)} %copy.542), channel_id=1, replica_groups=mesh['seq'=8,'pair'=2,'head'=2] {'pair'}, dimensions={0} | all-to-all | bytes 3211264 | tf_op jit(solution)/shard_map/all_to_all | solution.py:49
  174.8 1.6 copy.543
  176.6 26.3 %all_to_all.94 = f32[16,98,128]{2,1,0:T(8,128)S(1)} all-to-all(f32[16,98,128]{2,1,0:T(8,128)S(1)} %copy.544), channel_id=1, replica_groups=mesh['seq'=8,'pair'=2,'head'=2] {'seq','head'}, dimensions={0} | all-to-all | bytes 1605632 | tf_op jit(solution)/shard_map/all_to_all | solution.py:49
  203.2 6.5 %all_to_all.95 = bf16[2,192,64]{1,2,0:T(8,128)(2,1)S(1)} all-to-all(bf16[2,192,64]{1,2,0:T(8,128)(2,1)S(1)} %broadcast_in_dim.239), channel_id=1, replica_groups=mesh['seq'=8,'pair'=2,'head'=2] {'head'}, dimensions={0} | all-to-all | bytes 98304 | tf_op jit(solution)/shard_map/all_to_all | solution.py:62
  210.8 4.5 %all_to_all.96 = f32[2,8,12,1280]{3,1,2,0:T(8,128)S(1)} all-to-all(f32[2,8,12,1280]{3,1,2,0:T(8,128)S(1)} %copy.547), channel_id=1, replica_groups=mesh['seq'=8,'pair'=2,'head'=2] {'pair'}, dimensions={0} | all-to-all | bytes 1966080 | tf_op jit(solution)/shard_map/all_to_all | solution.py:49
  216.5 3.5 %all-to-all-start.7 = ((f32[8,120,128]{2,1,0:T(8,128)}), f32[8,120,128]{2,1,0:T(8,128)S(1)}, u32[]{:S(2)}, u32[]{:S(2)}) async-start(f32[8,120,128]{2,1,0:T(8,128)} %reshape.418), calls=%async_computation.8 | async-start | bytes 983040 | tf_op jit(solution)/shard_map/all_to_all | solution.py:49
  220.0 14.3 %all-to-all-done.7 = f32[8,120,128]{2,1,0:T(8,128)S(1)} async-done(((f32[8,120,128]{2,1,0:T(8,128)}), f32[8,120,128]{2,1,0:T(8,128)S(1)}, u32[]{:S(2)}, u32[]{:S(2)}) %all-to-all-start.7) | async-done | bytes 491552 | tf_op jit(solution)/shard_map/all_to_all | solution.py:49
  234.6 6.1 %all_to_all.97 = f32[2,1,12]{2,1,0:T(1,128)S(1)} all-to-all(f32[2,1,12]{2,1,0:T(1,128)S(1)} %broadcast_in_dim.240), channel_id=1, replica_groups=mesh['seq'=8,'pair'=2,'head'=2] {'head'}, dimensions={0} | all-to-all | bytes 192 | tf_op jit(solution)/shard_map/all_to_all | solution.py:62
  241.8 11.5 %all_to_all.98 = bf16[8,120,128]{2,1,0:T(8,128)(2,1)S(1)} all-to-all(bf16[8,120,128]{2,1,0:T(8,128)(2,1)S(1)} %broadcast_in_dim.242), channel_id=1, replica_groups=mesh['seq'=8,'pair'=2,'head'=2] {'seq'}, dimensions={0} | all-to-all | bytes 491520 | tf_op jit(solution)/shard_map/all_to_all | solution.py:62
  253.7 4.1 %all_to_all.99 = bf16[2,8,12,1280]{3,1,2,0:T(8,128)(2,1)S(1)} all-to-all(bf16[2,8,12,1280]{3,1,2,0:T(8,128)(2,1)S(1)} %broadcast_in_dim.244), channel_id=1, replica_groups=mesh['seq'=8,'pair'=2,'head'=2] {'pair'}, dimensions={0} | all-to-all | bytes 983040 | tf_op jit(solution)/shard_map/all_to_all | solution.py:62
  257.9 1.4 copy.551
  259.3 1.4 reshape.427
  260.8 2.9 fusion.44
  263.7 1.3 fusion.45
  265.4 1.3 select_maximum_fusion.1
  266.7 17.0 %all_to_all.100 = f32[2,96,1408]{2,1,0:T(8,128)S(1)} all-to-all(f32[2,96,1408]{2,1,0:T(8,128)S(1)} %bitcast.171), channel_id=1, replica_groups=mesh['seq'=8,'pair'=2,'head'=2] {'head'}, dimensions={0} | all-to-all | bytes 2162688 | tf_op jit(solution)/shard_map/all_to_all | solution.py:49
  284.1 7.5 %all_to_all.101 = bf16[2,96,640]{2,1,0:T(8,128)(2,1)S(1)} all-to-all(bf16[2,96,640]{2,1,0:T(8,128)(2,1)S(1)} %broadcast_in_dim.246), channel_id=1, replica_groups=mesh['seq'=8,'pair'=2,'head'=2] {'head'}, dimensions={0} | all-to-all | bytes 491520 | tf_op jit(solution)/shard_map/all_to_all | solution.py:62
  292.9 4.5 %all_to_all.102 = f32[2,8,12,1280]{3,1,2,0:T(8,128)S(1)} all-to-all(f32[2,8,12,1280]{3,1,2,0:T(8,128)S(1)} %copy.554), channel_id=1, replica_groups=mesh['seq'=8,'pair'=2,'head'=2] {'pair'}, dimensions={0} | all-to-all | bytes 1966080 | tf_op jit(solution)/shard_map/all_to_all | solution.py:49
  297.7 17.0 %all_to_all.103 = f32[8,120,128]{2,1,0:T(8,128)S(1)} all-to-all(f32[8,120,128]{2,1,0:T(8,128)S(1)} %reshape.421), channel_id=1, replica_groups=mesh['seq'=8,'pair'=2,'head'=2] {'seq'}, dimensions={0} | all-to-all | bytes 983040 | tf_op jit(solution)/shard_map/all_to_all | solution.py:49
  315.1 6.1 %all_to_all.104 = f32[2,1,12]{2,1,0:T(1,128)S(1)} all-to-all(f32[2,1,12]{2,1,0:T(1,128)S(1)} %broadcast_in_dim.247), channel_id=1, replica_groups=mesh['seq'=8,'pair'=2,'head'=2] {'head'}, dimensions={0} | all-to-all | bytes 192 | tf_op jit(solution)/shard_map/all_to_all | solution.py:62
  321.4 11.5 %all_to_all.105 = bf16[8,120,128]{2,1,0:T(8,128)(2,1)S(1)} all-to-all(bf16[8,120,128]{2,1,0:T(8,128)(2,1)S(1)} %broadcast_in_dim.249), channel_id=1, replica_groups=mesh['seq'=8,'pair'=2,'head'=2] {'seq'}, dimensions={0} | all-to-all | bytes 491520 | tf_op jit(solution)/shard_map/all_to_all | solution.py:62
  333.4 4.1 %all_to_all.106 = bf16[2,8,12,1280]{3,1,2,0:T(8,128)(2,1)S(1)} all-to-all(bf16[2,8,12,1280]{3,1,2,0:T(8,128)(2,1)S(1)} %broadcast_in_dim.251), channel_id=1, replica_groups=mesh['seq'=8,'pair'=2,'head'=2] {'pair'}, dimensions={0} | all-to-all | bytes 983040 | tf_op jit(solution)/shard_map/all_to_all | solution.py:62
  (238 shorter events, 33.3 us)
Async XLA Ops:
  6.5 285.1 %copy-start = (bf16[640,1280]{1,0:T(8,128)(2,1)S(1)}, bf16[640,1280]{1,0:T(8,128)(2,1)}, u32[]{:S(2)}) copy-start(bf16[640,1280]{1,0:T(8,128)(2,1)} %param.44) | copy-start | bytes 4915204
  6.5 2.8 copy-start.9
  6.5 2.8 copy-start.8
  6.5 2.8 copy-start.18
  6.5 3.1 copy-start.27
  6.5 45.1 %all-gather.5.cloned.1.call-start = ((), (), s32[]{:S(2)}) async-start(), calls=%async_computation.21 | async-start | bytes 2359296 | tf_op jit(solution)/shard_map/all_gather | solution.py:181
  7.3 107.9 %all-gather.3.cloned.1.call-start = ((), (), s32[]{:S(2)}) async-start(), calls=%async_computation.19 | async-start | bytes 5570560 | tf_op jit(solution)/shard_map/all_gather | solution.py:143
  9.2 5.7 %copy-start.13 = (s32[2,12,8]{1,2,0:T(8,128)S(1)}, s32[2,12,8]{1,2,0:T(8,128)}, u32[]{:S(2)}) copy-start(s32[2,12,8]{1,2,0:T(8,128)} %param.27) | copy-start | bytes 2308
  10.7 10.5 %all-to-all-start = ((f32[2,96,384]{2,1,0:T(8,128)}), f32[2,96,384]{2,1,0:T(8,128)S(1)}, u32[]{:S(2)}, u32[]{:S(2)}) async-start(f32[2,96,384]{2,1,0:T(8,128)} %bitcast.2), calls=%async_computation | async-start | bytes 589824 | tf_op jit(solution)/shard_map/all_to_all | solution.py:49
  18.2 1.3 copy-start.24
  22.7 9.1 %copy-start.11 = (bf16[4,8,1280]{2,1,0:T(8,128)(2,1)S(1)}, bf16[4,8,1280]{2,1,0:T(8,128)(2,1)}, u32[]{:S(2)}) copy-start(bf16[4,8,1280]{2,1,0:T(8,128)(2,1)} %param.32) | copy-start | bytes 245764
  22.7 9.9 %copy-start.21 = (s32[12]{0:T(128)S(1)}, s32[12]{0:T(128)}, u32[]{:S(2)}) copy-start(s32[12]{0:T(128)} %param.29) | copy-start | bytes 148
  22.7 10.9 %copy-start.29 = (u32[32]{0:T(128)S(1)}, u32[32]{0:T(128)}, u32[]{:S(2)}) copy-start(u32[32]{0:T(128)} %constant.271) | copy-start | bytes 388
  22.8 20.8 %copy-start.28 = (s32[4]{0:T(128)S(1)}, s32[4]{0:T(128)}, u32[]{:S(2)}) copy-start(s32[4]{0:T(128)} %param.33) | copy-start | bytes 52
  22.8 20.8 %copy-start.26 = (s32[8]{0:T(128)S(1)}, s32[8]{0:T(128)}, u32[]{:S(2)}) copy-start(s32[8]{0:T(128)} %param.31) | copy-start | bytes 100
  22.8 43.0 %all-to-all-start.1 = ((bf16[32,96,256]{2,1,0:T(8,128)(2,1)}), bf16[32,96,256]{2,1,0:T(8,128)(2,1)S(1)}, u32[]{:S(2)}, u32[]{:S(2)}) async-start(bf16[32,96,256]{2,1,0:T(8,128)(2,1)} %broadcast_in_dim.123), calls=%async_computation.1 | async-start | bytes 3145728 | tf_op jit(solution)/shard_map/all_to_all | solution.py:62
  28.3 101.7 %reduce-scatter.2.cloned.1.call-start = ((), (), s32[]{:S(2)}) async-start(), calls=%async_computation.20 | async-start | bytes 393216 | tf_op jit(solution)/shard_map/reduce_scatter | solution.py:147
  32.2 0.5 copy-start.22
  65.8 1.2 copy-start.1
  74.6 1.0 copy-start.6
  81.9 3.9 %copy-start.2 = (bf16[48,4,2048]{2,1,0:T(4,128)(2,1)S(1)}, bf16[48,4,2048]{2,1,0:T(4,128)(2,1)}, u32[]{:S(2)}) copy-start(bf16[48,4,2048]{2,1,0:T(4,128)(2,1)} %gather_fusion.7) | copy-start | bytes 2359300
  82.6 3.2 copy-start.14
  82.6 3.2 copy-start.15
  82.6 3.2 copy-start.16
  82.6 3.2 copy-start.17
  83.3 2.5 copy-start.3
  121.8 4.6 %copy-start.23 = (f32[256]{0:T(256)S(1)}, f32[256]{0:T(256)}, u32[]{:S(2)}) copy-start(f32[256]{0:T(256)} %param.37) | copy-start | bytes 3076
  126.3 3.7 %copy-start.25 = (f32[16]{0:T(128)S(1)}, f32[16]{0:T(128)}, u32[]{:S(2)}) copy-start(f32[16]{0:T(128)} %fusion.63) | copy-start | bytes 196
  134.6 1.9 copy-start.7
  137.6 15.3 %copy-start.4 = (f32[12,4,32,96]{3,2,1,0:T(8,128)}, f32[12,4,32,96]{3,2,1,0:T(8,128)S(1)}, u32[]{:S(2)}) copy-start(f32[12,4,32,96]{3,2,1,0:T(8,128)S(1)} %get-tuple-element.32) | copy-start | bytes 1769476
  176.6 33.4 %copy-start.10 = (bf16[128,1280]{1,0:T(8,128)(2,1)S(1)}, bf16[128,1280]{1,0:T(8,128)(2,1)}, u32[]{:S(2)}) copy-start(bf16[128,1280]{1,0:T(8,128)(2,1)} %param.39) | copy-start | bytes 983044
  215.6 25.1 %copy-start.19 = (f32[1280]{0:T(1024)S(1)}, f32[1280]{0:T(1024)}, u32[]{:S(2)}) copy-start(f32[1280]{0:T(1024)} %param.40) | copy-start | bytes 15364
  216.5 17.8 %all-to-all-start.7 = ((f32[8,120,128]{2,1,0:T(8,128)}), f32[8,120,128]{2,1,0:T(8,128)S(1)}, u32[]{:S(2)}, u32[]{:S(2)}) async-start(f32[8,120,128]{2,1,0:T(8,128)} %reshape.418), calls=%async_computation.8 | async-start | bytes 983040 | tf_op jit(solution)/shard_map/all_to_all | solution.py:49
  259.3 1.4 copy-start.12
  260.8 2.9 copy-start.5
  297.6 23.5 %copy-start.20 = (f32[1280]{0:T(1024)S(1)}, f32[1280]{0:T(1024)}, u32[]{:S(2)}) copy-start(f32[1280]{0:T(1024)} %param.45) | copy-start | bytes 15364
Sparse Core Ops, SparseCore 0:
  8.9 42.6 all-gather.4
  53.8 61.3 all-gather.2
  119.5 9.8 reduce-scatter.1

commit v14 on v9

--- a/solution.py
+++ b/solution.py
@@ -221,7 +221,7 @@
     scores = jnp.einsum("gkmd,gtkd->gkmt", grouped, all_keys, preferred_element_type=f32)
     scores = jnp.where(mask, scores, NEG)
     top = jnp.max(scores, -1).reshape(groups, KVH, steps, beams, repeat)
-    top = exchange_max(top, ALL, n_dev)
+    top = exchange_max(exchange_max(top, "pair", lax.axis_size("pair")), ("seq", "head"), n_dev // 2)
     weights = jnp.where(mask, jnp.exp(scores - top.reshape(groups, KVH, many)[..., None]), 0.0)
     total = jnp.sum(weights, -1).reshape(groups, KVH, steps, beams, repeat)
     weighted = jnp.einsum(

time: 344 us -> 346 us (level)
    all_to_all x1 -> x2, blocking collectives: 14.5 us -> 16.4 us  [exchange_max(): lax.all_to_all(spread, axes, 0, 0, tiled=True)]
where the time goes in v14:
time: 346 us; the launch traced here: 344 us
  blocking collectives  153 us (44%)
  local copies, waits for them, and re-layouts  67 us (19%)
  waiting for transfers between devices  53.8 us (16%)
  other arithmetic  28.2 us (8%)
  between operations  14.8 us (4%)
  matrix products  13.5 us (4%)
  starting transfers between devices  13.4 us (4%)
    all_to_all x6, blocking collectives, exchange_sum(): lax.all_to_all(parts.reshape((parts.shape[0],) + shape), axes, 0, 0, tile...  73.9 us
    all_to_all x6, blocking collectives, exchange_gather(): lax.all_to_all(spread, axes, 0, 0, tiled=True)  45.3 us
    all_gather x1, waiting for transfers between devices, shards(): lax.all_gather(w_keyval, SEQ, axis=1, tiled=True)  23.7 us
    all_to_all x2, blocking collectives, exchange_max(): lax.all_to_all(spread, axes, 0, 0, tiled=True)  16.4 us
    all_to_all x2, waiting for transfers between devices, exchange_sum(): lax.all_to_all(parts.reshape((parts.shape[0],) + shape), axes, 0, 0, tile...  15.8 us
    gather x6, local copies, waits for them, and re-layouts, shards(): tail_state = jnp.take_along_axis(everyone, picks[:, :, None, None], axis=1)  8.11 us
    unnamed x1, blocking collectives  8.04 us
    all_to_all x2, starting transfers between devices, exchange_sum(): lax.all_to_all(parts.reshape((parts.shape[0],) + shape), axes, 0, 0, tile...  7.72 us
  transfers between devices with their start and end apart: 6, of which 5 were waited for; matrix products, arithmetic and copies ran while one was open for 17% of the time, Pallas kernels for 0%

profile of v14, /device:TPU:0, one launch (start us, length us, event | category | flops | bytes accessed | tf_op | source)
XLA Modules:
  0.0 344.1 jit_solution(11240577725802673707)
XLA Ops:
  8.0 1.2 multiply_reduce_fusion.1
  10.7 4.2 %all-to-all-start = ((f32[2,96,384]{2,1,0:T(8,128)}), f32[2,96,384]{2,1,0:T(8,128)S(1)}, u32[]{:S(2)}, u32[]{:S(2)}) async-start(f32[2,96,384]{2,1,0:T(8,128)} %bitcast.2), calls=%async_computation | async-start | bytes 589824 | tf_op jit(solution)/shard_map/all_to_all | solution.py:49
  15.1 1.3 gather_fusion.4
  16.8 1.3 gather_fusion.1
  19.7 1.5 all-to-all-done
  21.4 1.3 broadcast_in_dim.121
  22.8 5.5 %all-to-all-start.1 = ((bf16[32,96,256]{2,1,0:T(8,128)(2,1)}), bf16[32,96,256]{2,1,0:T(8,128)(2,1)S(1)}, u32[]{:S(2)}, u32[]{:S(2)}) async-start(bf16[32,96,256]{2,1,0:T(8,128)(2,1)} %broadcast_in_dim.121), calls=%async_computation.1 | async-start | bytes 3145728 | tf_op jit(solution)/shard_map/all_to_all | solution.py:62
  34.9 8.0 %all-reduce.5 = f32[32]{0:T(128)S(1)} all-reduce(f32[32]{0:T(128)S(1)} %reshape.387), channel_id=3, replica_groups=mesh['seq'=8,'pair'=2,'head'=2] {'head'}, use_global_device_ids=true, to_apply=%region_6.7.clone | all-reduce | flops 32 | bytes 256
  43.8 1.3 subtract_compare_fusion.1
  45.2 6.4 %all-gather.5.cloned.1.call-done = bf16[12,8,4,2048]{3,2,1,0:T(4,128)(2,1)} async-done(((bf16[12,4,4,2048]{3,2,1,0:T(4,128)(2,1)}), bf16[12,8,4,2048]{3,2,1,0:T(4,128)(2,1)}) %all-gather.5.cloned.1.call-update) | async-done | bytes 1572880 | tf_op jit(solution)/shard_map/all_gather | solution.py:181
  51.6 3.9 %gather_fusion.7 = bf16[48,4,2048]{2,1,0:T(4,128)(2,1)} fusion(bf16[12,8,4,2048]{3,2,1,0:T(4,128)(2,1)} %all-gather.5.cloned.1.call-done, s32[48]{0:T(128)S(1)} %reshape.515), kind=kCustom, calls=%fused_computation.7.clone | custom fusion | bytes 1573248 | tf_op jit(solution)/shard_map/jit(take_along_axis)/gather | solution.py:197
  55.5 3.9 %gather_fusion.2 = bf16[48,4,2048]{2,1,0:T(4,128)(2,1)} fusion(bf16[12,8,4,2048]{3,2,1,0:T(4,128)(2,1)} %all-gather.5.cloned.1.call-done, s32[48]{0:T(128)S(1)} %reshape.492), kind=kCustom, calls=%fused_computation.2.clone | custom fusion | bytes 1573248 | tf_op jit(solution)/shard_map/jit(take_along_axis)/gather | solution.py:197
  59.4 6.4 %all-to-all-done.1 = bf16[32,96,256]{2,1,0:T(8,128)(2,1)S(1)} async-done(((bf16[32,96,256]{2,1,0:T(8,128)(2,1)}), bf16[32,96,256]{2,1,0:T(8,128)(2,1)S(1)}, u32[]{:S(2)}, u32[]{:S(2)}) %all-to-all-start.1) | async-done | bytes 1572896 | tf_op jit(solution)/shard_map/all_to_all | solution.py:62
  65.8 1.2 copy-done.1
  67.0 1.5 fusion.67
  70.5 2.4 mul.287
  72.9 1.4 reduce_sum.186
  75.6 1.6 gather_fusion
  78.0 1.6 gather_fusion.3
  80.3 1.6 gather_fusion.5
  83.3 1.2 broadcast_select_fusion
  84.5 1.3 broadcast_select_fusion.2
  85.8 1.7 fusion.21
  87.6 2.2 pad_maximum_fusion
  89.7 1.7 copy_convert_fusion
  91.4 23.7 %all-gather.3.cloned.1.call-done = bf16[1280,2048]{1,0:T(8,128)(2,1)} async-done(((bf16[1280,128]{1,0:T(8,128)(2,1)}), bf16[1280,2048]{1,0:T(8,128)(2,1)}) %all-gather.3.cloned.1.call-update) | async-done | bytes 5242896 | tf_op jit(solution)/shard_map/all_gather | solution.py:143
  115.1 4.2 %fusion.69 = f32[32,2048]{1,0:T(8,128)} fusion(bf16[32,1280]{1,0:T(8,128)(2,1)S(1)} %reshape.386, bf16[1280,2048]{1,0:T(8,128)(2,1)} %all-gather.3.cloned.1.call-done), kind=kOutput, calls=%fused_computation.174 | convolution fusion | flops 167772160 | bytes 5586944 | tf_op jit(solution)/shard_map/dot_general | solution.py:141
  119.4 2.4 reshape.388
  121.8 3.1 reshape.407
  124.9 1.4 copy.507
  126.3 2.2 fusion.22
  128.6 1.4 copy.508
  132.8 1.8 fusion.4
  134.6 1.9 fusion.66
  137.7 3.7 %all_to_all.85 = f32[2,12,128]{2,1,0:T(8,128)S(1)} all-to-all(f32[2,12,128]{2,1,0:T(8,128)S(1)} %broadcast_in_dim.229), channel_id=1, replica_groups=mesh['seq'=8,'pair'=2,'head'=2] {'pair'}, dimensions={0} | all-to-all | bytes 24576 | tf_op jit(solution)/shard_map/all_to_all | solution.py:56
  141.5 12.6 %all_to_all.86 = f32[16,12,128]{2,1,0:T(8,128)S(1)} all-to-all(f32[16,12,128]{2,1,0:T(8,128)S(1)} %broadcast_in_dim.230), channel_id=1, replica_groups=mesh['seq'=8,'pair'=2,'head'=2] {'seq','head'}, dimensions={0} | all-to-all | bytes 196608 | tf_op jit(solution)/shard_map/all_to_all | solution.py:56
  154.8 2.4 fusion.5
  157.2 2.5 reshape_reshape.4
  159.7 4.1 %copy.589 = f32[12,4,2,8,2,4,64]{6,3,0,2,5,4,1:T(8,128)} copy(f32[12,4,2,8,2,4,64]{6,5,4,3,2,1,0:T(4,128)} %reshape_reshape.4) | data formatting | bytes 3145728 | tf_op jit(solution)/shard_map/reshape;reshape | solution.py:234
  163.9 2.4 reshape.391
  166.7 1.3 select_maximum_fusion
  168.0 1.6 reshape.395
  170.5 5.0 %all_to_all.87 = f32[2,8,2,98,128]{4,1,3,2,0:T(8,128)S(1)} all-to-all(f32[2,8,2,98,128]{4,1,3,2,0:T(8,128)S(1)} %copy.541), channel_id=1, replica_groups=mesh['seq'=8,'pair'=2,'head'=2] {'pair'}, dimensions={0} | all-to-all | bytes 3211264 | tf_op jit(solution)/shard_map/all_to_all | solution.py:49
  176.6 1.6 copy.542
  178.4 25.9 %all_to_all.88 = f32[16,98,128]{2,1,0:T(8,128)S(1)} all-to-all(f32[16,98,128]{2,1,0:T(8,128)S(1)} %copy.543), channel_id=1, replica_groups=mesh['seq'=8,'pair'=2,'head'=2] {'seq','head'}, dimensions={0} | all-to-all | bytes 1605632 | tf_op jit(solution)/shard_map/all_to_all | solution.py:49
  204.7 6.5 %all_to_all.89 = bf16[2,192,64]{1,2,0:T(8,128)(2,1)S(1)} all-to-all(bf16[2,192,64]{1,2,0:T(8,128)(2,1)S(1)} %broadcast_in_dim.233), channel_id=1, replica_groups=mesh['seq'=8,'pair'=2,'head'=2] {'head'}, dimensions={0} | all-to-all | bytes 98304 | tf_op jit(solution)/shard_map/all_to_all | solution.py:62
  212.3 4.5 %all_to_all.90 = f32[2,8,12,1280]{3,1,2,0:T(8,128)S(1)} all-to-all(f32[2,8,12,1280]{3,1,2,0:T(8,128)S(1)} %copy.546), channel_id=1, replica_groups=mesh['seq'=8,'pair'=2,'head'=2] {'pair'}, dimensions={0} | all-to-all | bytes 1966080 | tf_op jit(solution)/shard_map/all_to_all | solution.py:49
  218.0 3.5 %all-to-all-start.8 = ((f32[8,120,128]{2,1,0:T(8,128)}), f32[8,120,128]{2,1,0:T(8,128)S(1)}, u32[]{:S(2)}, u32[]{:S(2)}) async-start(f32[8,120,128]{2,1,0:T(8,128)} %reshape.399), calls=%async_computation.9 | async-start | bytes 983040 | tf_op jit(solution)/shard_map/all_to_all | solution.py:49
  221.4 14.3 %all-to-all-done.8 = f32[8,120,128]{2,1,0:T(8,128)S(1)} async-done(((f32[8,120,128]{2,1,0:T(8,128)}), f32[8,120,128]{2,1,0:T(8,128)S(1)}, u32[]{:S(2)}, u32[]{:S(2)}) %all-to-all-start.8) | async-done | bytes 491552 | tf_op jit(solution)/shard_map/all_to_all | solution.py:49
  236.1 4.9 %psum.14 = f32[12]{0:T(128)S(1)} all-reduce(f32[12]{0:T(128)S(1)} %reduce_sum.194), channel_id=1, replica_groups=mesh['seq'=8,'pair'=2,'head'=2] {'head'}, use_global_device_ids=true, to_apply=%region_19.23 | all-reduce | flops 12 | bytes 96 | tf_op jit(solution)/shard_map/psum | solution.py:251
  242.1 11.5 %all_to_all.91 = bf16[8,120,128]{2,1,0:T(8,128)(2,1)S(1)} all-to-all(bf16[8,120,128]{2,1,0:T(8,128)(2,1)S(1)} %broadcast_in_dim.235), channel_id=1, replica_groups=mesh['seq'=8,'pair'=2,'head'=2] {'seq'}, dimensions={0} | all-to-all | bytes 491520 | tf_op jit(solution)/shard_map/all_to_all | solution.py:62
  254.1 4.1 %all_to_all.92 = bf16[2,8,12,1280]{3,1,2,0:T(8,128)(2,1)S(1)} all-to-all(bf16[2,8,12,1280]{3,1,2,0:T(8,128)(2,1)S(1)} %broadcast_in_dim.237), channel_id=1, replica_groups=mesh['seq'=8,'pair'=2,'head'=2] {'pair'}, dimensions={0} | all-to-all | bytes 983040 | tf_op jit(solution)/shard_map/all_to_all | solution.py:62
  258.2 1.4 copy.549
  259.6 1.4 reshape.408
  261.1 2.9 fusion.44
  264.0 1.3 fusion.45
  265.7 1.3 select_maximum_fusion.1
  267.0 17.0 %all_to_all.93 = f32[2,96,1408]{2,1,0:T(8,128)S(1)} all-to-all(f32[2,96,1408]{2,1,0:T(8,128)S(1)} %bitcast.169), channel_id=1, replica_groups=mesh['seq'=8,'pair'=2,'head'=2] {'head'}, dimensions={0} | all-to-all | bytes 2162688 | tf_op jit(solution)/shard_map/all_to_all | solution.py:49
  284.4 7.5 %all_to_all.94 = bf16[2,96,640]{2,1,0:T(8,128)(2,1)S(1)} all-to-all(bf16[2,96,640]{2,1,0:T(8,128)(2,1)S(1)} %broadcast_in_dim.239), channel_id=1, replica_groups=mesh['seq'=8,'pair'=2,'head'=2] {'head'}, dimensions={0} | all-to-all | bytes 491520 | tf_op jit(solution)/shard_map/all_to_all | solution.py:62
  293.2 4.5 %all_to_all.95 = f32[2,8,12,1280]{3,1,2,0:T(8,128)S(1)} all-to-all(f32[2,8,12,1280]{3,1,2,0:T(8,128)S(1)} %copy.552), channel_id=1, replica_groups=mesh['seq'=8,'pair'=2,'head'=2] {'pair'}, dimensions={0} | all-to-all | bytes 1966080 | tf_op jit(solution)/shard_map/all_to_all | solution.py:49
  298.0 17.0 %all_to_all.96 = f32[8,120,128]{2,1,0:T(8,128)S(1)} all-to-all(f32[8,120,128]{2,1,0:T(8,128)S(1)} %reshape.402), channel_id=1, replica_groups=mesh['seq'=8,'pair'=2,'head'=2] {'seq'}, dimensions={0} | all-to-all | bytes 983040 | tf_op jit(solution)/shard_map/all_to_all | solution.py:49
  315.4 4.9 %psum.15 = f32[12]{0:T(128)S(1)} all-reduce(f32[12]{0:T(128)S(1)} %reduce_sum.202), channel_id=1, replica_groups=mesh['seq'=8,'pair'=2,'head'=2] {'head'}, use_global_device_ids=true, to_apply=%region_26.30 | all-reduce | flops 12 | bytes 96 | tf_op jit(solution)/shard_map/psum | solution.py:274
  320.5 11.5 %all_to_all.97 = bf16[8,120,128]{2,1,0:T(8,128)(2,1)S(1)} all-to-all(bf16[8,120,128]{2,1,0:T(8,128)(2,1)S(1)} %broadcast_in_dim.241), channel_id=1, replica_groups=mesh['seq'=8,'pair'=2,'head'=2] {'seq'}, dimensions={0} | all-to-all | bytes 491520 | tf_op jit(solution)/shard_map/all_to_all | solution.py:62
  332.5 4.1 %all_to_all.98 = bf16[2,8,12,1280]{3,1,2,0:T(8,128)(2,1)S(1)} all-to-all(bf16[2,8,12,1280]{3,1,2,0:T(8,128)(2,1)S(1)} %broadcast_in_dim.243), channel_id=1, replica_groups=mesh['seq'=8,'pair'=2,'head'=2] {'pair'}, dimensions={0} | all-to-all | bytes 983040 | tf_op jit(solution)/shard_map/all_to_all | solution.py:62
  (237 shorter events, 34.3 us)
Async XLA Ops:
  6.5 285.4 %copy-start = (bf16[640,1280]{1,0:T(8,128)(2,1)S(1)}, bf16[640,1280]{1,0:T(8,128)(2,1)}, u32[]{:S(2)}) copy-start(bf16[640,1280]{1,0:T(8,128)(2,1)} %param.44) | copy-start | bytes 4915204
  6.5 2.8 copy-start.9
  6.5 2.8 copy-start.8
  6.5 2.8 copy-start.18
  6.5 3.1 copy-start.27
  6.5 45.1 %all-gather.5.cloned.1.call-start = ((), (), s32[]{:S(2)}) async-start(), calls=%async_computation.20 | async-start | bytes 2359296 | tf_op jit(solution)/shard_map/all_gather | solution.py:181
  7.3 107.9 %all-gather.3.cloned.1.call-start = ((), (), s32[]{:S(2)}) async-start(), calls=%async_computation.18 | async-start | bytes 5570560 | tf_op jit(solution)/shard_map/all_gather | solution.py:143
  9.2 5.7 %copy-start.13 = (s32[2,12,8]{1,2,0:T(8,128)S(1)}, s32[2,12,8]{1,2,0:T(8,128)}, u32[]{:S(2)}) copy-start(s32[2,12,8]{1,2,0:T(8,128)} %param.27) | copy-start | bytes 2308
  10.7 10.5 %all-to-all-start = ((f32[2,96,384]{2,1,0:T(8,128)}), f32[2,96,384]{2,1,0:T(8,128)S(1)}, u32[]{:S(2)}, u32[]{:S(2)}) async-start(f32[2,96,384]{2,1,0:T(8,128)} %bitcast.2), calls=%async_computation | async-start | bytes 589824 | tf_op jit(solution)/shard_map/all_to_all | solution.py:49
  18.2 1.3 copy-start.24
  22.7 9.1 %copy-start.11 = (bf16[4,8,1280]{2,1,0:T(8,128)(2,1)S(1)}, bf16[4,8,1280]{2,1,0:T(8,128)(2,1)}, u32[]{:S(2)}) copy-start(bf16[4,8,1280]{2,1,0:T(8,128)(2,1)} %param.32) | copy-start | bytes 245764
  22.7 9.9 %copy-start.21 = (s32[12]{0:T(128)S(1)}, s32[12]{0:T(128)}, u32[]{:S(2)}) copy-start(s32[12]{0:T(128)} %param.29) | copy-start | bytes 148
  22.7 10.9 %copy-start.29 = (u32[32]{0:T(128)S(1)}, u32[32]{0:T(128)}, u32[]{:S(2)}) copy-start(u32[32]{0:T(128)} %constant.271) | copy-start | bytes 388
  22.8 20.8 %copy-start.28 = (s32[4]{0:T(128)S(1)}, s32[4]{0:T(128)}, u32[]{:S(2)}) copy-start(s32[4]{0:T(128)} %param.33) | copy-start | bytes 52
  22.8 20.8 %copy-start.26 = (s32[8]{0:T(128)S(1)}, s32[8]{0:T(128)}, u32[]{:S(2)}) copy-start(s32[8]{0:T(128)} %param.31) | copy-start | bytes 100
  22.8 43.0 %all-to-all-start.1 = ((bf16[32,96,256]{2,1,0:T(8,128)(2,1)}), bf16[32,96,256]{2,1,0:T(8,128)(2,1)S(1)}, u32[]{:S(2)}, u32[]{:S(2)}) async-start(bf16[32,96,256]{2,1,0:T(8,128)(2,1)} %broadcast_in_dim.121), calls=%async_computation.1 | async-start | bytes 3145728 | tf_op jit(solution)/shard_map/all_to_all | solution.py:62
  28.3 101.7 %reduce-scatter.2.cloned.1.call-start = ((), (), s32[]{:S(2)}) async-start(), calls=%async_computation.19 | async-start | bytes 393216 | tf_op jit(solution)/shard_map/reduce_scatter | solution.py:147
  32.2 0.5 copy-start.22
  65.8 1.2 copy-start.1
  74.6 1.0 copy-start.6
  81.9 3.9 %copy-start.2 = (bf16[48,4,2048]{2,1,0:T(4,128)(2,1)S(1)}, bf16[48,4,2048]{2,1,0:T(4,128)(2,1)}, u32[]{:S(2)}) copy-start(bf16[48,4,2048]{2,1,0:T(4,128)(2,1)} %gather_fusion.7) | copy-start | bytes 2359300
  82.6 3.2 copy-start.14
  82.6 3.2 copy-start.15
  82.6 3.2 copy-start.16
  82.6 3.2 copy-start.17
  83.3 2.5 copy-start.3
  121.8 4.6 %copy-start.23 = (f32[256]{0:T(256)S(1)}, f32[256]{0:T(256)}, u32[]{:S(2)}) copy-start(f32[256]{0:T(256)} %param.37) | copy-start | bytes 3076
  126.3 3.7 %copy-start.25 = (f32[16]{0:T(128)S(1)}, f32[16]{0:T(128)}, u32[]{:S(2)}) copy-start(f32[16]{0:T(128)} %fusion.63) | copy-start | bytes 196
  134.6 1.9 copy-start.7
  137.6 17.1 %copy-start.4 = (f32[12,4,32,96]{3,2,1,0:T(8,128)}, f32[12,4,32,96]{3,2,1,0:T(8,128)S(1)}, u32[]{:S(2)}) copy-start(f32[12,4,32,96]{3,2,1,0:T(8,128)S(1)} %get-tuple-element.32) | copy-start | bytes 1769476
  178.4 33.0 %copy-start.10 = (bf16[128,1280]{1,0:T(8,128)(2,1)S(1)}, bf16[128,1280]{1,0:T(8,128)(2,1)}, u32[]{:S(2)}) copy-start(bf16[128,1280]{1,0:T(8,128)(2,1)} %param.39) | copy-start | bytes 983044
  217.1 24.0 %copy-start.19 = (f32[1280]{0:T(1024)S(1)}, f32[1280]{0:T(1024)}, u32[]{:S(2)}) copy-start(f32[1280]{0:T(1024)} %param.40) | copy-start | bytes 15364
  218.0 17.8 %all-to-all-start.8 = ((f32[8,120,128]{2,1,0:T(8,128)}), f32[8,120,128]{2,1,0:T(8,128)S(1)}, u32[]{:S(2)}, u32[]{:S(2)}) async-start(f32[8,120,128]{2,1,0:T(8,128)} %reshape.399), calls=%async_computation.9 | async-start | bytes 983040 | tf_op jit(solution)/shard_map/all_to_all | solution.py:49
  259.6 1.4 copy-start.12
  261.1 2.9 copy-start.5
  298.0 22.4 %copy-start.20 = (f32[1280]{0:T(1024)S(1)}, f32[1280]{0:T(1024)}, u32[]{:S(2)}) copy-start(f32[1280]{0:T(1024)} %param.45) | copy-start | bytes 15364
Sparse Core Ops, SparseCore 0:
  8.9 42.6 all-gather.4
  53.8 61.3 all-gather.2
  119.5 9.8 reduce-scatter.1

commit v15 on v9

--- a/solution.py
+++ b/solution.py
@@ -72,7 +72,7 @@
 def seq_gather(piece):
     pair = lax.axis_size("pair")
     outer = lax.axis_size("seq")
-    got = exchange_gather(exchange_gather(piece, "seq", outer, True), "pair", pair)
+    got = exchange_gather(exchange_gather(piece, "seq", outer, True), "pair", pair, True)
     return jnp.swapaxes(got, 0, 1).reshape((outer * pair,) + piece.shape)
 
 

time: 344 us -> 347 us (level)
  no operation moved by 1% of the time
where the time goes in v15:
time: 347 us; the launch traced here: 345 us
  blocking collectives  152 us (44%)
  local copies, waits for them, and re-layouts  68.4 us (20%)
  waiting for transfers between devices  53.8 us (16%)
  other arithmetic  29 us (8%)
  between operations  14.8 us (4%)
  matrix products  13.6 us (4%)
  starting transfers between devices  13.4 us (4%)
    all_to_all x6, blocking collectives, exchange_sum(): lax.all_to_all(parts.reshape((parts.shape[0],) + shape), axes, 0, 0, tile...  74.2 us
    all_to_all x6, blocking collectives, exchange_gather(): lax.all_to_all(spread, axes, 0, 0, tiled=True)  45.3 us
    all_gather x1, waiting for transfers between devices, shards(): lax.all_gather(w_keyval, SEQ, axis=1, tiled=True)  23.7 us
    all_to_all x2, waiting for transfers between devices, exchange_sum(): lax.all_to_all(parts.reshape((parts.shape[0],) + shape), axes, 0, 0, tile...  15.8 us
    all_to_all x1, blocking collectives, exchange_max(): lax.all_to_all(spread, axes, 0, 0, tiled=True)  14.5 us
    gather x6, local copies, waits for them, and re-layouts, shards(): tail_state = jnp.take_along_axis(everyone, picks[:, :, None, None], axis=1)  8.11 us
    unnamed x1, blocking collectives  8.04 us
    all_to_all x2, starting transfers between devices, exchange_sum(): lax.all_to_all(parts.reshape((parts.shape[0],) + shape), axes, 0, 0, tile...  7.72 us
  transfers between devices with their start and end apart: 6, of which 5 were waited for; matrix products, arithmetic and copies ran while one was open for 17% of the time, Pallas kernels for 0%

profile of v15, /device:TPU:0, one launch (start us, length us, event | category | flops | bytes accessed | tf_op | source)
XLA Modules:
  0.0 344.9 jit_solution(13360493407063177318)
XLA Ops:
  8.0 1.2 multiply_reduce_fusion.1
  10.7 4.2 %all-to-all-start = ((f32[2,96,384]{2,1,0:T(8,128)}), f32[2,96,384]{2,1,0:T(8,128)S(1)}, u32[]{:S(2)}, u32[]{:S(2)}) async-start(f32[2,96,384]{2,1,0:T(8,128)} %bitcast.2), calls=%async_computation | async-start | bytes 589824 | tf_op jit(solution)/shard_map/all_to_all | solution.py:49
  15.1 1.3 gather_fusion.4
  16.8 1.3 gather_fusion.1
  19.7 1.5 all-to-all-done
  21.4 1.3 broadcast_in_dim.119
  22.8 5.5 %all-to-all-start.1 = ((bf16[32,96,256]{2,1,0:T(8,128)(2,1)}), bf16[32,96,256]{2,1,0:T(8,128)(2,1)S(1)}, u32[]{:S(2)}, u32[]{:S(2)}) async-start(bf16[32,96,256]{2,1,0:T(8,128)(2,1)} %broadcast_in_dim.119), calls=%async_computation.1 | async-start | bytes 3145728 | tf_op jit(solution)/shard_map/all_to_all | solution.py:62
  34.9 8.0 %all-reduce.5 = f32[32]{0:T(128)S(1)} all-reduce(f32[32]{0:T(128)S(1)} %reshape.394), channel_id=3, replica_groups=mesh['seq'=8,'pair'=2,'head'=2] {'head'}, use_global_device_ids=true, to_apply=%region_6.7.clone | all-reduce | flops 32 | bytes 256
  43.8 1.3 subtract_compare_fusion.1
  45.2 6.4 %all-gather.5.cloned.1.call-done = bf16[12,8,4,2048]{3,2,1,0:T(4,128)(2,1)} async-done(((bf16[12,4,4,2048]{3,2,1,0:T(4,128)(2,1)}), bf16[12,8,4,2048]{3,2,1,0:T(4,128)(2,1)}) %all-gather.5.cloned.1.call-update) | async-done | bytes 1572880 | tf_op jit(solution)/shard_map/all_gather | solution.py:181
  51.6 3.9 %gather_fusion.7 = bf16[48,4,2048]{2,1,0:T(4,128)(2,1)} fusion(bf16[12,8,4,2048]{3,2,1,0:T(4,128)(2,1)} %all-gather.5.cloned.1.call-done, s32[48]{0:T(128)S(1)} %reshape.524), kind=kCustom, calls=%fused_computation.7.clone | custom fusion | bytes 1573248 | tf_op jit(solution)/shard_map/jit(take_along_axis)/gather | solution.py:197
  55.5 3.9 %gather_fusion.2 = bf16[48,4,2048]{2,1,0:T(4,128)(2,1)} fusion(bf16[12,8,4,2048]{3,2,1,0:T(4,128)(2,1)} %all-gather.5.cloned.1.call-done, s32[48]{0:T(128)S(1)} %reshape.501), kind=kCustom, calls=%fused_computation.2.clone | custom fusion | bytes 1573248 | tf_op jit(solution)/shard_map/jit(take_along_axis)/gather | solution.py:197
  59.4 6.4 %all-to-all-done.1 = bf16[32,96,256]{2,1,0:T(8,128)(2,1)S(1)} async-done(((bf16[32,96,256]{2,1,0:T(8,128)(2,1)}), bf16[32,96,256]{2,1,0:T(8,128)(2,1)S(1)}, u32[]{:S(2)}, u32[]{:S(2)}) %all-to-all-start.1) | async-done | bytes 1572896 | tf_op jit(solution)/shard_map/all_to_all | solution.py:62
  65.8 1.2 copy-done.1
  67.0 1.5 fusion.66
  70.5 2.4 mul.290
  72.9 1.4 reduce_sum.186
  75.6 1.6 gather_fusion
  78.0 1.6 gather_fusion.3
  80.3 1.6 gather_fusion.5
  83.3 1.2 broadcast_select_fusion
  84.5 1.3 broadcast_select_fusion.2
  85.8 1.7 fusion.20
  87.6 2.2 pad_maximum_fusion
  89.7 1.7 copy_convert_fusion
  91.4 23.7 %all-gather.3.cloned.1.call-done = bf16[1280,2048]{1,0:T(8,128)(2,1)} async-done(((bf16[1280,128]{1,0:T(8,128)(2,1)}), bf16[1280,2048]{1,0:T(8,128)(2,1)}) %all-gather.3.cloned.1.call-update) | async-done | bytes 5242896 | tf_op jit(solution)/shard_map/all_gather | solution.py:143
  115.1 4.2 %fusion.68 = f32[32,2048]{1,0:T(8,128)} fusion(bf16[32,1280]{1,0:T(8,128)(2,1)S(1)} %reshape.393, bf16[1280,2048]{1,0:T(8,128)(2,1)} %all-gather.3.cloned.1.call-done), kind=kOutput, calls=%fused_computation.172 | convolution fusion | flops 167772160 | bytes 5586944 | tf_op jit(solution)/shard_map/dot_general | solution.py:141
  119.4 2.4 reshape.395
  121.8 3.1 reshape.415
  124.9 1.4 copy.495
  126.3 2.2 fusion.21
  128.6 1.4 copy.496
  132.8 1.8 fusion.4
  134.6 1.9 fusion.65
  137.8 14.5 %all_to_all.80 = f32[32,12,128]{2,1,0:T(8,128)S(1)} all-to-all(f32[32,12,128]{2,1,0:T(8,128)S(1)} %broadcast_in_dim.224), channel_id=1, replica_groups=mesh['seq'=8,'pair'=2,'head'=2] {'seq','pair','head'}, dimensions={0} | all-to-all | bytes 393216 | tf_op jit(solution)/shard_map/all_to_all | solution.py:56
  153.0 2.4 fusion.5
  155.4 2.5 reshape_reshape.4
  157.9 4.1 %copy.573 = f32[12,4,2,8,2,4,64]{6,3,0,2,5,4,1:T(8,128)} copy(f32[12,4,2,8,2,4,64]{6,5,4,3,2,1,0:T(4,128)} %reshape_reshape.4) | data formatting | bytes 3145728 | tf_op jit(solution)/shard_map/reshape;reshape | solution.py:234
  162.0 2.4 reshape.398
  164.9 1.3 select_maximum_fusion
  166.2 1.6 reshape.402
  168.7 5.0 %all_to_all.81 = f32[2,8,2,98,128]{4,1,3,2,0:T(8,128)S(1)} all-to-all(f32[2,8,2,98,128]{4,1,3,2,0:T(8,128)S(1)} %copy.528), channel_id=1, replica_groups=mesh['seq'=8,'pair'=2,'head'=2] {'pair'}, dimensions={0} | all-to-all | bytes 3211264 | tf_op jit(solution)/shard_map/all_to_all | solution.py:49
  174.8 1.6 copy.529
  176.6 26.3 %all_to_all.82 = f32[16,98,128]{2,1,0:T(8,128)S(1)} all-to-all(f32[16,98,128]{2,1,0:T(8,128)S(1)} %copy.530), channel_id=1, replica_groups=mesh['seq'=8,'pair'=2,'head'=2] {'seq','head'}, dimensions={0} | all-to-all | bytes 1605632 | tf_op jit(solution)/shard_map/all_to_all | solution.py:49
  203.2 6.5 %all_to_all.83 = bf16[2,192,64]{1,2,0:T(8,128)(2,1)S(1)} all-to-all(bf16[2,192,64]{1,2,0:T(8,128)(2,1)S(1)} %broadcast_in_dim.227), channel_id=1, replica_groups=mesh['seq'=8,'pair'=2,'head'=2] {'head'}, dimensions={0} | all-to-all | bytes 98304 | tf_op jit(solution)/shard_map/all_to_all | solution.py:62
  210.8 4.5 %all_to_all.84 = f32[2,8,12,1280]{3,1,2,0:T(8,128)S(1)} all-to-all(f32[2,8,12,1280]{3,1,2,0:T(8,128)S(1)} %copy.533), channel_id=1, replica_groups=mesh['seq'=8,'pair'=2,'head'=2] {'pair'}, dimensions={0} | all-to-all | bytes 1966080 | tf_op jit(solution)/shard_map/all_to_all | solution.py:49
  216.5 3.5 %all-to-all-start.7 = ((f32[8,120,128]{2,1,0:T(8,128)}), f32[8,120,128]{2,1,0:T(8,128)S(1)}, u32[]{:S(2)}, u32[]{:S(2)}) async-start(f32[8,120,128]{2,1,0:T(8,128)} %reshape.406), calls=%async_computation.8 | async-start | bytes 983040 | tf_op jit(solution)/shard_map/all_to_all | solution.py:49
  220.0 14.3 %all-to-all-done.7 = f32[8,120,128]{2,1,0:T(8,128)S(1)} async-done(((f32[8,120,128]{2,1,0:T(8,128)}), f32[8,120,128]{2,1,0:T(8,128)S(1)}, u32[]{:S(2)}, u32[]{:S(2)}) %all-to-all-start.7) | async-done | bytes 491552 | tf_op jit(solution)/shard_map/all_to_all | solution.py:49
  234.6 4.9 %psum.14 = f32[12]{0:T(128)S(1)} all-reduce(f32[12]{0:T(128)S(1)} %reduce_sum.194), channel_id=1, replica_groups=mesh['seq'=8,'pair'=2,'head'=2] {'head'}, use_global_device_ids=true, to_apply=%region_18.22 | all-reduce | flops 12 | bytes 96 | tf_op jit(solution)/shard_map/psum | solution.py:251
  240.6 11.5 %all_to_all.85 = bf16[8,120,128]{2,1,0:T(8,128)(2,1)S(1)} all-to-all(bf16[8,120,128]{2,1,0:T(8,128)(2,1)S(1)} %broadcast_in_dim.229), channel_id=1, replica_groups=mesh['seq'=8,'pair'=2,'head'=2] {'seq'}, dimensions={0} | all-to-all | bytes 491520 | tf_op jit(solution)/shard_map/all_to_all | solution.py:62
  252.2 4.1 %all_to_all.86 = bf16[2,960,128]{2,1,0:T(8,128)(2,1)S(1)} all-to-all(bf16[2,960,128]{2,1,0:T(8,128)(2,1)S(1)} %broadcast_in_dim.231), channel_id=1, replica_groups=mesh['seq'=8,'pair'=2,'head'=2] {'pair'}, dimensions={0} | all-to-all | bytes 983040 | tf_op jit(solution)/shard_map/all_to_all | solution.py:62
  256.8 1.2 copy.535
  258.0 1.4 reshape.416
  259.4 2.9 fusion.43
  262.3 1.4 fusion.44
  264.7 1.5 mul.304
  266.5 1.1 select_maximum_fusion.1
  267.6 17.0 %all_to_all.87 = f32[2,96,1408]{2,1,0:T(8,128)S(1)} all-to-all(f32[2,96,1408]{2,1,0:T(8,128)S(1)} %bitcast.171), channel_id=1, replica_groups=mesh['seq'=8,'pair'=2,'head'=2] {'head'}, dimensions={0} | all-to-all | bytes 2162688 | tf_op jit(solution)/shard_map/all_to_all | solution.py:49
  285.0 7.5 %all_to_all.88 = bf16[2,96,640]{2,1,0:T(8,128)(2,1)S(1)} all-to-all(bf16[2,96,640]{2,1,0:T(8,128)(2,1)S(1)} %broadcast_in_dim.233), channel_id=1, replica_groups=mesh['seq'=8,'pair'=2,'head'=2] {'head'}, dimensions={0} | all-to-all | bytes 491520 | tf_op jit(solution)/shard_map/all_to_all | solution.py:62
  293.8 4.5 %all_to_all.89 = f32[2,8,12,1280]{3,1,2,0:T(8,128)S(1)} all-to-all(f32[2,8,12,1280]{3,1,2,0:T(8,128)S(1)} %copy.538), channel_id=1, replica_groups=mesh['seq'=8,'pair'=2,'head'=2] {'pair'}, dimensions={0} | all-to-all | bytes 1966080 | tf_op jit(solution)/shard_map/all_to_all | solution.py:49
  298.6 17.0 %all_to_all.90 = f32[8,120,128]{2,1,0:T(8,128)S(1)} all-to-all(f32[8,120,128]{2,1,0:T(8,128)S(1)} %reshape.409), channel_id=1, replica_groups=mesh['seq'=8,'pair'=2,'head'=2] {'seq'}, dimensions={0} | all-to-all | bytes 983040 | tf_op jit(solution)/shard_map/all_to_all | solution.py:49
  316.0 4.9 %psum.15 = f32[12]{0:T(128)S(1)} all-reduce(f32[12]{0:T(128)S(1)} %reduce_sum.202), channel_id=1, replica_groups=mesh['seq'=8,'pair'=2,'head'=2] {'head'}, use_global_device_ids=true, to_apply=%region_25.29 | all-reduce | flops 12 | bytes 96 | tf_op jit(solution)/shard_map/psum | solution.py:274
  321.1 11.5 %all_to_all.91 = bf16[8,120,128]{2,1,0:T(8,128)(2,1)S(1)} all-to-all(bf16[8,120,128]{2,1,0:T(8,128)(2,1)S(1)} %broadcast_in_dim.235), channel_id=1, replica_groups=mesh['seq'=8,'pair'=2,'head'=2] {'seq'}, dimensions={0} | all-to-all | bytes 491520 | tf_op jit(solution)/shard_map/all_to_all | solution.py:62
  332.7 4.1 %all_to_all.92 = bf16[2,960,128]{2,1,0:T(8,128)(2,1)S(1)} all-to-all(bf16[2,960,128]{2,1,0:T(8,128)(2,1)S(1)} %broadcast_in_dim.237), channel_id=1, replica_groups=mesh['seq'=8,'pair'=2,'head'=2] {'pair'}, dimensions={0} | all-to-all | bytes 983040 | tf_op jit(solution)/shard_map/all_to_all | solution.py:62
  (235 shorter events, 35.4 us)
Async XLA Ops:
  6.5 286.0 %copy-start = (bf16[640,1280]{1,0:T(8,128)(2,1)S(1)}, bf16[640,1280]{1,0:T(8,128)(2,1)}, u32[]{:S(2)}) copy-start(bf16[640,1280]{1,0:T(8,128)(2,1)} %param.44) | copy-start | bytes 4915204
  6.5 2.8 copy-start.10
  6.5 2.8 copy-start.9
  6.5 2.8 copy-start.19
  6.5 3.1 copy-start.28
  6.5 45.1 %all-gather.5.cloned.1.call-start = ((), (), s32[]{:S(2)}) async-start(), calls=%async_computation.19 | async-start | bytes 2359296 | tf_op jit(solution)/shard_map/all_gather | solution.py:181
  7.3 107.9 %all-gather.3.cloned.1.call-start = ((), (), s32[]{:S(2)}) async-start(), calls=%async_computation.17 | async-start | bytes 5570560 | tf_op jit(solution)/shard_map/all_gather | solution.py:143
  9.2 5.7 %copy-start.14 = (s32[2,12,8]{1,2,0:T(8,128)S(1)}, s32[2,12,8]{1,2,0:T(8,128)}, u32[]{:S(2)}) copy-start(s32[2,12,8]{1,2,0:T(8,128)} %param.27) | copy-start | bytes 2308
  10.7 10.5 %all-to-all-start = ((f32[2,96,384]{2,1,0:T(8,128)}), f32[2,96,384]{2,1,0:T(8,128)S(1)}, u32[]{:S(2)}, u32[]{:S(2)}) async-start(f32[2,96,384]{2,1,0:T(8,128)} %bitcast.2), calls=%async_computation | async-start | bytes 589824 | tf_op jit(solution)/shard_map/all_to_all | solution.py:49
  18.2 1.3 copy-start.25
  22.7 9.1 %copy-start.12 = (bf16[4,8,1280]{2,1,0:T(8,128)(2,1)S(1)}, bf16[4,8,1280]{2,1,0:T(8,128)(2,1)}, u32[]{:S(2)}) copy-start(bf16[4,8,1280]{2,1,0:T(8,128)(2,1)} %param.32) | copy-start | bytes 245764
  22.7 9.9 %copy-start.22 = (s32[12]{0:T(128)S(1)}, s32[12]{0:T(128)}, u32[]{:S(2)}) copy-start(s32[12]{0:T(128)} %param.29) | copy-start | bytes 148
  22.7 10.9 %copy-start.30 = (u32[32]{0:T(128)S(1)}, u32[32]{0:T(128)}, u32[]{:S(2)}) copy-start(u32[32]{0:T(128)} %constant.271) | copy-start | bytes 388
  22.8 20.8 %copy-start.29 = (s32[4]{0:T(128)S(1)}, s32[4]{0:T(128)}, u32[]{:S(2)}) copy-start(s32[4]{0:T(128)} %param.33) | copy-start | bytes 52
  22.8 20.8 %copy-start.27 = (s32[8]{0:T(128)S(1)}, s32[8]{0:T(128)}, u32[]{:S(2)}) copy-start(s32[8]{0:T(128)} %param.31) | copy-start | bytes 100
  22.8 43.0 %all-to-all-start.1 = ((bf16[32,96,256]{2,1,0:T(8,128)(2,1)}), bf16[32,96,256]{2,1,0:T(8,128)(2,1)S(1)}, u32[]{:S(2)}, u32[]{:S(2)}) async-start(bf16[32,96,256]{2,1,0:T(8,128)(2,1)} %broadcast_in_dim.119), calls=%async_computation.1 | async-start | bytes 3145728 | tf_op jit(solution)/shard_map/all_to_all | solution.py:62
  28.3 101.7 %reduce-scatter.2.cloned.1.call-start = ((), (), s32[]{:S(2)}) async-start(), calls=%async_computation.18 | async-start | bytes 393216 | tf_op jit(solution)/shard_map/reduce_scatter | solution.py:147
  32.2 0.5 copy-start.23
  65.8 1.2 copy-start.1
  74.6 1.0 copy-start.7
  81.9 3.9 %copy-start.2 = (bf16[48,4,2048]{2,1,0:T(4,128)(2,1)S(1)}, bf16[48,4,2048]{2,1,0:T(4,128)(2,1)}, u32[]{:S(2)}) copy-start(bf16[48,4,2048]{2,1,0:T(4,128)(2,1)} %gather_fusion.7) | copy-start | bytes 2359300
  82.6 3.2 copy-start.15
  82.6 3.2 copy-start.16
  82.6 3.2 copy-start.17
  82.6 3.2 copy-start.18
  83.3 2.5 copy-start.3
  121.8 4.6 %copy-start.24 = (f32[256]{0:T(256)S(1)}, f32[256]{0:T(256)}, u32[]{:S(2)}) copy-start(f32[256]{0:T(256)} %param.37) | copy-start | bytes 3076
  126.3 3.7 %copy-start.26 = (f32[16]{0:T(128)S(1)}, f32[16]{0:T(128)}, u32[]{:S(2)}) copy-start(f32[16]{0:T(128)} %fusion.62) | copy-start | bytes 196
  134.6 1.9 copy-start.8
  137.6 15.3 %copy-start.4 = (f32[12,4,32,96]{3,2,1,0:T(8,128)}, f32[12,4,32,96]{3,2,1,0:T(8,128)S(1)}, u32[]{:S(2)}) copy-start(f32[12,4,32,96]{3,2,1,0:T(8,128)S(1)} %get-tuple-element.32) | copy-start | bytes 1769476
  176.6 33.4 %copy-start.11 = (bf16[128,1280]{1,0:T(8,128)(2,1)S(1)}, bf16[128,1280]{1,0:T(8,128)(2,1)}, u32[]{:S(2)}) copy-start(bf16[128,1280]{1,0:T(8,128)(2,1)} %param.39) | copy-start | bytes 983044
  215.6 24.0 %copy-start.20 = (f32[1280]{0:T(1024)S(1)}, f32[1280]{0:T(1024)}, u32[]{:S(2)}) copy-start(f32[1280]{0:T(1024)} %param.40) | copy-start | bytes 15364
  216.5 17.8 %all-to-all-start.7 = ((f32[8,120,128]{2,1,0:T(8,128)}), f32[8,120,128]{2,1,0:T(8,128)S(1)}, u32[]{:S(2)}, u32[]{:S(2)}) async-start(f32[8,120,128]{2,1,0:T(8,128)} %reshape.406), calls=%async_computation.8 | async-start | bytes 983040 | tf_op jit(solution)/shard_map/all_to_all | solution.py:49
  258.0 1.4 copy-start.13
  259.4 2.9 copy-start.6
  264.7 1.7 copy-start.5
  298.6 22.4 %copy-start.21 = (f32[1280]{0:T(1024)S(1)}, f32[1280]{0:T(1024)}, u32[]{:S(2)}) copy-start(f32[1280]{0:T(1024)} %param.45) | copy-start | bytes 15364
Sparse Core Ops, SparseCore 0:
  8.9 42.6 all-gather.4
  53.8 61.3 all-gather.2
  119.5 9.8 reduce-scatter.1
